TPU v7x, 32 devices: a whole 2x2x4 slice. The times are simulated.
32 devices in a mesh: cand: 2 (over core), test: 8 (over z, x), feat: 2 (over y).
Axes of the slice: x: 2, y: 2, z: 4, core: 2. Of those that a mesh axis runs over, the one named last changes fastest.
Arguments:
- x_test: float32 [32768, 256], P(('test', 'cand'), 'feat'), may hold values from -6 to 6
- x_cand: float32 [8192, 256], P(('cand', 'test'), 'feat'), may hold values from -6 to 6
- w_self: float32 [256, 256], replicated, may hold values from -0.375 to 0.375
- w_neigh: float32 [256, 256], replicated, may hold values from -1.5 to 1.5
- d_out: float32 [8192, 256], P(('cand', 'test'), 'feat'), may hold values from -6 to 6
- block_row: int32 [2, 8, 512], P('cand', 'test'), may hold values from 0 to 31, as said below
- block_col: int32 [2, 8, 512], P('cand', 'test'), may hold values from 0 to 31, as said below
- block_mask: int32 [2, 8, 512, 16, 128], P('cand', 'test'), may hold values from 0 to 255, as said below
- block_live: int32 [2, 8], P('cand', 'test'), may hold values from 170 to 512, as said below
Outputs:
- output: float32 [8192, 256], P(('cand', 'test'), 'feat')
- grad_w_self: float32 [256, 256], P('feat')
- grad_w_neigh: float32 [256, 256], P('feat')
- grad_x_cand: float32 [8192, 256], P(('cand', 'test'), 'feat')
- grad_x_test: float32 [32768, 256], P(('test', 'cand'), 'feat')
Inputs may be any that keep to these rules, and one draw needn't show every extreme that they name: `block_row`: within one device's list the 512 slots name distinct (row block, column block) positions. `block_col`: within one device's list the 512 slots name distinct (row block, column block) positions. `block_mask`: each word holds 8 bits. `block_live`: some device has all 512 slots live in every draw.
All inputs are finite; a program needn't handle non-finite values.
Results may differ from a plain program's by a relative error of at most 0.0003.
Values sent between devices are 32-bit elements; how exact they have to be, the bound alone decides.
No kernel may reach another device: no remote copies, remote signals or barrier semaphores. Data moves between devices by JAX's collectives and lax.ppermute only.
A program may use at most 64 MiB of HBM per device.

v0:
```python
import math

import jax
import jax.numpy as jnp
from jax import lax
from jax.sharding import PartitionSpec as P

HIGHEST = lax.Precision.HIGHEST


def unpack_masks(packed):
    shifts = jnp.arange(8, dtype=jnp.int32)
    bit_cube = jnp.bitwise_and(jnp.right_shift(packed[..., :, None, :], shifts[:, None]), 1)
    return bit_cube.reshape(packed.shape[:-2] + (packed.shape[-2] * 8, packed.shape[-1])).astype(
        jnp.float32
    )


def slot_loop(live_count, offset, stride, slot_total, step_fn, initial):
    group_size = 16
    usable = (live_count - offset + stride - 1) // stride
    group_count = (usable + group_size - 1) // group_size

    def one_group(group_index, running):
        raw_slots = offset + stride * (
            group_index * group_size + jnp.arange(group_size, dtype=jnp.int32)
        )
        weights = (raw_slots < live_count).astype(jnp.float32)
        safe_slots = jnp.minimum(raw_slots, slot_total - 1)
        return step_fn(running, safe_slots, weights)

    return lax.fori_loop(0, group_count, one_group, initial)


def aggregate(
    packed_masks,
    block_rows,
    block_cols,
    live_count,
    offset,
    stride,
    fetch_tiles,
    row_blocks,
    feature_count,
):
    block_edge = packed_masks.shape[-1]

    def step_fn(running, safe_slots, weights):
        row_totals, row_counts = running
        dense_masks = unpack_masks(packed_masks[safe_slots])
        feature_tiles = fetch_tiles(block_cols[safe_slots])
        products = jnp.einsum("gij,gjh->gih", dense_masks, feature_tiles, precision=HIGHEST)
        selector = (
            block_rows[safe_slots][:, None] == jnp.arange(row_blocks, dtype=jnp.int32)[None, :]
        ).astype(jnp.float32) * weights[:, None]
        row_totals = row_totals + jnp.einsum("gk,gih->kih", selector, products, precision=HIGHEST)
        row_counts = row_counts + jnp.einsum(
            "gk,gi->ki", selector, jnp.sum(dense_masks, axis=2), precision=HIGHEST
        )
        return (row_totals, row_counts)

    initial = (
        jnp.zeros((row_blocks, block_edge, feature_count), jnp.float32),
        jnp.zeros((row_blocks, block_edge), jnp.float32),
    )
    return slot_loop(live_count, offset, stride, packed_masks.shape[0], step_fn, initial)


def transpose_product(packed_masks, block_rows, block_cols, live_count, gradient_tiles, col_blocks):
    block_edge = packed_masks.shape[-1]

    def step_fn(running, safe_slots, weights):
        dense_masks = unpack_masks(packed_masks[safe_slots])
        picked = gradient_tiles[block_rows[safe_slots]]
        products = jnp.einsum("gji,gjh->gih", dense_masks, picked, precision=HIGHEST)
        selector = (
            block_cols[safe_slots][:, None] == jnp.arange(col_blocks, dtype=jnp.int32)[None, :]
        ).astype(jnp.float32) * weights[:, None]
        return running + jnp.einsum("gk,gih->kih", selector, products, precision=HIGHEST)

    initial = jnp.zeros((col_blocks, block_edge, gradient_tiles.shape[-1]), jnp.float32)
    return slot_loop(live_count, 0, 1, packed_masks.shape[0], step_fn, initial)


def local(x_test, x_cand, w_self, w_neigh, d_out, block_row, block_col, block_mask, block_live):
    packed_masks = block_mask.reshape(block_mask.shape[2:])
    block_rows = block_row.reshape(-1)
    block_cols = block_col.reshape(-1)
    live_count = block_live.reshape(())
    block_edge = packed_masks.shape[-1]
    cand_count = lax.axis_size("cand")
    test_count = lax.axis_size("test")
    feat_index = lax.axis_index("feat")
    half_width = x_cand.shape[1]
    row_blocks = x_cand.shape[0] * test_count // block_edge
    col_blocks = x_test.shape[0] * cand_count // block_edge
    panel = lax.all_gather(x_test, "cand", axis=0, tiled=True)
    feature_tiles = panel.reshape(col_blocks, block_edge, half_width)

    def fetch_tiles(chosen):
        return feature_tiles[chosen]

    row_totals, row_counts = aggregate(
        packed_masks, block_rows, block_cols, live_count, 0, 1, fetch_tiles, row_blocks, half_width
    )
    own_totals, degree = (
        lax.psum_scatter(
            row_totals.reshape(-1, half_width), "test", scatter_dimension=0, tiled=True
        ),
        lax.psum_scatter(row_counts.reshape(-1), "test", scatter_dimension=0, tiled=True),
    )
    aggregated = own_totals / (1.0 + degree)[:, None]
    self_cols = lax.dynamic_slice_in_dim(w_self, feat_index * half_width, half_width, 1)
    neigh_cols = lax.dynamic_slice_in_dim(w_neigh, feat_index * half_width, half_width, 1)
    self_rows = lax.dynamic_slice_in_dim(w_self, feat_index * half_width, half_width, 0)
    neigh_rows = lax.dynamic_slice_in_dim(w_neigh, feat_index * half_width, half_width, 0)
    cand_full, aggregated_full = (
        lax.all_gather(x_cand, "feat", axis=1, tiled=True),
        lax.all_gather(aggregated, "feat", axis=1, tiled=True),
    )
    pre_act = jnp.dot(cand_full, self_cols, precision=HIGHEST) + jnp.dot(
        aggregated_full, neigh_cols, precision=HIGHEST
    )
    output = jax.nn.silu(pre_act)
    sigmoid_z = jax.nn.sigmoid(pre_act)
    grad_pre = d_out * (sigmoid_z * (1.0 + pre_act * (1.0 - sigmoid_z)))
    grad_full = lax.all_gather(grad_pre, "feat", axis=1, tiled=True)
    self_part = jnp.einsum("rk,rh->kh", x_cand, grad_full, precision=HIGHEST)
    neigh_part = jnp.einsum("rk,rh->kh", aggregated, grad_full, precision=HIGHEST)
    self_sum, neigh_sum = lax.psum((self_part, neigh_part), ("cand", "test"))
    root_count = math.sqrt(x_cand.shape[0] * cand_count * test_count)
    grad_w_self = self_sum / root_count
    grad_w_neigh = neigh_sum / root_count
    grad_x_cand = jnp.dot(grad_full, self_rows.T, precision=HIGHEST)
    grad_agg = jnp.dot(grad_full, neigh_rows.T, precision=HIGHEST)
    lifted = grad_agg / (1.0 + degree)[:, None]
    gathered_rows = lax.all_gather(lifted, "test", axis=0, tiled=True)
    gradient_tiles = gathered_rows.reshape(row_blocks, block_edge, half_width)
    column_terms = transpose_product(
        packed_masks, block_rows, block_cols, live_count, gradient_tiles, col_blocks
    )
    grad_x_test = lax.psum_scatter(
        column_terms.reshape(-1, half_width), "cand", scatter_dimension=0, tiled=True
    )
    return (output, grad_w_self, grad_w_neigh, grad_x_cand, grad_x_test)


def solution(mesh):
    return jax.shard_map(
        local,
        mesh=mesh,
        in_specs=(
            P(("test", "cand"), "feat"),
            P(("cand", "test"), "feat"),
            P(),
            P(),
            P(("cand", "test"), "feat"),
            P("cand", "test", None),
            P("cand", "test", None),
            P("cand", "test", None, None, None),
            P("cand", "test"),
        ),
        out_specs=(
            P(("cand", "test"), "feat"),
            P("feat", None),
            P("feat", None),
            P(("cand", "test"), "feat"),
            P(("test", "cand"), "feat"),
        ),
        check_vma=False,
    )
```

profile of v0, /device:TPU:31, one launch (start us, length us, event | category | flops | bytes accessed | tf_op | source)
XLA Modules:
  0.0 1030.6 jit_solution(8891889499213554505)
XLA Ops:
  8.6 13.1 %all-gather.3.cloned.1.call-done = f32[4096,128]{1,0:T(8,128)} async-done(((f32[2048,128]{1,0:T(8,128)}), f32[4096,128]{1,0:T(8,128)}) %all-gather.3.cloned.1.call-update) | async-done | bytes 2097168 | tf_op jit(solution)/shard_map/all_gather | solution.py:97
  22.7 433.2 %while.22 = (s32[]{:T(128)}, f32[32,128,128]{2,0,1:T(8,128)S(1)}, f32[32,128]{1,0:T(8,128)}, s32[]{:T(128)}, s32[512]{0:T(512)S(1)}, /*index=5*/s32[]{:T(128)}, ...) while((s32[]{:T(128)}, f32[32,128,128]{2,0,1:T(8,128)S(1)}, ...), condition=%wide.region_2.3_spmd, body=%wide.region_0.2_spmd.sunk | while | flops 506468544 | bytes 10039669 | solution.py:32
  60.4 2.9 convolution_add_fusion.7
  87.5 2.9 convolution_add_fusion.7
  195.8 2.9 convolution_add_fusion.7
  222.8 2.9 convolution_add_fusion.7
  460.8 8.4 all_gather.15
  469.9 26.1 %all-reduce = f32[4096]{0:T(1024)S(1)} all-reduce(f32[4096]{0:T(1024)} %bitcast.18), channel_id=3, replica_groups=mesh['cand'=2,'test'=8,'feat'=2] {'test'}, use_global_device_ids=true, to_apply=%region_4.5.clone | all-reduce | flops 4096 | bytes 32768
  496.1 28.0 %reduce-scatter.3.cloned.1.call-done = f32[512,128]{1,0:T(8,128)} async-done(((f32[4096,128]{1,0:T(8,128)}), f32[512,128]{1,0:T(8,128)}) %reduce-scatter.3.cloned.1.call-update) | async-done | bytes 262160 | tf_op jit(solution)/shard_map/reduce_scatter | solution.py:107
  525.2 6.5 all_gather.17
  533.1 5.9 all_gather.18
  543.4 48.1 %all-gather.5.cloned.1.call-done = f32[4096,128]{1,0:T(8,128)} async-done(((f32[512,128]{1,0:T(8,128)}), f32[4096,128]{1,0:T(8,128)}) %all-gather.5.cloned.1.call-update) | async-done | bytes 2097168 | tf_op jit(solution)/shard_map/all_gather | solution.py:137
  591.7 417.7 %while.23 = (s32[]{:T(128)}, f32[32,128,128]{2,0,1:T(8,128)S(1)}, s32[]{:T(128)}, s32[512]{0:T(512)S(1)}, s32[]{:T(128)}, /*index=5*/s32[512,16,128]{2,1,0:T(8,1...) while((s32[]{:T(128)}, f32[32,128,128]{2,0,1:T(8,128)S(1)}, s32[]{:T(128)}, ...), condition=%wide.region_8.9_spmd, body=%wide.region_7.8_spmd.sunk | while | flops 504630464 | bytes 9842357 | solution.py:32
  680.4 2.9 convolution_add_fusion.9
  693.4 2.9 convolution_add_fusion.9
  732.5 2.9 convolution_add_fusion.9
  771.7 2.9 convolution_add_fusion.9
  810.8 2.9 convolution_add_fusion.9
  849.9 2.9 convolution_add_fusion.9
  889.1 2.9 convolution_add_fusion.9
  928.2 2.9 convolution_add_fusion.9
  967.3 2.9 convolution_add_fusion.9
  1006.5 2.9 convolution_add_fusion.9
  1017.9 6.1 reduce-scatter.5.cloned.1.call-done
  (1350 shorter events, 825.5 us)
Async XLA Ops:
  7.2 524.5 %copy-start = (f32[256,256]{1,0:T(8,128)S(1)}, f32[256,256]{1,0:T(8,128)}, u32[]{:S(2)}) copy-start(f32[256,256]{1,0:T(8,128)} %param.16) | copy-start | bytes 786436
  7.2 15.5 %copy-start.2 = (s32[1,1,512]{2,1,0:T(1,128)S(1)}, s32[1,1,512]{2,1,0:T(1,128)}, u32[]{:S(2)}) copy-start(s32[1,1,512]{2,1,0:T(1,128)} %param.19) | copy-start | bytes 6148
  7.2 15.5 %copy-start.1 = (s32[1,1,512]{2,1,0:T(1,128)S(1)}, s32[1,1,512]{2,1,0:T(1,128)}, u32[]{:S(2)}) copy-start(s32[1,1,512]{2,1,0:T(1,128)} %param.18) | copy-start | bytes 6148
  7.2 14.6 %all-gather.3.cloned.1.call-start = ((), (), s32[]{:S(2)}) async-start(), calls=%async_computation.2 | async-start | bytes 3145728 | tf_op jit(solution)/shard_map/all_gather | solution.py:97
  7.9 516.1 %reduce-scatter.3.cloned.1.call-start = ((), (), s32[]{:S(2)}) async-start(), calls=%async_computation.3 | async-start | bytes 2359296 | tf_op jit(solution)/shard_map/reduce_scatter | solution.py:107
  23.4 4.7 copy-start.13
  36.9 4.7 copy-start.13
  50.4 4.7 copy-start.13
  64.0 4.7 copy-start.13
  77.5 4.7 copy-start.13
  91.0 4.7 copy-start.13
  104.6 4.7 copy-start.13
  118.1 4.7 copy-start.13
  131.6 4.7 copy-start.13
  145.2 4.7 copy-start.13
  158.7 4.7 copy-start.13
  172.3 4.7 copy-start.13
  185.8 4.7 copy-start.13
  348.2 4.7 copy-start.13
  458.4 10.8 %copy-start.7 = (f32[256,256]{1,0:T(8,128)S(1)}, f32[256,256]{1,0:T(8,128)}, u32[]{:S(2)}) copy-start(f32[256,256]{1,0:T(8,128)} %param.15) | copy-start | bytes 786436
  458.4 133.0 %all-gather.5.cloned.1.call-start = ((), (), s32[]{:S(2)}) async-start(), calls=%async_computation.4 | async-start | bytes 2359296 | tf_op jit(solution)/shard_map/all_gather | solution.py:137
  539.0 52.4 %copy-start.3 = (f32[512,256]{0,1:T(8,128)}, f32[512,256]{0,1:T(8,128)S(1)}, u32[]{:S(2)}) copy-start(f32[512,256]{0,1:T(8,128)S(1)} %all_gather.18) | copy-start | bytes 1572868
  540.8 474.7 %all-reduce.4.cloned.1.call-start = ((), (), s32[]{:S(2)}) async-start(), calls=%async_computation.6 | async-start | bytes 524288 | tf_op jit(solution)/shard_map/psum | solution.py:130
  543.3 480.7 %reduce-scatter.5.cloned.1.call-start = ((), (), s32[]{:S(2)}) async-start(), calls=%async_computation.5 | async-start | bytes 3145728 | tf_op jit(solution)/shard_map/reduce_scatter | solution.py:142
  (184 other events, 436.4 us)
Sparse Core Ops, SparseCore 0:
  9.6 12.1 all-gather.2
  458.6 65.4 reduce-scatter.2
  540.9 50.5 all-gather.4
  595.3 90.1 all-reduce.3
  1012.1 11.9 reduce-scatter.4
where the time goes:
time: 1040 us; the launch traced here: 1030 us
  local copies, waits for them, and re-layouts  441 us (42%)
  matrix products  351 us (34%)
  waiting for transfers between devices  96 us (9%)
  other arithmetic  73.2 us (7%)
  blocking collectives  46.9 us (5%)
  between operations  15.2 us (1%)
    dot_general x64, matrix products, step_fn(): jnp.einsum('gk,gih->kih', selector, products, precision=HIGHEST)  185 us
    gather x64, local copies, waits for them, and re-layouts, step_fn(): dense_masks = unpack_masks(packed_masks[safe_slots])  176 us
    gather x64, local copies, waits for them, and re-layouts, step_fn(): picked = gradient_tiles[block_rows[safe_slots]]  91.8 us
    gather x32, local copies, waits for them, and re-layouts, fetch_tiles(): return feature_tiles[chosen]  70.5 us
    dot_general x32, matrix products, step_fn(): jnp.einsum('gji,gjh->gih', dense_masks, picked, precision=HIGHEST)  62.9 us
    convert_element_type x64, other arithmetic, one_group(): weights = (raw_slots < live_count).astype(jnp.float32)  58 us
    dot_general x32, matrix products, step_fn(): jnp.einsum('gk,gi->ki', selector, jnp.sum(dense_masks, axis=2), precision...  53 us
    all_gather x1, waiting for transfers between devices, local(): gathered_rows = lax.all_gather(lifted, 'test', axis=0, tiled=True)  48.1 us
  transfers between devices with their start and end apart: 5, of which 4 were waited for; matrix products, arithmetic and copies ran while one was open for 41% of the time, Pallas kernels for 0%

commit v1 on v0

v1 whole, which is shorter than its diff:
```python
import math

import jax
import jax.numpy as jnp
from jax import lax
from jax.experimental import pallas as pl
from jax.experimental.pallas import tpu as pltpu
from jax.sharding import PartitionSpec as P

HIGHEST = lax.Precision.HIGHEST
SLOT_GROUP = 64


def split_hi_lo(values):
    high = lax.reduce_precision(values, exponent_bits=8, mantissa_bits=7)
    low = values - high
    return jnp.concatenate([high, low], axis=1).astype(jnp.bfloat16)


def unpack_block(words):
    word_rows, edge = words.shape
    cube = jnp.broadcast_to(words[:, None, :], (word_rows, 8, edge))
    shifts = lax.broadcasted_iota(jnp.int32, (word_rows, 8, edge), 1)
    bits = jnp.bitwise_and(jnp.right_shift(cube, shifts), 1)
    return bits.reshape(word_rows * 8, edge).astype(jnp.float32)


def slot_range(live_ref, group):
    base = pl.program_id(0) * group
    count = jnp.clip(live_ref[0] - base, 0, group)
    return base, count


def forward_kernel(live_ref, rows_ref, cols_ref, masks_ref, panel_ref, totals_ref, counts_ref):
    group, _, edge = masks_ref.shape
    row_limit = counts_ref.shape[0] - 1
    col_limit = panel_ref.shape[0] // edge - 1

    @pl.when(pl.program_id(0) == 0)
    def _():
        totals_ref[...] = jnp.zeros_like(totals_ref)
        counts_ref[...] = jnp.zeros_like(counts_ref)

    base, count = slot_range(live_ref, group)
    ones = jnp.ones((8, edge), jnp.bfloat16)
    half = totals_ref.shape[1]

    def body(k, carry):
        slot = base + k
        row = jnp.clip(rows_ref[slot], 0, row_limit)
        col = jnp.clip(cols_ref[slot], 0, col_limit)
        dense = unpack_block(masks_ref[k]).astype(jnp.bfloat16)
        tile = panel_ref[pl.ds(pl.multiple_of(col * edge, edge), edge), :]
        prod = jnp.dot(dense, tile, preferred_element_type=jnp.float32)
        start = pl.multiple_of(row * edge, edge)
        totals_ref[pl.ds(start, edge), :] += prod[:, :half] + prod[:, half:]
        counts_ref[row] += lax.dot_general(
            ones, dense, (((1,), (1,)), ((), ())), preferred_element_type=jnp.float32
        )
        return carry

    lax.fori_loop(0, count, body, 0)


def backward_kernel(live_ref, rows_ref, cols_ref, masks_ref, lifted_ref, out_ref):
    group, _, edge = masks_ref.shape
    row_limit = lifted_ref.shape[0] // edge - 1
    col_limit = out_ref.shape[0] // edge - 1

    @pl.when(pl.program_id(0) == 0)
    def _():
        out_ref[...] = jnp.zeros_like(out_ref)

    base, count = slot_range(live_ref, group)
    half = out_ref.shape[1]

    def body(k, carry):
        slot = base + k
        row = jnp.clip(rows_ref[slot], 0, row_limit)
        col = jnp.clip(cols_ref[slot], 0, col_limit)
        dense_t = unpack_block(masks_ref[k]).T.astype(jnp.bfloat16)
        tile = lifted_ref[pl.ds(pl.multiple_of(row * edge, edge), edge), :]
        prod = jnp.dot(dense_t, tile, preferred_element_type=jnp.float32)
        start = pl.multiple_of(col * edge, edge)
        out_ref[pl.ds(start, edge), :] += prod[:, :half] + prod[:, half:]
        return carry

    lax.fori_loop(0, count, body, 0)


def mask_spec(packed_masks, group):
    word_rows, edge = packed_masks.shape[1:]

    def index_map(chunk, live_ref, rows_ref, cols_ref):
        last = jnp.maximum(live_ref[0] - 1, 0) // group
        return (jnp.minimum(chunk, last), 0, 0)

    return pl.BlockSpec((group, word_rows, edge), index_map)


def whole_spec(shape):
    return pl.BlockSpec(shape, lambda chunk, live_ref, rows_ref, cols_ref: (0,) * len(shape))


def block_aggregate(live, block_rows, block_cols, packed_masks, panel_split, row_blocks):
    slot_total, _, edge = packed_masks.shape
    group = min(SLOT_GROUP, slot_total)
    half = panel_split.shape[1] // 2
    totals_shape = (row_blocks * edge, half)
    counts_shape = (row_blocks, 8, edge)
    grid_spec = pltpu.PrefetchScalarGridSpec(
        num_scalar_prefetch=3,
        grid=(slot_total // group,),
        in_specs=[mask_spec(packed_masks, group), whole_spec(panel_split.shape)],
        out_specs=[whole_spec(totals_shape), whole_spec(counts_shape)],
    )
    totals, counts = pl.pallas_call(
        forward_kernel,
        grid_spec=grid_spec,
        out_shape=[
            jax.ShapeDtypeStruct(totals_shape, jnp.float32),
            jax.ShapeDtypeStruct(counts_shape, jnp.float32),
        ],
        compiler_params=pltpu.CompilerParams(dimension_semantics=("arbitrary",)),
    )(live, block_rows, block_cols, packed_masks, panel_split)
    return totals, counts[:, 0, :].reshape(-1)


def block_transpose(live, block_rows, block_cols, packed_masks, lifted_split, col_blocks):
    slot_total, _, edge = packed_masks.shape
    group = min(SLOT_GROUP, slot_total)
    half = lifted_split.shape[1] // 2
    out_shape = (col_blocks * edge, half)
    grid_spec = pltpu.PrefetchScalarGridSpec(
        num_scalar_prefetch=3,
        grid=(slot_total // group,),
        in_specs=[mask_spec(packed_masks, group), whole_spec(lifted_split.shape)],
        out_specs=whole_spec(out_shape),
    )
    return pl.pallas_call(
        backward_kernel,
        grid_spec=grid_spec,
        out_shape=jax.ShapeDtypeStruct(out_shape, jnp.float32),
        compiler_params=pltpu.CompilerParams(dimension_semantics=("arbitrary",)),
    )(live, block_rows, block_cols, packed_masks, lifted_split)


def local(x_test, x_cand, w_self, w_neigh, d_out, block_row, block_col, block_mask, block_live):
    packed_masks = block_mask.reshape(block_mask.shape[2:])
    block_rows = block_row.reshape(-1)
    block_cols = block_col.reshape(-1)
    live = jnp.clip(block_live.reshape(1), 0, packed_masks.shape[0])
    block_edge = packed_masks.shape[-1]
    cand_count = lax.axis_size("cand")
    test_count = lax.axis_size("test")
    feat_index = lax.axis_index("feat")
    half_width = x_cand.shape[1]
    row_blocks = x_cand.shape[0] * test_count // block_edge
    col_blocks = x_test.shape[0] * cand_count // block_edge
    panel = lax.all_gather(x_test, "cand", axis=0, tiled=True)
    row_totals, row_counts = block_aggregate(
        live, block_rows, block_cols, packed_masks, split_hi_lo(panel), row_blocks
    )
    own_totals, degree = (
        lax.psum_scatter(row_totals, "test", scatter_dimension=0, tiled=True),
        lax.psum_scatter(row_counts, "test", scatter_dimension=0, tiled=True),
    )
    aggregated = own_totals / (1.0 + degree)[:, None]
    self_cols = lax.dynamic_slice_in_dim(w_self, feat_index * half_width, half_width, 1)
    neigh_cols = lax.dynamic_slice_in_dim(w_neigh, feat_index * half_width, half_width, 1)
    self_rows = lax.dynamic_slice_in_dim(w_self, feat_index * half_width, half_width, 0)
    neigh_rows = lax.dynamic_slice_in_dim(w_neigh, feat_index * half_width, half_width, 0)
    cand_full, aggregated_full = (
        lax.all_gather(x_cand, "feat", axis=1, tiled=True),
        lax.all_gather(aggregated, "feat", axis=1, tiled=True),
    )
    pre_act = jnp.dot(cand_full, self_cols, precision=HIGHEST) + jnp.dot(
        aggregated_full, neigh_cols, precision=HIGHEST
    )
    output = jax.nn.silu(pre_act)
    sigmoid_z = jax.nn.sigmoid(pre_act)
    grad_pre = d_out * (sigmoid_z * (1.0 + pre_act * (1.0 - sigmoid_z)))
    grad_full = lax.all_gather(grad_pre, "feat", axis=1, tiled=True)
    self_part = jnp.einsum("rk,rh->kh", x_cand, grad_full, precision=HIGHEST)
    neigh_part = jnp.einsum("rk,rh->kh", aggregated, grad_full, precision=HIGHEST)
    self_sum, neigh_sum = lax.psum((self_part, neigh_part), ("cand", "test"))
    root_count = math.sqrt(x_cand.shape[0] * cand_count * test_count)
    grad_w_self = self_sum / root_count
    grad_w_neigh = neigh_sum / root_count
    grad_x_cand = jnp.dot(grad_full, self_rows.T, precision=HIGHEST)
    grad_agg = jnp.dot(grad_full, neigh_rows.T, precision=HIGHEST)
    lifted = grad_agg / (1.0 + degree)[:, None]
    gathered_rows = lax.all_gather(lifted, "test", axis=0, tiled=True)
    column_terms = block_transpose(
        live, block_rows, block_cols, packed_masks, split_hi_lo(gathered_rows), col_blocks
    )
    grad_x_test = lax.psum_scatter(column_terms, "cand", scatter_dimension=0, tiled=True)
    return (output, grad_w_self, grad_w_neigh, grad_x_cand, grad_x_test)


def solution(mesh):
    return jax.shard_map(
        local,
        mesh=mesh,
        in_specs=(
            P(("test", "cand"), "feat"),
            P(("cand", "test"), "feat"),
            P(),
            P(),
            P(("cand", "test"), "feat"),
            P("cand", "test", None),
            P("cand", "test", None),
            P("cand", "test", None, None, None),
            P("cand", "test"),
        ),
        out_specs=(
            P(("cand", "test"), "feat"),
            P("feat", None),
            P("feat", None),
            P(("cand", "test"), "feat"),
            P(("test", "cand"), "feat"),
        ),
        check_vma=False,
    )
```

time: 1040 us -> 397 us (0.38)
  local copies, waits for them, and re-layouts: 441 us -> 4.84 us
  matrix products: 351 us -> 7.37 us
  Pallas kernels: 0 us -> 215 us
  other arithmetic: 73.2 us -> 9.08 us
    gather x256 -> x0, local copies, waits for them, and re-layouts: 419 us -> none  [the longest x64 176 us: step_fn(): dense_masks = unpack_masks(packed_masks[safe_slots])]
    dot_general x160 -> x0, matrix products: 343 us -> none  [the longest x64 185 us: step_fn(): jnp.einsum('gk,gih->kih', selector, products, precision=HIGHEST)]
    pallas_call x0 -> x2, Pallas kernels: none -> 215 us  [the longest x1 123 us: block_transpose(): pl.pallas_call(backward_kernel, grid_spec=grid_spec, out_shape=jax.ShapeD...]
    convert_element_type x64 -> x0, other arithmetic: 58 us -> none  [one_group(): weights = (raw_slots < live_count).astype(jnp.float32)]
    reduce_sum x32 -> x0, other arithmetic: 11 us -> none  [step_fn(): jnp.sum(dense_masks, axis=2)]
  transfers between devices with their start and end apart: 5 -> 5, of which waited for: 4 -> 4; matrix products, arithmetic and copies ran while one was open for 41% -> 3% of each run, Pallas kernels for 0% -> 31%
where the time goes in v1:
time: 397 us; the launch traced here: 395 us
  Pallas kernels  215 us (54%)
  waiting for transfers between devices  96.1 us (24%)
  blocking collectives  47 us (12%)
  between operations  15.2 us (4%)
  other arithmetic  9.08 us (2%)
  matrix products  7.37 us (2%)
  local copies, waits for them, and re-layouts  4.84 us (1%)
    pallas_call x1, Pallas kernels, block_transpose(): pl.pallas_call(backward_kernel, grid_spec=grid_spec, out_shape=jax.ShapeD...  123 us
    pallas_call x1, Pallas kernels, block_aggregate(): pl.pallas_call(forward_kernel, grid_spec=grid_spec, out_shape=[jax.ShapeD...  92.6 us
    all_gather x1, waiting for transfers between devices, local(): gathered_rows = lax.all_gather(lifted, 'test', axis=0, tiled=True)  48.1 us
    reduce_scatter x1, waiting for transfers between devices, local(): lax.psum_scatter(row_totals, 'test', scatter_dimension=0, tiled=True)  27 us
    unnamed x1, blocking collectives  26.2 us
    all_gather x1, waiting for transfers between devices, local(): panel = lax.all_gather(x_test, 'cand', axis=0, tiled=True)  13.2 us
    all_gather x1, blocking collectives, local(): lax.all_gather(x_cand, 'feat', axis=1, tiled=True)  8.41 us
  transfers between devices with their start and end apart: 5, of which 4 were waited for; matrix products, arithmetic and copies ran while one was open for 3% of the time, Pallas kernels for 31%

profile of v1, /device:TPU:31, one launch (start us, length us, event | category | flops | bytes accessed | tf_op | source)
XLA Modules:
  0.0 395.0 jit_solution(1297808450914456491)
XLA Ops:
  8.6 13.2 %all-gather.3.cloned.1.call-done = f32[4096,128]{1,0:T(8,128)} async-done(((f32[2048,128]{1,0:T(8,128)}), f32[4096,128]{1,0:T(8,128)}) %all-gather.3.cloned.1.call-update) | async-done | bytes 2097168 | tf_op jit(solution)/shard_map/all_gather | solution.py:160
  21.8 1.9 reduce-precision_convert_fusion.1
  23.7 1.5 pad_maximum_fusion.panel_ref
  25.2 92.6 %shard_map.128 = (f32[4096,128]{1,0:T(8,128)}, f32[32,8,128]{2,1,0:T(8,128)}) custom-call(s32[1]{0:T(128)} %bitcast.1.live_ref, s32[512]{0:T(512)} %bitcast.21, s32[512]{0:T(512)} %bitcast.23, s32[512,16,128]{2,1,0:T(8,128)} %bitcast.18, bf16[4096,256]{1,0:T(8,128)(2,1)} %pad_maximum_fusion.panel_ref), custom_call_target="tpu_custom_call" | custom-call | tf_op jit(solution)/shard_map/pallas_call | solution.py:117
  118.0 0.8 copy-done.3
  120.2 8.4 %all_gather.15 = f32[512,256]{1,0:T(8,128)S(1)} all-gather(f32[512,128]{1,0:T(8,128)S(1)} %copy-done.1), channel_id=1, replica_groups=mesh['cand'=2,'test'=8,'feat'=2] {'feat'}, dimensions={1}, use_global_device_ids=true | all-gather | bytes 786432 | tf_op jit(solution)/shard_map/all_gather | solution.py:174
  129.4 0.9 slice.3
  130.3 26.2 %all-reduce = f32[4096]{0:T(1024)S(1)} all-reduce(f32[4096]{0:T(1024)S(1)} %bitcast.20), channel_id=3, replica_groups=mesh['cand'=2,'test'=8,'feat'=2] {'test'}, use_global_device_ids=true, to_apply=%region_1.2.clone | all-reduce | flops 4096 | bytes 32768
  156.5 27.0 %reduce-scatter.3.cloned.1.call-done = f32[512,128]{1,0:T(8,128)} async-done(((f32[4096,128]{1,0:T(8,128)}), f32[512,128]{1,0:T(8,128)}) %reduce-scatter.3.cloned.1.call-update) | async-done | bytes 262160 | tf_op jit(solution)/shard_map/reduce_scatter | solution.py:165
  183.6 1.1 broadcast_divide_fusion
  184.7 6.5 %all_gather.17 = f32[512,256]{1,0:T(8,128)S(1)} all-gather(f32[512,128]{1,0:T(8,128)S(1)} %broadcast_divide_fusion), channel_id=1, replica_groups=mesh['cand'=2,'test'=8,'feat'=2] {'feat'}, dimensions={1}, use_global_device_ids=true | all-gather | bytes 786432 | tf_op jit(solution)/shard_map/all_gather | solution.py:175
  191.1 0.8 multiply_multiply_fusion
  191.9 5.9 %all_gather.18 = f32[512,256]{0,1:T(8,128)S(1)} all-gather(f32[512,128]{0,1:T(8,128)S(1)} %get-tuple-element.25), channel_id=1, replica_groups=mesh['cand'=2,'test'=8,'feat'=2] {'feat'}, dimensions={1}, use_global_device_ids=true | all-gather | bytes 786432 | tf_op jit(solution)/shard_map/all_gather | solution.py:183
  197.8 1.7 convolution_divide_fusion
  199.6 1.2 fusion.12
  200.8 1.2 convolution_bitcast_fusion.1
  202.1 48.1 %all-gather.5.cloned.1.call-done = f32[4096,128]{1,0:T(8,128)} async-done(((f32[512,128]{1,0:T(8,128)}), f32[4096,128]{1,0:T(8,128)}) %all-gather.5.cloned.1.call-update) | async-done | bytes 2097168 | tf_op jit(solution)/shard_map/all_gather | solution.py:193
  250.3 1.9 reduce-precision_convert_fusion
  252.2 1.5 pad_maximum_fusion.1.lifted_ref
  253.7 122.6 %shard_map.129 = f32[4096,128]{1,0:T(8,128)} custom-call(s32[1]{0:T(128)} %bitcast.1.live_ref, s32[512]{0:T(512)} %bitcast.22, s32[512]{0:T(512)} %bitcast.24, s32[512,16,128]{2,1,0:T(8,128)} %bitcast.19, bf16[4096,256]{1,0:T(8,128)(2,1)} %pad_maximum_fusion.1.lifted_ref), custom_call_target="tpu_custom_call" | custom-call | tf_op jit(solution)/shard_map/pallas_call | solution.py:140
  376.4 0.8 copy.23
  377.2 1.7 fusion.4
  378.9 1.0 broadcast_multiply_fusion
  381.4 7.0 %reduce-scatter.5.cloned.1.call-done = f32[2048,128]{1,0:T(8,128)} async-done(((f32[4096,128]{1,0:T(8,128)}), f32[2048,128]{1,0:T(8,128)}) %reduce-scatter.5.cloned.1.call-update) | async-done | bytes 1048592 | tf_op jit(solution)/shard_map/reduce_scatter | solution.py:197
  (26 shorter events, 4.0 us)
Async XLA Ops:
  7.2 184.0 %copy-start = (f32[256,256]{1,0:T(8,128)S(1)}, f32[256,256]{1,0:T(8,128)}, u32[]{:S(2)}) copy-start(f32[256,256]{1,0:T(8,128)} %param.12) | copy-start | bytes 786436
  7.2 14.6 %all-gather.3.cloned.1.call-start = ((), (), s32[]{:S(2)}) async-start(), calls=%async_computation.2 | async-start | bytes 3145728 | tf_op jit(solution)/shard_map/all_gather | solution.py:160
  7.9 175.7 %reduce-scatter.3.cloned.1.call-start = ((), (), s32[]{:S(2)}) async-start(), calls=%async_computation.3 | async-start | bytes 2359296 | tf_op jit(solution)/shard_map/reduce_scatter | solution.py:165
  117.9 0.9 copy-start.3
  117.9 1.1 copy-start.4
  117.9 2.3 copy-start.1
  117.9 10.8 %copy-start.2 = (f32[256,256]{1,0:T(8,128)S(1)}, f32[256,256]{1,0:T(8,128)}, u32[]{:S(2)}) copy-start(f32[256,256]{1,0:T(8,128)} %param.11) | copy-start | bytes 786436
  117.9 132.3 %all-gather.5.cloned.1.call-start = ((), (), s32[]{:S(2)}) async-start(), calls=%async_computation.4 | async-start | bytes 2359296 | tf_op jit(solution)/shard_map/all_gather | solution.py:193
  199.5 179.3 %all-reduce.4.cloned.1.call-start = ((), (), s32[]{:S(2)}) async-start(), calls=%async_computation.6 | async-start | bytes 524288 | tf_op jit(solution)/shard_map/psum | solution.py:186
  202.1 186.3 %reduce-scatter.5.cloned.1.call-start = ((), (), s32[]{:S(2)}) async-start(), calls=%async_computation.5 | async-start | bytes 3145728 | tf_op jit(solution)/shard_map/reduce_scatter | solution.py:197
Sparse Core Ops, SparseCore 0:
  9.5 12.1 all-gather.2
  118.0 65.4 reduce-scatter.2
  199.7 50.5 all-gather.4
  254.1 91.1 all-reduce.3
  376.5 11.9 reduce-scatter.4

commit v2 on v1

--- a/solution.py
+++ b/solution.py
@@ -145,6 +145,46 @@
     )(live, block_rows, block_cols, packed_masks, lifted_split)
 
 
+def swap(values, axis):
+    return lax.ppermute(values, axis, [(0, 1), (1, 0)])
+
+
+def gather_axis(values, axis, dim):
+    if lax.axis_size(axis) != 2:
+        return lax.all_gather(values, axis, axis=dim, tiled=True)
+    other = swap(values, axis)
+    first = lax.axis_index(axis) == 0
+    return jnp.concatenate(
+        [jnp.where(first, values, other), jnp.where(first, other, values)], axis=dim
+    )
+
+
+def scatter_sum_axis(values, axis):
+    if lax.axis_size(axis) != 2:
+        return lax.psum_scatter(values, axis, scatter_dimension=0, tiled=True)
+    rows = values.shape[0] // 2
+    index = lax.axis_index(axis)
+    own = lax.dynamic_slice_in_dim(values, index * rows, rows, 0)
+    other = lax.dynamic_slice_in_dim(values, (1 - index) * rows, rows, 0)
+    return own + swap(other, axis)
+
+
+def scatter_totals_and_counts(row_totals, row_counts, test_count):
+    width = row_totals.shape[1]
+    chunk_rows = row_totals.shape[0] // test_count
+    count_rows = chunk_rows // width
+    padded = -(-count_rows // 16) * 16
+    pieces = [
+        row_totals.reshape(test_count, chunk_rows, width),
+        row_counts.reshape(test_count, count_rows, width),
+    ]
+    if padded > count_rows:
+        pieces.append(jnp.zeros((test_count, padded - count_rows, width), jnp.float32))
+    combined = jnp.concatenate(pieces, axis=1).reshape(-1, width)
+    own = lax.psum_scatter(combined, "test", scatter_dimension=0, tiled=True)
+    return own[:chunk_rows], own[chunk_rows : chunk_rows + count_rows].reshape(-1)
+
+
 def local(x_test, x_cand, w_self, w_neigh, d_out, block_row, block_col, block_mask, block_live):
     packed_masks = block_mask.reshape(block_mask.shape[2:])
     block_rows = block_row.reshape(-1)
@@ -157,30 +197,25 @@
     half_width = x_cand.shape[1]
     row_blocks = x_cand.shape[0] * test_count // block_edge
     col_blocks = x_test.shape[0] * cand_count // block_edge
-    panel = lax.all_gather(x_test, "cand", axis=0, tiled=True)
+    panel = gather_axis(x_test, "cand", 0)
+    cand_full = gather_axis(x_cand, "feat", 1)
     row_totals, row_counts = block_aggregate(
         live, block_rows, block_cols, packed_masks, split_hi_lo(panel), row_blocks
     )
-    own_totals, degree = (
-        lax.psum_scatter(row_totals, "test", scatter_dimension=0, tiled=True),
-        lax.psum_scatter(row_counts, "test", scatter_dimension=0, tiled=True),
-    )
+    own_totals, degree = scatter_totals_and_counts(row_totals, row_counts, test_count)
     aggregated = own_totals / (1.0 + degree)[:, None]
     self_cols = lax.dynamic_slice_in_dim(w_self, feat_index * half_width, half_width, 1)
     neigh_cols = lax.dynamic_slice_in_dim(w_neigh, feat_index * half_width, half_width, 1)
     self_rows = lax.dynamic_slice_in_dim(w_self, feat_index * half_width, half_width, 0)
     neigh_rows = lax.dynamic_slice_in_dim(w_neigh, feat_index * half_width, half_width, 0)
-    cand_full, aggregated_full = (
-        lax.all_gather(x_cand, "feat", axis=1, tiled=True),
-        lax.all_gather(aggregated, "feat", axis=1, tiled=True),
-    )
+    aggregated_full = gather_axis(aggregated, "feat", 1)
     pre_act = jnp.dot(cand_full, self_cols, precision=HIGHEST) + jnp.dot(
         aggregated_full, neigh_cols, precision=HIGHEST
     )
     output = jax.nn.silu(pre_act)
     sigmoid_z = jax.nn.sigmoid(pre_act)
     grad_pre = d_out * (sigmoid_z * (1.0 + pre_act * (1.0 - sigmoid_z)))
-    grad_full = lax.all_gather(grad_pre, "feat", axis=1, tiled=True)
+    grad_full = gather_axis(grad_pre, "feat", 1)
     self_part = jnp.einsum("rk,rh->kh", x_cand, grad_full, precision=HIGHEST)
     neigh_part = jnp.einsum("rk,rh->kh", aggregated, grad_full, precision=HIGHEST)
     self_sum, neigh_sum = lax.psum((self_part, neigh_part), ("cand", "test"))
@@ -194,7 +229,7 @@
     column_terms = block_transpose(
         live, block_rows, block_cols, packed_masks, split_hi_lo(gathered_rows), col_blocks
     )
-    grad_x_test = lax.psum_scatter(column_terms, "cand", scatter_dimension=0, tiled=True)
+    grad_x_test = scatter_sum_axis(column_terms, "cand")
     return (output, grad_w_self, grad_w_neigh, grad_x_cand, grad_x_test)
 
 

time: 397 us -> 482 us (1.21)
  waiting for transfers between devices: 96.1 us -> 216 us
  blocking collectives: 47 us -> 0 us
  other arithmetic: 9.08 us -> 16.1 us
    psum x1, waiting for transfers between devices: 0.01 us -> 88 us  [local(): self_sum, neigh_sum = lax.psum((self_part, neigh_part), ('cand', 'test'))]
    reduce_scatter x2 -> x1, waiting for transfers between devices: 34.1 us -> 65.3 us  [scatter_totals_and_counts(): own = lax.psum_scatter(combined, 'test', scatter_dimension=0, tiled=True)]
    unnamed x1 -> x0, blocking collectives: 26.2 us -> none
    all_gather x3 -> x0, blocking collectives: 20.8 us -> none  [the longest x1 8.41 us: local(): lax.all_gather(x_cand, 'feat', axis=1, tiled=True)]
    all_gather x1 -> x0, waiting for transfers between devices: 13.2 us -> none  [local(): panel = lax.all_gather(x_test, 'cand', axis=0, tiled=True)]
    ppermute x0 -> x5, waiting for transfers between devices: none -> 12.4 us  [swap(): return lax.ppermute(values, axis, [(0, 1), (1, 0)])]
  transfers between devices with their start and end apart: 5 -> 8, of which waited for: 4 -> 6; matrix products, arithmetic and copies ran while one was open for 3% -> 2% of each run, Pallas kernels for 31% -> 0%
where the time goes in v2:
time: 482 us; the launch traced here: 478 us
  waiting for transfers between devices  216 us (45%)
  Pallas kernels  215 us (45%)
  other arithmetic  16.1 us (3%)
  between operations  14.5 us (3%)
  matrix products  7.79 us (2%)
  local copies, waits for them, and re-layouts  5.65 us (1%)
    pallas_call x1, Pallas kernels, block_transpose(): pl.pallas_call(backward_kernel, grid_spec=grid_spec, out_shape=jax.ShapeD...  123 us
    pallas_call x1, Pallas kernels, block_aggregate(): pl.pallas_call(forward_kernel, grid_spec=grid_spec, out_shape=[jax.ShapeD...  92.6 us
    psum x1, waiting for transfers between devices, local(): self_sum, neigh_sum = lax.psum((self_part, neigh_part), ('cand', 'test'))  88 us
    reduce_scatter x1, waiting for transfers between devices, scatter_totals_and_counts(): own = lax.psum_scatter(combined, 'test', scatter_dimension=0, tiled=True)  65.3 us
    all_gather x1, waiting for transfers between devices, local(): gathered_rows = lax.all_gather(lifted, 'test', axis=0, tiled=True)  50.4 us
    ppermute x5, waiting for transfers between devices, swap(): return lax.ppermute(values, axis, [(0, 1), (1, 0)])  12.4 us
  transfers between devices with their start and end apart: 8, of which 6 were waited for; matrix products, arithmetic and copies ran while one was open for 2% of the time, Pallas kernels for 0%

profile of v2, /device:TPU:31, one launch (start us, length us, event | category | flops | bytes accessed | tf_op | source)
XLA Modules:
  0.0 478.3 jit_solution(11057432130074976530)
XLA Ops:
  8.7 1.8 collective-permute-done.1
  10.5 1.4 broadcast_select_fusion.1
  12.2 1.6 pad_maximum_fusion.1.panel_ref
  13.7 92.6 %shard_map.128 = (f32[4096,128]{1,0:T(8,128)}, f32[32,8,128]{2,1,0:T(8,128)}) custom-call(s32[1]{0:T(128)} %bitcast.live_ref, s32[512]{0:T(512)} %bitcast.18, s32[512]{0:T(512)} %bitcast.20, s32[512,16,128]{2,1,0:T(8,128)} %bitcast.13, bf16[4096,256]{1,0:T(8,128)(2,1)} %pad_maximum_fusion.1.panel_ref), custom_call_target="tpu_custom_call" | custom-call | tf_op jit(solution)/shard_map/pallas_call | solution.py:117
  107.3 3.2 maximum_maximum_fusion
  111.6 65.3 %reduce-scatter.2.cloned.1.call-done = f32[528,128]{1,0:T(8,128)} async-done(((f32[4224,128]{1,0:T(8,128)}), f32[528,128]{1,0:T(8,128)}) %reduce-scatter.2.cloned.1.call-update) | async-done | bytes 270352 | tf_op jit(solution)/shard_map/reduce_scatter | solution.py:184
  177.6 1.1 slice_divide_fusion
  179.1 5.7 %collective-permute-done.2 = f32[512,128]{1,0:T(8,128)S(1)} collective-permute-done((f32[512,128]{1,0:T(8,128)S(1)}, f32[512,128]{1,0:T(8,128)S(1)}, u32[]{:S(2)}, u32[]{:S(2)}) %collective-permute-start.2) | collective-permute-done | bytes 262176 | tf_op jit(solution)/shard_map/ppermute | solution.py:149
  184.7 1.1 broadcast_select_fusion.5
  186.5 1.3 multiply_multiply_fusion
  188.0 5.0 %collective-permute-done.3 = f32[512,128]{1,0:T(8,128)S(1)} collective-permute-done((f32[512,128]{1,0:T(8,128)S(1)}, f32[512,128]{1,0:T(8,128)S(1)}, u32[]{:S(2)}, u32[]{:S(2)}) %collective-permute-start.3) | collective-permute-done | bytes 262176 | tf_op jit(solution)/shard_map/ppermute | solution.py:149
  193.0 1.3 convolution_divide_fusion
  194.4 50.4 %all-gather.2.cloned.1.call-done = f32[4096,128]{1,0:T(8,128)} async-done(((f32[512,128]{1,0:T(8,128)}), f32[4096,128]{1,0:T(8,128)}) %all-gather.2.cloned.1.call-update) | async-done | bytes 2097168 | tf_op jit(solution)/shard_map/all_gather | solution.py:228
  244.8 1.9 reduce-precision_convert_fusion
  246.7 1.5 pad_maximum_fusion.2.lifted_ref
  248.2 122.6 %shard_map.129 = f32[4096,128]{1,0:T(8,128)} custom-call(s32[1]{0:T(128)} %bitcast.live_ref, s32[512]{0:T(512)} %bitcast.19, s32[512]{0:T(512)} %bitcast.21, s32[512,16,128]{2,1,0:T(8,128)} %bitcast.14, bf16[4096,256]{1,0:T(8,128)(2,1)} %pad_maximum_fusion.2.lifted_ref), custom_call_target="tpu_custom_call" | custom-call | tf_op jit(solution)/shard_map/pallas_call | solution.py:140
  370.8 2.3 constant_dynamic-slice_fusion
  373.1 1.2 collective-permute-start.4
  374.3 1.7 fusion.11
  376.0 1.7 convolution_bitcast_fusion
  377.7 1.3 fusion.10
  379.0 88.0 %all-reduce.3.cloned.1.call-done = (f32[128,256]{0,1:T(8,128)}, f32[128,256]{0,1:T(8,128)}) async-done(((f32[128,256]{0,1:T(8,128)}, f32[128,256]{0,1:T(8,128)}), (f32[128,256]{0,1:T(8,128)}, f32[128,256]{0,1:T(8,128)})) %all-reduce.3.cloned.1.call-update) | async-done | bytes 262160 | tf_op jit(solution)/shard_map/psum | solution.py:221
  466.9 1.0 broadcast_multiply_fusion
  469.5 2.3 dynamic-slice_add_fusion
  (32 shorter events, 6.8 us)
Async XLA Ops:
  7.2 179.3 %copy-start = (f32[256,256]{1,0:T(8,128)S(1)}, f32[256,256]{1,0:T(8,128)}, u32[]{:S(2)}) copy-start(f32[256,256]{1,0:T(8,128)} %param.11) | copy-start | bytes 786436
  7.2 169.7 %reduce-scatter.2.cloned.1.call-start = ((), (), s32[]{:S(2)}) async-start(), calls=%async_computation.1 | async-start | bytes 2433024 | tf_op jit(solution)/shard_map/reduce_scatter | solution.py:184
  7.2 3.2 collective-permute-start.1
  110.4 0.9 copy-start.2
  110.4 75.4 %copy-start.3 = (f32[256,256]{1,0:T(8,128)S(1)}, f32[256,256]{1,0:T(8,128)}, u32[]{:S(2)}) copy-start(f32[256,256]{1,0:T(8,128)} %param.12) | copy-start | bytes 786436
  110.5 76.0 %copy-start.4 = (f32[512,128]{1,0:T(8,128)S(1)}, f32[512,128]{1,0:T(8,128)}, u32[]{:S(2)}) copy-start(f32[512,128]{1,0:T(8,128)} %param.13) | copy-start | bytes 786436
  110.5 134.3 %all-gather.2.cloned.1.call-start = ((), (), s32[]{:S(2)}) async-start(), calls=%async_computation.2 | async-start | bytes 2359296 | tf_op jit(solution)/shard_map/all_gather | solution.py:228
  111.4 67.6 %collective-permute-start = (f32[512,128]{1,0:T(8,128)S(1)}, f32[512,128]{1,0:T(8,128)S(1)}, u32[]{:S(2)}, u32[]{:S(2)}) collective-permute-start(f32[512,128]{1,0:T(8,128)S(1)} %copy-done.2), channel_id=1, source_target_pairs={{0,1},{1,0},{2,3},{3,2},{4,5},{5,4},{6,7},{7,6},{8,9},{9,8},{10,11... | collective-permute-start | bytes 786440 | tf_op jit(solution)/shard_map/ppermute | solution.py:149
  178.7 6.0 %collective-permute-start.2 = (f32[512,128]{1,0:T(8,128)S(1)}, f32[512,128]{1,0:T(8,128)S(1)}, u32[]{:S(2)}, u32[]{:S(2)}) collective-permute-start(f32[512,128]{1,0:T(8,128)S(1)} %slice_divide_fusion), channel_id=1, source_target_pairs={{0,1},{1,0},{2,3},{3,2},{4,5},{5,4},{6,7},{7,6},{8,9},{9,8},{10,11... | collective-permute-start | bytes 786440 | tf_op jit(solution)/shard_map/ppermute | solution.py:149
  187.8 5.2 %collective-permute-start.3 = (f32[512,128]{1,0:T(8,128)S(1)}, f32[512,128]{1,0:T(8,128)S(1)}, u32[]{:S(2)}, u32[]{:S(2)}) collective-permute-start(f32[512,128]{1,0:T(8,128)S(1)} %get-tuple-element.28), channel_id=1, source_target_pairs={{0,1},{1,0},{2,3},{3,2},{4,5},{5,4},{6,7},{7,6},{8,9},{9,8},{10,11... | collective-permute-start | bytes 786440 | tf_op jit(solution)/shard_map/ppermute | solution.py:149
  194.4 272.6 %all-reduce.3.cloned.1.call-start = ((), (), s32[]{:S(2)}) async-start(), calls=%async_computation.3 | async-start | bytes 524288 | tf_op jit(solution)/shard_map/psum | solution.py:221
  373.1 96.3 %copy-start.1 = (f32[4096,128]{1,0:T(8,128)S(1)}, f32[4096,128]{1,0:T(8,128)}, u32[]{:S(2)}) copy-start(f32[4096,128]{1,0:T(8,128)} %shard_map.129) | copy-start | bytes 6291460
  373.1 96.3 %collective-permute-start.4 = (f32[2048,128]{1,0:T(8,128)}, f32[2048,128]{1,0:T(8,128)}, u32[]{:S(2)}, u32[]{:S(2)}) collective-permute-start(f32[2048,128]{1,0:T(8,128)} %constant_dynamic-slice_fusion), channel_id=1, source_target_pairs={{0,16},{16,0},{1,17},{17,1},{2,18},{18,2},{3,19},{19,3},{4,20},{20... | collective-permute-start | bytes 3145736 | tf_op jit(solution)/shard_map/ppermute | solution.py:149
Sparse Core Ops, SparseCore 0:
  110.6 66.2 reduce-scatter.1
  194.5 50.2 all-gather.1
  377.8 89.0 all-reduce.2

commit v3 on v2

--- a/solution.py
+++ b/solution.py
@@ -145,35 +145,69 @@
     )(live, block_rows, block_cols, packed_masks, lifted_split)
 
 
-def swap(values, axis):
-    return lax.ppermute(values, axis, [(0, 1), (1, 0)])
+def axis_bits(axis):
+    count = lax.axis_size(axis)
+    bits = count.bit_length() - 1
+    assert count == 1 << bits
+    return bits
+
+
+def exchange(values, axis, bit):
+    count = lax.axis_size(axis)
+    return lax.ppermute(values, axis, [(i, i ^ (1 << bit)) for i in range(count)])
+
+
+def axis_bit(axis, bit):
+    return (lax.axis_index(axis) >> bit) & 1
 
 
 def gather_axis(values, axis, dim):
     if lax.axis_size(axis) != 2:
         return lax.all_gather(values, axis, axis=dim, tiled=True)
-    other = swap(values, axis)
+    other = exchange(values, axis, 0)
     first = lax.axis_index(axis) == 0
     return jnp.concatenate(
         [jnp.where(first, values, other), jnp.where(first, other, values)], axis=dim
     )
 
 
-def scatter_sum_axis(values, axis):
-    if lax.axis_size(axis) != 2:
-        return lax.psum_scatter(values, axis, scatter_dimension=0, tiled=True)
-    rows = values.shape[0] // 2
-    index = lax.axis_index(axis)
-    own = lax.dynamic_slice_in_dim(values, index * rows, rows, 0)
-    other = lax.dynamic_slice_in_dim(values, (1 - index) * rows, rows, 0)
-    return own + swap(other, axis)
+def halving_scatter(values, axis):
+    bits = axis_bits(axis)
+    chunk = values.shape[0] >> bits
+    data = values.reshape((2,) * bits + (chunk,) + values.shape[1:])
+    for bit in range(bits):
+        position = bits - 1 - bit
+        mine = axis_bit(axis, bit)
+        keep = lax.dynamic_index_in_dim(data, mine, position, keepdims=False)
+        send = lax.dynamic_index_in_dim(data, 1 - mine, position, keepdims=False)
+        data = keep + exchange(send, axis, bit)
+    return data
+
+
+def doubling_gather(values, axis):
+    bits = axis_bits(axis)
+    data = values
+    for stacked, bit in enumerate(reversed(range(bits))):
+        other = exchange(data, axis, bit)
+        first = axis_bit(axis, bit) == 0
+        data = jnp.where(
+            first, jnp.stack([data, other], axis=stacked), jnp.stack([other, data], axis=stacked)
+        )
+    return data.reshape((-1,) + values.shape[1:])
+
+
+def butterfly_sum(values, axes):
+    for axis in axes:
+        for bit in range(axis_bits(axis)):
+            values = values + exchange(values, axis, bit)
+    return values
 
 
 def scatter_totals_and_counts(row_totals, row_counts, test_count):
     width = row_totals.shape[1]
     chunk_rows = row_totals.shape[0] // test_count
     count_rows = chunk_rows // width
-    padded = -(-count_rows // 16) * 16
+    padded = -(-count_rows // 8) * 8
     pieces = [
         row_totals.reshape(test_count, chunk_rows, width),
         row_counts.reshape(test_count, count_rows, width),
@@ -181,7 +215,7 @@
     if padded > count_rows:
         pieces.append(jnp.zeros((test_count, padded - count_rows, width), jnp.float32))
     combined = jnp.concatenate(pieces, axis=1).reshape(-1, width)
-    own = lax.psum_scatter(combined, "test", scatter_dimension=0, tiled=True)
+    own = halving_scatter(combined, "test")
     return own[:chunk_rows], own[chunk_rows : chunk_rows + count_rows].reshape(-1)
 
 
@@ -197,7 +231,7 @@
     half_width = x_cand.shape[1]
     row_blocks = x_cand.shape[0] * test_count // block_edge
     col_blocks = x_test.shape[0] * cand_count // block_edge
-    panel = gather_axis(x_test, "cand", 0)
+    panel = doubling_gather(x_test, "cand")
     cand_full = gather_axis(x_cand, "feat", 1)
     row_totals, row_counts = block_aggregate(
         live, block_rows, block_cols, packed_masks, split_hi_lo(panel), row_blocks
@@ -218,18 +252,18 @@
     grad_full = gather_axis(grad_pre, "feat", 1)
     self_part = jnp.einsum("rk,rh->kh", x_cand, grad_full, precision=HIGHEST)
     neigh_part = jnp.einsum("rk,rh->kh", aggregated, grad_full, precision=HIGHEST)
-    self_sum, neigh_sum = lax.psum((self_part, neigh_part), ("cand", "test"))
+    self_sum, neigh_sum = butterfly_sum(jnp.stack([self_part, neigh_part]), ("cand", "test"))
     root_count = math.sqrt(x_cand.shape[0] * cand_count * test_count)
     grad_w_self = self_sum / root_count
     grad_w_neigh = neigh_sum / root_count
     grad_x_cand = jnp.dot(grad_full, self_rows.T, precision=HIGHEST)
     grad_agg = jnp.dot(grad_full, neigh_rows.T, precision=HIGHEST)
     lifted = grad_agg / (1.0 + degree)[:, None]
-    gathered_rows = lax.all_gather(lifted, "test", axis=0, tiled=True)
+    gathered_rows = doubling_gather(lifted, "test")
     column_terms = block_transpose(
         live, block_rows, block_cols, packed_masks, split_hi_lo(gathered_rows), col_blocks
     )
-    grad_x_test = scatter_sum_axis(column_terms, "cand")
+    grad_x_test = halving_scatter(column_terms, "cand")
     return (output, grad_w_self, grad_w_neigh, grad_x_cand, grad_x_test)
 
 

time: 482 us -> 379 us (0.79)
  waiting for transfers between devices: 216 us -> 121 us
  between operations: 14.5 us -> 1.61 us
  starting transfers between devices: 2.89 us -> 13 us
    ppermute x5 -> x15, waiting for transfers between devices: 12.4 us -> 121 us  [exchange(): return lax.ppermute(values, axis, [(i, i ^ 1 << bit) for i in range(count)])]
    psum x1 -> x0, waiting for transfers between devices: 88 us -> none  [local(): self_sum, neigh_sum = lax.psum((self_part, neigh_part), ('cand', 'test'))]
    reduce_scatter x1 -> x0, waiting for transfers between devices: 65.3 us -> none  [scatter_totals_and_counts(): own = lax.psum_scatter(combined, 'test', scatter_dimension=0, tiled=True)]
    all_gather x1 -> x0, waiting for transfers between devices: 50.4 us -> none  [local(): gathered_rows = lax.all_gather(lifted, 'test', axis=0, tiled=True)]
    ppermute x5 -> x15, starting transfers between devices: 2.77 us -> 13 us  [exchange(): return lax.ppermute(values, axis, [(i, i ^ 1 << bit) for i in range(count)])]
  transfers between devices with their start and end apart: 8 -> 15, of which waited for: 6 -> 12; matrix products, arithmetic and copies ran while one was open for 2% -> 3% of each run, Pallas kernels for 0% -> 32%
where the time goes in v3:
time: 379 us; the launch traced here: 378 us
  Pallas kernels  215 us (57%)
  waiting for transfers between devices  121 us (32%)
  other arithmetic  15.3 us (4%)
  starting transfers between devices  13 us (3%)
  matrix products  6.71 us (2%)
  local copies, waits for them, and re-layouts  5.08 us (1%)
    pallas_call x1, Pallas kernels, block_transpose(): pl.pallas_call(backward_kernel, grid_spec=grid_spec, out_shape=jax.ShapeD...  123 us
    ppermute x15, waiting for transfers between devices, exchange(): return lax.ppermute(values, axis, [(i, i ^ 1 << bit) for i in range(count)])  121 us
    pallas_call x1, Pallas kernels, block_aggregate(): pl.pallas_call(forward_kernel, grid_spec=grid_spec, out_shape=[jax.ShapeD...  92.6 us
    ppermute x15, starting transfers between devices, exchange(): return lax.ppermute(values, axis, [(i, i ^ 1 << bit) for i in range(count)])  13 us
  transfers between devices with their start and end apart: 15, of which 12 were waited for; matrix products, arithmetic and copies ran while one was open for 3% of the time, Pallas kernels for 32%

profile of v3, /device:TPU:31, one launch (start us, length us, event | category | flops | bytes accessed | tf_op | source)
XLA Modules:
  0.0 378.4 jit_solution(8329645522815367751)
XLA Ops:
  2.1 1.8 collective-permute-done.1
  3.9 1.7 maximum_select_fusion
  6.0 1.6 pad_maximum_fusion.panel_ref
  7.5 92.6 %shard_map.128 = (f32[4096,128]{1,0:T(8,128)}, f32[32,8,128]{2,1,0:T(8,128)}) custom-call(s32[1]{0:T(128)} %bitcast.live_ref, s32[512]{0:T(512)} %bitcast.71, s32[512]{0:T(512)} %bitcast.73, s32[512,16,128]{2,1,0:T(8,128)} %bitcast.54, bf16[4096,256]{1,0:T(8,128)(2,1)} %pad_maximum_fusion.panel_ref), custom_call_target="tpu_custom_call" | custom-call | tf_op jit(solution)/shard_map/pallas_call | solution.py:117
  101.1 1.8 maximum_maximum_fusion
  103.1 24.8 %collective-permute-done.2 = f32[2,2,520,128]{3,2,1,0:T(8,128)} collective-permute-done((f32[2,2,520,128]{3,2,1,0:T(8,128)S(1)}, f32[2,2,520,128]{3,2,1,0:T(8,128)}, u32[]{:S(2)}, u32[]{:S(2)}) %collective-permute-start.2) | collective-permute-done | bytes 1064992 | tf_op jit(solution)/shard_map/ppermute | solution.py:157
  127.8 1.3 bitcast_add_fusion
  129.3 12.4 %collective-permute-done.3 = f32[2,520,128]{2,1,0:T(8,128)S(1)} collective-permute-done((f32[2,520,128]{2,1,0:T(8,128)S(1)}, f32[2,520,128]{2,1,0:T(8,128)S(1)}, u32[]{:S(2)}, u32[]{:S(2)}) %collective-permute-start.3) | collective-permute-done | bytes 532512 | tf_op jit(solution)/shard_map/ppermute | solution.py:157
  142.2 14.6 %collective-permute-done.4 = f32[520,128]{1,0:T(8,128)S(1)} collective-permute-done((f32[520,128]{1,0:T(8,128)S(1)}, f32[520,128]{1,0:T(8,128)S(1)}, u32[]{:S(2)}, u32[]{:S(2)}) %collective-permute-start.4) | collective-permute-done | bytes 266272 | tf_op jit(solution)/shard_map/ppermute | solution.py:157
  157.4 7.1 %collective-permute-done.5 = f32[512,128]{1,0:T(8,128)S(1)} collective-permute-done((f32[512,128]{1,0:T(8,128)S(1)}, f32[512,128]{1,0:T(8,128)S(1)}, u32[]{:S(2)}, u32[]{:S(2)}) %collective-permute-start.5) | collective-permute-done | bytes 262176 | tf_op jit(solution)/shard_map/ppermute | solution.py:157
  166.7 6.3 %collective-permute-done.6 = f32[512,128]{1,0:T(8,128)S(1)} collective-permute-done((f32[512,128]{1,0:T(8,128)S(1)}, f32[512,128]{1,0:T(8,128)S(1)}, u32[]{:S(2)}, u32[]{:S(2)}) %collective-permute-start.6) | collective-permute-done | bytes 262176 | tf_op jit(solution)/shard_map/ppermute | solution.py:157
  173.7 8.8 %collective-permute-done.11 = f32[512,128]{1,0:T(8,128)S(1)} collective-permute-done((f32[512,128]{1,0:T(8,128)S(1)}, f32[512,128]{1,0:T(8,128)S(1)}, u32[]{:S(2)}, u32[]{:S(2)}) %collective-permute-start.11) | collective-permute-done | bytes 262176 | tf_op jit(solution)/shard_map/ppermute | solution.py:157
  182.7 11.5 %collective-permute-done.12 = f32[2,512,128]{2,1,0:T(8,128)S(1)} collective-permute-done((f32[2,512,128]{2,1,0:T(8,128)S(1)}, f32[2,512,128]{2,1,0:T(8,128)S(1)}, u32[]{:S(2)}, u32[]{:S(2)}) %collective-permute-start.12) | collective-permute-done | bytes 524320 | tf_op jit(solution)/shard_map/ppermute | solution.py:157
  195.8 1.9 convolution_bitcast_fusion.1
  199.5 3.1 collective-permute-start.7
  202.6 1.4 collective-permute-done.7
  205.7 11.7 %collective-permute-done.13 = f32[2,2,512,128]{3,2,0,1:T(8,128)S(1)} collective-permute-done((f32[2,2,512,128]{3,2,0,1:T(8,128)}, f32[2,2,512,128]{3,2,0,1:T(8,128)S(1)}, u32[]{:S(2)}, u32[]{:S(2)}) %collective-permute-start.13) | collective-permute-done | bytes 1048608 | tf_op jit(solution)/shard_map/ppermute | solution.py:157
  218.0 1.5 pad_maximum_fusion.1.lifted_ref
  219.5 122.6 %shard_map.129 = f32[4096,128]{1,0:T(8,128)} custom-call(s32[1]{0:T(128)} %bitcast.live_ref, s32[512]{0:T(512)} %bitcast.72, s32[512]{0:T(512)} %bitcast.74, s32[512,16,128]{2,1,0:T(8,128)} %bitcast.55, bf16[4096,256]{1,0:T(8,128)(2,1)} %pad_maximum_fusion.1.lifted_ref), custom_call_target="tpu_custom_call" | custom-call | tf_op jit(solution)/shard_map/pallas_call | solution.py:140
  342.1 2.3 dynamic-slice_bitcast_fusion.1
  344.4 6.5 %collective-permute-start.14 = (f32[2048,128]{1,0:T(8,128)}, f32[2048,128]{1,0:T(8,128)}, u32[]{:S(2)}, u32[]{:S(2)}) collective-permute-start(f32[2048,128]{1,0:T(8,128)} %dynamic-slice_bitcast_fusion.1), channel_id=1, source_target_pairs={{0,16},{16,0},{1,17},{17,1},{2,18},{18,2},{3,19},{19,3},{4,20},{20... | collective-permute-start | bytes 3145736 | tf_op jit(solution)/shard_map/ppermute | solution.py:157
  351.9 7.7 %collective-permute-done.9 = f32[2,128,256]{1,2,0:T(8,128)S(1)} collective-permute-done((f32[2,128,256]{1,2,0:T(8,128)S(1)}, f32[2,128,256]{1,2,0:T(8,128)S(1)}, u32[]{:S(2)}, u32[]{:S(2)}) %collective-permute-start.9) | collective-permute-done | bytes 262176 | tf_op jit(solution)/shard_map/ppermute | solution.py:157
  361.0 13.4 %collective-permute-done.10 = f32[2,128,256]{1,2,0:T(8,128)S(1)} collective-permute-done((f32[2,128,256]{1,2,0:T(8,128)S(1)}, f32[2,128,256]{1,2,0:T(8,128)S(1)}, u32[]{:S(2)}, u32[]{:S(2)}) %collective-permute-start.10) | collective-permute-done | bytes 262176 | tf_op jit(solution)/shard_map/ppermute | solution.py:157
  376.1 2.3 bitcast_add_fusion.1
  (61 shorter events, 16.2 us)
Async XLA Ops:
  0.6 164.5 %copy-start = (f32[256,256]{1,0:T(8,128)S(1)}, f32[256,256]{1,0:T(8,128)}, u32[]{:S(2)}) copy-start(f32[256,256]{1,0:T(8,128)} %param.11) | copy-start | bytes 786436
  0.6 3.2 collective-permute-start.1
  103.0 24.9 %collective-permute-start.2 = (f32[2,2,520,128]{3,2,1,0:T(8,128)S(1)}, f32[2,2,520,128]{3,2,1,0:T(8,128)}, u32[]{:S(2)}, u32[]{:S(2)}) collective-permute-start(f32[2,2,520,128]{3,2,1,0:T(8,128)S(1)} %dynamic-slice_bitcast_fusion), channel_id=1, source_target_pairs={{0,2},{2,0},{4,6},{6,4},{8,10},{10,8},{12,14},{14,12},{1,3},{3,1},... | collective-permute-start | bytes 3194888 | tf_op jit(solution)/shard_map/ppermute | solution.py:157
  129.2 12.8 %copy-start.2 = (f32[512,128]{1,0:T(8,128)S(1)}, f32[512,128]{1,0:T(8,128)}, u32[]{:S(2)}) copy-start(f32[512,128]{1,0:T(8,128)} %param.10) | copy-start | bytes 786436
  129.2 12.5 %collective-permute-start.3 = (f32[2,520,128]{2,1,0:T(8,128)S(1)}, f32[2,520,128]{2,1,0:T(8,128)S(1)}, u32[]{:S(2)}, u32[]{:S(2)}) collective-permute-start(f32[2,520,128]{2,1,0:T(8,128)S(1)} %dynamic-slice_bitcast_fusion.2), channel_id=1, source_target_pairs={{0,4},{2,6},{4,0},{6,2},{8,12},{10,14},{12,8},{14,10},{1,5},{3,7},... | collective-permute-start | bytes 1597448 | tf_op jit(solution)/shard_map/ppermute | solution.py:157
  141.8 22.8 %copy-start.3 = (f32[256,256]{1,0:T(8,128)S(1)}, f32[256,256]{1,0:T(8,128)}, u32[]{:S(2)}) copy-start(f32[256,256]{1,0:T(8,128)} %param.12) | copy-start | bytes 786436
  141.8 15.0 %collective-permute-start.4 = (f32[520,128]{1,0:T(8,128)S(1)}, f32[520,128]{1,0:T(8,128)S(1)}, u32[]{:S(2)}, u32[]{:S(2)}) collective-permute-start(f32[520,128]{1,0:T(8,128)S(1)} %dynamic-slice_bitcast_fusion.3), channel_id=1, source_target_pairs={{0,8},{2,10},{4,12},{6,14},{8,0},{10,2},{12,4},{14,6},{1,9},{3,11}... | collective-permute-start | bytes 798728 | tf_op jit(solution)/shard_map/ppermute | solution.py:157
  141.9 15.4 %collective-permute-start = (f32[512,128]{1,0:T(8,128)S(1)}, f32[512,128]{1,0:T(8,128)S(1)}, u32[]{:S(2)}, u32[]{:S(2)}) collective-permute-start(f32[512,128]{1,0:T(8,128)S(1)} %copy-done.2), channel_id=1, source_target_pairs={{0,1},{1,0},{2,3},{3,2},{4,5},{5,4},{6,7},{7,6},{8,9},{9,8},{10,11... | collective-permute-start | bytes 786440 | tf_op jit(solution)/shard_map/ppermute | solution.py:157
  142.2 23.0 %copy-start.4 = (f32[512,128]{1,0:T(8,128)S(1)}, f32[512,128]{1,0:T(8,128)}, u32[]{:S(2)}) copy-start(f32[512,128]{1,0:T(8,128)} %param.13) | copy-start | bytes 786436
  157.0 7.4 %collective-permute-start.5 = (f32[512,128]{1,0:T(8,128)S(1)}, f32[512,128]{1,0:T(8,128)S(1)}, u32[]{:S(2)}, u32[]{:S(2)}) collective-permute-start(f32[512,128]{1,0:T(8,128)S(1)} %slice_divide_fusion), channel_id=1, source_target_pairs={{0,1},{1,0},{2,3},{3,2},{4,5},{5,4},{6,7},{7,6},{8,9},{9,8},{10,11... | collective-permute-start | bytes 786440 | tf_op jit(solution)/shard_map/ppermute | solution.py:157
  166.5 6.5 %collective-permute-start.6 = (f32[512,128]{1,0:T(8,128)S(1)}, f32[512,128]{1,0:T(8,128)S(1)}, u32[]{:S(2)}, u32[]{:S(2)}) collective-permute-start(f32[512,128]{1,0:T(8,128)S(1)} %get-tuple-element.46), channel_id=1, source_target_pairs={{0,1},{1,0},{2,3},{3,2},{4,5},{5,4},{6,7},{7,6},{8,9},{9,8},{10,11... | collective-permute-start | bytes 786440 | tf_op jit(solution)/shard_map/ppermute | solution.py:157
  173.6 8.9 %collective-permute-start.11 = (f32[512,128]{1,0:T(8,128)S(1)}, f32[512,128]{1,0:T(8,128)S(1)}, u32[]{:S(2)}, u32[]{:S(2)}) collective-permute-start(f32[512,128]{1,0:T(8,128)S(1)} %convolution_divide_fusion), channel_id=1, source_target_pairs={{0,8},{2,10},{4,12},{6,14},{8,0},{10,2},{12,4},{14,6},{1,9},{3,11}... | collective-permute-start | bytes 786440 | tf_op jit(solution)/shard_map/ppermute | solution.py:157
  182.6 11.6 %collective-permute-start.12 = (f32[2,512,128]{2,1,0:T(8,128)S(1)}, f32[2,512,128]{2,1,0:T(8,128)S(1)}, u32[]{:S(2)}, u32[]{:S(2)}) collective-permute-start(f32[2,512,128]{2,1,0:T(8,128)S(1)} %maximum_select_fusion.5), channel_id=1, source_target_pairs={{0,4},{2,6},{4,0},{6,2},{8,12},{10,14},{12,8},{14,10},{1,5},{3,7},... | collective-permute-start | bytes 1572872 | tf_op jit(solution)/shard_map/ppermute | solution.py:157
  195.2 22.1 %collective-permute-start.13 = (f32[2,2,512,128]{3,2,0,1:T(8,128)}, f32[2,2,512,128]{3,2,0,1:T(8,128)S(1)}, u32[]{:S(2)}, u32[]{:S(2)}) collective-permute-start(f32[2,2,512,128]{3,2,0,1:T(8,128)} %maximum_select_fusion.3), channel_id=1, source_target_pairs={{0,2},{2,0},{4,6},{6,4},{8,10},{10,8},{12,14},{14,12},{1,3},{3,1},... | collective-permute-start | bytes 3145736 | tf_op jit(solution)/shard_map/ppermute | solution.py:157
  199.5 4.4 %collective-permute-start.7 = (f32[2,128,256]{1,2,0:T(8,128)}, f32[2,128,256]{1,2,0:T(8,128)S(1)}, u32[]{:S(2)}, u32[]{:S(2)}) collective-permute-start(f32[2,128,256]{1,2,0:T(8,128)} %pad_maximum_fusion.3), channel_id=1, source_target_pairs={{0,16},{16,0},{1,17},{17,1},{2,18},{18,2},{3,19},{19,3},{4,20},{20... | collective-permute-start | bytes 786440 | tf_op jit(solution)/shard_map/ppermute | solution.py:157
  204.7 146.2 %collective-permute-start.8 = (f32[2,128,256]{1,2,0:T(8,128)}, f32[2,128,256]{1,2,0:T(8,128)}, u32[]{:S(2)}, u32[]{:S(2)}) collective-permute-start(f32[2,128,256]{1,2,0:T(8,128)} %fusion.28), channel_id=1, source_target_pairs={{0,2},{2,0},{4,6},{6,4},{8,10},{10,8},{12,14},{14,12},{1,3},{3,1},... | collective-permute-start | bytes 786440 | tf_op jit(solution)/shard_map/ppermute | solution.py:157
  344.4 31.6 %copy-start.1 = (f32[4096,128]{1,0:T(8,128)S(1)}, f32[4096,128]{1,0:T(8,128)}, u32[]{:S(2)}) copy-start(f32[4096,128]{1,0:T(8,128)} %shard_map.129) | copy-start | bytes 6291460
  344.4 31.6 %collective-permute-start.14 = (f32[2048,128]{1,0:T(8,128)}, f32[2048,128]{1,0:T(8,128)}, u32[]{:S(2)}, u32[]{:S(2)}) collective-permute-start(f32[2048,128]{1,0:T(8,128)} %dynamic-slice_bitcast_fusion.1), channel_id=1, source_target_pairs={{0,16},{16,0},{1,17},{17,1},{2,18},{18,2},{3,19},{19,3},{4,20},{20... | collective-permute-start | bytes 3145736 | tf_op jit(solution)/shard_map/ppermute | solution.py:157
  351.9 7.8 %collective-permute-start.9 = (f32[2,128,256]{1,2,0:T(8,128)S(1)}, f32[2,128,256]{1,2,0:T(8,128)S(1)}, u32[]{:S(2)}, u32[]{:S(2)}) collective-permute-start(f32[2,128,256]{1,2,0:T(8,128)S(1)} %fusion.32), channel_id=1, source_target_pairs={{0,4},{2,6},{4,0},{6,2},{8,12},{10,14},{12,8},{14,10},{1,5},{3,7},... | collective-permute-start | bytes 786440 | tf_op jit(solution)/shard_map/ppermute | solution.py:157
  359.7 14.8 %collective-permute-start.10 = (f32[2,128,256]{1,2,0:T(8,128)S(1)}, f32[2,128,256]{1,2,0:T(8,128)S(1)}, u32[]{:S(2)}, u32[]{:S(2)}) collective-permute-start(f32[2,128,256]{1,2,0:T(8,128)S(1)} %add.101), channel_id=1, source_target_pairs={{0,8},{2,10},{4,12},{6,14},{8,0},{10,2},{12,4},{14,6},{1,9},{3,11}... | collective-permute-start | bytes 786440 | tf_op jit(solution)/shard_map/ppermute | solution.py:157

commit v4 on v3

--- a/solution.py
+++ b/solution.py
@@ -25,67 +25,73 @@
     return bits.reshape(word_rows * 8, edge).astype(jnp.float32)
 
 
-def slot_range(live_ref, group):
+UNROLL = 8
+
+
+def live_chunk(live_ref, group):
     base = pl.program_id(0) * group
-    count = jnp.clip(live_ref[0] - base, 0, group)
-    return base, count
-
-
-def forward_kernel(live_ref, rows_ref, cols_ref, masks_ref, panel_ref, totals_ref, counts_ref):
+    return base, base < live_ref[0]
+
+
+def slot_words(masks_ref, live_ref, base, k):
+    keep = jnp.where(base + k < live_ref[0], -1, 0).astype(jnp.int32)
+    return unpack_block(jnp.bitwise_and(masks_ref[k], keep)).astype(jnp.bfloat16)
+
+
+def forward_kernel(live_ref, rows_ref, cols_ref, masks_ref, panel_ref, totals_ref):
     group, _, edge = masks_ref.shape
-    row_limit = counts_ref.shape[0] - 1
+    row_limit = totals_ref.shape[0] // edge - 1
     col_limit = panel_ref.shape[0] // edge - 1
+    half = totals_ref.shape[1]
 
     @pl.when(pl.program_id(0) == 0)
     def _():
         totals_ref[...] = jnp.zeros_like(totals_ref)
-        counts_ref[...] = jnp.zeros_like(counts_ref)
-
-    base, count = slot_range(live_ref, group)
-    ones = jnp.ones((8, edge), jnp.bfloat16)
-    half = totals_ref.shape[1]
-
-    def body(k, carry):
-        slot = base + k
-        row = jnp.clip(rows_ref[slot], 0, row_limit)
-        col = jnp.clip(cols_ref[slot], 0, col_limit)
-        dense = unpack_block(masks_ref[k]).astype(jnp.bfloat16)
-        tile = panel_ref[pl.ds(pl.multiple_of(col * edge, edge), edge), :]
-        prod = jnp.dot(dense, tile, preferred_element_type=jnp.float32)
-        start = pl.multiple_of(row * edge, edge)
-        totals_ref[pl.ds(start, edge), :] += prod[:, :half] + prod[:, half:]
-        counts_ref[row] += lax.dot_general(
-            ones, dense, (((1,), (1,)), ((), ())), preferred_element_type=jnp.float32
-        )
-        return carry
-
-    lax.fori_loop(0, count, body, 0)
+
+    base, active = live_chunk(live_ref, group)
+
+    @pl.when(active)
+    def _():
+        def body(k, carry):
+            slot = base + k
+            row = jnp.clip(rows_ref[slot], 0, row_limit)
+            col = jnp.clip(cols_ref[slot], 0, col_limit)
+            dense = slot_words(masks_ref, live_ref, base, k)
+            tile = panel_ref[pl.ds(pl.multiple_of(col * edge, edge), edge), :]
+            prod = jnp.dot(dense, tile, preferred_element_type=jnp.float32)
+            start = pl.multiple_of(row * edge, edge)
+            totals_ref[pl.ds(start, edge), :] += prod[:, :half] + prod[:, half:]
+            return carry
+
+        lax.fori_loop(0, group, body, 0, unroll=UNROLL)
 
 
 def backward_kernel(live_ref, rows_ref, cols_ref, masks_ref, lifted_ref, out_ref):
     group, _, edge = masks_ref.shape
-    row_limit = lifted_ref.shape[0] // edge - 1
-    col_limit = out_ref.shape[0] // edge - 1
+    row_limit = lifted_ref.shape[1] // edge - 1
+    col_limit = out_ref.shape[1] // edge - 1
+    half = out_ref.shape[0]
 
     @pl.when(pl.program_id(0) == 0)
     def _():
         out_ref[...] = jnp.zeros_like(out_ref)
 
-    base, count = slot_range(live_ref, group)
-    half = out_ref.shape[1]
-
-    def body(k, carry):
-        slot = base + k
-        row = jnp.clip(rows_ref[slot], 0, row_limit)
-        col = jnp.clip(cols_ref[slot], 0, col_limit)
-        dense_t = unpack_block(masks_ref[k]).T.astype(jnp.bfloat16)
-        tile = lifted_ref[pl.ds(pl.multiple_of(row * edge, edge), edge), :]
-        prod = jnp.dot(dense_t, tile, preferred_element_type=jnp.float32)
-        start = pl.multiple_of(col * edge, edge)
-        out_ref[pl.ds(start, edge), :] += prod[:, :half] + prod[:, half:]
-        return carry
-
-    lax.fori_loop(0, count, body, 0)
+    base, active = live_chunk(live_ref, group)
+
+    @pl.when(active)
+    def _():
+        def body(k, carry):
+            slot = base + k
+            row = jnp.clip(rows_ref[slot], 0, row_limit)
+            col = jnp.clip(cols_ref[slot], 0, col_limit)
+            dense = slot_words(masks_ref, live_ref, base, k)
+            tile = lifted_ref[:, pl.ds(pl.multiple_of(row * edge, edge), edge)]
+            prod = jnp.dot(tile, dense, preferred_element_type=jnp.float32)
+            start = pl.multiple_of(col * edge, edge)
+            out_ref[:, pl.ds(start, edge)] += prod[:half] + prod[half:]
+            return carry
+
+        lax.fori_loop(0, group, body, 0, unroll=UNROLL)
 
 
 def mask_spec(packed_masks, group):
@@ -102,47 +108,55 @@
     return pl.BlockSpec(shape, lambda chunk, live_ref, rows_ref, cols_ref: (0,) * len(shape))
 
 
-def block_aggregate(live, block_rows, block_cols, packed_masks, panel_split, row_blocks):
-    slot_total, _, edge = packed_masks.shape
+def slot_pallas(kernel, live, block_rows, block_cols, packed_masks, dense_input, out_shape):
+    slot_total = packed_masks.shape[0]
     group = min(SLOT_GROUP, slot_total)
-    half = panel_split.shape[1] // 2
-    totals_shape = (row_blocks * edge, half)
-    counts_shape = (row_blocks, 8, edge)
     grid_spec = pltpu.PrefetchScalarGridSpec(
         num_scalar_prefetch=3,
         grid=(slot_total // group,),
-        in_specs=[mask_spec(packed_masks, group), whole_spec(panel_split.shape)],
-        out_specs=[whole_spec(totals_shape), whole_spec(counts_shape)],
-    )
-    totals, counts = pl.pallas_call(
-        forward_kernel,
-        grid_spec=grid_spec,
-        out_shape=[
-            jax.ShapeDtypeStruct(totals_shape, jnp.float32),
-            jax.ShapeDtypeStruct(counts_shape, jnp.float32),
-        ],
-        compiler_params=pltpu.CompilerParams(dimension_semantics=("arbitrary",)),
-    )(live, block_rows, block_cols, packed_masks, panel_split)
-    return totals, counts[:, 0, :].reshape(-1)
-
-
-def block_transpose(live, block_rows, block_cols, packed_masks, lifted_split, col_blocks):
-    slot_total, _, edge = packed_masks.shape
-    group = min(SLOT_GROUP, slot_total)
-    half = lifted_split.shape[1] // 2
-    out_shape = (col_blocks * edge, half)
-    grid_spec = pltpu.PrefetchScalarGridSpec(
-        num_scalar_prefetch=3,
-        grid=(slot_total // group,),
-        in_specs=[mask_spec(packed_masks, group), whole_spec(lifted_split.shape)],
+        in_specs=[mask_spec(packed_masks, group), whole_spec(dense_input.shape)],
         out_specs=whole_spec(out_shape),
     )
     return pl.pallas_call(
-        backward_kernel,
+        kernel,
         grid_spec=grid_spec,
         out_shape=jax.ShapeDtypeStruct(out_shape, jnp.float32),
         compiler_params=pltpu.CompilerParams(dimension_semantics=("arbitrary",)),
-    )(live, block_rows, block_cols, packed_masks, lifted_split)
+    )(live, block_rows, block_cols, packed_masks, dense_input)
+
+
+def block_row_counts(live, block_rows, packed_masks, row_blocks):
+    slot_total, word_rows, edge = packed_masks.shape
+    shifts = jnp.arange(8, dtype=jnp.int32)
+    bits = jnp.bitwise_and(jnp.right_shift(packed_masks[:, :, None, :], shifts[:, None]), 1)
+    slot_counts = jnp.sum(bits, axis=-1).reshape(slot_total, word_rows * 8).astype(jnp.float32)
+    live_slots = jnp.arange(slot_total, dtype=jnp.int32) < live[0]
+    selector = jnp.logical_and(
+        block_rows[:, None] == jnp.arange(row_blocks, dtype=jnp.int32)[None, :], live_slots[:, None]
+    ).astype(jnp.float32)
+    counts = jnp.einsum("sb,sr->br", selector, slot_counts, precision=HIGHEST)
+    return counts.reshape(-1)
+
+
+def block_aggregate(live, block_rows, block_cols, packed_masks, panel_split, row_blocks):
+    edge = packed_masks.shape[-1]
+    totals_shape = (row_blocks * edge, panel_split.shape[1] // 2)
+    totals = slot_pallas(
+        forward_kernel, live, block_rows, block_cols, packed_masks, panel_split, totals_shape
+    )
+    return totals, block_row_counts(live, block_rows, packed_masks, row_blocks)
+
+
+def block_transpose(live, block_rows, block_cols, packed_masks, lifted_rows, col_blocks):
+    edge = packed_masks.shape[-1]
+    lifted_t = lifted_rows.T
+    high = lax.reduce_precision(lifted_t, exponent_bits=8, mantissa_bits=7)
+    split_t = jnp.concatenate([high, lifted_t - high], axis=0).astype(jnp.bfloat16)
+    out_shape = (lifted_rows.shape[1], col_blocks * edge)
+    out_t = slot_pallas(
+        backward_kernel, live, block_rows, block_cols, packed_masks, split_t, out_shape
+    )
+    return out_t.T
 
 
 def axis_bits(axis):
@@ -261,7 +275,7 @@
     lifted = grad_agg / (1.0 + degree)[:, None]
     gathered_rows = doubling_gather(lifted, "test")
     column_terms = block_transpose(
-        live, block_rows, block_cols, packed_masks, split_hi_lo(gathered_rows), col_blocks
+        live, block_rows, block_cols, packed_masks, gathered_rows, col_blocks
     )
     grad_x_test = halving_scatter(column_terms, "cand")
     return (output, grad_w_self, grad_w_neigh, grad_x_cand, grad_x_test)

time: 379 us -> 367 us (0.968)
  Pallas kernels: 215 us -> 48.6 us
  other arithmetic: 15.3 us -> 154 us
  local copies, waits for them, and re-layouts: 5.08 us -> 21.2 us
    pallas_call x2, Pallas kernels: 215 us -> 48.6 us  [slot_pallas(): pl.pallas_call(kernel, grid_spec=grid_spec, out_shape=jax.ShapeDtypeStruc...]
    reduce_sum x0 -> x1, other arithmetic: none -> 142 us  [block_row_counts(): jnp.sum(bits, axis=-1).reshape(slot_total, word_rows * 8)]
    dynamic_slice x0 -> x3, local copies, waits for them, and re-layouts: none -> 7.54 us  [the longest x2 3.87 us: halving_scatter(): keep = lax.dynamic_index_in_dim(data, mine, position, keepdims=False)]
    select_n x1 -> x2, local copies, waits for them, and re-layouts: 0.14 us -> 5.52 us  [doubling_gather(): jnp.where(first, jnp.stack([data, other], axis=stacked), jnp.stack([other...]
  transfers between devices with their start and end apart: 15 -> 15, of which waited for: 12 -> 11; matrix products, arithmetic and copies ran while one was open for 3% -> 47% of each run, Pallas kernels for 32% -> 7%
where the time goes in v4:
time: 367 us; the launch traced here: 366 us
  other arithmetic  154 us (42%)
  waiting for transfers between devices  121 us (33%)
  Pallas kernels  48.6 us (13%)
  local copies, waits for them, and re-layouts  21.2 us (6%)
  starting transfers between devices  13.2 us (4%)
  matrix products  7.01 us (2%)
    reduce_sum x1, other arithmetic, block_row_counts(): jnp.sum(bits, axis=-1).reshape(slot_total, word_rows * 8)  142 us
    ppermute x15, waiting for transfers between devices, exchange(): return lax.ppermute(values, axis, [(i, i ^ 1 << bit) for i in range(count)])  121 us
    pallas_call x2, Pallas kernels, slot_pallas(): pl.pallas_call(kernel, grid_spec=grid_spec, out_shape=jax.ShapeDtypeStruc...  48.6 us
    ppermute x15, starting transfers between devices, exchange(): return lax.ppermute(values, axis, [(i, i ^ 1 << bit) for i in range(count)])  13.2 us
  transfers between devices with their start and end apart: 15, of which 11 were waited for; matrix products, arithmetic and copies ran while one was open for 47% of the time, Pallas kernels for 7%

profile of v4, /device:TPU:31, one launch (start us, length us, event | category | flops | bytes accessed | tf_op | source)
XLA Modules:
  0.0 366.5 jit_solution(12024012644317687929)
XLA Ops:
  1.4 141.9 %and_reduce_fusion = s32[512,16,8]{2,1,0:T(8,128)} fusion(s32[512,16,128]{2,1,0:T(8,128)} %bitcast.66), kind=kLoop, calls=%fused_computation | loop fusion | flops 25100288 | bytes 4456448 | tf_op jit(solution)/shard_map/reduce_sum | solution.py:132
  143.3 3.0 copy.97
  148.0 1.6 pad_maximum_fusion.panel_ref
  149.6 23.6 %shard_map.128 = f32[4096,128]{1,0:T(8,128)} custom-call(s32[1]{0:T(128)} %bitcast.live_ref, s32[512]{0:T(512)} %bitcast.83, s32[512]{0:T(512)} %bitcast.86, s32[512,16,128]{2,1,0:T(8,128)} %bitcast.67, bf16[4096,256]{1,0:T(8,128)(2,1)} %pad_maximum_fusion.panel_ref), custom_call_target="tpu_custom_call" | custom-call | tf_op jit(solution)/shard_map/pallas_call | solution.py:120
  173.2 1.8 maximum_maximum_fusion
  175.2 25.1 %collective-permute-done.2 = f32[2,2,520,128]{3,2,1,0:T(8,128)} collective-permute-done((f32[2,2,520,128]{3,2,1,0:T(8,128)S(1)}, f32[2,2,520,128]{3,2,1,0:T(8,128)}, u32[]{:S(2)}, u32[]{:S(2)}) %collective-permute-start.2) | collective-permute-done | bytes 1064992 | tf_op jit(solution)/shard_map/ppermute | solution.py:171
  201.8 12.8 %collective-permute-done.3 = f32[2,520,128]{2,1,0:T(8,128)S(1)} collective-permute-done((f32[2,520,128]{2,1,0:T(8,128)S(1)}, f32[2,520,128]{2,1,0:T(8,128)S(1)}, u32[]{:S(2)}, u32[]{:S(2)}) %collective-permute-start.3) | collective-permute-done | bytes 532512 | tf_op jit(solution)/shard_map/ppermute | solution.py:171
  215.1 14.5 %collective-permute-done.4 = f32[520,128]{1,0:T(8,128)S(1)} collective-permute-done((f32[520,128]{1,0:T(8,128)S(1)}, f32[520,128]{1,0:T(8,128)S(1)}, u32[]{:S(2)}, u32[]{:S(2)}) %collective-permute-start.4) | collective-permute-done | bytes 266272 | tf_op jit(solution)/shard_map/ppermute | solution.py:171
  230.2 7.0 %collective-permute-done.5 = f32[512,128]{1,0:T(8,128)S(1)} collective-permute-done((f32[512,128]{1,0:T(8,128)S(1)}, f32[512,128]{1,0:T(8,128)S(1)}, u32[]{:S(2)}, u32[]{:S(2)}) %collective-permute-start.5) | collective-permute-done | bytes 262176 | tf_op jit(solution)/shard_map/ppermute | solution.py:171
  239.6 6.2 %collective-permute-done.6 = f32[512,128]{1,0:T(8,128)S(1)} collective-permute-done((f32[512,128]{1,0:T(8,128)S(1)}, f32[512,128]{1,0:T(8,128)S(1)}, u32[]{:S(2)}, u32[]{:S(2)}) %collective-permute-start.6) | collective-permute-done | bytes 262176 | tf_op jit(solution)/shard_map/ppermute | solution.py:171
  246.6 8.8 %collective-permute-done.11 = f32[512,128]{1,0:T(8,128)S(1)} collective-permute-done((f32[512,128]{1,0:T(8,128)S(1)}, f32[512,128]{1,0:T(8,128)S(1)}, u32[]{:S(2)}, u32[]{:S(2)}) %collective-permute-start.11) | collective-permute-done | bytes 262176 | tf_op jit(solution)/shard_map/ppermute | solution.py:171
  255.6 11.5 %collective-permute-done.12 = f32[2,512,128]{2,1,0:T(8,128)S(1)} collective-permute-done((f32[2,512,128]{2,1,0:T(8,128)S(1)}, f32[2,512,128]{2,1,0:T(8,128)S(1)}, u32[]{:S(2)}, u32[]{:S(2)}) %collective-permute-start.12) | collective-permute-done | bytes 524320 | tf_op jit(solution)/shard_map/ppermute | solution.py:171
  268.7 1.9 convolution_bitcast_fusion.1
  271.7 3.1 collective-permute-start.7
  277.8 12.4 %collective-permute-done.13 = f32[2,2,512,128]{3,2,0,1:T(8,128)S(1)} collective-permute-done((f32[2,2,512,128]{3,2,0,1:T(8,128)}, f32[2,2,512,128]{3,2,0,1:T(8,128)S(1)}, u32[]{:S(2)}, u32[]{:S(2)}) %collective-permute-start.13) | collective-permute-done | bytes 1048608 | tf_op jit(solution)/shard_map/ppermute | solution.py:171
  290.4 2.5 copy.104
  292.8 3.1 select_n.160
  297.8 25.0 %shard_map.129 = f32[128,4096]{1,0:T(8,128)} custom-call(s32[1]{0:T(128)} %bitcast.live_ref, s32[512]{0:T(512)} %bitcast.84, s32[512]{0:T(512)} %bitcast.87, s32[512,16,128]{2,1,0:T(8,128)} %bitcast.68, bf16[256,4096]{1,0:T(8,128)(2,1)} %pad_maximum_fusion.1.lifted_ref), custom_call_target="tpu_custom_call" | custom-call | tf_op jit(solution)/shard_map/pallas_call | solution.py:120
  322.8 3.2 reshape.278
  326.1 3.1 constant_dynamic-slice_fusion.1
  329.2 3.7 %copy.106 = f32[1,2048,128]{2,1,0:T(8,128)} copy(f32[1,2048,128]{1,0,2:T(1,128)} %get-tuple-element.36) | data formatting | bytes 2097152 | tf_op jit(solution)/shard_map/jit(dynamic_index_in_dim)/dynamic_slice | solution.py:196
  332.9 6.4 %collective-permute-start.14 = (f32[2048,128]{1,0:T(8,128)}, f32[2048,128]{1,0:T(8,128)S(1)}, u32[]{:S(2)}, u32[]{:S(2)}) collective-permute-start(f32[2048,128]{1,0:T(8,128)} %bitcast.82), channel_id=1, source_target_pairs={{0,16},{16,0},{1,17},{17,1},{2,18},{18,2},{3,19},{19,3},{4,20},{20... | collective-permute-start | bytes 3145736 | tf_op jit(solution)/shard_map/ppermute | solution.py:171
  340.3 7.8 %collective-permute-done.9 = f32[2,128,256]{1,2,0:T(8,128)S(1)} collective-permute-done((f32[2,128,256]{1,2,0:T(8,128)S(1)}, f32[2,128,256]{1,2,0:T(8,128)S(1)}, u32[]{:S(2)}, u32[]{:S(2)}) %collective-permute-start.9) | collective-permute-done | bytes 262176 | tf_op jit(solution)/shard_map/ppermute | solution.py:171
  349.6 13.4 %collective-permute-done.10 = f32[2,128,256]{1,2,0:T(8,128)S(1)} collective-permute-done((f32[2,128,256]{1,2,0:T(8,128)S(1)}, f32[2,128,256]{1,2,0:T(8,128)S(1)}, u32[]{:S(2)}, u32[]{:S(2)}) %collective-permute-start.10) | collective-permute-done | bytes 262176 | tf_op jit(solution)/shard_map/ppermute | solution.py:171
  (88 shorter events, 21.1 us)
Async XLA Ops:
  0.6 237.4 %copy-start = (f32[256,256]{1,0:T(8,128)S(1)}, f32[256,256]{1,0:T(8,128)}, u32[]{:S(2)}) copy-start(f32[256,256]{1,0:T(8,128)} %param.11) | copy-start | bytes 786436
  0.6 146.9 %collective-permute-start.1 = (f32[2048,128]{1,0:T(8,128)}, f32[2048,128]{1,0:T(8,128)S(1)}, u32[]{:S(2)}, u32[]{:S(2)}) collective-permute-start(f32[2048,128]{1,0:T(8,128)} %param.9), channel_id=1, source_target_pairs={{0,16},{16,0},{1,17},{17,1},{2,18},{18,2},{3,19},{19,3},{4,20},{20... | collective-permute-start | bytes 3145736 | tf_op jit(solution)/shard_map/ppermute | solution.py:171
  175.1 25.2 %collective-permute-start.2 = (f32[2,2,520,128]{3,2,1,0:T(8,128)S(1)}, f32[2,2,520,128]{3,2,1,0:T(8,128)}, u32[]{:S(2)}, u32[]{:S(2)}) collective-permute-start(f32[2,2,520,128]{3,2,1,0:T(8,128)S(1)} %dynamic-slice_bitcast_fusion), channel_id=1, source_target_pairs={{0,2},{2,0},{4,6},{6,4},{8,10},{10,8},{12,14},{14,12},{1,3},{3,1},... | collective-permute-start | bytes 3194888 | tf_op jit(solution)/shard_map/ppermute | solution.py:171
  201.6 13.1 %copy-start.8 = (f32[512,128]{1,0:T(8,128)S(1)}, f32[512,128]{1,0:T(8,128)}, u32[]{:S(2)}) copy-start(f32[512,128]{1,0:T(8,128)} %param.10) | copy-start | bytes 786436
  201.7 12.9 %collective-permute-start.3 = (f32[2,520,128]{2,1,0:T(8,128)S(1)}, f32[2,520,128]{2,1,0:T(8,128)S(1)}, u32[]{:S(2)}, u32[]{:S(2)}) collective-permute-start(f32[2,520,128]{2,1,0:T(8,128)S(1)} %dynamic-slice_bitcast_fusion.1), channel_id=1, source_target_pairs={{0,4},{2,6},{4,0},{6,2},{8,12},{10,14},{12,8},{14,10},{1,5},{3,7},... | collective-permute-start | bytes 1597448 | tf_op jit(solution)/shard_map/ppermute | solution.py:171
  214.6 22.8 %copy-start.11 = (f32[256,256]{1,0:T(8,128)S(1)}, f32[256,256]{1,0:T(8,128)}, u32[]{:S(2)}) copy-start(f32[256,256]{1,0:T(8,128)} %param.12) | copy-start | bytes 786436
  214.7 15.0 %collective-permute-start.4 = (f32[520,128]{1,0:T(8,128)S(1)}, f32[520,128]{1,0:T(8,128)S(1)}, u32[]{:S(2)}, u32[]{:S(2)}) collective-permute-start(f32[520,128]{1,0:T(8,128)S(1)} %dynamic-slice_bitcast_fusion.2), channel_id=1, source_target_pairs={{0,8},{2,10},{4,12},{6,14},{8,0},{10,2},{12,4},{14,6},{1,9},{3,11}... | collective-permute-start | bytes 798728 | tf_op jit(solution)/shard_map/ppermute | solution.py:171
  214.8 15.4 %collective-permute-start = (f32[512,128]{1,0:T(8,128)S(1)}, f32[512,128]{1,0:T(8,128)S(1)}, u32[]{:S(2)}, u32[]{:S(2)}) collective-permute-start(f32[512,128]{1,0:T(8,128)S(1)} %copy-done.8), channel_id=1, source_target_pairs={{0,1},{1,0},{2,3},{3,2},{4,5},{5,4},{6,7},{7,6},{8,9},{9,8},{10,11... | collective-permute-start | bytes 786440 | tf_op jit(solution)/shard_map/ppermute | solution.py:171
  215.1 22.9 %copy-start.13 = (f32[512,128]{1,0:T(8,128)S(1)}, f32[512,128]{1,0:T(8,128)}, u32[]{:S(2)}) copy-start(f32[512,128]{1,0:T(8,128)} %param.13) | copy-start | bytes 786436
  229.8 7.4 %collective-permute-start.5 = (f32[512,128]{1,0:T(8,128)S(1)}, f32[512,128]{1,0:T(8,128)S(1)}, u32[]{:S(2)}, u32[]{:S(2)}) collective-permute-start(f32[512,128]{1,0:T(8,128)S(1)} %slice_divide_fusion), channel_id=1, source_target_pairs={{0,1},{1,0},{2,3},{3,2},{4,5},{5,4},{6,7},{7,6},{8,9},{9,8},{10,11... | collective-permute-start | bytes 786440 | tf_op jit(solution)/shard_map/ppermute | solution.py:171
  239.3 6.5 %collective-permute-start.6 = (f32[512,128]{1,0:T(8,128)S(1)}, f32[512,128]{1,0:T(8,128)S(1)}, u32[]{:S(2)}, u32[]{:S(2)}) collective-permute-start(f32[512,128]{1,0:T(8,128)S(1)} %get-tuple-element.49), channel_id=1, source_target_pairs={{0,1},{1,0},{2,3},{3,2},{4,5},{5,4},{6,7},{7,6},{8,9},{9,8},{10,11... | collective-permute-start | bytes 786440 | tf_op jit(solution)/shard_map/ppermute | solution.py:171
  245.9 24.8 %copy-start.1 = (f32[512,128]{1,0:T(8,128)}, f32[512,128]{1,0:T(8,128)S(1)}, u32[]{:S(2)}) copy-start(f32[512,128]{1,0:T(8,128)S(1)} %get-tuple-element.41) | copy-start | bytes 786436
  245.9 24.8 %copy-start.3 = (f32[512,128]{1,0:T(8,128)}, f32[512,128]{1,0:T(8,128)S(1)}, u32[]{:S(2)}) copy-start(f32[512,128]{1,0:T(8,128)S(1)} %get-tuple-element.42) | copy-start | bytes 786436
  246.5 8.9 %collective-permute-start.11 = (f32[512,128]{1,0:T(8,128)S(1)}, f32[512,128]{1,0:T(8,128)S(1)}, u32[]{:S(2)}, u32[]{:S(2)}) collective-permute-start(f32[512,128]{1,0:T(8,128)S(1)} %convolution_divide_fusion), channel_id=1, source_target_pairs={{0,8},{2,10},{4,12},{6,14},{8,0},{10,2},{12,4},{14,6},{1,9},{3,11}... | collective-permute-start | bytes 786440 | tf_op jit(solution)/shard_map/ppermute | solution.py:171
  255.4 11.6 %collective-permute-start.12 = (f32[2,512,128]{2,1,0:T(8,128)S(1)}, f32[2,512,128]{2,1,0:T(8,128)S(1)}, u32[]{:S(2)}, u32[]{:S(2)}) collective-permute-start(f32[2,512,128]{2,1,0:T(8,128)S(1)} %maximum_select_fusion.5), channel_id=1, source_target_pairs={{0,4},{2,6},{4,0},{6,2},{8,12},{10,14},{12,8},{14,10},{1,5},{3,7},... | collective-permute-start | bytes 1572872 | tf_op jit(solution)/shard_map/ppermute | solution.py:171
  268.1 22.1 %collective-permute-start.13 = (f32[2,2,512,128]{3,2,0,1:T(8,128)}, f32[2,2,512,128]{3,2,0,1:T(8,128)S(1)}, u32[]{:S(2)}, u32[]{:S(2)}) collective-permute-start(f32[2,2,512,128]{3,2,0,1:T(8,128)} %maximum_select_fusion.3), channel_id=1, source_target_pairs={{0,2},{2,0},{4,6},{6,4},{8,10},{10,8},{12,14},{14,12},{1,3},{3,1},... | collective-permute-start | bytes 3145736 | tf_op jit(solution)/shard_map/ppermute | solution.py:171
  271.7 4.3 %collective-permute-start.7 = (f32[2,128,256]{1,2,0:T(8,128)S(1)}, f32[2,128,256]{1,2,0:T(8,128)S(1)}, u32[]{:S(2)}, u32[]{:S(2)}) collective-permute-start(f32[2,128,256]{1,2,0:T(8,128)S(1)} %pad_maximum_fusion.3), channel_id=1, source_target_pairs={{0,16},{16,0},{1,17},{17,1},{2,18},{18,2},{3,19},{19,3},{4,20},{20... | collective-permute-start | bytes 786440 | tf_op jit(solution)/shard_map/ppermute | solution.py:171
  276.0 14.3 %copy-start.9 = (f32[2,128,256]{1,2,0:T(8,128)}, f32[2,128,256]{1,2,0:T(8,128)S(1)}, u32[]{:S(2)}) copy-start(f32[2,128,256]{1,2,0:T(8,128)S(1)} %collective-permute-done.7) | copy-start | bytes 786436
  276.8 62.5 %collective-permute-start.8 = (f32[2,128,256]{1,2,0:T(8,128)}, f32[2,128,256]{1,2,0:T(8,128)}, u32[]{:S(2)}, u32[]{:S(2)}) collective-permute-start(f32[2,128,256]{1,2,0:T(8,128)} %fusion.32), channel_id=1, source_target_pairs={{0,2},{2,0},{4,6},{6,4},{8,10},{10,8},{12,14},{14,12},{1,3},{3,1},... | collective-permute-start | bytes 786440 | tf_op jit(solution)/shard_map/ppermute | solution.py:171
  329.2 19.1 %copy-start.2 = (f32[512,128]{1,0:T(8,128)S(1)}, f32[512,128]{1,0:T(8,128)}, u32[]{:S(2)}) copy-start(f32[512,128]{1,0:T(8,128)} %copy-done.1) | copy-start | bytes 786436
  329.2 19.1 %copy-start.4 = (f32[512,128]{1,0:T(8,128)S(1)}, f32[512,128]{1,0:T(8,128)}, u32[]{:S(2)}) copy-start(f32[512,128]{1,0:T(8,128)} %copy-done.3) | copy-start | bytes 786436
  332.9 32.5 %collective-permute-start.14 = (f32[2048,128]{1,0:T(8,128)}, f32[2048,128]{1,0:T(8,128)S(1)}, u32[]{:S(2)}, u32[]{:S(2)}) collective-permute-start(f32[2048,128]{1,0:T(8,128)} %bitcast.82), channel_id=1, source_target_pairs={{0,16},{16,0},{1,17},{17,1},{2,18},{18,2},{3,19},{19,3},{4,20},{20... | collective-permute-start | bytes 3145736 | tf_op jit(solution)/shard_map/ppermute | solution.py:171
  340.3 7.9 %collective-permute-start.9 = (f32[2,128,256]{1,2,0:T(8,128)S(1)}, f32[2,128,256]{1,2,0:T(8,128)S(1)}, u32[]{:S(2)}, u32[]{:S(2)}) collective-permute-start(f32[2,128,256]{1,2,0:T(8,128)S(1)} %fusion.36), channel_id=1, source_target_pairs={{0,4},{2,6},{4,0},{6,2},{8,12},{10,14},{12,8},{14,10},{1,5},{3,7},... | collective-permute-start | bytes 786440 | tf_op jit(solution)/shard_map/ppermute | solution.py:171
  348.2 14.8 %collective-permute-start.10 = (f32[2,128,256]{1,2,0:T(8,128)S(1)}, f32[2,128,256]{1,2,0:T(8,128)S(1)}, u32[]{:S(2)}, u32[]{:S(2)}) collective-permute-start(f32[2,128,256]{1,2,0:T(8,128)S(1)} %add.108), channel_id=1, source_target_pairs={{0,8},{2,10},{4,12},{6,14},{8,0},{10,2},{12,4},{14,6},{1,9},{3,11}... | collective-permute-start | bytes 786440 | tf_op jit(solution)/shard_map/ppermute | solution.py:171
  (5 other events, 34.4 us)

commit v5 on v4

--- a/solution.py
+++ b/solution.py
@@ -17,12 +17,16 @@
     return jnp.concatenate([high, low], axis=1).astype(jnp.bfloat16)
 
 
-def unpack_block(words):
+def unpack_bits(words):
     word_rows, edge = words.shape
     cube = jnp.broadcast_to(words[:, None, :], (word_rows, 8, edge))
     shifts = lax.broadcasted_iota(jnp.int32, (word_rows, 8, edge), 1)
     bits = jnp.bitwise_and(jnp.right_shift(cube, shifts), 1)
-    return bits.reshape(word_rows * 8, edge).astype(jnp.float32)
+    return bits.reshape(word_rows * 8, edge)
+
+
+def unpack_block(words):
+    return unpack_bits(words).astype(jnp.float32)
 
 
 UNROLL = 8
@@ -38,7 +42,7 @@
     return unpack_block(jnp.bitwise_and(masks_ref[k], keep)).astype(jnp.bfloat16)
 
 
-def forward_kernel(live_ref, rows_ref, cols_ref, masks_ref, panel_ref, totals_ref):
+def forward_kernel(live_ref, rows_ref, cols_ref, masks_ref, panel_ref, totals_ref, bits_ref):
     group, _, edge = masks_ref.shape
     row_limit = totals_ref.shape[0] // edge - 1
     col_limit = panel_ref.shape[0] // edge - 1
@@ -47,6 +51,7 @@
     @pl.when(pl.program_id(0) == 0)
     def _():
         totals_ref[...] = jnp.zeros_like(totals_ref)
+        bits_ref[...] = jnp.zeros_like(bits_ref)
 
     base, active = live_chunk(live_ref, group)
 
@@ -56,7 +61,10 @@
             slot = base + k
             row = jnp.clip(rows_ref[slot], 0, row_limit)
             col = jnp.clip(cols_ref[slot], 0, col_limit)
-            dense = slot_words(masks_ref, live_ref, base, k)
+            keep = jnp.where(slot < live_ref[0], -1, 0).astype(jnp.int32)
+            bits = unpack_bits(jnp.bitwise_and(masks_ref[k], keep))
+            bits_ref[row] += bits
+            dense = bits.astype(jnp.float32).astype(jnp.bfloat16)
             tile = panel_ref[pl.ds(pl.multiple_of(col * edge, edge), edge), :]
             prod = jnp.dot(dense, tile, preferred_element_type=jnp.float32)
             start = pl.multiple_of(row * edge, edge)
@@ -108,43 +116,32 @@
     return pl.BlockSpec(shape, lambda chunk, live_ref, rows_ref, cols_ref: (0,) * len(shape))
 
 
-def slot_pallas(kernel, live, block_rows, block_cols, packed_masks, dense_input, out_shape):
+def slot_pallas(kernel, live, block_rows, block_cols, packed_masks, dense_input, out_shapes):
     slot_total = packed_masks.shape[0]
     group = min(SLOT_GROUP, slot_total)
     grid_spec = pltpu.PrefetchScalarGridSpec(
         num_scalar_prefetch=3,
         grid=(slot_total // group,),
         in_specs=[mask_spec(packed_masks, group), whole_spec(dense_input.shape)],
-        out_specs=whole_spec(out_shape),
+        out_specs=[whole_spec(shape.shape) for shape in out_shapes],
     )
     return pl.pallas_call(
         kernel,
         grid_spec=grid_spec,
-        out_shape=jax.ShapeDtypeStruct(out_shape, jnp.float32),
+        out_shape=out_shapes,
         compiler_params=pltpu.CompilerParams(dimension_semantics=("arbitrary",)),
     )(live, block_rows, block_cols, packed_masks, dense_input)
 
 
-def block_row_counts(live, block_rows, packed_masks, row_blocks):
-    slot_total, word_rows, edge = packed_masks.shape
-    shifts = jnp.arange(8, dtype=jnp.int32)
-    bits = jnp.bitwise_and(jnp.right_shift(packed_masks[:, :, None, :], shifts[:, None]), 1)
-    slot_counts = jnp.sum(bits, axis=-1).reshape(slot_total, word_rows * 8).astype(jnp.float32)
-    live_slots = jnp.arange(slot_total, dtype=jnp.int32) < live[0]
-    selector = jnp.logical_and(
-        block_rows[:, None] == jnp.arange(row_blocks, dtype=jnp.int32)[None, :], live_slots[:, None]
-    ).astype(jnp.float32)
-    counts = jnp.einsum("sb,sr->br", selector, slot_counts, precision=HIGHEST)
-    return counts.reshape(-1)
-
-
 def block_aggregate(live, block_rows, block_cols, packed_masks, panel_split, row_blocks):
     edge = packed_masks.shape[-1]
-    totals_shape = (row_blocks * edge, panel_split.shape[1] // 2)
-    totals = slot_pallas(
-        forward_kernel, live, block_rows, block_cols, packed_masks, panel_split, totals_shape
-    )
-    return totals, block_row_counts(live, block_rows, packed_masks, row_blocks)
+    totals_shape = jax.ShapeDtypeStruct((row_blocks * edge, panel_split.shape[1] // 2), jnp.float32)
+    bits_shape = jax.ShapeDtypeStruct((row_blocks, edge, edge), jnp.int32)
+    totals, bit_sums = slot_pallas(
+        forward_kernel, live, block_rows, block_cols, packed_masks, panel_split,
+        [totals_shape, bits_shape],
+    )
+    return totals, jnp.sum(bit_sums, axis=-1).astype(jnp.float32).reshape(-1)
 
 
 def block_transpose(live, block_rows, block_cols, packed_masks, lifted_rows, col_blocks):
@@ -152,9 +149,9 @@
     lifted_t = lifted_rows.T
     high = lax.reduce_precision(lifted_t, exponent_bits=8, mantissa_bits=7)
     split_t = jnp.concatenate([high, lifted_t - high], axis=0).astype(jnp.bfloat16)
-    out_shape = (lifted_rows.shape[1], col_blocks * edge)
-    out_t = slot_pallas(
-        backward_kernel, live, block_rows, block_cols, packed_masks, split_t, out_shape
+    out_shape = jax.ShapeDtypeStruct((lifted_rows.shape[1], col_blocks * edge), jnp.float32)
+    (out_t,) = slot_pallas(
+        backward_kernel, live, block_rows, block_cols, packed_masks, split_t, [out_shape]
     )
     return out_t.T
 

time: 367 us -> 228 us (0.62)
  other arithmetic: 154 us -> 15.8 us
    reduce_sum x1, other arithmetic: 142 us -> 2.2 us  [block_aggregate(): return (totals, jnp.sum(bit_sums, axis=-1).astype(jnp.float32).reshape(-1))]
  transfers between devices with their start and end apart: 15 -> 15, of which waited for: 11 -> 12; matrix products, arithmetic and copies ran while one was open for 47% -> 12% of each run, Pallas kernels for 7% -> 11%
where the time goes in v5:
time: 228 us; the launch traced here: 227 us
  waiting for transfers between devices  122 us (54%)
  Pallas kernels  49.6 us (22%)
  local copies, waits for them, and re-layouts  18.1 us (8%)
  other arithmetic  15.8 us (7%)
  starting transfers between devices  13.3 us (6%)
  matrix products  6.71 us (3%)
    ppermute x15, waiting for transfers between devices, exchange(): return lax.ppermute(values, axis, [(i, i ^ 1 << bit) for i in range(count)])  122 us
    pallas_call x2, Pallas kernels, slot_pallas(): pl.pallas_call(kernel, grid_spec=grid_spec, out_shape=out_shapes, compile...  49.6 us
    ppermute x15, starting transfers between devices, exchange(): return lax.ppermute(values, axis, [(i, i ^ 1 << bit) for i in range(count)])  13.3 us
    select_n x2, local copies, waits for them, and re-layouts, doubling_gather(): jnp.where(first, jnp.stack([data, other], axis=stacked), jnp.stack([other...  5.52 us
  transfers between devices with their start and end apart: 15, of which 12 were waited for; matrix products, arithmetic and copies ran while one was open for 12% of the time, Pallas kernels for 11%

profile of v5, /device:TPU:31, one launch (start us, length us, event | category | flops | bytes accessed | tf_op | source)
XLA Modules:
  0.0 227.0 jit_solution(18055288863701062678)
XLA Ops:
  2.1 1.8 collective-permute-done.1
  3.9 1.7 maximum_select_fusion
  7.6 24.7 %shard_map.128 = (f32[4096,128]{1,0:T(8,128)}, s32[32,128,128]{2,1,0:T(8,128)}) custom-call(s32[1]{0:T(128)} %bitcast.live_ref, s32[512]{0:T(512)} %bitcast.74, s32[512]{0:T(512)} %bitcast.76, s32[512,16,128]{2,1,0:T(8,128)} %bitcast.57, bf16[4096,256]{1,0:T(8,128)(2,1)} %pad_maximum_fusion.panel_ref), custom_call_target="tpu_custom_call" | custom-call | tf_op jit(solution)/shard_map/pallas_call | solution.py:128
  32.3 2.2 reduce_sum.9
  34.5 1.8 maximum_maximum_fusion
  36.5 24.8 %collective-permute-done.2 = f32[2,2,520,128]{3,2,1,0:T(8,128)} collective-permute-done((f32[2,2,520,128]{3,2,1,0:T(8,128)S(1)}, f32[2,2,520,128]{3,2,1,0:T(8,128)}, u32[]{:S(2)}, u32[]{:S(2)}) %collective-permute-start.2) | collective-permute-done | bytes 1064992 | tf_op jit(solution)/shard_map/ppermute | solution.py:168
  62.8 12.4 %collective-permute-done.3 = f32[2,520,128]{2,1,0:T(8,128)S(1)} collective-permute-done((f32[2,520,128]{2,1,0:T(8,128)S(1)}, f32[2,520,128]{2,1,0:T(8,128)S(1)}, u32[]{:S(2)}, u32[]{:S(2)}) %collective-permute-start.3) | collective-permute-done | bytes 532512 | tf_op jit(solution)/shard_map/ppermute | solution.py:168
  75.8 14.5 %collective-permute-done.4 = f32[520,128]{1,0:T(8,128)S(1)} collective-permute-done((f32[520,128]{1,0:T(8,128)S(1)}, f32[520,128]{1,0:T(8,128)S(1)}, u32[]{:S(2)}, u32[]{:S(2)}) %collective-permute-start.4) | collective-permute-done | bytes 266272 | tf_op jit(solution)/shard_map/ppermute | solution.py:168
  90.9 7.0 %collective-permute-done.5 = f32[512,128]{1,0:T(8,128)S(1)} collective-permute-done((f32[512,128]{1,0:T(8,128)S(1)}, f32[512,128]{1,0:T(8,128)S(1)}, u32[]{:S(2)}, u32[]{:S(2)}) %collective-permute-start.5) | collective-permute-done | bytes 262176 | tf_op jit(solution)/shard_map/ppermute | solution.py:168
  100.3 6.2 %collective-permute-done.6 = f32[512,128]{1,0:T(8,128)S(1)} collective-permute-done((f32[512,128]{1,0:T(8,128)S(1)}, f32[512,128]{1,0:T(8,128)S(1)}, u32[]{:S(2)}, u32[]{:S(2)}) %collective-permute-start.6) | collective-permute-done | bytes 262176 | tf_op jit(solution)/shard_map/ppermute | solution.py:168
  107.2 8.8 %collective-permute-done.11 = f32[512,128]{1,0:T(8,128)S(1)} collective-permute-done((f32[512,128]{1,0:T(8,128)S(1)}, f32[512,128]{1,0:T(8,128)S(1)}, u32[]{:S(2)}, u32[]{:S(2)}) %collective-permute-start.11) | collective-permute-done | bytes 262176 | tf_op jit(solution)/shard_map/ppermute | solution.py:168
  116.2 11.5 %collective-permute-done.12 = f32[2,512,128]{2,1,0:T(8,128)S(1)} collective-permute-done((f32[2,512,128]{2,1,0:T(8,128)S(1)}, f32[2,512,128]{2,1,0:T(8,128)S(1)}, u32[]{:S(2)}, u32[]{:S(2)}) %collective-permute-start.12) | collective-permute-done | bytes 524320 | tf_op jit(solution)/shard_map/ppermute | solution.py:168
  129.3 1.9 convolution_bitcast_fusion.1
  132.3 3.1 %collective-permute-start.7 = (f32[2,128,256]{1,2,0:T(8,128)S(1)}, f32[2,128,256]{1,2,0:T(8,128)S(1)}, u32[]{:S(2)}, u32[]{:S(2)}) collective-permute-start(f32[2,128,256]{1,2,0:T(8,128)S(1)} %pad_maximum_fusion.3), channel_id=1, source_target_pairs={{0,16},{16,0},{1,17},{17,1},{2,18},{18,2},{3,19},{19,3},{4,20},{20... | collective-permute-start | bytes 786440 | tf_op jit(solution)/shard_map/ppermute | solution.py:168
  138.4 12.4 %collective-permute-done.13 = f32[2,2,512,128]{3,2,0,1:T(8,128)S(1)} collective-permute-done((f32[2,2,512,128]{3,2,0,1:T(8,128)}, f32[2,2,512,128]{3,2,0,1:T(8,128)S(1)}, u32[]{:S(2)}, u32[]{:S(2)}) %collective-permute-start.13) | collective-permute-done | bytes 1048608 | tf_op jit(solution)/shard_map/ppermute | solution.py:168
  151.0 2.5 %copy.96 = f32[2,2,2,512,128]{3,2,1,0,4:T(2,128)} copy(f32[2,2,2,512,128]{4,3,0,1,2:T(8,128)S(1)} %maximum_select_fusion.1) | data formatting | bytes 4194304 | tf_op jit(solution)/shard_map/jit(_where)/select_n | solution.py:204
  153.5 3.1 %select_n.160 = f32[4096,128]{0,1:T(8,128)S(1)} reshape(f32[2,2,2,512,128]{3,2,1,0,4:T(2,128)} %copy.96) | data formatting | bytes 4194304 | tf_op jit(solution)/shard_map/jit(_where)/select_n | solution.py:204
  158.5 24.9 %shard_map.129 = f32[128,4096]{1,0:T(8,128)} custom-call(s32[1]{0:T(128)} %bitcast.live_ref, s32[512]{0:T(512)} %bitcast.75, s32[512]{0:T(512)} %bitcast.77, s32[512,16,128]{2,1,0:T(8,128)} %bitcast.58, bf16[256,4096]{1,0:T(8,128)(2,1)} %pad_maximum_fusion.1.lifted_ref), custom_call_target="tpu_custom_call" | custom-call | tf_op jit(solution)/shard_map/pallas_call | solution.py:128
  183.4 3.2 %reshape.236 = f32[2,2048,128]{1,0,2:T(2,128)S(1)} reshape(f32[4096,128]{0,1:T(8,128)} %bitcast.59) | data formatting | bytes 4194304 | tf_op jit(solution)/shard_map/reshape | solution.py:188
  186.6 3.1 %constant_dynamic-slice_fusion.1 = (f32[1,2048,128]{1,0,2:T(1,128)S(1)}, f32[1,2048,128]{1,0,2:T(1,128)}) fusion(f32[2,2048,128]{1,0,2:T(2,128)S(1)} %reshape.236, s32[]{:T(128)S(6)} %select_n.161, s32[]{:T(128)S(6)} %select_n.162), kind=kLoop, calls=%fused_computation.55 | loop fusion | bytes 4194312 | tf_op jit(solution)/shard_map/jit(dynamic_index_in_dim)/dynamic_slice | solution.py:192
  189.7 3.7 %copy.98 = f32[1,2048,128]{2,1,0:T(8,128)} copy(f32[1,2048,128]{1,0,2:T(1,128)} %get-tuple-element.40) | data formatting | bytes 2097152 | tf_op jit(solution)/shard_map/jit(dynamic_index_in_dim)/dynamic_slice | solution.py:193
  193.4 6.4 %collective-permute-start.14 = (f32[2048,128]{1,0:T(8,128)}, f32[2048,128]{1,0:T(8,128)S(1)}, u32[]{:S(2)}, u32[]{:S(2)}) collective-permute-start(f32[2048,128]{1,0:T(8,128)} %bitcast.72), channel_id=1, source_target_pairs={{0,16},{16,0},{1,17},{17,1},{2,18},{18,2},{3,19},{19,3},{4,20},{20... | collective-permute-start | bytes 3145736 | tf_op jit(solution)/shard_map/ppermute | solution.py:168
  200.9 7.8 %collective-permute-done.9 = f32[2,128,256]{1,2,0:T(8,128)S(1)} collective-permute-done((f32[2,128,256]{1,2,0:T(8,128)S(1)}, f32[2,128,256]{1,2,0:T(8,128)S(1)}, u32[]{:S(2)}, u32[]{:S(2)}) %collective-permute-start.9) | collective-permute-done | bytes 262176 | tf_op jit(solution)/shard_map/ppermute | solution.py:168
  210.2 13.4 %collective-permute-done.10 = f32[2,128,256]{1,2,0:T(8,128)S(1)} collective-permute-done((f32[2,128,256]{1,2,0:T(8,128)S(1)}, f32[2,128,256]{1,2,0:T(8,128)S(1)}, u32[]{:S(2)}, u32[]{:S(2)}) %collective-permute-start.10) | collective-permute-done | bytes 262176 | tf_op jit(solution)/shard_map/ppermute | solution.py:168
  (80 shorter events, 22.3 us)
Async XLA Ops:
  0.6 98.0 %copy-start = (f32[256,256]{1,0:T(8,128)S(1)}, f32[256,256]{1,0:T(8,128)}, u32[]{:S(2)}) copy-start(f32[256,256]{1,0:T(8,128)} %param.11) | copy-start | bytes 786436
  0.6 3.2 %collective-permute-start.1 = (f32[2048,128]{1,0:T(8,128)}, f32[2048,128]{1,0:T(8,128)S(1)}, u32[]{:S(2)}, u32[]{:S(2)}) collective-permute-start(f32[2048,128]{1,0:T(8,128)} %param.9), channel_id=1, source_target_pairs={{0,16},{16,0},{1,17},{17,1},{2,18},{18,2},{3,19},{19,3},{4,20},{20... | collective-permute-start | bytes 3145736 | tf_op jit(solution)/shard_map/ppermute | solution.py:168
  36.4 24.9 %collective-permute-start.2 = (f32[2,2,520,128]{3,2,1,0:T(8,128)S(1)}, f32[2,2,520,128]{3,2,1,0:T(8,128)}, u32[]{:S(2)}, u32[]{:S(2)}) collective-permute-start(f32[2,2,520,128]{3,2,1,0:T(8,128)S(1)} %dynamic-slice_bitcast_fusion), channel_id=1, source_target_pairs={{0,2},{2,0},{4,6},{6,4},{8,10},{10,8},{12,14},{14,12},{1,3},{3,1},... | collective-permute-start | bytes 3194888 | tf_op jit(solution)/shard_map/ppermute | solution.py:168
  62.6 12.8 %copy-start.7 = (f32[512,128]{1,0:T(8,128)S(1)}, f32[512,128]{1,0:T(8,128)}, u32[]{:S(2)}) copy-start(f32[512,128]{1,0:T(8,128)} %param.10) | copy-start | bytes 786436
  62.7 12.5 %collective-permute-start.3 = (f32[2,520,128]{2,1,0:T(8,128)S(1)}, f32[2,520,128]{2,1,0:T(8,128)S(1)}, u32[]{:S(2)}, u32[]{:S(2)}) collective-permute-start(f32[2,520,128]{2,1,0:T(8,128)S(1)} %dynamic-slice_bitcast_fusion.1), channel_id=1, source_target_pairs={{0,4},{2,6},{4,0},{6,2},{8,12},{10,14},{12,8},{14,10},{1,5},{3,7},... | collective-permute-start | bytes 1597448 | tf_op jit(solution)/shard_map/ppermute | solution.py:168
  75.2 22.8 %copy-start.10 = (f32[256,256]{1,0:T(8,128)S(1)}, f32[256,256]{1,0:T(8,128)}, u32[]{:S(2)}) copy-start(f32[256,256]{1,0:T(8,128)} %param.12) | copy-start | bytes 786436
  75.3 15.0 %collective-permute-start.4 = (f32[520,128]{1,0:T(8,128)S(1)}, f32[520,128]{1,0:T(8,128)S(1)}, u32[]{:S(2)}, u32[]{:S(2)}) collective-permute-start(f32[520,128]{1,0:T(8,128)S(1)} %dynamic-slice_bitcast_fusion.2), channel_id=1, source_target_pairs={{0,8},{2,10},{4,12},{6,14},{8,0},{10,2},{12,4},{14,6},{1,9},{3,11}... | collective-permute-start | bytes 798728 | tf_op jit(solution)/shard_map/ppermute | solution.py:168
  75.4 15.4 %collective-permute-start = (f32[512,128]{1,0:T(8,128)S(1)}, f32[512,128]{1,0:T(8,128)S(1)}, u32[]{:S(2)}, u32[]{:S(2)}) collective-permute-start(f32[512,128]{1,0:T(8,128)S(1)} %copy-done.7), channel_id=1, source_target_pairs={{0,1},{1,0},{2,3},{3,2},{4,5},{5,4},{6,7},{7,6},{8,9},{9,8},{10,11... | collective-permute-start | bytes 786440 | tf_op jit(solution)/shard_map/ppermute | solution.py:168
  75.8 22.9 %copy-start.11 = (f32[512,128]{1,0:T(8,128)S(1)}, f32[512,128]{1,0:T(8,128)}, u32[]{:S(2)}) copy-start(f32[512,128]{1,0:T(8,128)} %param.13) | copy-start | bytes 786436
  90.5 7.4 %collective-permute-start.5 = (f32[512,128]{1,0:T(8,128)S(1)}, f32[512,128]{1,0:T(8,128)S(1)}, u32[]{:S(2)}, u32[]{:S(2)}) collective-permute-start(f32[512,128]{1,0:T(8,128)S(1)} %slice_divide_fusion), channel_id=1, source_target_pairs={{0,1},{1,0},{2,3},{3,2},{4,5},{5,4},{6,7},{7,6},{8,9},{9,8},{10,11... | collective-permute-start | bytes 786440 | tf_op jit(solution)/shard_map/ppermute | solution.py:168
  100.0 6.5 %collective-permute-start.6 = (f32[512,128]{1,0:T(8,128)S(1)}, f32[512,128]{1,0:T(8,128)S(1)}, u32[]{:S(2)}, u32[]{:S(2)}) collective-permute-start(f32[512,128]{1,0:T(8,128)S(1)} %get-tuple-element.53), channel_id=1, source_target_pairs={{0,1},{1,0},{2,3},{3,2},{4,5},{5,4},{6,7},{7,6},{8,9},{9,8},{10,11... | collective-permute-start | bytes 786440 | tf_op jit(solution)/shard_map/ppermute | solution.py:168
  106.5 24.7 %copy-start.1 = (f32[512,128]{1,0:T(8,128)}, f32[512,128]{1,0:T(8,128)S(1)}, u32[]{:S(2)}) copy-start(f32[512,128]{1,0:T(8,128)S(1)} %get-tuple-element.45) | copy-start | bytes 786436
  106.5 24.7 %copy-start.3 = (f32[512,128]{1,0:T(8,128)}, f32[512,128]{1,0:T(8,128)S(1)}, u32[]{:S(2)}) copy-start(f32[512,128]{1,0:T(8,128)S(1)} %get-tuple-element.46) | copy-start | bytes 786436
  107.1 8.9 %collective-permute-start.11 = (f32[512,128]{1,0:T(8,128)S(1)}, f32[512,128]{1,0:T(8,128)S(1)}, u32[]{:S(2)}, u32[]{:S(2)}) collective-permute-start(f32[512,128]{1,0:T(8,128)S(1)} %convolution_divide_fusion), channel_id=1, source_target_pairs={{0,8},{2,10},{4,12},{6,14},{8,0},{10,2},{12,4},{14,6},{1,9},{3,11}... | collective-permute-start | bytes 786440 | tf_op jit(solution)/shard_map/ppermute | solution.py:168
  116.1 11.6 %collective-permute-start.12 = (f32[2,512,128]{2,1,0:T(8,128)S(1)}, f32[2,512,128]{2,1,0:T(8,128)S(1)}, u32[]{:S(2)}, u32[]{:S(2)}) collective-permute-start(f32[2,512,128]{2,1,0:T(8,128)S(1)} %maximum_select_fusion.5), channel_id=1, source_target_pairs={{0,4},{2,6},{4,0},{6,2},{8,12},{10,14},{12,8},{14,10},{1,5},{3,7},... | collective-permute-start | bytes 1572872 | tf_op jit(solution)/shard_map/ppermute | solution.py:168
  128.7 22.1 %collective-permute-start.13 = (f32[2,2,512,128]{3,2,0,1:T(8,128)}, f32[2,2,512,128]{3,2,0,1:T(8,128)S(1)}, u32[]{:S(2)}, u32[]{:S(2)}) collective-permute-start(f32[2,2,512,128]{3,2,0,1:T(8,128)} %maximum_select_fusion.3), channel_id=1, source_target_pairs={{0,2},{2,0},{4,6},{6,4},{8,10},{10,8},{12,14},{14,12},{1,3},{3,1},... | collective-permute-start | bytes 3145736 | tf_op jit(solution)/shard_map/ppermute | solution.py:168
  132.3 4.3 %collective-permute-start.7 = (f32[2,128,256]{1,2,0:T(8,128)S(1)}, f32[2,128,256]{1,2,0:T(8,128)S(1)}, u32[]{:S(2)}, u32[]{:S(2)}) collective-permute-start(f32[2,128,256]{1,2,0:T(8,128)S(1)} %pad_maximum_fusion.3), channel_id=1, source_target_pairs={{0,16},{16,0},{1,17},{17,1},{2,18},{18,2},{3,19},{19,3},{4,20},{20... | collective-permute-start | bytes 786440 | tf_op jit(solution)/shard_map/ppermute | solution.py:168
  136.6 14.3 %copy-start.8 = (f32[2,128,256]{1,2,0:T(8,128)}, f32[2,128,256]{1,2,0:T(8,128)S(1)}, u32[]{:S(2)}) copy-start(f32[2,128,256]{1,2,0:T(8,128)S(1)} %collective-permute-done.7) | copy-start | bytes 786436
  137.4 62.5 %collective-permute-start.8 = (f32[2,128,256]{1,2,0:T(8,128)}, f32[2,128,256]{1,2,0:T(8,128)}, u32[]{:S(2)}, u32[]{:S(2)}) collective-permute-start(f32[2,128,256]{1,2,0:T(8,128)} %fusion.28), channel_id=1, source_target_pairs={{0,2},{2,0},{4,6},{6,4},{8,10},{10,8},{12,14},{14,12},{1,3},{3,1},... | collective-permute-start | bytes 786440 | tf_op jit(solution)/shard_map/ppermute | solution.py:168
  189.7 19.2 %copy-start.2 = (f32[512,128]{1,0:T(8,128)S(1)}, f32[512,128]{1,0:T(8,128)}, u32[]{:S(2)}) copy-start(f32[512,128]{1,0:T(8,128)} %copy-done.1) | copy-start | bytes 786436
  189.7 19.2 %copy-start.4 = (f32[512,128]{1,0:T(8,128)S(1)}, f32[512,128]{1,0:T(8,128)}, u32[]{:S(2)}) copy-start(f32[512,128]{1,0:T(8,128)} %copy-done.3) | copy-start | bytes 786436
  193.4 32.5 %collective-permute-start.14 = (f32[2048,128]{1,0:T(8,128)}, f32[2048,128]{1,0:T(8,128)S(1)}, u32[]{:S(2)}, u32[]{:S(2)}) collective-permute-start(f32[2048,128]{1,0:T(8,128)} %bitcast.72), channel_id=1, source_target_pairs={{0,16},{16,0},{1,17},{17,1},{2,18},{18,2},{3,19},{19,3},{4,20},{20... | collective-permute-start | bytes 3145736 | tf_op jit(solution)/shard_map/ppermute | solution.py:168
  200.9 7.9 %collective-permute-start.9 = (f32[2,128,256]{1,2,0:T(8,128)S(1)}, f32[2,128,256]{1,2,0:T(8,128)S(1)}, u32[]{:S(2)}, u32[]{:S(2)}) collective-permute-start(f32[2,128,256]{1,2,0:T(8,128)S(1)} %fusion.32), channel_id=1, source_target_pairs={{0,4},{2,6},{4,0},{6,2},{8,12},{10,14},{12,8},{14,10},{1,5},{3,7},... | collective-permute-start | bytes 786440 | tf_op jit(solution)/shard_map/ppermute | solution.py:168
  208.8 14.8 %collective-permute-start.10 = (f32[2,128,256]{1,2,0:T(8,128)S(1)}, f32[2,128,256]{1,2,0:T(8,128)S(1)}, u32[]{:S(2)}, u32[]{:S(2)}) collective-permute-start(f32[2,128,256]{1,2,0:T(8,128)S(1)} %add.101), channel_id=1, source_target_pairs={{0,8},{2,10},{4,12},{6,14},{8,0},{10,2},{12,4},{14,6},{1,9},{3,11}... | collective-permute-start | bytes 786440 | tf_op jit(solution)/shard_map/ppermute | solution.py:168
  (3 other events, 26.4 us)

commit v6 on v5

--- a/solution.py
+++ b/solution.py
@@ -182,12 +182,14 @@
     )
 
 
-def halving_scatter(values, axis):
+def halving_steps(values, axis, order):
     bits = axis_bits(axis)
     chunk = values.shape[0] >> bits
     data = values.reshape((2,) * bits + (chunk,) + values.shape[1:])
-    for bit in range(bits):
-        position = bits - 1 - bit
+    remaining = list(reversed(range(bits)))
+    for bit in order:
+        position = remaining.index(bit)
+        remaining.remove(bit)
         mine = axis_bit(axis, bit)
         keep = lax.dynamic_index_in_dim(data, mine, position, keepdims=False)
         send = lax.dynamic_index_in_dim(data, 1 - mine, position, keepdims=False)
@@ -195,16 +197,48 @@
     return data
 
 
-def doubling_gather(values, axis):
-    bits = axis_bits(axis)
+def doubling_steps(values, axis, order):
     data = values
-    for stacked, bit in enumerate(reversed(range(bits))):
+    present = []
+    for bit in order:
+        position = sum(1 for other in present if other > bit)
+        present.insert(position, bit)
         other = exchange(data, axis, bit)
         first = axis_bit(axis, bit) == 0
         data = jnp.where(
-            first, jnp.stack([data, other], axis=stacked), jnp.stack([other, data], axis=stacked)
+            first, jnp.stack([data, other], axis=position), jnp.stack([other, data], axis=position)
         )
-    return data.reshape((-1,) + values.shape[1:])
+    return data
+
+
+def bit_orders(axis):
+    bits = axis_bits(axis)
+    ascending = list(range(bits))
+    if bits < 2:
+        return [ascending]
+    return [ascending, [1, 0] + ascending[2:]]
+
+
+def halving_scatter(values, axis):
+    orders = bit_orders(axis)
+    bits = axis_bits(axis)
+    shaped = values.reshape((1 << bits, -1) + values.shape[1:])
+    pieces = jnp.split(shaped, len(orders), axis=1)
+    results = [
+        halving_steps(piece.reshape((-1,) + values.shape[1:]), axis, order)
+        for piece, order in zip(pieces, orders)
+    ]
+    return jnp.concatenate(results, axis=0)
+
+
+def doubling_gather(values, axis):
+    orders = [list(reversed(order)) for order in bit_orders(axis)]
+    pieces = jnp.split(values, len(orders), axis=0)
+    results = [doubling_steps(piece, axis, order) for piece, order in zip(pieces, orders)]
+    stacked = jnp.concatenate(
+        [result.reshape((-1,) + result.shape[-2:]) for result in results], axis=1
+    )
+    return stacked.reshape((-1,) + values.shape[1:])
 
 
 def butterfly_sum(values, axes):
@@ -218,7 +252,7 @@
     width = row_totals.shape[1]
     chunk_rows = row_totals.shape[0] // test_count
     count_rows = chunk_rows // width
-    padded = -(-count_rows // 8) * 8
+    padded = -(-count_rows // 16) * 16
     pieces = [
         row_totals.reshape(test_count, chunk_rows, width),
         row_counts.reshape(test_count, count_rows, width),

time: 228 us -> 193 us (0.85)
  waiting for transfers between devices: 122 us -> 83.4 us
  starting transfers between devices: 13.3 us -> 18.8 us
    ppermute x15 -> x21, waiting for transfers between devices: 122 us -> 83.4 us  [exchange(): return lax.ppermute(values, axis, [(i, i ^ 1 << bit) for i in range(count)])]
    ppermute x15 -> x21, starting transfers between devices: 13.3 us -> 18.8 us  [exchange(): return lax.ppermute(values, axis, [(i, i ^ 1 << bit) for i in range(count)])]
    select_n x2, local copies, waits for them, and re-layouts: 5.52 us -> 0.14 us  [doubling_steps(): jnp.where(first, jnp.stack([data, other], axis=position), jnp.stack([othe...]
    reshape x1 -> x2, local copies, waits for them, and re-layouts: 3.21 us -> 5.13 us  [the longest x1 3.21 us: halving_scatter(): shaped = values.reshape((1 << bits, -1) + values.shape[1:])]
  transfers between devices with their start and end apart: 15 -> 21, of which waited for: 12 -> 15; matrix products, arithmetic and copies ran while one was open for 12% -> 14% of each run, Pallas kernels for 11% -> 13%
where the time goes in v6:
time: 193 us; the launch traced here: 192 us
  waiting for transfers between devices  83.4 us (43%)
  Pallas kernels  49.7 us (26%)
  starting transfers between devices  18.8 us (10%)
  local copies, waits for them, and re-layouts  16.5 us (9%)
  other arithmetic  16.3 us (8%)
  matrix products  5.79 us (3%)
    ppermute x21, waiting for transfers between devices, exchange(): return lax.ppermute(values, axis, [(i, i ^ 1 << bit) for i in range(count)])  83.4 us
    pallas_call x2, Pallas kernels, slot_pallas(): pl.pallas_call(kernel, grid_spec=grid_spec, out_shape=out_shapes, compile...  49.7 us
    ppermute x21, starting transfers between devices, exchange(): return lax.ppermute(values, axis, [(i, i ^ 1 << bit) for i in range(count)])  18.8 us
    dynamic_slice x2, local copies, waits for them, and re-layouts, halving_steps(): keep = lax.dynamic_index_in_dim(data, mine, position, keepdims=False)  3.87 us
  transfers between devices with their start and end apart: 21, of which 15 were waited for; matrix products, arithmetic and copies ran while one was open for 14% of the time, Pallas kernels for 13%

profile of v6, /device:TPU:31, one launch (start us, length us, event | category | flops | bytes accessed | tf_op | source)
XLA Modules:
  0.0 192.2 jit_solution(16102646777612706858)
XLA Ops:
  2.1 1.8 collective-permute-done.1
  3.9 1.7 maximum_select_fusion
  7.6 24.7 %shard_map.128 = (f32[4096,128]{1,0:T(8,128)}, s32[32,128,128]{2,1,0:T(8,128)}) custom-call(s32[1]{0:T(128)} %bitcast.live_ref, s32[512]{0:T(512)} %bitcast.124, s32[512]{0:T(512)} %bitcast.126, s32[512,16,128]{2,1,0:T(8,128)} %bitcast.97, bf16[4096,256]{1,0:T(8,128)(2,1)} %pad_maximum_fusion.panel_ref), custom_call_target="tpu_custom_call" | custom-call | tf_op jit(solution)/shard_map/pallas_call | solution.py:128
  32.3 2.4 %reduce_sum.9 = s32[32,128]{1,0:T(8,128)S(1)} reduce(s32[32,128,128]{2,1,0:T(8,128)} %get-tuple-element.8, s32[]{:T(128)} %constant.70.clone.1), dimensions={2}, to_apply=%region_0.1 | reduce | flops 520192 | bytes 2113540 | tf_op jit(solution)/shard_map/reduce_sum | solution.py:144
  37.3 12.1 %collective-permute-done.2 = f32[2,2,264,128]{3,2,1,0:T(8,128)S(1)} collective-permute-done((f32[2,2,264,128]{3,2,1,0:T(8,128)S(1)}, f32[2,2,264,128]{3,2,1,0:T(8,128)S(1)}, u32[]{:S(2)}, u32[]{:S(2)}) %collective-permute-start.2) | collective-permute-done | bytes 540704 | tf_op jit(solution)/shard_map/ppermute | solution.py:168
  51.9 5.6 %collective-permute-done.3 = f32[2,264,128]{2,1,0:T(8,128)S(1)} collective-permute-done((f32[2,264,128]{2,1,0:T(8,128)S(1)}, f32[2,264,128]{2,1,0:T(8,128)S(1)}, u32[]{:S(2)}, u32[]{:S(2)}) %collective-permute-start.3) | collective-permute-done | bytes 270368 | tf_op jit(solution)/shard_map/ppermute | solution.py:168
  58.3 1.8 collective-permute-start.7
  60.1 9.7 %collective-permute-done.4 = f32[264,128]{1,0:T(8,128)S(1)} collective-permute-done((f32[264,128]{1,0:T(8,128)S(1)}, f32[264,128]{1,0:T(8,128)S(1)}, u32[]{:S(2)}, u32[]{:S(2)}) %collective-permute-start.4) | collective-permute-done | bytes 135200 | tf_op jit(solution)/shard_map/ppermute | solution.py:168
  69.8 2.9 %collective-permute-done.7 = f32[264,128]{1,0:T(8,128)S(1)} collective-permute-done((f32[264,128]{1,0:T(8,128)S(1)}, f32[264,128]{1,0:T(8,128)S(1)}, u32[]{:S(2)}, u32[]{:S(2)}) %collective-permute-start.7) | collective-permute-done | bytes 135200 | tf_op jit(solution)/shard_map/ppermute | solution.py:168
  73.2 7.1 %collective-permute-done.8 = f32[512,128]{1,0:T(8,128)S(1)} collective-permute-done((f32[512,128]{1,0:T(8,128)S(1)}, f32[512,128]{1,0:T(8,128)S(1)}, u32[]{:S(2)}, u32[]{:S(2)}) %collective-permute-start.8) | collective-permute-done | bytes 262176 | tf_op jit(solution)/shard_map/ppermute | solution.py:168
  82.5 6.3 %collective-permute-done.9 = f32[512,128]{1,0:T(8,128)S(1)} collective-permute-done((f32[512,128]{1,0:T(8,128)S(1)}, f32[512,128]{1,0:T(8,128)S(1)}, u32[]{:S(2)}, u32[]{:S(2)}) %collective-permute-start.9) | collective-permute-done | bytes 262176 | tf_op jit(solution)/shard_map/ppermute | solution.py:168
  91.7 2.4 %collective-permute-start.17 = (f32[256,128]{1,0:T(8,128)S(1)}, f32[256,128]{1,0:T(8,128)S(1)}, u32[]{:S(2)}, u32[]{:S(2)}) collective-permute-start(f32[256,128]{1,0:T(8,128)S(1)} %get-tuple-element.47), channel_id=1, source_target_pairs={{0,8},{2,10},{4,12},{6,14},{8,0},{10,2},{12,4},{14,6},{1,9},{3,11}... | collective-permute-start | bytes 393224 | tf_op jit(solution)/shard_map/ppermute | solution.py:168
  94.1 2.8 %collective-permute-start.10 = (f32[2,128,256]{1,2,0:T(8,128)S(1)}, f32[2,128,256]{1,2,0:T(8,128)S(1)}, u32[]{:S(2)}, u32[]{:S(2)}) collective-permute-start(f32[2,128,256]{1,2,0:T(8,128)S(1)} %pad_maximum_fusion.6), channel_id=1, source_target_pairs={{0,16},{16,0},{1,17},{17,1},{2,18},{18,2},{3,19},{19,3},{4,20},{20... | collective-permute-start | bytes 786440 | tf_op jit(solution)/shard_map/ppermute | solution.py:168
  98.3 2.6 %collective-permute-done.17 = f32[256,128]{1,0:T(8,128)S(1)} collective-permute-done((f32[256,128]{1,0:T(8,128)S(1)}, f32[256,128]{1,0:T(8,128)S(1)}, u32[]{:S(2)}, u32[]{:S(2)}) %collective-permute-start.17) | collective-permute-done | bytes 131104 | tf_op jit(solution)/shard_map/ppermute | solution.py:168
  102.5 3.3 %collective-permute-done.15 = f32[2,256,128]{2,1,0:T(8,128)S(1)} collective-permute-done((f32[2,256,128]{2,1,0:T(8,128)S(1)}, f32[2,256,128]{2,1,0:T(8,128)S(1)}, u32[]{:S(2)}, u32[]{:S(2)}) %collective-permute-start.15) | collective-permute-done | bytes 262176 | tf_op jit(solution)/shard_map/ppermute | solution.py:168
  109.5 8.9 %collective-permute-done.16 = f32[2,2,256,128]{3,2,0,1:T(8,128)S(1)} collective-permute-done((f32[2,2,256,128]{3,2,0,1:T(8,128)S(1)}, f32[2,2,256,128]{3,2,0,1:T(8,128)S(1)}, u32[]{:S(2)}, u32[]{:S(2)}) %collective-permute-start.16) | collective-permute-done | bytes 524320 | tf_op jit(solution)/shard_map/ppermute | solution.py:168
  120.3 1.9 copy.80
  124.1 24.9 %shard_map.129 = f32[128,4096]{1,0:T(8,128)} custom-call(s32[1]{0:T(128)} %bitcast.live_ref, s32[512]{0:T(512)} %bitcast.125, s32[512]{0:T(512)} %bitcast.127, s32[512,16,128]{2,1,0:T(8,128)} %bitcast.98, bf16[256,4096]{1,0:T(8,128)(2,1)} %pad_maximum_fusion.2.lifted_ref), custom_call_target="tpu_custom_call" | custom-call | tf_op jit(solution)/shard_map/pallas_call | solution.py:128
  149.1 3.2 %reshape.419 = f32[2,2048,128]{1,0,2:T(2,128)S(1)} reshape(f32[4096,128]{0,1:T(8,128)} %bitcast.100) | data formatting | bytes 4194304 | tf_op jit(solution)/shard_map/reshape | solution.py:225
  152.3 3.1 %constant_dynamic-slice_fusion.1 = (f32[1,2048,128]{1,0,2:T(1,128)S(1)}, f32[1,2048,128]{1,0,2:T(1,128)}) fusion(f32[2,2048,128]{1,0,2:T(2,128)S(1)} %reshape.419, s32[]{:T(128)S(6)} %select_n.226, s32[]{:T(128)S(6)} %select_n.227), kind=kLoop, calls=%fused_computation.71 | loop fusion | bytes 4194312 | tf_op jit(solution)/shard_map/jit(dynamic_index_in_dim)/dynamic_slice | solution.py:194
  155.4 3.7 %copy.74 = f32[1,2048,128]{2,1,0:T(8,128)} copy(f32[1,2048,128]{1,0,2:T(1,128)} %get-tuple-element.30) | data formatting | bytes 2097152 | tf_op jit(solution)/shard_map/jit(dynamic_index_in_dim)/dynamic_slice | solution.py:195
  159.1 4.7 %collective-permute-start.20 = (f32[2048,128]{1,0:T(8,128)}, f32[2048,128]{1,0:T(8,128)S(1)}, u32[]{:S(2)}, u32[]{:S(2)}) collective-permute-start(f32[2048,128]{1,0:T(8,128)} %bitcast.116), channel_id=1, source_target_pairs={{0,16},{16,0},{1,17},{17,1},{2,18},{18,2},{3,19},{19,3},{4,20},{20... | collective-permute-start | bytes 3145736 | tf_op jit(solution)/shard_map/ppermute | solution.py:168
  164.9 7.8 %collective-permute-done.12 = f32[2,128,256]{1,2,0:T(8,128)S(1)} collective-permute-done((f32[2,128,256]{1,2,0:T(8,128)S(1)}, f32[2,128,256]{1,2,0:T(8,128)S(1)}, u32[]{:S(2)}, u32[]{:S(2)}) %collective-permute-start.12) | collective-permute-done | bytes 262176 | tf_op jit(solution)/shard_map/ppermute | solution.py:168
  175.5 13.0 %collective-permute-done.13 = f32[2,128,256]{1,2,0:T(8,128)} collective-permute-done((f32[2,128,256]{1,2,0:T(8,128)}, f32[2,128,256]{1,2,0:T(8,128)}, u32[]{:S(2)}, u32[]{:S(2)}) %collective-permute-start.13) | collective-permute-done | bytes 262176 | tf_op jit(solution)/shard_map/ppermute | solution.py:168
  (111 shorter events, 31.7 us)
Async XLA Ops:
  0.6 80.3 %copy-start = (f32[256,256]{1,0:T(8,128)S(1)}, f32[256,256]{1,0:T(8,128)}, u32[]{:S(2)}) copy-start(f32[256,256]{1,0:T(8,128)} %param.11) | copy-start | bytes 786436
  0.6 3.2 %collective-permute-start.1 = (f32[2048,128]{1,0:T(8,128)}, f32[2048,128]{1,0:T(8,128)S(1)}, u32[]{:S(2)}, u32[]{:S(2)}) collective-permute-start(f32[2048,128]{1,0:T(8,128)} %param.9), channel_id=1, source_target_pairs={{0,16},{16,0},{1,17},{17,1},{2,18},{18,2},{3,19},{19,3},{4,20},{20... | collective-permute-start | bytes 3145736 | tf_op jit(solution)/shard_map/ppermute | solution.py:168
  35.9 13.5 %collective-permute-start.2 = (f32[2,2,264,128]{3,2,1,0:T(8,128)S(1)}, f32[2,2,264,128]{3,2,1,0:T(8,128)S(1)}, u32[]{:S(2)}, u32[]{:S(2)}) collective-permute-start(f32[2,2,264,128]{3,2,1,0:T(8,128)S(1)} %dynamic-slice_bitcast_fusion.1), channel_id=1, source_target_pairs={{0,2},{2,0},{4,6},{6,4},{8,10},{10,8},{12,14},{14,12},{1,3},{3,1},... | collective-permute-start | bytes 1622024 | tf_op jit(solution)/shard_map/ppermute | solution.py:168
  37.1 13.9 %collective-permute-start.5 = (f32[2,2,264,128]{3,2,1,0:T(8,128)}, f32[2,2,264,128]{3,2,1,0:T(8,128)S(1)}, u32[]{:S(2)}, u32[]{:S(2)}) collective-permute-start(f32[2,2,264,128]{3,2,1,0:T(8,128)} %dynamic-slice_bitcast_fusion), channel_id=1, source_target_pairs={{0,4},{2,6},{4,0},{6,2},{8,12},{10,14},{12,8},{14,10},{1,5},{3,7},... | collective-permute-start | bytes 1622024 | tf_op jit(solution)/shard_map/ppermute | solution.py:168
  37.1 36.1 %collective-permute-start = (f32[512,128]{1,0:T(8,128)S(1)}, f32[512,128]{1,0:T(8,128)S(1)}, u32[]{:S(2)}, u32[]{:S(2)}) collective-permute-start(f32[512,128]{1,0:T(8,128)S(1)} %copy-done.9), channel_id=1, source_target_pairs={{0,1},{1,0},{2,3},{3,2},{4,5},{5,4},{6,7},{7,6},{8,9},{9,8},{10,11... | collective-permute-start | bytes 786440 | tf_op jit(solution)/shard_map/ppermute | solution.py:168
  50.6 6.9 %collective-permute-start.3 = (f32[2,264,128]{2,1,0:T(8,128)S(1)}, f32[2,264,128]{2,1,0:T(8,128)S(1)}, u32[]{:S(2)}, u32[]{:S(2)}) collective-permute-start(f32[2,264,128]{2,1,0:T(8,128)S(1)} %dynamic-slice_bitcast_fusion.3), channel_id=1, source_target_pairs={{0,4},{2,6},{4,0},{6,2},{8,12},{10,14},{12,8},{14,10},{1,5},{3,7},... | collective-permute-start | bytes 811016 | tf_op jit(solution)/shard_map/ppermute | solution.py:168
  51.1 7.1 %collective-permute-start.6 = (f32[2,264,128]{2,1,0:T(8,128)S(1)}, f32[2,264,128]{2,1,0:T(8,128)S(1)}, u32[]{:S(2)}, u32[]{:S(2)}) collective-permute-start(f32[2,264,128]{2,1,0:T(8,128)S(1)} %dynamic-slice_bitcast_fusion.2), channel_id=1, source_target_pairs={{0,2},{2,0},{4,6},{6,4},{8,10},{10,8},{12,14},{14,12},{1,3},{3,1},... | collective-permute-start | bytes 811016 | tf_op jit(solution)/shard_map/ppermute | solution.py:168
  57.5 22.8 %copy-start.12 = (f32[256,256]{1,0:T(8,128)S(1)}, f32[256,256]{1,0:T(8,128)}, u32[]{:S(2)}) copy-start(f32[256,256]{1,0:T(8,128)} %param.12) | copy-start | bytes 786436
  57.6 12.3 %collective-permute-start.4 = (f32[264,128]{1,0:T(8,128)S(1)}, f32[264,128]{1,0:T(8,128)S(1)}, u32[]{:S(2)}, u32[]{:S(2)}) collective-permute-start(f32[264,128]{1,0:T(8,128)S(1)} %dynamic-slice_bitcast_fusion.5), channel_id=1, source_target_pairs={{0,8},{2,10},{4,12},{6,14},{8,0},{10,2},{12,4},{14,6},{1,9},{3,11}... | collective-permute-start | bytes 405512 | tf_op jit(solution)/shard_map/ppermute | solution.py:168
  58.3 22.7 %copy-start.13 = (f32[512,128]{1,0:T(8,128)S(1)}, f32[512,128]{1,0:T(8,128)}, u32[]{:S(2)}) copy-start(f32[512,128]{1,0:T(8,128)} %param.13) | copy-start | bytes 786436
  58.3 14.4 %collective-permute-start.7 = (f32[264,128]{1,0:T(8,128)S(1)}, f32[264,128]{1,0:T(8,128)S(1)}, u32[]{:S(2)}, u32[]{:S(2)}) collective-permute-start(f32[264,128]{1,0:T(8,128)S(1)} %dynamic-slice_bitcast_fusion.4), channel_id=1, source_target_pairs={{0,8},{2,10},{4,12},{6,14},{8,0},{10,2},{12,4},{14,6},{1,9},{3,11}... | collective-permute-start | bytes 405512 | tf_op jit(solution)/shard_map/ppermute | solution.py:168
  72.9 7.4 %collective-permute-start.8 = (f32[512,128]{1,0:T(8,128)S(1)}, f32[512,128]{1,0:T(8,128)S(1)}, u32[]{:S(2)}, u32[]{:S(2)}) collective-permute-start(f32[512,128]{1,0:T(8,128)S(1)} %fusion.10), channel_id=1, source_target_pairs={{0,1},{1,0},{2,3},{3,2},{4,5},{5,4},{6,7},{7,6},{8,9},{9,8},{10,11... | collective-permute-start | bytes 786440 | tf_op jit(solution)/shard_map/ppermute | solution.py:168
  82.3 6.5 %collective-permute-start.9 = (f32[512,128]{1,0:T(8,128)S(1)}, f32[512,128]{1,0:T(8,128)S(1)}, u32[]{:S(2)}, u32[]{:S(2)}) collective-permute-start(f32[512,128]{1,0:T(8,128)S(1)} %get-tuple-element.51), channel_id=1, source_target_pairs={{0,1},{1,0},{2,3},{3,2},{4,5},{5,4},{6,7},{7,6},{8,9},{9,8},{10,11... | collective-permute-start | bytes 786440 | tf_op jit(solution)/shard_map/ppermute | solution.py:168
  90.5 7.6 %collective-permute-start.14 = (f32[256,128]{1,0:T(8,128)S(1)}, f32[256,128]{1,0:T(8,128)S(1)}, u32[]{:S(2)}, u32[]{:S(2)}) collective-permute-start(f32[256,128]{1,0:T(8,128)S(1)} %get-tuple-element.48), channel_id=1, source_target_pairs={{0,8},{2,10},{4,12},{6,14},{8,0},{10,2},{12,4},{14,6},{1,9},{3,11}... | collective-permute-start | bytes 393224 | tf_op jit(solution)/shard_map/ppermute | solution.py:168
  91.7 9.3 %collective-permute-start.17 = (f32[256,128]{1,0:T(8,128)S(1)}, f32[256,128]{1,0:T(8,128)S(1)}, u32[]{:S(2)}, u32[]{:S(2)}) collective-permute-start(f32[256,128]{1,0:T(8,128)S(1)} %get-tuple-element.47), channel_id=1, source_target_pairs={{0,8},{2,10},{4,12},{6,14},{8,0},{10,2},{12,4},{14,6},{1,9},{3,11}... | collective-permute-start | bytes 393224 | tf_op jit(solution)/shard_map/ppermute | solution.py:168
  94.1 13.2 %collective-permute-start.10 = (f32[2,128,256]{1,2,0:T(8,128)S(1)}, f32[2,128,256]{1,2,0:T(8,128)S(1)}, u32[]{:S(2)}, u32[]{:S(2)}) collective-permute-start(f32[2,128,256]{1,2,0:T(8,128)S(1)} %pad_maximum_fusion.6), channel_id=1, source_target_pairs={{0,16},{16,0},{1,17},{17,1},{2,18},{18,2},{3,19},{19,3},{4,20},{20... | collective-permute-start | bytes 786440 | tf_op jit(solution)/shard_map/ppermute | solution.py:168
  98.2 7.5 %collective-permute-start.15 = (f32[2,256,128]{2,1,0:T(8,128)S(1)}, f32[2,256,128]{2,1,0:T(8,128)S(1)}, u32[]{:S(2)}, u32[]{:S(2)}) collective-permute-start(f32[2,256,128]{2,1,0:T(8,128)S(1)} %maximum_select_fusion.7), channel_id=1, source_target_pairs={{0,4},{2,6},{4,0},{6,2},{8,12},{10,14},{12,8},{14,10},{1,5},{3,7},... | collective-permute-start | bytes 786440 | tf_op jit(solution)/shard_map/ppermute | solution.py:168
  101.0 6.2 %collective-permute-start.18 = (f32[2,256,128]{2,1,0:T(8,128)S(1)}, f32[2,256,128]{2,1,0:T(8,128)S(1)}, u32[]{:S(2)}, u32[]{:S(2)}) collective-permute-start(f32[2,256,128]{2,1,0:T(8,128)S(1)} %maximum_select_fusion.9), channel_id=1, source_target_pairs={{0,2},{2,0},{4,6},{6,4},{8,10},{10,8},{12,14},{14,12},{1,3},{3,1},... | collective-permute-start | bytes 786440 | tf_op jit(solution)/shard_map/ppermute | solution.py:168
  105.8 12.7 %collective-permute-start.16 = (f32[2,2,256,128]{3,2,0,1:T(8,128)S(1)}, f32[2,2,256,128]{3,2,0,1:T(8,128)S(1)}, u32[]{:S(2)}, u32[]{:S(2)}) collective-permute-start(f32[2,2,256,128]{3,2,0,1:T(8,128)S(1)} %maximum_select_fusion.4), channel_id=1, source_target_pairs={{0,2},{2,0},{4,6},{6,4},{8,10},{10,8},{12,14},{14,12},{1,3},{3,1},... | collective-permute-start | bytes 1572872 | tf_op jit(solution)/shard_map/ppermute | solution.py:168
  107.3 11.3 %collective-permute-start.19 = (f32[2,2,256,128]{3,2,0,1:T(8,128)S(1)}, f32[2,2,256,128]{3,2,0,1:T(8,128)S(1)}, u32[]{:S(2)}, u32[]{:S(2)}) collective-permute-start(f32[2,2,256,128]{3,2,0,1:T(8,128)S(1)} %maximum_select_fusion.6), channel_id=1, source_target_pairs={{0,4},{2,6},{4,0},{6,2},{8,12},{10,14},{12,8},{14,10},{1,5},{3,7},... | collective-permute-start | bytes 1572872 | tf_op jit(solution)/shard_map/ppermute | solution.py:168
  108.1 55.7 %collective-permute-start.11 = (f32[2,128,256]{1,2,0:T(8,128)}, f32[2,128,256]{1,2,0:T(8,128)}, u32[]{:S(2)}, u32[]{:S(2)}) collective-permute-start(f32[2,128,256]{1,2,0:T(8,128)} %fusion.31), channel_id=1, source_target_pairs={{0,2},{2,0},{4,6},{6,4},{8,10},{10,8},{12,14},{14,12},{1,3},{3,1},... | collective-permute-start | bytes 786440 | tf_op jit(solution)/shard_map/ppermute | solution.py:168
  159.1 32.1 %collective-permute-start.20 = (f32[2048,128]{1,0:T(8,128)}, f32[2048,128]{1,0:T(8,128)S(1)}, u32[]{:S(2)}, u32[]{:S(2)}) collective-permute-start(f32[2048,128]{1,0:T(8,128)} %bitcast.116), channel_id=1, source_target_pairs={{0,16},{16,0},{1,17},{17,1},{2,18},{18,2},{3,19},{19,3},{4,20},{20... | collective-permute-start | bytes 3145736 | tf_op jit(solution)/shard_map/ppermute | solution.py:168
  164.8 7.9 %collective-permute-start.12 = (f32[2,128,256]{1,2,0:T(8,128)S(1)}, f32[2,128,256]{1,2,0:T(8,128)S(1)}, u32[]{:S(2)}, u32[]{:S(2)}) collective-permute-start(f32[2,128,256]{1,2,0:T(8,128)S(1)} %fusion.37), channel_id=1, source_target_pairs={{0,4},{2,6},{4,0},{6,2},{8,12},{10,14},{12,8},{14,10},{1,5},{3,7},... | collective-permute-start | bytes 786440 | tf_op jit(solution)/shard_map/ppermute | solution.py:168
  173.5 15.1 %collective-permute-start.13 = (f32[2,128,256]{1,2,0:T(8,128)}, f32[2,128,256]{1,2,0:T(8,128)}, u32[]{:S(2)}, u32[]{:S(2)}) collective-permute-start(f32[2,128,256]{1,2,0:T(8,128)} %add.120), channel_id=1, source_target_pairs={{0,8},{2,10},{4,12},{6,14},{8,0},{10,2},{12,4},{14,6},{1,9},{3,11}... | collective-permute-start | bytes 786440 | tf_op jit(solution)/shard_map/ppermute | solution.py:168
  (11 other events, 91.0 us)

commit v7 on v6

--- a/solution.py
+++ b/solution.py
@@ -76,9 +76,11 @@
 
 def backward_kernel(live_ref, rows_ref, cols_ref, masks_ref, lifted_ref, out_ref):
     group, _, edge = masks_ref.shape
-    row_limit = lifted_ref.shape[1] // edge - 1
-    col_limit = out_ref.shape[1] // edge - 1
-    half = out_ref.shape[0]
+    row_chunk = lifted_ref.shape[2] // edge
+    col_chunk = out_ref.shape[2] // edge
+    row_limit = lifted_ref.shape[0] * row_chunk - 1
+    col_limit = out_ref.shape[0] * col_chunk - 1
+    half = out_ref.shape[1]
 
     @pl.when(pl.program_id(0) == 0)
     def _():
@@ -93,10 +95,11 @@
             row = jnp.clip(rows_ref[slot], 0, row_limit)
             col = jnp.clip(cols_ref[slot], 0, col_limit)
             dense = slot_words(masks_ref, live_ref, base, k)
-            tile = lifted_ref[:, pl.ds(pl.multiple_of(row * edge, edge), edge)]
+            row_start = pl.multiple_of((row % row_chunk) * edge, edge)
+            tile = lifted_ref[row // row_chunk, :, pl.ds(row_start, edge)]
             prod = jnp.dot(tile, dense, preferred_element_type=jnp.float32)
-            start = pl.multiple_of(col * edge, edge)
-            out_ref[:, pl.ds(start, edge)] += prod[:half] + prod[half:]
+            col_start = pl.multiple_of((col % col_chunk) * edge, edge)
+            out_ref[col // col_chunk, :, pl.ds(col_start, edge)] += prod[:half] + prod[half:]
             return carry
 
         lax.fori_loop(0, group, body, 0, unroll=UNROLL)
@@ -144,16 +147,17 @@
     return totals, jnp.sum(bit_sums, axis=-1).astype(jnp.float32).reshape(-1)
 
 
-def block_transpose(live, block_rows, block_cols, packed_masks, lifted_rows, col_blocks):
+def block_transpose(live, block_rows, block_cols, packed_masks, lifted_chunks, cand_count):
     edge = packed_masks.shape[-1]
-    lifted_t = lifted_rows.T
-    high = lax.reduce_precision(lifted_t, exponent_bits=8, mantissa_bits=7)
-    split_t = jnp.concatenate([high, lifted_t - high], axis=0).astype(jnp.bfloat16)
-    out_shape = jax.ShapeDtypeStruct((lifted_rows.shape[1], col_blocks * edge), jnp.float32)
+    high = lax.reduce_precision(lifted_chunks, exponent_bits=8, mantissa_bits=7)
+    split_t = jnp.concatenate([high, lifted_chunks - high], axis=1).astype(jnp.bfloat16)
+    width = lifted_chunks.shape[1]
+    panel_cols = lifted_chunks.shape[0] * lifted_chunks.shape[2]
+    out_shape = jax.ShapeDtypeStruct((cand_count, width, panel_cols // cand_count), jnp.float32)
     (out_t,) = slot_pallas(
         backward_kernel, live, block_rows, block_cols, packed_masks, split_t, [out_shape]
     )
-    return out_t.T
+    return out_t
 
 
 def axis_bits(axis):
@@ -239,6 +243,15 @@
         [result.reshape((-1,) + result.shape[-2:]) for result in results], axis=1
     )
     return stacked.reshape((-1,) + values.shape[1:])
+
+
+def doubling_gather_lanes(values, axis):
+    orders = [list(reversed(order)) for order in bit_orders(axis)]
+    pieces = jnp.split(values, len(orders), axis=1)
+    results = [doubling_steps(piece, axis, order) for piece, order in zip(pieces, orders)]
+    return jnp.concatenate(
+        [result.reshape((-1,) + result.shape[-2:]) for result in results], axis=2
+    )
 
 
 def butterfly_sum(values, axes):
@@ -297,18 +310,18 @@
     grad_full = gather_axis(grad_pre, "feat", 1)
     self_part = jnp.einsum("rk,rh->kh", x_cand, grad_full, precision=HIGHEST)
     neigh_part = jnp.einsum("rk,rh->kh", aggregated, grad_full, precision=HIGHEST)
-    self_sum, neigh_sum = butterfly_sum(jnp.stack([self_part, neigh_part]), ("cand", "test"))
+    grad_w_pair = butterfly_sum(jnp.stack([self_part, neigh_part]), ("cand", "test"))
     root_count = math.sqrt(x_cand.shape[0] * cand_count * test_count)
-    grad_w_self = self_sum / root_count
-    grad_w_neigh = neigh_sum / root_count
     grad_x_cand = jnp.dot(grad_full, self_rows.T, precision=HIGHEST)
     grad_agg = jnp.dot(grad_full, neigh_rows.T, precision=HIGHEST)
     lifted = grad_agg / (1.0 + degree)[:, None]
-    gathered_rows = doubling_gather(lifted, "test")
-    column_terms = block_transpose(
-        live, block_rows, block_cols, packed_masks, gathered_rows, col_blocks
-    )
-    grad_x_test = halving_scatter(column_terms, "cand")
+    lifted_chunks = doubling_gather_lanes(lifted.T, "test")
+    grad_w_pair, lifted_chunks = lax.optimization_barrier((grad_w_pair, lifted_chunks))
+    grad_w_self = grad_w_pair[0] / root_count
+    grad_w_neigh = grad_w_pair[1] / root_count
+    out_t = block_transpose(live, block_rows, block_cols, packed_masks, lifted_chunks, cand_count)
+    own_t = halving_scatter(out_t.reshape(-1, out_t.shape[2]), "cand")
+    grad_x_test = own_t.T
     return (output, grad_w_self, grad_w_neigh, grad_x_cand, grad_x_test)
 
 

time: 193 us -> 172 us (0.89)
  local copies, waits for them, and re-layouts: 16.5 us -> 7.55 us
  waiting for transfers between devices: 83.4 us -> 75.5 us
  other arithmetic: 16.3 us -> 11.9 us
    ppermute x21, waiting for transfers between devices: 83.4 us -> 75.5 us  [exchange(): return lax.ppermute(values, axis, [(i, i ^ 1 << bit) for i in range(count)])]
    dynamic_slice x3 -> x0, local copies, waits for them, and re-layouts: 7.53 us -> none  [the longest x2 3.87 us: halving_steps(): keep = lax.dynamic_index_in_dim(data, mine, position, keepdims=False)]
    reshape x2 -> x0, local copies, waits for them, and re-layouts: 5.13 us -> none  [the longest x1 3.21 us: halving_scatter(): shaped = values.reshape((1 << bits, -1) + values.shape[1:])]
    add x4, other arithmetic: 3.56 us -> 0.14 us  [butterfly_sum(): values = values + exchange(values, axis, bit)]
    squeeze x6 -> x7, local copies, waits for them, and re-layouts: 0.97 us -> 3.41 us  [halving_steps(): send = lax.dynamic_index_in_dim(data, 1 - mine, position, keepdims=False)]
  transfers between devices with their start and end apart: 21 -> 21, of which waited for: 15 -> 17; matrix products, arithmetic and copies ran while one was open for 14% -> 4% of each run, Pallas kernels for 13% -> 0%
where the time goes in v7:
time: 172 us
  waiting for transfers between devices  75.5 us (44%)
  Pallas kernels  48.8 us (28%)
  starting transfers between devices  20.6 us (12%)
  other arithmetic  11.9 us (7%)
  local copies, waits for them, and re-layouts  7.55 us (4%)
  matrix products  5.82 us (3%)
  between operations  1.74 us (1%)
    ppermute x21, waiting for transfers between devices, exchange(): return lax.ppermute(values, axis, [(i, i ^ 1 << bit) for i in range(count)])  75.5 us
    pallas_call x2, Pallas kernels, slot_pallas(): pl.pallas_call(kernel, grid_spec=grid_spec, out_shape=out_shapes, compile...  48.8 us
    ppermute x21, starting transfers between devices, exchange(): return lax.ppermute(values, axis, [(i, i ^ 1 << bit) for i in range(count)])  20.6 us
    unnamed x17, local copies, waits for them, and re-layouts  3.82 us
  transfers between devices with their start and end apart: 21, of which 17 were waited for; matrix products, arithmetic and copies ran while one was open for 4% of the time, Pallas kernels for 0%

profile of v7, /device:TPU:31, one launch (start us, length us, event | category | flops | bytes accessed | tf_op | source)
XLA Modules:
  0.0 171.9 jit_solution(11961711751551668714)
XLA Ops:
  2.1 1.8 %collective-permute-done.1 = f32[2048,128]{1,0:T(8,128)S(1)} collective-permute-done((f32[2048,128]{1,0:T(8,128)}, f32[2048,128]{1,0:T(8,128)S(1)}, u32[]{:S(2)}, u32[]{:S(2)}) %collective-permute-start.1) | collective-permute-done | bytes 1048608 | tf_op jit(solution)/shard_map/ppermute | solution.py:172
  3.9 1.7 %maximum_select_fusion = f32[2,2048,128]{2,1,0:T(8,128)S(1)} fusion(f32[1,2048,128]{2,1,0:T(8,128)S(1)} %bitcast.111, f32[1,2048,128]{2,1,0:T(8,128)} %bitcast.110, pred[]{:T(512)S(6)} %eq.21), kind=kLoop, calls=%fused_computation.6 | loop fusion | flops 1572864 | bytes 4194305 | tf_op jit(solution)/shard_map/jit(_where)/select_n | solution.py:212
  6.0 1.6 pad_maximum_fusion.panel_ref
  7.5 24.7 %shard_map.128 = (f32[4096,128]{1,0:T(8,128)}, s32[32,128,128]{2,1,0:T(8,128)}) custom-call(s32[1]{0:T(128)} %bitcast.live_ref, s32[512]{0:T(512)} %bitcast.119, s32[512]{0:T(512)} %bitcast.121, s32[512,16,128]{2,1,0:T(8,128)} %bitcast.95, bf16[4096,256]{1,0:T(8,128)(2,1)} %pad_maximum_fusion.panel_ref), custom_call_target="tpu_custom_call" | custom-call | tf_op jit(solution)/shard_map/pallas_call | solution.py:131
  32.3 2.4 %reduce_sum.9 = s32[32,128]{1,0:T(8,128)S(1)} reduce(s32[32,128,128]{2,1,0:T(8,128)} %get-tuple-element.10, s32[]{:T(128)} %constant.70.clone.1), dimensions={2}, to_apply=%region_0.1 | reduce | flops 520192 | bytes 2113540 | tf_op jit(solution)/shard_map/reduce_sum | solution.py:147
  37.2 12.2 %collective-permute-done.2 = f32[2,2,264,128]{3,2,1,0:T(8,128)S(1)} collective-permute-done((f32[2,2,264,128]{3,2,1,0:T(8,128)S(1)}, f32[2,2,264,128]{3,2,1,0:T(8,128)S(1)}, u32[]{:S(2)}, u32[]{:S(2)}) %collective-permute-start.2) | collective-permute-done | bytes 540704 | tf_op jit(solution)/shard_map/ppermute | solution.py:172
  51.8 5.7 %collective-permute-done.3 = f32[2,264,128]{2,1,0:T(8,128)S(1)} collective-permute-done((f32[2,264,128]{2,1,0:T(8,128)S(1)}, f32[2,264,128]{2,1,0:T(8,128)S(1)}, u32[]{:S(2)}, u32[]{:S(2)}) %collective-permute-start.3) | collective-permute-done | bytes 270368 | tf_op jit(solution)/shard_map/ppermute | solution.py:172
  58.2 2.0 %collective-permute-start.7 = (f32[264,128]{1,0:T(8,128)S(1)}, f32[264,128]{1,0:T(8,128)S(1)}, u32[]{:S(2)}, u32[]{:S(2)}) collective-permute-start(f32[264,128]{1,0:T(8,128)S(1)} %dynamic-slice_bitcast_fusion.5), channel_id=1, source_target_pairs={{0,8},{2,10},{4,12},{6,14},{8,0},{10,2},{12,4},{14,6},{1,9},{3,11}... | collective-permute-start | bytes 405512 | tf_op jit(solution)/shard_map/ppermute | solution.py:172
  60.1 9.7 %collective-permute-done.4 = f32[264,128]{1,0:T(8,128)S(1)} collective-permute-done((f32[264,128]{1,0:T(8,128)S(1)}, f32[264,128]{1,0:T(8,128)S(1)}, u32[]{:S(2)}, u32[]{:S(2)}) %collective-permute-start.4) | collective-permute-done | bytes 135200 | tf_op jit(solution)/shard_map/ppermute | solution.py:172
  69.8 2.9 %collective-permute-done.7 = f32[264,128]{1,0:T(8,128)S(1)} collective-permute-done((f32[264,128]{1,0:T(8,128)S(1)}, f32[264,128]{1,0:T(8,128)S(1)}, u32[]{:S(2)}, u32[]{:S(2)}) %collective-permute-start.7) | collective-permute-done | bytes 135200 | tf_op jit(solution)/shard_map/ppermute | solution.py:172
  73.2 7.2 %collective-permute-done.8 = f32[512,128]{1,0:T(8,128)S(1)} collective-permute-done((f32[512,128]{1,0:T(8,128)S(1)}, f32[512,128]{1,0:T(8,128)S(1)}, u32[]{:S(2)}, u32[]{:S(2)}) %collective-permute-start.8) | collective-permute-done | bytes 262176 | tf_op jit(solution)/shard_map/ppermute | solution.py:172
  82.5 6.3 %collective-permute-done.9 = f32[512,128]{1,0:T(8,128)S(1)} collective-permute-done((f32[512,128]{1,0:T(8,128)S(1)}, f32[512,128]{1,0:T(8,128)S(1)}, u32[]{:S(2)}, u32[]{:S(2)}) %collective-permute-start.9) | collective-permute-done | bytes 262176 | tf_op jit(solution)/shard_map/ppermute | solution.py:172
  91.7 2.4 %collective-permute-start.17 = (f32[128,256]{1,0:T(8,128)S(1)}, f32[128,256]{1,0:T(8,128)S(1)}, u32[]{:S(2)}, u32[]{:S(2)}) collective-permute-start(f32[128,256]{1,0:T(8,128)S(1)} %get-tuple-element.51), channel_id=1, source_target_pairs={{0,8},{2,10},{4,12},{6,14},{8,0},{10,2},{12,4},{14,6},{1,9},{3,11}... | collective-permute-start | bytes 393224 | tf_op jit(solution)/shard_map/ppermute | solution.py:172
  94.1 2.8 %collective-permute-start.10 = (f32[2,128,256]{1,2,0:T(8,128)S(1)}, f32[2,128,256]{1,2,0:T(8,128)S(1)}, u32[]{:S(2)}, u32[]{:S(2)}) collective-permute-start(f32[2,128,256]{1,2,0:T(8,128)S(1)} %pad_maximum_fusion.6), channel_id=1, source_target_pairs={{0,16},{16,0},{1,17},{17,1},{2,18},{18,2},{3,19},{19,3},{4,20},{20... | collective-permute-start | bytes 786440 | tf_op jit(solution)/shard_map/ppermute | solution.py:172
  98.3 2.7 %collective-permute-done.17 = f32[128,256]{1,0:T(8,128)S(1)} collective-permute-done((f32[128,256]{1,0:T(8,128)S(1)}, f32[128,256]{1,0:T(8,128)S(1)}, u32[]{:S(2)}, u32[]{:S(2)}) %collective-permute-start.17) | collective-permute-done | bytes 131104 | tf_op jit(solution)/shard_map/ppermute | solution.py:172
  102.8 3.0 %collective-permute-done.15 = f32[2,128,256]{2,1,0:T(8,128)S(1)} collective-permute-done((f32[2,128,256]{2,1,0:T(8,128)S(1)}, f32[2,128,256]{2,1,0:T(8,128)S(1)}, u32[]{:S(2)}, u32[]{:S(2)}) %collective-permute-start.15) | collective-permute-done | bytes 262176 | tf_op jit(solution)/shard_map/ppermute | solution.py:172
  107.4 5.5 %collective-permute-done.11 = f32[2,128,256]{1,2,0:T(8,128)S(1)} collective-permute-done((f32[2,128,256]{1,2,0:T(8,128)S(1)}, f32[2,128,256]{1,2,0:T(8,128)S(1)}, u32[]{:S(2)}, u32[]{:S(2)}) %collective-permute-start.11) | collective-permute-done | bytes 262176 | tf_op jit(solution)/shard_map/ppermute | solution.py:172
  113.1 8.5 %collective-permute-done.12 = f32[2,128,256]{1,2,0:T(8,128)S(1)} collective-permute-done((f32[2,128,256]{1,2,0:T(8,128)S(1)}, f32[2,128,256]{1,2,0:T(8,128)S(1)}, u32[]{:S(2)}, u32[]{:S(2)}) %collective-permute-start.12) | collective-permute-done | bytes 262176 | tf_op jit(solution)/shard_map/ppermute | solution.py:172
  121.7 2.4 %collective-permute-done.16 = f32[2,2,128,256]{3,2,0,1:T(8,128)S(1)} collective-permute-done((f32[2,2,128,256]{3,2,0,1:T(8,128)S(1)}, f32[2,2,128,256]{3,2,0,1:T(8,128)S(1)}, u32[]{:S(2)}, u32[]{:S(2)}) %collective-permute-start.16) | collective-permute-done | bytes 524320 | tf_op jit(solution)/shard_map/ppermute | solution.py:172
  124.8 5.6 %collective-permute-done.13 = f32[2,128,256]{1,2,0:T(8,128)S(1)} collective-permute-done((f32[2,128,256]{1,2,0:T(8,128)S(1)}, f32[2,128,256]{1,2,0:T(8,128)S(1)}, u32[]{:S(2)}, u32[]{:S(2)}) %collective-permute-start.13) | collective-permute-done | bytes 262176 | tf_op jit(solution)/shard_map/ppermute | solution.py:172
  130.9 1.5 pad_maximum_fusion.2.lifted_ref
  132.3 24.1 %shard_map.129 = f32[2,128,2048]{2,1,0:T(8,128)} custom-call(s32[1]{0:T(128)} %bitcast.live_ref, s32[512]{0:T(512)} %bitcast.120, s32[512]{0:T(512)} %bitcast.122, s32[512,16,128]{2,1,0:T(8,128)} %bitcast.96, bf16[8,256,512]{2,1,0:T(8,128)(2,1)} %pad_maximum_fusion.2.lifted_ref), custom_call_target="tpu_custom_call" | custom-call | tf_op jit(solution)/shard_map/pallas_call | solution.py:131
  156.4 2.4 %dynamic-slice_bitcast_fusion = f32[128,2048]{1,0:T(8,128)} fusion(f32[2,128,2048]{2,1,0:T(8,128)} %shard_map.129, s32[]{:T(128)S(6)} %select_n.227), kind=kLoop, calls=%fused_computation.20 | loop fusion | bytes 2097156 | tf_op jit(solution)/shard_map/jit(dynamic_index_in_dim)/squeeze | solution.py:199
  158.9 7.5 %collective-permute-start.20 = (f32[128,2048]{1,0:T(8,128)}, f32[128,2048]{1,0:T(8,128)}, u32[]{:S(2)}, u32[]{:S(2)}) collective-permute-start(f32[128,2048]{1,0:T(8,128)} %dynamic-slice_bitcast_fusion), channel_id=1, source_target_pairs={{0,16},{16,0},{1,17},{17,1},{2,18},{18,2},{3,19},{19,3},{4,20},{20... | collective-permute-start | bytes 3145736 | tf_op jit(solution)/shard_map/ppermute | solution.py:172
  (94 shorter events, 23.6 us)
Async XLA Ops:
  0.6 80.3 %copy-start = (f32[256,256]{1,0:T(8,128)S(1)}, f32[256,256]{1,0:T(8,128)}, u32[]{:S(2)}) copy-start(f32[256,256]{1,0:T(8,128)} %param.11) | copy-start | bytes 786436
  0.6 3.2 %collective-permute-start.1 = (f32[2048,128]{1,0:T(8,128)}, f32[2048,128]{1,0:T(8,128)S(1)}, u32[]{:S(2)}, u32[]{:S(2)}) collective-permute-start(f32[2048,128]{1,0:T(8,128)} %param.9), channel_id=1, source_target_pairs={{0,16},{16,0},{1,17},{17,1},{2,18},{18,2},{3,19},{19,3},{4,20},{20... | collective-permute-start | bytes 3145736 | tf_op jit(solution)/shard_map/ppermute | solution.py:172
  35.9 13.6 %collective-permute-start.2 = (f32[2,2,264,128]{3,2,1,0:T(8,128)S(1)}, f32[2,2,264,128]{3,2,1,0:T(8,128)S(1)}, u32[]{:S(2)}, u32[]{:S(2)}) collective-permute-start(f32[2,2,264,128]{3,2,1,0:T(8,128)S(1)} %dynamic-slice_bitcast_fusion.2), channel_id=1, source_target_pairs={{0,2},{2,0},{4,6},{6,4},{8,10},{10,8},{12,14},{14,12},{1,3},{3,1},... | collective-permute-start | bytes 1622024 | tf_op jit(solution)/shard_map/ppermute | solution.py:172
  37.0 13.9 %collective-permute-start.5 = (f32[2,2,264,128]{3,2,1,0:T(8,128)}, f32[2,2,264,128]{3,2,1,0:T(8,128)S(1)}, u32[]{:S(2)}, u32[]{:S(2)}) collective-permute-start(f32[2,2,264,128]{3,2,1,0:T(8,128)} %dynamic-slice_bitcast_fusion.1), channel_id=1, source_target_pairs={{0,4},{2,6},{4,0},{6,2},{8,12},{10,14},{12,8},{14,10},{1,5},{3,7},... | collective-permute-start | bytes 1622024 | tf_op jit(solution)/shard_map/ppermute | solution.py:172
  37.0 36.1 %collective-permute-start = (f32[512,128]{1,0:T(8,128)S(1)}, f32[512,128]{1,0:T(8,128)S(1)}, u32[]{:S(2)}, u32[]{:S(2)}) collective-permute-start(f32[512,128]{1,0:T(8,128)S(1)} %copy-done.4), channel_id=1, source_target_pairs={{0,1},{1,0},{2,3},{3,2},{4,5},{5,4},{6,7},{7,6},{8,9},{9,8},{10,11... | collective-permute-start | bytes 786440 | tf_op jit(solution)/shard_map/ppermute | solution.py:172
  50.6 6.9 %collective-permute-start.3 = (f32[2,264,128]{2,1,0:T(8,128)S(1)}, f32[2,264,128]{2,1,0:T(8,128)S(1)}, u32[]{:S(2)}, u32[]{:S(2)}) collective-permute-start(f32[2,264,128]{2,1,0:T(8,128)S(1)} %dynamic-slice_bitcast_fusion.4), channel_id=1, source_target_pairs={{0,4},{2,6},{4,0},{6,2},{8,12},{10,14},{12,8},{14,10},{1,5},{3,7},... | collective-permute-start | bytes 811016 | tf_op jit(solution)/shard_map/ppermute | solution.py:172
  51.0 7.1 %collective-permute-start.6 = (f32[2,264,128]{2,1,0:T(8,128)S(1)}, f32[2,264,128]{2,1,0:T(8,128)S(1)}, u32[]{:S(2)}, u32[]{:S(2)}) collective-permute-start(f32[2,264,128]{2,1,0:T(8,128)S(1)} %dynamic-slice_bitcast_fusion.3), channel_id=1, source_target_pairs={{0,2},{2,0},{4,6},{6,4},{8,10},{10,8},{12,14},{14,12},{1,3},{3,1},... | collective-permute-start | bytes 811016 | tf_op jit(solution)/shard_map/ppermute | solution.py:172
  57.6 22.8 %copy-start.5 = (f32[256,256]{1,0:T(8,128)S(1)}, f32[256,256]{1,0:T(8,128)}, u32[]{:S(2)}) copy-start(f32[256,256]{1,0:T(8,128)} %param.12) | copy-start | bytes 786436
  57.6 12.3 %collective-permute-start.4 = (f32[264,128]{1,0:T(8,128)S(1)}, f32[264,128]{1,0:T(8,128)S(1)}, u32[]{:S(2)}, u32[]{:S(2)}) collective-permute-start(f32[264,128]{1,0:T(8,128)S(1)} %dynamic-slice_bitcast_fusion.6), channel_id=1, source_target_pairs={{0,8},{2,10},{4,12},{6,14},{8,0},{10,2},{12,4},{14,6},{1,9},{3,11}... | collective-permute-start | bytes 405512 | tf_op jit(solution)/shard_map/ppermute | solution.py:172
  58.2 22.8 %copy-start.6 = (f32[512,128]{1,0:T(8,128)S(1)}, f32[512,128]{1,0:T(8,128)}, u32[]{:S(2)}) copy-start(f32[512,128]{1,0:T(8,128)} %param.13) | copy-start | bytes 786436
  58.2 14.6 %collective-permute-start.7 = (f32[264,128]{1,0:T(8,128)S(1)}, f32[264,128]{1,0:T(8,128)S(1)}, u32[]{:S(2)}, u32[]{:S(2)}) collective-permute-start(f32[264,128]{1,0:T(8,128)S(1)} %dynamic-slice_bitcast_fusion.5), channel_id=1, source_target_pairs={{0,8},{2,10},{4,12},{6,14},{8,0},{10,2},{12,4},{14,6},{1,9},{3,11}... | collective-permute-start | bytes 405512 | tf_op jit(solution)/shard_map/ppermute | solution.py:172
  72.9 7.4 %collective-permute-start.8 = (f32[512,128]{1,0:T(8,128)S(1)}, f32[512,128]{1,0:T(8,128)S(1)}, u32[]{:S(2)}, u32[]{:S(2)}) collective-permute-start(f32[512,128]{1,0:T(8,128)S(1)} %fusion.11), channel_id=1, source_target_pairs={{0,1},{1,0},{2,3},{3,2},{4,5},{5,4},{6,7},{7,6},{8,9},{9,8},{10,11... | collective-permute-start | bytes 786440 | tf_op jit(solution)/shard_map/ppermute | solution.py:172
  82.3 6.5 %collective-permute-start.9 = (f32[512,128]{1,0:T(8,128)S(1)}, f32[512,128]{1,0:T(8,128)S(1)}, u32[]{:S(2)}, u32[]{:S(2)}) collective-permute-start(f32[512,128]{1,0:T(8,128)S(1)} %get-tuple-element.53), channel_id=1, source_target_pairs={{0,1},{1,0},{2,3},{3,2},{4,5},{5,4},{6,7},{7,6},{8,9},{9,8},{10,11... | collective-permute-start | bytes 786440 | tf_op jit(solution)/shard_map/ppermute | solution.py:172
  90.6 7.7 %collective-permute-start.14 = (f32[128,256]{1,0:T(8,128)S(1)}, f32[128,256]{1,0:T(8,128)S(1)}, u32[]{:S(2)}, u32[]{:S(2)}) collective-permute-start(f32[128,256]{1,0:T(8,128)S(1)} %get-tuple-element.52), channel_id=1, source_target_pairs={{0,8},{2,10},{4,12},{6,14},{8,0},{10,2},{12,4},{14,6},{1,9},{3,11}... | collective-permute-start | bytes 393224 | tf_op jit(solution)/shard_map/ppermute | solution.py:172
  91.7 9.4 %collective-permute-start.17 = (f32[128,256]{1,0:T(8,128)S(1)}, f32[128,256]{1,0:T(8,128)S(1)}, u32[]{:S(2)}, u32[]{:S(2)}) collective-permute-start(f32[128,256]{1,0:T(8,128)S(1)} %get-tuple-element.51), channel_id=1, source_target_pairs={{0,8},{2,10},{4,12},{6,14},{8,0},{10,2},{12,4},{14,6},{1,9},{3,11}... | collective-permute-start | bytes 393224 | tf_op jit(solution)/shard_map/ppermute | solution.py:172
  94.1 8.3 %collective-permute-start.10 = (f32[2,128,256]{1,2,0:T(8,128)S(1)}, f32[2,128,256]{1,2,0:T(8,128)S(1)}, u32[]{:S(2)}, u32[]{:S(2)}) collective-permute-start(f32[2,128,256]{1,2,0:T(8,128)S(1)} %pad_maximum_fusion.6), channel_id=1, source_target_pairs={{0,16},{16,0},{1,17},{17,1},{2,18},{18,2},{3,19},{19,3},{4,20},{20... | collective-permute-start | bytes 786440 | tf_op jit(solution)/shard_map/ppermute | solution.py:172
  98.3 7.6 %collective-permute-start.15 = (f32[2,128,256]{2,1,0:T(8,128)S(1)}, f32[2,128,256]{2,1,0:T(8,128)S(1)}, u32[]{:S(2)}, u32[]{:S(2)}) collective-permute-start(f32[2,128,256]{2,1,0:T(8,128)S(1)} %maximum_select_fusion.7), channel_id=1, source_target_pairs={{0,4},{2,6},{4,0},{6,2},{8,12},{10,14},{12,8},{14,10},{1,5},{3,7},... | collective-permute-start | bytes 786440 | tf_op jit(solution)/shard_map/ppermute | solution.py:172
  101.1 6.2 %collective-permute-start.18 = (f32[2,128,256]{2,1,0:T(8,128)S(1)}, f32[2,128,256]{2,1,0:T(8,128)S(1)}, u32[]{:S(2)}, u32[]{:S(2)}) collective-permute-start(f32[2,128,256]{2,1,0:T(8,128)S(1)} %maximum_select_fusion.9), channel_id=1, source_target_pairs={{0,2},{2,0},{4,6},{6,4},{8,10},{10,8},{12,14},{14,12},{1,3},{3,1},... | collective-permute-start | bytes 786440 | tf_op jit(solution)/shard_map/ppermute | solution.py:172
  102.4 10.4 %collective-permute-start.11 = (f32[2,128,256]{1,2,0:T(8,128)S(1)}, f32[2,128,256]{1,2,0:T(8,128)S(1)}, u32[]{:S(2)}, u32[]{:S(2)}) collective-permute-start(f32[2,128,256]{1,2,0:T(8,128)S(1)} %fusion.30), channel_id=1, source_target_pairs={{0,2},{2,0},{4,6},{6,4},{8,10},{10,8},{12,14},{14,12},{1,3},{3,1},... | collective-permute-start | bytes 786440 | tf_op jit(solution)/shard_map/ppermute | solution.py:172
  105.9 18.2 %collective-permute-start.16 = (f32[2,2,128,256]{3,2,0,1:T(8,128)S(1)}, f32[2,2,128,256]{3,2,0,1:T(8,128)S(1)}, u32[]{:S(2)}, u32[]{:S(2)}) collective-permute-start(f32[2,2,128,256]{3,2,0,1:T(8,128)S(1)} %maximum_select_fusion.4), channel_id=1, source_target_pairs={{0,2},{2,0},{4,6},{6,4},{8,10},{10,8},{12,14},{14,12},{1,3},{3,1},... | collective-permute-start | bytes 1572872 | tf_op jit(solution)/shard_map/ppermute | solution.py:172
  107.3 17.0 %collective-permute-start.19 = (f32[2,2,128,256]{3,2,0,1:T(8,128)S(1)}, f32[2,2,128,256]{3,2,0,1:T(8,128)S(1)}, u32[]{:S(2)}, u32[]{:S(2)}) collective-permute-start(f32[2,2,128,256]{3,2,0,1:T(8,128)S(1)} %maximum_select_fusion.6), channel_id=1, source_target_pairs={{0,4},{2,6},{4,0},{6,2},{8,12},{10,14},{12,8},{14,10},{1,5},{3,7},... | collective-permute-start | bytes 1572872 | tf_op jit(solution)/shard_map/ppermute | solution.py:172
  112.9 8.7 %collective-permute-start.12 = (f32[2,128,256]{1,2,0:T(8,128)S(1)}, f32[2,128,256]{1,2,0:T(8,128)S(1)}, u32[]{:S(2)}, u32[]{:S(2)}) collective-permute-start(f32[2,128,256]{1,2,0:T(8,128)S(1)} %fusion.36), channel_id=1, source_target_pairs={{0,4},{2,6},{4,0},{6,2},{8,12},{10,14},{12,8},{14,10},{1,5},{3,7},... | collective-permute-start | bytes 786440 | tf_op jit(solution)/shard_map/ppermute | solution.py:172
  121.6 8.8 %collective-permute-start.13 = (f32[2,128,256]{1,2,0:T(8,128)S(1)}, f32[2,128,256]{1,2,0:T(8,128)S(1)}, u32[]{:S(2)}, u32[]{:S(2)}) collective-permute-start(f32[2,128,256]{1,2,0:T(8,128)S(1)} %add.120), channel_id=1, source_target_pairs={{0,8},{2,10},{4,12},{6,14},{8,0},{10,2},{12,4},{14,6},{1,9},{3,11}... | collective-permute-start | bytes 786440 | tf_op jit(solution)/shard_map/ppermute | solution.py:172
  158.9 10.4 %collective-permute-start.20 = (f32[128,2048]{1,0:T(8,128)}, f32[128,2048]{1,0:T(8,128)}, u32[]{:S(2)}, u32[]{:S(2)}) collective-permute-start(f32[128,2048]{1,0:T(8,128)} %dynamic-slice_bitcast_fusion), channel_id=1, source_target_pairs={{0,16},{16,0},{1,17},{17,1},{2,18},{18,2},{3,19},{19,3},{4,20},{20... | collective-permute-start | bytes 3145736 | tf_op jit(solution)/shard_map/ppermute | solution.py:172
  (4 other events, 18.3 us)

commit v8 on v7

--- a/solution.py
+++ b/solution.py
@@ -8,7 +8,7 @@
 from jax.sharding import PartitionSpec as P
 
 HIGHEST = lax.Precision.HIGHEST
-SLOT_GROUP = 64
+SLOT_GROUP = 128
 
 
 def split_hi_lo(values):
@@ -23,6 +23,15 @@
     shifts = lax.broadcasted_iota(jnp.int32, (word_rows, 8, edge), 1)
     bits = jnp.bitwise_and(jnp.right_shift(cube, shifts), 1)
     return bits.reshape(word_rows * 8, edge)
+
+
+def spread_bytes(words):
+    low = jnp.zeros_like(words)
+    high = jnp.zeros_like(words)
+    for bit in range(4):
+        low = low + jnp.left_shift(jnp.bitwise_and(jnp.right_shift(words, bit), 1), 8 * bit)
+        high = high + jnp.left_shift(jnp.bitwise_and(jnp.right_shift(words, bit + 4), 1), 8 * bit)
+    return jnp.concatenate([low, high], axis=0)
 
 
 def unpack_block(words):
@@ -62,9 +71,9 @@
             row = jnp.clip(rows_ref[slot], 0, row_limit)
             col = jnp.clip(cols_ref[slot], 0, col_limit)
             keep = jnp.where(slot < live_ref[0], -1, 0).astype(jnp.int32)
-            bits = unpack_bits(jnp.bitwise_and(masks_ref[k], keep))
-            bits_ref[row] += bits
-            dense = bits.astype(jnp.float32).astype(jnp.bfloat16)
+            words = jnp.bitwise_and(masks_ref[k], keep)
+            bits_ref[row] += spread_bytes(words)
+            dense = unpack_bits(words).astype(jnp.float32).astype(jnp.bfloat16)
             tile = panel_ref[pl.ds(pl.multiple_of(col * edge, edge), edge), :]
             prod = jnp.dot(dense, tile, preferred_element_type=jnp.float32)
             start = pl.multiple_of(row * edge, edge)
@@ -139,12 +148,19 @@
 def block_aggregate(live, block_rows, block_cols, packed_masks, panel_split, row_blocks):
     edge = packed_masks.shape[-1]
     totals_shape = jax.ShapeDtypeStruct((row_blocks * edge, panel_split.shape[1] // 2), jnp.float32)
-    bits_shape = jax.ShapeDtypeStruct((row_blocks, edge, edge), jnp.int32)
-    totals, bit_sums = slot_pallas(
+    word_rows = packed_masks.shape[1]
+    bits_shape = jax.ShapeDtypeStruct((row_blocks, 2 * word_rows, edge), jnp.int32)
+    totals, byte_sums = slot_pallas(
         forward_kernel, live, block_rows, block_cols, packed_masks, panel_split,
         [totals_shape, bits_shape],
     )
-    return totals, jnp.sum(bit_sums, axis=-1).astype(jnp.float32).reshape(-1)
+    fields = [
+        jnp.sum(jnp.bitwise_and(jnp.right_shift(byte_sums, 8 * field), 255), axis=2)
+        for field in range(4)
+    ]
+    per_row = jnp.stack(fields, axis=-1).reshape(row_blocks, 2, word_rows, 4)
+    counts = jnp.transpose(per_row, (0, 2, 1, 3)).reshape(-1).astype(jnp.float32)
+    return totals, counts
 
 
 def block_transpose(live, block_rows, block_cols, packed_masks, lifted_chunks, cand_count):

time: 172 us -> 177 us (1.029)
  starting transfers between devices: 20.6 us -> 12.5 us
  waiting for transfers between devices: 75.5 us -> 82.2 us
  other arithmetic: 11.9 us -> 15.4 us
    ppermute x21, starting transfers between devices: 20.6 us -> 12.5 us  [exchange(): return lax.ppermute(values, axis, [(i, i ^ 1 << bit) for i in range(count)])]
    ppermute x21, waiting for transfers between devices: 75.5 us -> 82.2 us  [exchange(): return lax.ppermute(values, axis, [(i, i ^ 1 << bit) for i in range(count)])]
    unnamed x17 -> x13, local copies, waits for them, and re-layouts: 3.82 us -> 2.85 us
  transfers between devices with their start and end apart: 21 -> 21, of which waited for: 17 -> 15; matrix products, arithmetic and copies ran while one was open for 4% -> 5% of each run, Pallas kernels for 0% -> 0%
where the time goes in v8:
time: 177 us
  waiting for transfers between devices  82.2 us (46%)
  Pallas kernels  50.1 us (28%)
  other arithmetic  15.4 us (9%)
  starting transfers between devices  12.5 us (7%)
  local copies, waits for them, and re-layouts  9.12 us (5%)
  matrix products  5.82 us (3%)
    ppermute x21, waiting for transfers between devices, exchange(): return lax.ppermute(values, axis, [(i, i ^ 1 << bit) for i in range(count)])  82.2 us
    pallas_call x2, Pallas kernels, slot_pallas(): pl.pallas_call(kernel, grid_spec=grid_spec, out_shape=out_shapes, compile...  50.1 us
    ppermute x21, starting transfers between devices, exchange(): return lax.ppermute(values, axis, [(i, i ^ 1 << bit) for i in range(count)])  12.5 us
    squeeze x7, local copies, waits for them, and re-layouts, halving_steps(): send = lax.dynamic_index_in_dim(data, 1 - mine, position, keepdims=False)  4.23 us
  transfers between devices with their start and end apart: 21, of which 15 were waited for; matrix products, arithmetic and copies ran while one was open for 5% of the time, Pallas kernels for 0%

profile of v8, /device:TPU:31, one launch (start us, length us, event | category | flops | bytes accessed | tf_op | source)
XLA Modules:
  0.0 176.8 jit_solution(13536729534731980111)
XLA Ops:
  2.1 1.7 collective-permute-done.1
  3.9 1.7 maximum_select_fusion
  6.0 1.6 pad_maximum_fusion.panel_ref
  7.5 26.0 %shard_map.128 = (f32[4096,128]{1,0:T(8,128)}, s32[32,32,128]{2,1,0:T(8,128)}) custom-call(s32[1]{0:T(128)} %bitcast.live_ref, s32[512]{0:T(512)} %bitcast.127, s32[512]{0:T(512)} %bitcast.129, s32[512,16,128]{2,1,0:T(8,128)} %bitcast.100, bf16[4096,256]{1,0:T(8,128)(2,1)} %pad_maximum_fusion.panel_ref), custom_call_target="tpu_custom_call" | custom-call | tf_op jit(solution)/shard_map/pallas_call | solution.py:140
  33.5 3.3 %and_reduce_fusion.3 = (s32[32,32]{1,0:T(8,128)S(1)}, s32[32,32]{1,0:T(8,128)S(1)}, s32[32,32]{1,0:T(8,128)S(1)}, s32[32,32]{1,0:T(8,128)S(1)}) fusion(s32[32,32,128]{2,1,0:T(8,128)} %get-tuple-element.10), kind=kLoop, calls=%fused_computation.40 | loop fusion | flops 1568768 | bytes 540672 | tf_op jit(solution)/shard_map/reduce_sum | solution.py:158
  38.5 1.7 fusion.32
  42.5 12.4 %collective-permute-done.5 = f32[2,2,264,128]{3,2,1,0:T(8,128)} collective-permute-done((f32[2,2,264,128]{3,2,1,0:T(8,128)}, f32[2,2,264,128]{3,2,1,0:T(8,128)}, u32[]{:S(2)}, u32[]{:S(2)}) %collective-permute-start.5) | collective-permute-done | bytes 540704 | tf_op jit(solution)/shard_map/ppermute | solution.py:188
  58.2 4.8 %collective-permute-done.6 = f32[2,264,128]{2,1,0:T(8,128)S(1)} collective-permute-done((f32[2,264,128]{2,1,0:T(8,128)S(1)}, f32[2,264,128]{2,1,0:T(8,128)S(1)}, u32[]{:S(2)}, u32[]{:S(2)}) %collective-permute-start.6) | collective-permute-done | bytes 270368 | tf_op jit(solution)/shard_map/ppermute | solution.py:188
  65.6 8.4 %collective-permute-done.7 = f32[264,128]{1,0:T(8,128)S(1)} collective-permute-done((f32[264,128]{1,0:T(8,128)S(1)}, f32[264,128]{1,0:T(8,128)S(1)}, u32[]{:S(2)}, u32[]{:S(2)}) %collective-permute-start.7) | collective-permute-done | bytes 135200 | tf_op jit(solution)/shard_map/ppermute | solution.py:188
  74.0 2.9 %collective-permute-done.4 = f32[264,128]{1,0:T(8,128)S(1)} collective-permute-done((f32[264,128]{1,0:T(8,128)S(1)}, f32[264,128]{1,0:T(8,128)S(1)}, u32[]{:S(2)}, u32[]{:S(2)}) %collective-permute-start.4) | collective-permute-done | bytes 135200 | tf_op jit(solution)/shard_map/ppermute | solution.py:188
  77.4 6.5 %collective-permute-done.8 = f32[512,128]{1,0:T(8,128)S(1)} collective-permute-done((f32[512,128]{1,0:T(8,128)S(1)}, f32[512,128]{1,0:T(8,128)S(1)}, u32[]{:S(2)}, u32[]{:S(2)}) %collective-permute-start.8) | collective-permute-done | bytes 262176 | tf_op jit(solution)/shard_map/ppermute | solution.py:188
  86.0 5.7 %collective-permute-done.9 = f32[512,128]{1,0:T(8,128)S(1)} collective-permute-done((f32[512,128]{1,0:T(8,128)S(1)}, f32[512,128]{1,0:T(8,128)S(1)}, u32[]{:S(2)}, u32[]{:S(2)}) %collective-permute-start.9) | collective-permute-done | bytes 262176 | tf_op jit(solution)/shard_map/ppermute | solution.py:188
  94.5 2.4 %collective-permute-start.14 = (f32[128,256]{1,0:T(8,128)S(1)}, f32[128,256]{1,0:T(8,128)S(1)}, u32[]{:S(2)}, u32[]{:S(2)}) collective-permute-start(f32[128,256]{1,0:T(8,128)S(1)} %get-tuple-element.61), channel_id=1, source_target_pairs={{0,8},{2,10},{4,12},{6,14},{8,0},{10,2},{12,4},{14,6},{1,9},{3,11}... | collective-permute-start | bytes 393224 | tf_op jit(solution)/shard_map/ppermute | solution.py:188
  96.9 3.5 %collective-permute-start.10 = (f32[2,128,256]{1,2,0:T(8,128)S(1)}, f32[2,128,256]{1,2,0:T(8,128)S(1)}, u32[]{:S(2)}, u32[]{:S(2)}) collective-permute-start(f32[2,128,256]{1,2,0:T(8,128)S(1)} %pad_maximum_fusion.6), channel_id=1, source_target_pairs={{0,16},{16,0},{1,17},{17,1},{2,18},{18,2},{3,19},{19,3},{4,20},{20... | collective-permute-start | bytes 786440 | tf_op jit(solution)/shard_map/ppermute | solution.py:188
  100.4 2.5 %collective-permute-done.17 = f32[128,256]{1,0:T(8,128)S(1)} collective-permute-done((f32[128,256]{1,0:T(8,128)S(1)}, f32[128,256]{1,0:T(8,128)S(1)}, u32[]{:S(2)}, u32[]{:S(2)}) %collective-permute-start.17) | collective-permute-done | bytes 131104 | tf_op jit(solution)/shard_map/ppermute | solution.py:188
  103.0 2.7 %collective-permute-done.14 = f32[128,256]{1,0:T(8,128)S(1)} collective-permute-done((f32[128,256]{1,0:T(8,128)S(1)}, f32[128,256]{1,0:T(8,128)S(1)}, u32[]{:S(2)}, u32[]{:S(2)}) %collective-permute-start.14) | collective-permute-done | bytes 131104 | tf_op jit(solution)/shard_map/ppermute | solution.py:188
  106.1 2.6 %collective-permute-done.18 = f32[2,128,256]{2,1,0:T(8,128)S(1)} collective-permute-done((f32[2,128,256]{2,1,0:T(8,128)S(1)}, f32[2,128,256]{2,1,0:T(8,128)S(1)}, u32[]{:S(2)}, u32[]{:S(2)}) %collective-permute-start.18) | collective-permute-done | bytes 262176 | tf_op jit(solution)/shard_map/ppermute | solution.py:188
  108.9 3.5 %collective-permute-done.15 = f32[2,128,256]{2,1,0:T(8,128)S(1)} collective-permute-done((f32[2,128,256]{2,1,0:T(8,128)S(1)}, f32[2,128,256]{2,1,0:T(8,128)S(1)}, u32[]{:S(2)}, u32[]{:S(2)}) %collective-permute-start.15) | collective-permute-done | bytes 262176 | tf_op jit(solution)/shard_map/ppermute | solution.py:188
  112.5 1.8 %collective-permute-done.11 = f32[2,128,256]{1,2,0:T(8,128)S(1)} collective-permute-done((f32[2,128,256]{1,2,0:T(8,128)S(1)}, f32[2,128,256]{1,2,0:T(8,128)S(1)}, u32[]{:S(2)}, u32[]{:S(2)}) %collective-permute-start.11) | collective-permute-done | bytes 262176 | tf_op jit(solution)/shard_map/ppermute | solution.py:188
  114.6 12.9 %collective-permute-done.12 = f32[2,128,256]{1,2,0:T(8,128)S(1)} collective-permute-done((f32[2,128,256]{1,2,0:T(8,128)S(1)}, f32[2,128,256]{1,2,0:T(8,128)S(1)}, u32[]{:S(2)}, u32[]{:S(2)}) %collective-permute-start.12) | collective-permute-done | bytes 262176 | tf_op jit(solution)/shard_map/ppermute | solution.py:188
  128.4 12.6 %collective-permute-done.13 = f32[2,128,256]{1,2,0:T(8,128)S(1)} collective-permute-done((f32[2,128,256]{1,2,0:T(8,128)S(1)}, f32[2,128,256]{1,2,0:T(8,128)S(1)}, u32[]{:S(2)}, u32[]{:S(2)}) %collective-permute-start.13) | collective-permute-done | bytes 262176 | tf_op jit(solution)/shard_map/ppermute | solution.py:188
  142.9 24.1 %shard_map.129 = f32[2,128,2048]{2,1,0:T(8,128)} custom-call(s32[1]{0:T(128)} %bitcast.live_ref, s32[512]{0:T(512)} %bitcast.128, s32[512]{0:T(512)} %bitcast.130, s32[512,16,128]{2,1,0:T(8,128)} %bitcast.101, bf16[8,256,512]{2,1,0:T(8,128)(2,1)} %pad_maximum_fusion.2.lifted_ref), custom_call_target="tpu_custom_call" | custom-call | tf_op jit(solution)/shard_map/pallas_call | solution.py:140
  167.0 2.4 %dynamic-slice_bitcast_fusion = f32[128,2048]{1,0:T(8,128)} fusion(f32[2,128,2048]{2,1,0:T(8,128)} %shard_map.129, s32[]{:T(128)S(6)} %select_n.227), kind=kLoop, calls=%fused_computation.20 | loop fusion | bytes 2097156 | tf_op jit(solution)/shard_map/jit(dynamic_index_in_dim)/squeeze | solution.py:215
  169.5 1.9 %collective-permute-start.20 = (f32[128,2048]{1,0:T(8,128)}, f32[128,2048]{1,0:T(8,128)}, u32[]{:S(2)}, u32[]{:S(2)}) collective-permute-start(f32[128,2048]{1,0:T(8,128)} %dynamic-slice_bitcast_fusion), channel_id=1, source_target_pairs={{0,16},{16,0},{1,17},{17,1},{2,18},{18,2},{3,19},{19,3},{4,20},{20... | collective-permute-start | bytes 3145736 | tf_op jit(solution)/shard_map/ppermute | solution.py:188
  (96 shorter events, 25.4 us)
Async XLA Ops:
  0.6 83.8 %copy-start = (f32[256,256]{1,0:T(8,128)S(1)}, f32[256,256]{1,0:T(8,128)}, u32[]{:S(2)}) copy-start(f32[256,256]{1,0:T(8,128)} %param.11) | copy-start | bytes 786436
  0.6 3.2 %collective-permute-start.1 = (f32[2048,128]{1,0:T(8,128)}, f32[2048,128]{1,0:T(8,128)S(1)}, u32[]{:S(2)}, u32[]{:S(2)}) collective-permute-start(f32[2048,128]{1,0:T(8,128)} %param.9), channel_id=1, source_target_pairs={{0,16},{16,0},{1,17},{17,1},{2,18},{18,2},{3,19},{19,3},{4,20},{20... | collective-permute-start | bytes 3145736 | tf_op jit(solution)/shard_map/ppermute | solution.py:188
  41.1 13.8 %collective-permute-start.5 = (f32[2,2,264,128]{3,2,1,0:T(8,128)}, f32[2,2,264,128]{3,2,1,0:T(8,128)}, u32[]{:S(2)}, u32[]{:S(2)}) collective-permute-start(f32[2,2,264,128]{3,2,1,0:T(8,128)} %dynamic-slice_bitcast_fusion.1), channel_id=1, source_target_pairs={{0,4},{2,6},{4,0},{6,2},{8,12},{10,14},{12,8},{14,10},{1,5},{3,7},... | collective-permute-start | bytes 1622024 | tf_op jit(solution)/shard_map/ppermute | solution.py:188
  42.0 14.4 %collective-permute-start.2 = (f32[2,2,264,128]{3,2,1,0:T(8,128)}, f32[2,2,264,128]{3,2,1,0:T(8,128)}, u32[]{:S(2)}, u32[]{:S(2)}) collective-permute-start(f32[2,2,264,128]{3,2,1,0:T(8,128)} %dynamic-slice_bitcast_fusion.2), channel_id=1, source_target_pairs={{0,2},{2,0},{4,6},{6,4},{8,10},{10,8},{12,14},{14,12},{1,3},{3,1},... | collective-permute-start | bytes 1622024 | tf_op jit(solution)/shard_map/ppermute | solution.py:188
  42.2 35.1 %collective-permute-start = (f32[512,128]{1,0:T(8,128)S(1)}, f32[512,128]{1,0:T(8,128)S(1)}, u32[]{:S(2)}, u32[]{:S(2)}) collective-permute-start(f32[512,128]{1,0:T(8,128)S(1)} %copy-done.2), channel_id=1, source_target_pairs={{0,1},{1,0},{2,3},{3,2},{4,5},{5,4},{6,7},{7,6},{8,9},{9,8},{10,11... | collective-permute-start | bytes 786440 | tf_op jit(solution)/shard_map/ppermute | solution.py:188
  56.0 6.9 %collective-permute-start.6 = (f32[2,264,128]{2,1,0:T(8,128)S(1)}, f32[2,264,128]{2,1,0:T(8,128)S(1)}, u32[]{:S(2)}, u32[]{:S(2)}) collective-permute-start(f32[2,264,128]{2,1,0:T(8,128)S(1)} %dynamic-slice_bitcast_fusion.3), channel_id=1, source_target_pairs={{0,2},{2,0},{4,6},{6,4},{8,10},{10,8},{12,14},{14,12},{1,3},{3,1},... | collective-permute-start | bytes 811016 | tf_op jit(solution)/shard_map/ppermute | solution.py:188
  57.5 6.6 %collective-permute-start.3 = (f32[2,264,128]{2,1,0:T(8,128)S(1)}, f32[2,264,128]{2,1,0:T(8,128)S(1)}, u32[]{:S(2)}, u32[]{:S(2)}) collective-permute-start(f32[2,264,128]{2,1,0:T(8,128)S(1)} %dynamic-slice_bitcast_fusion.4), channel_id=1, source_target_pairs={{0,4},{2,6},{4,0},{6,2},{8,12},{10,14},{12,8},{14,10},{1,5},{3,7},... | collective-permute-start | bytes 811016 | tf_op jit(solution)/shard_map/ppermute | solution.py:188
  63.0 20.9 %copy-start.3 = (f32[256,256]{1,0:T(8,128)S(1)}, f32[256,256]{1,0:T(8,128)}, u32[]{:S(2)}) copy-start(f32[256,256]{1,0:T(8,128)} %param.12) | copy-start | bytes 786436
  63.0 11.0 %collective-permute-start.7 = (f32[264,128]{1,0:T(8,128)S(1)}, f32[264,128]{1,0:T(8,128)S(1)}, u32[]{:S(2)}, u32[]{:S(2)}) collective-permute-start(f32[264,128]{1,0:T(8,128)S(1)} %dynamic-slice_bitcast_fusion.5), channel_id=1, source_target_pairs={{0,8},{2,10},{4,12},{6,14},{8,0},{10,2},{12,4},{14,6},{1,9},{3,11}... | collective-permute-start | bytes 405512 | tf_op jit(solution)/shard_map/ppermute | solution.py:188
  64.2 20.3 %copy-start.4 = (f32[512,128]{1,0:T(8,128)S(1)}, f32[512,128]{1,0:T(8,128)}, u32[]{:S(2)}) copy-start(f32[512,128]{1,0:T(8,128)} %param.13) | copy-start | bytes 786436
  64.2 12.7 %collective-permute-start.4 = (f32[264,128]{1,0:T(8,128)S(1)}, f32[264,128]{1,0:T(8,128)S(1)}, u32[]{:S(2)}, u32[]{:S(2)}) collective-permute-start(f32[264,128]{1,0:T(8,128)S(1)} %dynamic-slice_bitcast_fusion.6), channel_id=1, source_target_pairs={{0,8},{2,10},{4,12},{6,14},{8,0},{10,2},{12,4},{14,6},{1,9},{3,11}... | collective-permute-start | bytes 405512 | tf_op jit(solution)/shard_map/ppermute | solution.py:188
  77.0 6.8 %collective-permute-start.8 = (f32[512,128]{1,0:T(8,128)S(1)}, f32[512,128]{1,0:T(8,128)S(1)}, u32[]{:S(2)}, u32[]{:S(2)}) collective-permute-start(f32[512,128]{1,0:T(8,128)S(1)} %fusion.11), channel_id=1, source_target_pairs={{0,1},{1,0},{2,3},{3,2},{4,5},{5,4},{6,7},{7,6},{8,9},{9,8},{10,11... | collective-permute-start | bytes 786440 | tf_op jit(solution)/shard_map/ppermute | solution.py:188
  85.8 5.9 %collective-permute-start.9 = (f32[512,128]{1,0:T(8,128)S(1)}, f32[512,128]{1,0:T(8,128)S(1)}, u32[]{:S(2)}, u32[]{:S(2)}) collective-permute-start(f32[512,128]{1,0:T(8,128)S(1)} %get-tuple-element.62), channel_id=1, source_target_pairs={{0,1},{1,0},{2,3},{3,2},{4,5},{5,4},{6,7},{7,6},{8,9},{9,8},{10,11... | collective-permute-start | bytes 786440 | tf_op jit(solution)/shard_map/ppermute | solution.py:188
  93.4 9.5 %collective-permute-start.17 = (f32[128,256]{1,0:T(8,128)S(1)}, f32[128,256]{1,0:T(8,128)S(1)}, u32[]{:S(2)}, u32[]{:S(2)}) collective-permute-start(f32[128,256]{1,0:T(8,128)S(1)} %get-tuple-element.60), channel_id=1, source_target_pairs={{0,8},{2,10},{4,12},{6,14},{8,0},{10,2},{12,4},{14,6},{1,9},{3,11}... | collective-permute-start | bytes 393224 | tf_op jit(solution)/shard_map/ppermute | solution.py:188
  94.5 11.2 %collective-permute-start.14 = (f32[128,256]{1,0:T(8,128)S(1)}, f32[128,256]{1,0:T(8,128)S(1)}, u32[]{:S(2)}, u32[]{:S(2)}) collective-permute-start(f32[128,256]{1,0:T(8,128)S(1)} %get-tuple-element.61), channel_id=1, source_target_pairs={{0,8},{2,10},{4,12},{6,14},{8,0},{10,2},{12,4},{14,6},{1,9},{3,11}... | collective-permute-start | bytes 393224 | tf_op jit(solution)/shard_map/ppermute | solution.py:188
  96.9 8.9 %collective-permute-start.10 = (f32[2,128,256]{1,2,0:T(8,128)S(1)}, f32[2,128,256]{1,2,0:T(8,128)S(1)}, u32[]{:S(2)}, u32[]{:S(2)}) collective-permute-start(f32[2,128,256]{1,2,0:T(8,128)S(1)} %pad_maximum_fusion.6), channel_id=1, source_target_pairs={{0,16},{16,0},{1,17},{17,1},{2,18},{18,2},{3,19},{19,3},{4,20},{20... | collective-permute-start | bytes 786440 | tf_op jit(solution)/shard_map/ppermute | solution.py:188
  102.9 5.8 %collective-permute-start.18 = (f32[2,128,256]{2,1,0:T(8,128)S(1)}, f32[2,128,256]{2,1,0:T(8,128)S(1)}, u32[]{:S(2)}, u32[]{:S(2)}) collective-permute-start(f32[2,128,256]{2,1,0:T(8,128)S(1)} %maximum_select_fusion.9), channel_id=1, source_target_pairs={{0,2},{2,0},{4,6},{6,4},{8,10},{10,8},{12,14},{14,12},{1,3},{3,1},... | collective-permute-start | bytes 786440 | tf_op jit(solution)/shard_map/ppermute | solution.py:188
  105.7 6.7 %collective-permute-start.15 = (f32[2,128,256]{2,1,0:T(8,128)S(1)}, f32[2,128,256]{2,1,0:T(8,128)S(1)}, u32[]{:S(2)}, u32[]{:S(2)}) collective-permute-start(f32[2,128,256]{2,1,0:T(8,128)S(1)} %maximum_select_fusion.7), channel_id=1, source_target_pairs={{0,4},{2,6},{4,0},{6,2},{8,12},{10,14},{12,8},{14,10},{1,5},{3,7},... | collective-permute-start | bytes 786440 | tf_op jit(solution)/shard_map/ppermute | solution.py:188
  105.9 8.4 %collective-permute-start.11 = (f32[2,128,256]{1,2,0:T(8,128)S(1)}, f32[2,128,256]{1,2,0:T(8,128)S(1)}, u32[]{:S(2)}, u32[]{:S(2)}) collective-permute-start(f32[2,128,256]{1,2,0:T(8,128)S(1)} %fusion.31), channel_id=1, source_target_pairs={{0,2},{2,0},{4,6},{6,4},{8,10},{10,8},{12,14},{14,12},{1,3},{3,1},... | collective-permute-start | bytes 786440 | tf_op jit(solution)/shard_map/ppermute | solution.py:188
  108.8 18.9 %collective-permute-start.19 = (f32[2,2,128,256]{3,2,0,1:T(8,128)S(1)}, f32[2,2,128,256]{3,2,0,1:T(8,128)S(1)}, u32[]{:S(2)}, u32[]{:S(2)}) collective-permute-start(f32[2,2,128,256]{3,2,0,1:T(8,128)S(1)} %maximum_select_fusion.6), channel_id=1, source_target_pairs={{0,4},{2,6},{4,0},{6,2},{8,12},{10,14},{12,8},{14,10},{1,5},{3,7},... | collective-permute-start | bytes 1572872 | tf_op jit(solution)/shard_map/ppermute | solution.py:188
  112.5 15.4 %collective-permute-start.16 = (f32[2,2,128,256]{3,2,0,1:T(8,128)S(1)}, f32[2,2,128,256]{3,2,0,1:T(8,128)S(1)}, u32[]{:S(2)}, u32[]{:S(2)}) collective-permute-start(f32[2,2,128,256]{3,2,0,1:T(8,128)S(1)} %maximum_select_fusion.4), channel_id=1, source_target_pairs={{0,2},{2,0},{4,6},{6,4},{8,10},{10,8},{12,14},{14,12},{1,3},{3,1},... | collective-permute-start | bytes 1572872 | tf_op jit(solution)/shard_map/ppermute | solution.py:188
  114.4 13.1 %collective-permute-start.12 = (f32[2,128,256]{1,2,0:T(8,128)S(1)}, f32[2,128,256]{1,2,0:T(8,128)S(1)}, u32[]{:S(2)}, u32[]{:S(2)}) collective-permute-start(f32[2,128,256]{1,2,0:T(8,128)S(1)} %fusion.37), channel_id=1, source_target_pairs={{0,4},{2,6},{4,0},{6,2},{8,12},{10,14},{12,8},{14,10},{1,5},{3,7},... | collective-permute-start | bytes 786440 | tf_op jit(solution)/shard_map/ppermute | solution.py:188
  127.6 13.4 %collective-permute-start.13 = (f32[2,128,256]{1,2,0:T(8,128)S(1)}, f32[2,128,256]{1,2,0:T(8,128)S(1)}, u32[]{:S(2)}, u32[]{:S(2)}) collective-permute-start(f32[2,128,256]{1,2,0:T(8,128)S(1)} %add.120), channel_id=1, source_target_pairs={{0,8},{2,10},{4,12},{6,14},{8,0},{10,2},{12,4},{14,6},{1,9},{3,11}... | collective-permute-start | bytes 786440 | tf_op jit(solution)/shard_map/ppermute | solution.py:188
  169.5 4.7 %collective-permute-start.20 = (f32[128,2048]{1,0:T(8,128)}, f32[128,2048]{1,0:T(8,128)}, u32[]{:S(2)}, u32[]{:S(2)}) collective-permute-start(f32[128,2048]{1,0:T(8,128)} %dynamic-slice_bitcast_fusion), channel_id=1, source_target_pairs={{0,16},{16,0},{1,17},{17,1},{2,18},{18,2},{3,19},{19,3},{4,20},{20... | collective-permute-start | bytes 3145736 | tf_op jit(solution)/shard_map/ppermute | solution.py:188
  (2 other events, 9.1 us)

commit v9 on v7

--- a/solution.py
+++ b/solution.py
@@ -11,10 +11,9 @@
 SLOT_GROUP = 64
 
 
-def split_hi_lo(values):
+def split_hi_lo(values, axis):
     high = lax.reduce_precision(values, exponent_bits=8, mantissa_bits=7)
-    low = values - high
-    return jnp.concatenate([high, low], axis=1).astype(jnp.bfloat16)
+    return jnp.stack([high, values - high], axis=axis).astype(jnp.bfloat16)
 
 
 def unpack_bits(words):
@@ -25,6 +24,24 @@
     return bits.reshape(word_rows * 8, edge)
 
 
+def unpack_bit_major(words):
+    return jnp.concatenate(
+        [jnp.bitwise_and(jnp.right_shift(words, bit), 1) for bit in range(8)], axis=0
+    )
+
+
+def to_bit_major(rows, edge):
+    count, width = rows.shape
+    shaped = rows.reshape(count // edge, edge // 8, 8, width)
+    return jnp.swapaxes(shaped, 1, 2).reshape(count, width)
+
+
+def from_bit_major(rows, edge):
+    count, width = rows.shape
+    shaped = rows.reshape(count // edge, 8, edge // 8, width)
+    return jnp.swapaxes(shaped, 1, 2).reshape(count, width)
+
+
 def unpack_block(words):
     return unpack_bits(words).astype(jnp.float32)
 
@@ -45,8 +62,7 @@
 def forward_kernel(live_ref, rows_ref, cols_ref, masks_ref, panel_ref, totals_ref, bits_ref):
     group, _, edge = masks_ref.shape
     row_limit = totals_ref.shape[0] // edge - 1
-    col_limit = panel_ref.shape[0] // edge - 1
-    half = totals_ref.shape[1]
+    col_limit = panel_ref.shape[1] // edge - 1
 
     @pl.when(pl.program_id(0) == 0)
     def _():
@@ -62,13 +78,19 @@
             row = jnp.clip(rows_ref[slot], 0, row_limit)
             col = jnp.clip(cols_ref[slot], 0, col_limit)
             keep = jnp.where(slot < live_ref[0], -1, 0).astype(jnp.int32)
-            bits = unpack_bits(jnp.bitwise_and(masks_ref[k], keep))
+            bits = unpack_bit_major(jnp.bitwise_and(masks_ref[k], keep))
             bits_ref[row] += bits
             dense = bits.astype(jnp.float32).astype(jnp.bfloat16)
-            tile = panel_ref[pl.ds(pl.multiple_of(col * edge, edge), edge), :]
-            prod = jnp.dot(dense, tile, preferred_element_type=jnp.float32)
+            col_start = pl.multiple_of(col * edge, edge)
+            tile = jnp.concatenate(
+                [panel_ref[0, pl.ds(col_start, edge), :], panel_ref[1, pl.ds(col_start, edge), :]],
+                axis=0,
+            )
+            prod = jnp.dot(
+                jnp.concatenate([dense, dense], axis=1), tile, preferred_element_type=jnp.float32
+            )
             start = pl.multiple_of(row * edge, edge)
-            totals_ref[pl.ds(start, edge), :] += prod[:, :half] + prod[:, half:]
+            totals_ref[pl.ds(start, edge), :] += prod
             return carry
 
         lax.fori_loop(0, group, body, 0, unroll=UNROLL)
@@ -76,11 +98,10 @@
 
 def backward_kernel(live_ref, rows_ref, cols_ref, masks_ref, lifted_ref, out_ref):
     group, _, edge = masks_ref.shape
-    row_chunk = lifted_ref.shape[2] // edge
+    row_chunk = lifted_ref.shape[3] // edge
     col_chunk = out_ref.shape[2] // edge
     row_limit = lifted_ref.shape[0] * row_chunk - 1
     col_limit = out_ref.shape[0] * col_chunk - 1
-    half = out_ref.shape[1]
 
     @pl.when(pl.program_id(0) == 0)
     def _():
@@ -94,12 +115,23 @@
             slot = base + k
             row = jnp.clip(rows_ref[slot], 0, row_limit)
             col = jnp.clip(cols_ref[slot], 0, col_limit)
-            dense = slot_words(masks_ref, live_ref, base, k)
+            keep = jnp.where(slot < live_ref[0], -1, 0).astype(jnp.int32)
+            bits = unpack_bit_major(jnp.bitwise_and(masks_ref[k], keep))
+            dense = bits.astype(jnp.float32).astype(jnp.bfloat16)
             row_start = pl.multiple_of((row % row_chunk) * edge, edge)
-            tile = lifted_ref[row // row_chunk, :, pl.ds(row_start, edge)]
-            prod = jnp.dot(tile, dense, preferred_element_type=jnp.float32)
+            chunk = row // row_chunk
+            tile = jnp.concatenate(
+                [
+                    lifted_ref[chunk, 0, :, pl.ds(row_start, edge)],
+                    lifted_ref[chunk, 1, :, pl.ds(row_start, edge)],
+                ],
+                axis=1,
+            )
+            prod = jnp.dot(
+                tile, jnp.concatenate([dense, dense], axis=0), preferred_element_type=jnp.float32
+            )
             col_start = pl.multiple_of((col % col_chunk) * edge, edge)
-            out_ref[col // col_chunk, :, pl.ds(col_start, edge)] += prod[:half] + prod[half:]
+            out_ref[col // col_chunk, :, pl.ds(col_start, edge)] += prod
             return carry
 
         lax.fori_loop(0, group, body, 0, unroll=UNROLL)
@@ -138,19 +170,19 @@
 
 def block_aggregate(live, block_rows, block_cols, packed_masks, panel_split, row_blocks):
     edge = packed_masks.shape[-1]
-    totals_shape = jax.ShapeDtypeStruct((row_blocks * edge, panel_split.shape[1] // 2), jnp.float32)
+    totals_shape = jax.ShapeDtypeStruct((row_blocks * edge, panel_split.shape[2]), jnp.float32)
     bits_shape = jax.ShapeDtypeStruct((row_blocks, edge, edge), jnp.int32)
     totals, bit_sums = slot_pallas(
         forward_kernel, live, block_rows, block_cols, packed_masks, panel_split,
         [totals_shape, bits_shape],
     )
-    return totals, jnp.sum(bit_sums, axis=-1).astype(jnp.float32).reshape(-1)
+    counts = jnp.sum(bit_sums, axis=-1).astype(jnp.float32).reshape(-1, 1)
+    return totals, from_bit_major(counts, edge).reshape(-1)
 
 
 def block_transpose(live, block_rows, block_cols, packed_masks, lifted_chunks, cand_count):
     edge = packed_masks.shape[-1]
-    high = lax.reduce_precision(lifted_chunks, exponent_bits=8, mantissa_bits=7)
-    split_t = jnp.concatenate([high, lifted_chunks - high], axis=1).astype(jnp.bfloat16)
+    split_t = split_hi_lo(lifted_chunks, 1)
     width = lifted_chunks.shape[1]
     panel_cols = lifted_chunks.shape[0] * lifted_chunks.shape[2]
     out_shape = jax.ShapeDtypeStruct((cand_count, width, panel_cols // cand_count), jnp.float32)
@@ -292,10 +324,10 @@
     panel = doubling_gather(x_test, "cand")
     cand_full = gather_axis(x_cand, "feat", 1)
     row_totals, row_counts = block_aggregate(
-        live, block_rows, block_cols, packed_masks, split_hi_lo(panel), row_blocks
+        live, block_rows, block_cols, packed_masks, split_hi_lo(panel, 0), row_blocks
     )
     own_totals, degree = scatter_totals_and_counts(row_totals, row_counts, test_count)
-    aggregated = own_totals / (1.0 + degree)[:, None]
+    aggregated = from_bit_major(own_totals, block_edge) / (1.0 + degree)[:, None]
     self_cols = lax.dynamic_slice_in_dim(w_self, feat_index * half_width, half_width, 1)
     neigh_cols = lax.dynamic_slice_in_dim(w_neigh, feat_index * half_width, half_width, 1)
     self_rows = lax.dynamic_slice_in_dim(w_self, feat_index * half_width, half_width, 0)
@@ -315,7 +347,7 @@
     grad_x_cand = jnp.dot(grad_full, self_rows.T, precision=HIGHEST)
     grad_agg = jnp.dot(grad_full, neigh_rows.T, precision=HIGHEST)
     lifted = grad_agg / (1.0 + degree)[:, None]
-    lifted_chunks = doubling_gather_lanes(lifted.T, "test")
+    lifted_chunks = doubling_gather_lanes(to_bit_major(lifted, block_edge).T, "test")
     grad_w_pair, lifted_chunks = lax.optimization_barrier((grad_w_pair, lifted_chunks))
     grad_w_self = grad_w_pair[0] / root_count
     grad_w_neigh = grad_w_pair[1] / root_count

time: 172 us -> 182 us (1.058)
  starting transfers between devices: 20.6 us -> 14.1 us
  other arithmetic: 11.9 us -> 17.8 us
  waiting for transfers between devices: 75.5 us -> 81.3 us
  local copies, waits for them, and re-layouts: 7.55 us -> 10.9 us
    ppermute x21, starting transfers between devices: 20.6 us -> 14.1 us  [exchange(): return lax.ppermute(values, axis, [(i, i ^ 1 << bit) for i in range(count)])]
    ppermute x21, waiting for transfers between devices: 75.5 us -> 81.3 us  [exchange(): return lax.ppermute(values, axis, [(i, i ^ 1 << bit) for i in range(count)])]
    another operation x2 -> x4, other arithmetic: 0.73 us -> 3.77 us  [the longest x3 3.44 us: split_hi_lo(): return jnp.stack([high, values - high], axis=axis).astype(jnp.bfloat16)]
    concatenate x2 -> x1, other arithmetic: 3.04 us -> 0.02 us  [halving_scatter(): return jnp.concatenate(results, axis=0)]
    select_n x11, other arithmetic: 2.19 us -> 4.27 us  [doubling_steps(): jnp.where(first, jnp.stack([data, other], axis=position), jnp.stack([othe...]
    unnamed x17 -> x22, local copies, waits for them, and re-layouts: 3.82 us -> 4.91 us
  transfers between devices with their start and end apart: 21 -> 21, of which waited for: 17 -> 15; matrix products, arithmetic and copies ran while one was open for 4% -> 8% of each run, Pallas kernels for 0% -> 0%
where the time goes in v9:
time: 182 us; the launch traced here: 181 us
  waiting for transfers between devices  81.3 us (45%)
  Pallas kernels  50.2 us (28%)
  other arithmetic  17.8 us (10%)
  starting transfers between devices  14.1 us (8%)
  local copies, waits for them, and re-layouts  10.9 us (6%)
  matrix products  5.08 us (3%)
    ppermute x21, waiting for transfers between devices, exchange(): return lax.ppermute(values, axis, [(i, i ^ 1 << bit) for i in range(count)])  81.3 us
    pallas_call x2, Pallas kernels, slot_pallas(): pl.pallas_call(kernel, grid_spec=grid_spec, out_shape=out_shapes, compile...  50.2 us
    ppermute x21, starting transfers between devices, exchange(): return lax.ppermute(values, axis, [(i, i ^ 1 << bit) for i in range(count)])  14.1 us
    unnamed x22, local copies, waits for them, and re-layouts  4.91 us
    select_n x11, other arithmetic, doubling_steps(): jnp.where(first, jnp.stack([data, other], axis=position), jnp.stack([othe...  4.27 us
  transfers between devices with their start and end apart: 21, of which 15 were waited for; matrix products, arithmetic and copies ran while one was open for 8% of the time, Pallas kernels for 0%

profile of v9, /device:TPU:31, one launch (start us, length us, event | category | flops | bytes accessed | tf_op | source)
XLA Modules:
  0.0 181.1 jit_solution(13291404896092303877)
XLA Ops:
  2.1 1.8 collective-permute-done.1
  3.9 1.7 maximum_select_fusion
  6.0 1.5 pad_maximum_fusion.panel_ref
  7.5 24.6 %shard_map.128 = (f32[4096,128]{1,0:T(8,128)}, s32[32,128,128]{2,1,0:T(8,128)}) custom-call(s32[1]{0:T(128)} %bitcast.live_ref, s32[512]{0:T(512)} %bitcast.146, s32[512]{0:T(512)} %bitcast.148, s32[512,16,128]{2,1,0:T(8,128)} %bitcast.118, bf16[2,4096,128]{2,1,0:T(8,128)(2,1)} %pad_maximum_fusion.panel_ref), custom_call_target="tpu_custom_call" | custom-call | tf_op jit(solution)/shard_map/pallas_call | solution.py:163
  32.1 2.4 %reduce_sum.9 = s32[32,128]{1,0:T(8,128)S(1)} reduce(s32[32,128,128]{2,1,0:T(8,128)} %get-tuple-element.10, s32[]{:T(128)} %constant.70.clone.1), dimensions={2}, to_apply=%region_0.1 | reduce | flops 520192 | bytes 2113540 | tf_op jit(solution)/shard_map/reduce_sum | solution.py:179
  37.5 12.2 %collective-permute-done.5 = f32[2,2,264,128]{3,2,1,0:T(8,128)S(1)} collective-permute-done((f32[2,2,264,128]{3,2,1,0:T(8,128)S(1)}, f32[2,2,264,128]{3,2,1,0:T(8,128)S(1)}, u32[]{:S(2)}, u32[]{:S(2)}) %collective-permute-start.5) | collective-permute-done | bytes 540704 | tf_op jit(solution)/shard_map/ppermute | solution.py:204
  52.1 5.6 %collective-permute-done.6 = f32[2,264,128]{2,1,0:T(8,128)S(1)} collective-permute-done((f32[2,264,128]{2,1,0:T(8,128)S(1)}, f32[2,264,128]{2,1,0:T(8,128)S(1)}, u32[]{:S(2)}, u32[]{:S(2)}) %collective-permute-start.6) | collective-permute-done | bytes 270368 | tf_op jit(solution)/shard_map/ppermute | solution.py:204
  57.9 2.4 %collective-permute-start.4 = (f32[264,128]{1,0:T(8,128)S(1)}, f32[264,128]{1,0:T(8,128)S(1)}, u32[]{:S(2)}, u32[]{:S(2)}) collective-permute-start(f32[264,128]{1,0:T(8,128)S(1)} %dynamic-slice_bitcast_fusion.6), channel_id=1, source_target_pairs={{0,8},{2,10},{4,12},{6,14},{8,0},{10,2},{12,4},{14,6},{1,9},{3,11}... | collective-permute-start | bytes 405512 | tf_op jit(solution)/shard_map/ppermute | solution.py:204
  60.3 9.4 %collective-permute-done.7 = f32[264,128]{1,0:T(8,128)S(1)} collective-permute-done((f32[264,128]{1,0:T(8,128)S(1)}, f32[264,128]{1,0:T(8,128)S(1)}, u32[]{:S(2)}, u32[]{:S(2)}) %collective-permute-start.7) | collective-permute-done | bytes 135200 | tf_op jit(solution)/shard_map/ppermute | solution.py:204
  69.8 2.9 %collective-permute-done.4 = f32[264,128]{1,0:T(8,128)S(1)} collective-permute-done((f32[264,128]{1,0:T(8,128)S(1)}, f32[264,128]{1,0:T(8,128)S(1)}, u32[]{:S(2)}, u32[]{:S(2)}) %collective-permute-start.4) | collective-permute-done | bytes 135200 | tf_op jit(solution)/shard_map/ppermute | solution.py:204
  74.4 5.7 %collective-permute-done.8 = f32[512,128]{0,1:T(8,128)S(1)} collective-permute-done((f32[512,128]{0,1:T(8,128)S(1)}, f32[512,128]{0,1:T(8,128)S(1)}, u32[]{:S(2)}, u32[]{:S(2)}) %collective-permute-start.8) | collective-permute-done | bytes 262176 | tf_op jit(solution)/shard_map/ppermute | solution.py:204
  82.2 6.0 %collective-permute-done.9 = f32[512,128]{0,1:T(8,128)S(1)} collective-permute-done((f32[512,128]{0,1:T(8,128)S(1)}, f32[512,128]{0,1:T(8,128)S(1)}, u32[]{:S(2)}, u32[]{:S(2)}) %collective-permute-start.9) | collective-permute-done | bytes 262176 | tf_op jit(solution)/shard_map/ppermute | solution.py:204
  90.2 2.4 %collective-permute-start.17 = (f32[128,256]{0,1:T(8,128)S(1)}, f32[128,256]{0,1:T(8,128)S(1)}, u32[]{:S(2)}, u32[]{:S(2)}) collective-permute-start(f32[128,256]{0,1:T(8,128)S(1)} %get-tuple-element.56), channel_id=1, source_target_pairs={{0,8},{2,10},{4,12},{6,14},{8,0},{10,2},{12,4},{14,6},{1,9},{3,11}... | collective-permute-start | bytes 393224 | tf_op jit(solution)/shard_map/ppermute | solution.py:204
  92.7 3.1 %collective-permute-start.10 = (f32[2,128,256]{1,2,0:T(8,128)S(1)}, f32[2,128,256]{1,2,0:T(8,128)S(1)}, u32[]{:S(2)}, u32[]{:S(2)}) collective-permute-start(f32[2,128,256]{1,2,0:T(8,128)S(1)} %pad_maximum_fusion.6), channel_id=1, source_target_pairs={{0,16},{16,0},{1,17},{17,1},{2,18},{18,2},{3,19},{19,3},{4,20},{20... | collective-permute-start | bytes 786440 | tf_op jit(solution)/shard_map/ppermute | solution.py:204
  95.8 3.9 %collective-permute-done.14 = f32[128,256]{0,1:T(8,128)S(1)} collective-permute-done((f32[128,256]{0,1:T(8,128)S(1)}, f32[128,256]{0,1:T(8,128)S(1)}, u32[]{:S(2)}, u32[]{:S(2)}) %collective-permute-start.14) | collective-permute-done | bytes 131104 | tf_op jit(solution)/shard_map/ppermute | solution.py:204
  99.8 2.7 %collective-permute-done.17 = f32[128,256]{0,1:T(8,128)S(1)} collective-permute-done((f32[128,256]{0,1:T(8,128)S(1)}, f32[128,256]{0,1:T(8,128)S(1)}, u32[]{:S(2)}, u32[]{:S(2)}) %collective-permute-start.17) | collective-permute-done | bytes 131104 | tf_op jit(solution)/shard_map/ppermute | solution.py:204
  104.3 3.0 %collective-permute-done.15 = f32[2,128,256]{1,2,0:T(8,128)S(1)} collective-permute-done((f32[2,128,256]{1,2,0:T(8,128)S(1)}, f32[2,128,256]{1,2,0:T(8,128)S(1)}, u32[]{:S(2)}, u32[]{:S(2)}) %collective-permute-start.15) | collective-permute-done | bytes 262176 | tf_op jit(solution)/shard_map/ppermute | solution.py:204
  107.4 2.3 %collective-permute-done.18 = f32[2,128,256]{1,2,0:T(8,128)S(1)} collective-permute-done((f32[2,128,256]{1,2,0:T(8,128)S(1)}, f32[2,128,256]{1,2,0:T(8,128)S(1)}, u32[]{:S(2)}, u32[]{:S(2)}) %collective-permute-start.18) | collective-permute-done | bytes 262176 | tf_op jit(solution)/shard_map/ppermute | solution.py:204
  110.6 4.8 %collective-permute-done.11 = f32[2,128,256]{1,2,0:T(8,128)S(1)} collective-permute-done((f32[2,128,256]{1,2,0:T(8,128)S(1)}, f32[2,128,256]{1,2,0:T(8,128)S(1)}, u32[]{:S(2)}, u32[]{:S(2)}) %collective-permute-start.11) | collective-permute-done | bytes 262176 | tf_op jit(solution)/shard_map/ppermute | solution.py:204
  115.6 11.5 %collective-permute-done.12 = f32[2,128,256]{1,2,0:T(8,128)S(1)} collective-permute-done((f32[2,128,256]{1,2,0:T(8,128)S(1)}, f32[2,128,256]{1,2,0:T(8,128)S(1)}, u32[]{:S(2)}, u32[]{:S(2)}) %collective-permute-start.12) | collective-permute-done | bytes 262176 | tf_op jit(solution)/shard_map/ppermute | solution.py:204
  132.4 9.5 %collective-permute-done.13 = f32[2,128,256]{1,2,0:T(8,128)} collective-permute-done((f32[2,128,256]{1,2,0:T(8,128)}, f32[2,128,256]{1,2,0:T(8,128)}, u32[]{:S(2)}, u32[]{:S(2)}) %collective-permute-start.13) | collective-permute-done | bytes 262176 | tf_op jit(solution)/shard_map/ppermute | solution.py:204
  145.0 25.6 %shard_map.129 = f32[2,128,2048]{2,1,0:T(8,128)} custom-call(s32[1]{0:T(128)} %bitcast.live_ref, s32[512]{0:T(512)} %bitcast.147, s32[512]{0:T(512)} %bitcast.149, s32[512,16,128]{2,1,0:T(8,128)} %bitcast.119, bf16[8,2,128,512]{3,2,1,0:T(8,128)(2,1)} %pad_maximum_fusion.2.lifted_ref), custom_call_target="tpu_custom_call" | custom-call | tf_op jit(solution)/shard_map/pallas_call | solution.py:163
  170.5 2.4 %dynamic-slice_bitcast_fusion = f32[128,2048]{1,0:T(8,128)} fusion(f32[2,128,2048]{2,1,0:T(8,128)} %shard_map.129, s32[]{:T(128)S(6)} %select_n.238), kind=kLoop, calls=%fused_computation.22 | loop fusion | bytes 2097156 | tf_op jit(solution)/shard_map/jit(dynamic_index_in_dim)/squeeze | solution.py:231
  175.2 1.7 fusion.15
  (107 shorter events, 30.2 us)
Async XLA Ops:
  0.6 80.1 %copy-start = (f32[256,256]{1,0:T(8,128)S(1)}, f32[256,256]{1,0:T(8,128)}, u32[]{:S(2)}) copy-start(f32[256,256]{1,0:T(8,128)} %param.11) | copy-start | bytes 786436
  0.6 3.2 %collective-permute-start.1 = (f32[2048,128]{1,0:T(8,128)}, f32[2048,128]{1,0:T(8,128)S(1)}, u32[]{:S(2)}, u32[]{:S(2)}) collective-permute-start(f32[2048,128]{1,0:T(8,128)} %param.9), channel_id=1, source_target_pairs={{0,16},{16,0},{1,17},{17,1},{2,18},{18,2},{3,19},{19,3},{4,20},{20... | collective-permute-start | bytes 3145736 | tf_op jit(solution)/shard_map/ppermute | solution.py:204
  36.2 13.5 %collective-permute-start.5 = (f32[2,2,264,128]{3,2,1,0:T(8,128)S(1)}, f32[2,2,264,128]{3,2,1,0:T(8,128)S(1)}, u32[]{:S(2)}, u32[]{:S(2)}) collective-permute-start(f32[2,2,264,128]{3,2,1,0:T(8,128)S(1)} %dynamic-slice_bitcast_fusion.1), channel_id=1, source_target_pairs={{0,4},{2,6},{4,0},{6,2},{8,12},{10,14},{12,8},{14,10},{1,5},{3,7},... | collective-permute-start | bytes 1622024 | tf_op jit(solution)/shard_map/ppermute | solution.py:204
  37.1 13.8 %collective-permute-start.2 = (f32[2,2,264,128]{3,2,1,0:T(8,128)}, f32[2,2,264,128]{3,2,1,0:T(8,128)S(1)}, u32[]{:S(2)}, u32[]{:S(2)}) collective-permute-start(f32[2,2,264,128]{3,2,1,0:T(8,128)} %dynamic-slice_bitcast_fusion.2), channel_id=1, source_target_pairs={{0,2},{2,0},{4,6},{6,4},{8,10},{10,8},{12,14},{14,12},{1,3},{3,1},... | collective-permute-start | bytes 1622024 | tf_op jit(solution)/shard_map/ppermute | solution.py:204
  37.2 36.2 %collective-permute-start = (f32[512,128]{0,1:T(8,128)S(1)}, f32[512,128]{0,1:T(8,128)}, u32[]{:S(2)}, u32[]{:S(2)}) collective-permute-start(f32[512,128]{0,1:T(8,128)S(1)} %copy.90), channel_id=1, source_target_pairs={{0,1},{1,0},{2,3},{3,2},{4,5},{5,4},{6,7},{7,6},{8,9},{9,8},{10,11... | collective-permute-start | bytes 786440 | tf_op jit(solution)/shard_map/ppermute | solution.py:204
  50.8 6.9 %collective-permute-start.6 = (f32[2,264,128]{2,1,0:T(8,128)S(1)}, f32[2,264,128]{2,1,0:T(8,128)S(1)}, u32[]{:S(2)}, u32[]{:S(2)}) collective-permute-start(f32[2,264,128]{2,1,0:T(8,128)S(1)} %dynamic-slice_bitcast_fusion.3), channel_id=1, source_target_pairs={{0,2},{2,0},{4,6},{6,4},{8,10},{10,8},{12,14},{14,12},{1,3},{3,1},... | collective-permute-start | bytes 811016 | tf_op jit(solution)/shard_map/ppermute | solution.py:204
  51.0 6.9 %collective-permute-start.3 = (f32[2,264,128]{2,1,0:T(8,128)S(1)}, f32[2,264,128]{2,1,0:T(8,128)S(1)}, u32[]{:S(2)}, u32[]{:S(2)}) collective-permute-start(f32[2,264,128]{2,1,0:T(8,128)S(1)} %dynamic-slice_bitcast_fusion.4), channel_id=1, source_target_pairs={{0,4},{2,6},{4,0},{6,2},{8,12},{10,14},{12,8},{14,10},{1,5},{3,7},... | collective-permute-start | bytes 811016 | tf_op jit(solution)/shard_map/ppermute | solution.py:204
  57.7 15.5 %copy-start.5 = (f32[512,128]{1,0:T(8,128)S(1)}, f32[512,128]{1,0:T(8,128)}, u32[]{:S(2)}) copy-start(f32[512,128]{1,0:T(8,128)} %param.13) | copy-start | bytes 786436
  57.8 12.0 %collective-permute-start.7 = (f32[264,128]{1,0:T(8,128)S(1)}, f32[264,128]{1,0:T(8,128)S(1)}, u32[]{:S(2)}, u32[]{:S(2)}) collective-permute-start(f32[264,128]{1,0:T(8,128)S(1)} %dynamic-slice_bitcast_fusion.5), channel_id=1, source_target_pairs={{0,8},{2,10},{4,12},{6,14},{8,0},{10,2},{12,4},{14,6},{1,9},{3,11}... | collective-permute-start | bytes 405512 | tf_op jit(solution)/shard_map/ppermute | solution.py:204
  57.9 14.7 %collective-permute-start.4 = (f32[264,128]{1,0:T(8,128)S(1)}, f32[264,128]{1,0:T(8,128)S(1)}, u32[]{:S(2)}, u32[]{:S(2)}) collective-permute-start(f32[264,128]{1,0:T(8,128)S(1)} %dynamic-slice_bitcast_fusion.6), channel_id=1, source_target_pairs={{0,8},{2,10},{4,12},{6,14},{8,0},{10,2},{12,4},{14,6},{1,9},{3,11}... | collective-permute-start | bytes 405512 | tf_op jit(solution)/shard_map/ppermute | solution.py:204
  73.0 7.2 %collective-permute-start.8 = (f32[512,128]{0,1:T(8,128)S(1)}, f32[512,128]{0,1:T(8,128)S(1)}, u32[]{:S(2)}, u32[]{:S(2)}) collective-permute-start(f32[512,128]{0,1:T(8,128)S(1)} %broadcast_divide_fusion), channel_id=1, source_target_pairs={{0,1},{1,0},{2,3},{3,2},{4,5},{5,4},{6,7},{7,6},{8,9},{9,8},{10,11... | collective-permute-start | bytes 786440 | tf_op jit(solution)/shard_map/ppermute | solution.py:204
  82.0 6.2 %collective-permute-start.9 = (f32[512,128]{0,1:T(8,128)S(1)}, f32[512,128]{0,1:T(8,128)S(1)}, u32[]{:S(2)}, u32[]{:S(2)}) collective-permute-start(f32[512,128]{0,1:T(8,128)S(1)} %get-tuple-element.58), channel_id=1, source_target_pairs={{0,1},{1,0},{2,3},{3,2},{4,5},{5,4},{6,7},{7,6},{8,9},{9,8},{10,11... | collective-permute-start | bytes 786440 | tf_op jit(solution)/shard_map/ppermute | solution.py:204
  89.6 10.2 %collective-permute-start.14 = (f32[128,256]{0,1:T(8,128)S(1)}, f32[128,256]{0,1:T(8,128)S(1)}, u32[]{:S(2)}, u32[]{:S(2)}) collective-permute-start(f32[128,256]{0,1:T(8,128)S(1)} %get-tuple-element.57), channel_id=1, source_target_pairs={{0,8},{2,10},{4,12},{6,14},{8,0},{10,2},{12,4},{14,6},{1,9},{3,11}... | collective-permute-start | bytes 393224 | tf_op jit(solution)/shard_map/ppermute | solution.py:204
  90.2 12.3 %collective-permute-start.17 = (f32[128,256]{0,1:T(8,128)S(1)}, f32[128,256]{0,1:T(8,128)S(1)}, u32[]{:S(2)}, u32[]{:S(2)}) collective-permute-start(f32[128,256]{0,1:T(8,128)S(1)} %get-tuple-element.56), channel_id=1, source_target_pairs={{0,8},{2,10},{4,12},{6,14},{8,0},{10,2},{12,4},{14,6},{1,9},{3,11}... | collective-permute-start | bytes 393224 | tf_op jit(solution)/shard_map/ppermute | solution.py:204
  92.7 10.0 %collective-permute-start.10 = (f32[2,128,256]{1,2,0:T(8,128)S(1)}, f32[2,128,256]{1,2,0:T(8,128)S(1)}, u32[]{:S(2)}, u32[]{:S(2)}) collective-permute-start(f32[2,128,256]{1,2,0:T(8,128)S(1)} %pad_maximum_fusion.6), channel_id=1, source_target_pairs={{0,16},{16,0},{1,17},{17,1},{2,18},{18,2},{3,19},{19,3},{4,20},{20... | collective-permute-start | bytes 786440 | tf_op jit(solution)/shard_map/ppermute | solution.py:204
  99.7 7.6 %collective-permute-start.15 = (f32[2,128,256]{1,2,0:T(8,128)S(1)}, f32[2,128,256]{1,2,0:T(8,128)S(1)}, u32[]{:S(2)}, u32[]{:S(2)}) collective-permute-start(f32[2,128,256]{1,2,0:T(8,128)S(1)} %maximum_select_fusion.7), channel_id=1, source_target_pairs={{0,4},{2,6},{4,0},{6,2},{8,12},{10,14},{12,8},{14,10},{1,5},{3,7},... | collective-permute-start | bytes 786440 | tf_op jit(solution)/shard_map/ppermute | solution.py:204
  102.6 7.2 %collective-permute-start.18 = (f32[2,128,256]{1,2,0:T(8,128)S(1)}, f32[2,128,256]{1,2,0:T(8,128)S(1)}, u32[]{:S(2)}, u32[]{:S(2)}) collective-permute-start(f32[2,128,256]{1,2,0:T(8,128)S(1)} %maximum_select_fusion.9), channel_id=1, source_target_pairs={{0,2},{2,0},{4,6},{6,4},{8,10},{10,8},{12,14},{14,12},{1,3},{3,1},... | collective-permute-start | bytes 786440 | tf_op jit(solution)/shard_map/ppermute | solution.py:204
  102.7 12.6 %collective-permute-start.11 = (f32[2,128,256]{1,2,0:T(8,128)S(1)}, f32[2,128,256]{1,2,0:T(8,128)S(1)}, u32[]{:S(2)}, u32[]{:S(2)}) collective-permute-start(f32[2,128,256]{1,2,0:T(8,128)S(1)} %fusion.31), channel_id=1, source_target_pairs={{0,2},{2,0},{4,6},{6,4},{8,10},{10,8},{12,14},{14,12},{1,3},{3,1},... | collective-permute-start | bytes 786440 | tf_op jit(solution)/shard_map/ppermute | solution.py:204
  107.4 20.5 %collective-permute-start.16 = (f32[2,2,128,256]{2,3,0,1:T(8,128)S(1)}, f32[2,2,128,256]{2,3,0,1:T(8,128)S(1)}, u32[]{:S(2)}, u32[]{:S(2)}) collective-permute-start(f32[2,2,128,256]{2,3,0,1:T(8,128)S(1)} %maximum_select_fusion.4), channel_id=1, source_target_pairs={{0,2},{2,0},{4,6},{6,4},{8,10},{10,8},{12,14},{14,12},{1,3},{3,1},... | collective-permute-start | bytes 1572872 | tf_op jit(solution)/shard_map/ppermute | solution.py:204
  110.6 17.7 %collective-permute-start.19 = (f32[2,2,128,256]{2,3,0,1:T(8,128)}, f32[2,2,128,256]{2,3,0,1:T(8,128)}, u32[]{:S(2)}, u32[]{:S(2)}) collective-permute-start(f32[2,2,128,256]{2,3,0,1:T(8,128)} %maximum_select_fusion.6), channel_id=1, source_target_pairs={{0,4},{2,6},{4,0},{6,2},{8,12},{10,14},{12,8},{14,10},{1,5},{3,7},... | collective-permute-start | bytes 1572872 | tf_op jit(solution)/shard_map/ppermute | solution.py:204
  115.4 11.7 %collective-permute-start.12 = (f32[2,128,256]{1,2,0:T(8,128)S(1)}, f32[2,128,256]{1,2,0:T(8,128)S(1)}, u32[]{:S(2)}, u32[]{:S(2)}) collective-permute-start(f32[2,128,256]{1,2,0:T(8,128)S(1)} %fusion.37), channel_id=1, source_target_pairs={{0,4},{2,6},{4,0},{6,2},{8,12},{10,14},{12,8},{14,10},{1,5},{3,7},... | collective-permute-start | bytes 786440 | tf_op jit(solution)/shard_map/ppermute | solution.py:204
  127.9 14.1 %collective-permute-start.13 = (f32[2,128,256]{1,2,0:T(8,128)}, f32[2,128,256]{1,2,0:T(8,128)}, u32[]{:S(2)}, u32[]{:S(2)}) collective-permute-start(f32[2,128,256]{1,2,0:T(8,128)} %add.120), channel_id=1, source_target_pairs={{0,8},{2,10},{4,12},{6,14},{8,0},{10,2},{12,4},{14,6},{1,9},{3,11}... | collective-permute-start | bytes 786440 | tf_op jit(solution)/shard_map/ppermute | solution.py:204
  145.0 29.5 %copy-start.6 = (f32[512,128]{0,1:T(8,128)S(1)}, f32[512,128]{0,1:T(8,128)}, u32[]{:S(2)}) copy-start(f32[512,128]{0,1:T(8,128)} %get-tuple-element.59) | copy-start | bytes 786436
  173.0 5.5 %collective-permute-start.20 = (f32[128,2048]{1,0:T(8,128)}, f32[128,2048]{1,0:T(8,128)}, u32[]{:S(2)}, u32[]{:S(2)}) collective-permute-start(f32[128,2048]{1,0:T(8,128)} %dynamic-slice_bitcast_fusion), channel_id=1, source_target_pairs={{0,16},{16,0},{1,17},{17,1},{2,18},{18,2},{3,19},{19,3},{4,20},{20... | collective-permute-start | bytes 3145736 | tf_op jit(solution)/shard_map/ppermute | solution.py:204
  (5 other events, 21.2 us)

commit v10 on v7

--- a/solution.py
+++ b/solution.py
@@ -42,7 +42,13 @@
     return unpack_block(jnp.bitwise_and(masks_ref[k], keep)).astype(jnp.bfloat16)
 
 
-def forward_kernel(live_ref, rows_ref, cols_ref, masks_ref, panel_ref, totals_ref, bits_ref):
+def last_step():
+    return pl.program_id(0) == pl.num_programs(0) - 1
+
+
+def forward_kernel(
+    live_ref, rows_ref, cols_ref, masks_ref, panel_ref, totals_ref, bits_ref, totals_odd, bits_odd
+):
     group, _, edge = masks_ref.shape
     row_limit = totals_ref.shape[0] // edge - 1
     col_limit = panel_ref.shape[0] // edge - 1
@@ -52,29 +58,40 @@
     def _():
         totals_ref[...] = jnp.zeros_like(totals_ref)
         bits_ref[...] = jnp.zeros_like(bits_ref)
+        totals_odd[...] = jnp.zeros_like(totals_odd)
+        bits_odd[...] = jnp.zeros_like(bits_odd)
 
     base, active = live_chunk(live_ref, group)
 
+    def one_slot(k, totals_acc, bits_acc):
+        slot = base + k
+        row = jnp.clip(rows_ref[slot], 0, row_limit)
+        col = jnp.clip(cols_ref[slot], 0, col_limit)
+        keep = jnp.where(slot < live_ref[0], -1, 0).astype(jnp.int32)
+        bits = unpack_bits(jnp.bitwise_and(masks_ref[k], keep))
+        bits_acc[row] += bits
+        dense = bits.astype(jnp.float32).astype(jnp.bfloat16)
+        tile = panel_ref[pl.ds(pl.multiple_of(col * edge, edge), edge), :]
+        prod = jnp.dot(dense, tile, preferred_element_type=jnp.float32)
+        start = pl.multiple_of(row * edge, edge)
+        totals_acc[pl.ds(start, edge), :] += prod[:, :half] + prod[:, half:]
+
     @pl.when(active)
     def _():
-        def body(k, carry):
-            slot = base + k
-            row = jnp.clip(rows_ref[slot], 0, row_limit)
-            col = jnp.clip(cols_ref[slot], 0, col_limit)
-            keep = jnp.where(slot < live_ref[0], -1, 0).astype(jnp.int32)
-            bits = unpack_bits(jnp.bitwise_and(masks_ref[k], keep))
-            bits_ref[row] += bits
-            dense = bits.astype(jnp.float32).astype(jnp.bfloat16)
-            tile = panel_ref[pl.ds(pl.multiple_of(col * edge, edge), edge), :]
-            prod = jnp.dot(dense, tile, preferred_element_type=jnp.float32)
-            start = pl.multiple_of(row * edge, edge)
-            totals_ref[pl.ds(start, edge), :] += prod[:, :half] + prod[:, half:]
+        def body(pair, carry):
+            one_slot(2 * pair, totals_ref, bits_ref)
+            one_slot(2 * pair + 1, totals_odd, bits_odd)
             return carry
 
-        lax.fori_loop(0, group, body, 0, unroll=UNROLL)
-
-
-def backward_kernel(live_ref, rows_ref, cols_ref, masks_ref, lifted_ref, out_ref):
+        lax.fori_loop(0, group // 2, body, 0, unroll=UNROLL // 2)
+
+    @pl.when(last_step())
+    def _():
+        totals_ref[...] += totals_odd[...]
+        bits_ref[...] += bits_odd[...]
+
+
+def backward_kernel(live_ref, rows_ref, cols_ref, masks_ref, lifted_ref, out_ref, out_odd):
     group, _, edge = masks_ref.shape
     row_chunk = lifted_ref.shape[2] // edge
     col_chunk = out_ref.shape[2] // edge
@@ -85,24 +102,33 @@
     @pl.when(pl.program_id(0) == 0)
     def _():
         out_ref[...] = jnp.zeros_like(out_ref)
+        out_odd[...] = jnp.zeros_like(out_odd)
 
     base, active = live_chunk(live_ref, group)
 
+    def one_slot(k, out_acc):
+        slot = base + k
+        row = jnp.clip(rows_ref[slot], 0, row_limit)
+        col = jnp.clip(cols_ref[slot], 0, col_limit)
+        dense = slot_words(masks_ref, live_ref, base, k)
+        row_start = pl.multiple_of((row % row_chunk) * edge, edge)
+        tile = lifted_ref[row // row_chunk, :, pl.ds(row_start, edge)]
+        prod = jnp.dot(tile, dense, preferred_element_type=jnp.float32)
+        col_start = pl.multiple_of((col % col_chunk) * edge, edge)
+        out_acc[col // col_chunk, :, pl.ds(col_start, edge)] += prod[:half] + prod[half:]
+
     @pl.when(active)
     def _():
-        def body(k, carry):
-            slot = base + k
-            row = jnp.clip(rows_ref[slot], 0, row_limit)
-            col = jnp.clip(cols_ref[slot], 0, col_limit)
-            dense = slot_words(masks_ref, live_ref, base, k)
-            row_start = pl.multiple_of((row % row_chunk) * edge, edge)
-            tile = lifted_ref[row // row_chunk, :, pl.ds(row_start, edge)]
-            prod = jnp.dot(tile, dense, preferred_element_type=jnp.float32)
-            col_start = pl.multiple_of((col % col_chunk) * edge, edge)
-            out_ref[col // col_chunk, :, pl.ds(col_start, edge)] += prod[:half] + prod[half:]
+        def body(pair, carry):
+            one_slot(2 * pair, out_ref)
+            one_slot(2 * pair + 1, out_odd)
             return carry
 
-        lax.fori_loop(0, group, body, 0, unroll=UNROLL)
+        lax.fori_loop(0, group // 2, body, 0, unroll=UNROLL // 2)
+
+    @pl.when(last_step())
+    def _():
+        out_ref[...] += out_odd[...]
 
 
 def mask_spec(packed_masks, group):
@@ -127,6 +153,7 @@
         grid=(slot_total // group,),
         in_specs=[mask_spec(packed_masks, group), whole_spec(dense_input.shape)],
         out_specs=[whole_spec(shape.shape) for shape in out_shapes],
+        scratch_shapes=[pltpu.VMEM(shape.shape, shape.dtype) for shape in out_shapes],
     )
     return pl.pallas_call(
         kernel,

time: 172 us -> 173 us (level)
  transfers between devices with their start and end apart: 21 -> 21, of which waited for: 17 -> 15; matrix products, arithmetic and copies ran while one was open for 4% -> 4% of each run, Pallas kernels for 0% -> 0%
where the time goes in v10:
time: 173 us
  waiting for transfers between devices  75.5 us (44%)
  Pallas kernels  49.6 us (29%)
  starting transfers between devices  20.5 us (12%)
  other arithmetic  11.9 us (7%)
  local copies, waits for them, and re-layouts  7.56 us (4%)
  matrix products  5.81 us (3%)
  between operations  1.76 us (1%)
    ppermute x21, waiting for transfers between devices, exchange(): return lax.ppermute(values, axis, [(i, i ^ 1 << bit) for i in range(count)])  75.5 us
    pallas_call x2, Pallas kernels, slot_pallas(): pl.pallas_call(kernel, grid_spec=grid_spec, out_shape=out_shapes, compile...  49.6 us
    ppermute x21, starting transfers between devices, exchange(): return lax.ppermute(values, axis, [(i, i ^ 1 << bit) for i in range(count)])  20.5 us
    unnamed x17, local copies, waits for them, and re-layouts  3.82 us
  transfers between devices with their start and end apart: 21, of which 15 were waited for; matrix products, arithmetic and copies ran while one was open for 4% of the time, Pallas kernels for 0%

profile of v10, /device:TPU:31, one launch (start us, length us, event | category | flops | bytes accessed | tf_op | source)
XLA Modules:
  0.0 172.6 jit_solution(8059631708433373881)
XLA Ops:
  2.1 1.8 %collective-permute-done.1 = f32[2048,128]{1,0:T(8,128)S(1)} collective-permute-done((f32[2048,128]{1,0:T(8,128)}, f32[2048,128]{1,0:T(8,128)S(1)}, u32[]{:S(2)}, u32[]{:S(2)}) %collective-permute-start.1) | collective-permute-done | bytes 1048608 | tf_op jit(solution)/shard_map/ppermute | solution.py:199
  3.9 1.7 %maximum_select_fusion = f32[2,2048,128]{2,1,0:T(8,128)S(1)} fusion(f32[1,2048,128]{2,1,0:T(8,128)S(1)} %bitcast.111, f32[1,2048,128]{2,1,0:T(8,128)} %bitcast.110, pred[]{:T(512)S(6)} %eq.21), kind=kLoop, calls=%fused_computation.6 | loop fusion | flops 1572864 | bytes 4194305 | tf_op jit(solution)/shard_map/jit(_where)/select_n | solution.py:239
  6.0 1.6 pad_maximum_fusion.panel_ref
  7.5 25.2 %shard_map.128 = (f32[4096,128]{1,0:T(8,128)}, s32[32,128,128]{2,1,0:T(8,128)}) custom-call(s32[1]{0:T(128)} %bitcast.live_ref, s32[512]{0:T(512)} %bitcast.119, s32[512]{0:T(512)} %bitcast.121, s32[512,16,128]{2,1,0:T(8,128)} %bitcast.95, bf16[4096,256]{1,0:T(8,128)(2,1)} %pad_maximum_fusion.panel_ref), custom_call_target="tpu_custom_call" | custom-call | tf_op jit(solution)/shard_map/pallas_call | solution.py:158
  32.8 2.4 %reduce_sum.9 = s32[32,128]{1,0:T(8,128)S(1)} reduce(s32[32,128,128]{2,1,0:T(8,128)} %get-tuple-element.10, s32[]{:T(128)} %constant.70.clone.1), dimensions={2}, to_apply=%region_0.1 | reduce | flops 520192 | bytes 2113540 | tf_op jit(solution)/shard_map/reduce_sum | solution.py:174
  37.5 12.4 %collective-permute-done.2 = f32[2,2,264,128]{3,2,1,0:T(8,128)S(1)} collective-permute-done((f32[2,2,264,128]{3,2,1,0:T(8,128)S(1)}, f32[2,2,264,128]{3,2,1,0:T(8,128)S(1)}, u32[]{:S(2)}, u32[]{:S(2)}) %collective-permute-start.2) | collective-permute-done | bytes 540704 | tf_op jit(solution)/shard_map/ppermute | solution.py:199
  52.3 5.6 %collective-permute-done.3 = f32[2,264,128]{2,1,0:T(8,128)S(1)} collective-permute-done((f32[2,264,128]{2,1,0:T(8,128)S(1)}, f32[2,264,128]{2,1,0:T(8,128)S(1)}, u32[]{:S(2)}, u32[]{:S(2)}) %collective-permute-start.3) | collective-permute-done | bytes 270368 | tf_op jit(solution)/shard_map/ppermute | solution.py:199
  58.2 2.4 %collective-permute-start.7 = (f32[264,128]{1,0:T(8,128)S(1)}, f32[264,128]{1,0:T(8,128)S(1)}, u32[]{:S(2)}, u32[]{:S(2)}) collective-permute-start(f32[264,128]{1,0:T(8,128)S(1)} %dynamic-slice_bitcast_fusion.5), channel_id=1, source_target_pairs={{0,8},{2,10},{4,12},{6,14},{8,0},{10,2},{12,4},{14,6},{1,9},{3,11}... | collective-permute-start | bytes 405512 | tf_op jit(solution)/shard_map/ppermute | solution.py:199
  60.6 9.7 %collective-permute-done.4 = f32[264,128]{1,0:T(8,128)S(1)} collective-permute-done((f32[264,128]{1,0:T(8,128)S(1)}, f32[264,128]{1,0:T(8,128)S(1)}, u32[]{:S(2)}, u32[]{:S(2)}) %collective-permute-start.4) | collective-permute-done | bytes 135200 | tf_op jit(solution)/shard_map/ppermute | solution.py:199
  70.3 2.9 %collective-permute-done.7 = f32[264,128]{1,0:T(8,128)S(1)} collective-permute-done((f32[264,128]{1,0:T(8,128)S(1)}, f32[264,128]{1,0:T(8,128)S(1)}, u32[]{:S(2)}, u32[]{:S(2)}) %collective-permute-start.7) | collective-permute-done | bytes 135200 | tf_op jit(solution)/shard_map/ppermute | solution.py:199
  73.7 7.1 %collective-permute-done.8 = f32[512,128]{1,0:T(8,128)S(1)} collective-permute-done((f32[512,128]{1,0:T(8,128)S(1)}, f32[512,128]{1,0:T(8,128)S(1)}, u32[]{:S(2)}, u32[]{:S(2)}) %collective-permute-start.8) | collective-permute-done | bytes 262176 | tf_op jit(solution)/shard_map/ppermute | solution.py:199
  83.0 6.3 %collective-permute-done.9 = f32[512,128]{1,0:T(8,128)S(1)} collective-permute-done((f32[512,128]{1,0:T(8,128)S(1)}, f32[512,128]{1,0:T(8,128)S(1)}, u32[]{:S(2)}, u32[]{:S(2)}) %collective-permute-start.9) | collective-permute-done | bytes 262176 | tf_op jit(solution)/shard_map/ppermute | solution.py:199
  92.1 2.4 %collective-permute-start.17 = (f32[128,256]{1,0:T(8,128)S(1)}, f32[128,256]{1,0:T(8,128)S(1)}, u32[]{:S(2)}, u32[]{:S(2)}) collective-permute-start(f32[128,256]{1,0:T(8,128)S(1)} %get-tuple-element.51), channel_id=1, source_target_pairs={{0,8},{2,10},{4,12},{6,14},{8,0},{10,2},{12,4},{14,6},{1,9},{3,11}... | collective-permute-start | bytes 393224 | tf_op jit(solution)/shard_map/ppermute | solution.py:199
  94.5 2.8 %collective-permute-start.10 = (f32[2,128,256]{1,2,0:T(8,128)S(1)}, f32[2,128,256]{1,2,0:T(8,128)S(1)}, u32[]{:S(2)}, u32[]{:S(2)}) collective-permute-start(f32[2,128,256]{1,2,0:T(8,128)S(1)} %pad_maximum_fusion.6), channel_id=1, source_target_pairs={{0,16},{16,0},{1,17},{17,1},{2,18},{18,2},{3,19},{19,3},{4,20},{20... | collective-permute-start | bytes 786440 | tf_op jit(solution)/shard_map/ppermute | solution.py:199
  98.8 2.7 %collective-permute-done.17 = f32[128,256]{1,0:T(8,128)S(1)} collective-permute-done((f32[128,256]{1,0:T(8,128)S(1)}, f32[128,256]{1,0:T(8,128)S(1)}, u32[]{:S(2)}, u32[]{:S(2)}) %collective-permute-start.17) | collective-permute-done | bytes 131104 | tf_op jit(solution)/shard_map/ppermute | solution.py:199
  103.2 3.0 %collective-permute-done.15 = f32[2,128,256]{2,1,0:T(8,128)S(1)} collective-permute-done((f32[2,128,256]{2,1,0:T(8,128)S(1)}, f32[2,128,256]{2,1,0:T(8,128)S(1)}, u32[]{:S(2)}, u32[]{:S(2)}) %collective-permute-start.15) | collective-permute-done | bytes 262176 | tf_op jit(solution)/shard_map/ppermute | solution.py:199
  107.8 5.5 %collective-permute-done.11 = f32[2,128,256]{1,2,0:T(8,128)S(1)} collective-permute-done((f32[2,128,256]{1,2,0:T(8,128)S(1)}, f32[2,128,256]{1,2,0:T(8,128)S(1)}, u32[]{:S(2)}, u32[]{:S(2)}) %collective-permute-start.11) | collective-permute-done | bytes 262176 | tf_op jit(solution)/shard_map/ppermute | solution.py:199
  113.5 8.5 %collective-permute-done.12 = f32[2,128,256]{1,2,0:T(8,128)S(1)} collective-permute-done((f32[2,128,256]{1,2,0:T(8,128)S(1)}, f32[2,128,256]{1,2,0:T(8,128)S(1)}, u32[]{:S(2)}, u32[]{:S(2)}) %collective-permute-start.12) | collective-permute-done | bytes 262176 | tf_op jit(solution)/shard_map/ppermute | solution.py:199
  122.2 2.4 %collective-permute-done.16 = f32[2,2,128,256]{3,2,0,1:T(8,128)S(1)} collective-permute-done((f32[2,2,128,256]{3,2,0,1:T(8,128)S(1)}, f32[2,2,128,256]{3,2,0,1:T(8,128)S(1)}, u32[]{:S(2)}, u32[]{:S(2)}) %collective-permute-start.16) | collective-permute-done | bytes 524320 | tf_op jit(solution)/shard_map/ppermute | solution.py:199
  125.3 5.6 %collective-permute-done.13 = f32[2,128,256]{1,2,0:T(8,128)S(1)} collective-permute-done((f32[2,128,256]{1,2,0:T(8,128)S(1)}, f32[2,128,256]{1,2,0:T(8,128)S(1)}, u32[]{:S(2)}, u32[]{:S(2)}) %collective-permute-start.13) | collective-permute-done | bytes 262176 | tf_op jit(solution)/shard_map/ppermute | solution.py:199
  131.3 1.5 pad_maximum_fusion.2.lifted_ref
  132.7 24.4 %shard_map.129 = f32[2,128,2048]{2,1,0:T(8,128)} custom-call(s32[1]{0:T(128)} %bitcast.live_ref, s32[512]{0:T(512)} %bitcast.120, s32[512]{0:T(512)} %bitcast.122, s32[512,16,128]{2,1,0:T(8,128)} %bitcast.96, bf16[8,256,512]{2,1,0:T(8,128)(2,1)} %pad_maximum_fusion.2.lifted_ref), custom_call_target="tpu_custom_call" | custom-call | tf_op jit(solution)/shard_map/pallas_call | solution.py:158
  157.1 2.4 %dynamic-slice_bitcast_fusion = f32[128,2048]{1,0:T(8,128)} fusion(f32[2,128,2048]{2,1,0:T(8,128)} %shard_map.129, s32[]{:T(128)S(6)} %select_n.227), kind=kLoop, calls=%fused_computation.20 | loop fusion | bytes 2097156 | tf_op jit(solution)/shard_map/jit(dynamic_index_in_dim)/squeeze | solution.py:226
  159.6 7.6 %collective-permute-start.20 = (f32[128,2048]{1,0:T(8,128)}, f32[128,2048]{1,0:T(8,128)}, u32[]{:S(2)}, u32[]{:S(2)}) collective-permute-start(f32[128,2048]{1,0:T(8,128)} %dynamic-slice_bitcast_fusion), channel_id=1, source_target_pairs={{0,16},{16,0},{1,17},{17,1},{2,18},{18,2},{3,19},{19,3},{4,20},{20... | collective-permute-start | bytes 3145736 | tf_op jit(solution)/shard_map/ppermute | solution.py:199
  (94 shorter events, 23.1 us)
Async XLA Ops:
  0.6 80.8 %copy-start = (f32[256,256]{1,0:T(8,128)S(1)}, f32[256,256]{1,0:T(8,128)}, u32[]{:S(2)}) copy-start(f32[256,256]{1,0:T(8,128)} %param.11) | copy-start | bytes 786436
  0.6 3.2 %collective-permute-start.1 = (f32[2048,128]{1,0:T(8,128)}, f32[2048,128]{1,0:T(8,128)S(1)}, u32[]{:S(2)}, u32[]{:S(2)}) collective-permute-start(f32[2048,128]{1,0:T(8,128)} %param.9), channel_id=1, source_target_pairs={{0,16},{16,0},{1,17},{17,1},{2,18},{18,2},{3,19},{19,3},{4,20},{20... | collective-permute-start | bytes 3145736 | tf_op jit(solution)/shard_map/ppermute | solution.py:199
  36.4 13.5 %collective-permute-start.2 = (f32[2,2,264,128]{3,2,1,0:T(8,128)S(1)}, f32[2,2,264,128]{3,2,1,0:T(8,128)S(1)}, u32[]{:S(2)}, u32[]{:S(2)}) collective-permute-start(f32[2,2,264,128]{3,2,1,0:T(8,128)S(1)} %dynamic-slice_bitcast_fusion.2), channel_id=1, source_target_pairs={{0,2},{2,0},{4,6},{6,4},{8,10},{10,8},{12,14},{14,12},{1,3},{3,1},... | collective-permute-start | bytes 1622024 | tf_op jit(solution)/shard_map/ppermute | solution.py:199
  37.3 13.8 %collective-permute-start.5 = (f32[2,2,264,128]{3,2,1,0:T(8,128)}, f32[2,2,264,128]{3,2,1,0:T(8,128)S(1)}, u32[]{:S(2)}, u32[]{:S(2)}) collective-permute-start(f32[2,2,264,128]{3,2,1,0:T(8,128)} %dynamic-slice_bitcast_fusion.1), channel_id=1, source_target_pairs={{0,4},{2,6},{4,0},{6,2},{8,12},{10,14},{12,8},{14,10},{1,5},{3,7},... | collective-permute-start | bytes 1622024 | tf_op jit(solution)/shard_map/ppermute | solution.py:199
  37.3 36.3 %collective-permute-start = (f32[512,128]{1,0:T(8,128)S(1)}, f32[512,128]{1,0:T(8,128)S(1)}, u32[]{:S(2)}, u32[]{:S(2)}) collective-permute-start(f32[512,128]{1,0:T(8,128)S(1)} %copy-done.4), channel_id=1, source_target_pairs={{0,1},{1,0},{2,3},{3,2},{4,5},{5,4},{6,7},{7,6},{8,9},{9,8},{10,11... | collective-permute-start | bytes 786440 | tf_op jit(solution)/shard_map/ppermute | solution.py:199
  51.0 6.9 %collective-permute-start.3 = (f32[2,264,128]{2,1,0:T(8,128)S(1)}, f32[2,264,128]{2,1,0:T(8,128)S(1)}, u32[]{:S(2)}, u32[]{:S(2)}) collective-permute-start(f32[2,264,128]{2,1,0:T(8,128)S(1)} %dynamic-slice_bitcast_fusion.4), channel_id=1, source_target_pairs={{0,4},{2,6},{4,0},{6,2},{8,12},{10,14},{12,8},{14,10},{1,5},{3,7},... | collective-permute-start | bytes 811016 | tf_op jit(solution)/shard_map/ppermute | solution.py:199
  51.2 6.9 %collective-permute-start.6 = (f32[2,264,128]{2,1,0:T(8,128)S(1)}, f32[2,264,128]{2,1,0:T(8,128)S(1)}, u32[]{:S(2)}, u32[]{:S(2)}) collective-permute-start(f32[2,264,128]{2,1,0:T(8,128)S(1)} %dynamic-slice_bitcast_fusion.3), channel_id=1, source_target_pairs={{0,2},{2,0},{4,6},{6,4},{8,10},{10,8},{12,14},{14,12},{1,3},{3,1},... | collective-permute-start | bytes 811016 | tf_op jit(solution)/shard_map/ppermute | solution.py:199
  58.0 22.8 %copy-start.5 = (f32[256,256]{1,0:T(8,128)S(1)}, f32[256,256]{1,0:T(8,128)}, u32[]{:S(2)}) copy-start(f32[256,256]{1,0:T(8,128)} %param.12) | copy-start | bytes 786436
  58.0 12.3 %collective-permute-start.4 = (f32[264,128]{1,0:T(8,128)S(1)}, f32[264,128]{1,0:T(8,128)S(1)}, u32[]{:S(2)}, u32[]{:S(2)}) collective-permute-start(f32[264,128]{1,0:T(8,128)S(1)} %dynamic-slice_bitcast_fusion.6), channel_id=1, source_target_pairs={{0,8},{2,10},{4,12},{6,14},{8,0},{10,2},{12,4},{14,6},{1,9},{3,11}... | collective-permute-start | bytes 405512 | tf_op jit(solution)/shard_map/ppermute | solution.py:199
  58.2 23.2 %copy-start.6 = (f32[512,128]{1,0:T(8,128)S(1)}, f32[512,128]{1,0:T(8,128)}, u32[]{:S(2)}) copy-start(f32[512,128]{1,0:T(8,128)} %param.13) | copy-start | bytes 786436
  58.2 15.0 %collective-permute-start.7 = (f32[264,128]{1,0:T(8,128)S(1)}, f32[264,128]{1,0:T(8,128)S(1)}, u32[]{:S(2)}, u32[]{:S(2)}) collective-permute-start(f32[264,128]{1,0:T(8,128)S(1)} %dynamic-slice_bitcast_fusion.5), channel_id=1, source_target_pairs={{0,8},{2,10},{4,12},{6,14},{8,0},{10,2},{12,4},{14,6},{1,9},{3,11}... | collective-permute-start | bytes 405512 | tf_op jit(solution)/shard_map/ppermute | solution.py:199
  73.3 7.4 %collective-permute-start.8 = (f32[512,128]{1,0:T(8,128)S(1)}, f32[512,128]{1,0:T(8,128)S(1)}, u32[]{:S(2)}, u32[]{:S(2)}) collective-permute-start(f32[512,128]{1,0:T(8,128)S(1)} %fusion.11), channel_id=1, source_target_pairs={{0,1},{1,0},{2,3},{3,2},{4,5},{5,4},{6,7},{7,6},{8,9},{9,8},{10,11... | collective-permute-start | bytes 786440 | tf_op jit(solution)/shard_map/ppermute | solution.py:199
  82.7 6.5 %collective-permute-start.9 = (f32[512,128]{1,0:T(8,128)S(1)}, f32[512,128]{1,0:T(8,128)S(1)}, u32[]{:S(2)}, u32[]{:S(2)}) collective-permute-start(f32[512,128]{1,0:T(8,128)S(1)} %get-tuple-element.53), channel_id=1, source_target_pairs={{0,1},{1,0},{2,3},{3,2},{4,5},{5,4},{6,7},{7,6},{8,9},{9,8},{10,11... | collective-permute-start | bytes 786440 | tf_op jit(solution)/shard_map/ppermute | solution.py:199
  91.0 7.7 %collective-permute-start.14 = (f32[128,256]{1,0:T(8,128)S(1)}, f32[128,256]{1,0:T(8,128)S(1)}, u32[]{:S(2)}, u32[]{:S(2)}) collective-permute-start(f32[128,256]{1,0:T(8,128)S(1)} %get-tuple-element.52), channel_id=1, source_target_pairs={{0,8},{2,10},{4,12},{6,14},{8,0},{10,2},{12,4},{14,6},{1,9},{3,11}... | collective-permute-start | bytes 393224 | tf_op jit(solution)/shard_map/ppermute | solution.py:199
  92.1 9.4 %collective-permute-start.17 = (f32[128,256]{1,0:T(8,128)S(1)}, f32[128,256]{1,0:T(8,128)S(1)}, u32[]{:S(2)}, u32[]{:S(2)}) collective-permute-start(f32[128,256]{1,0:T(8,128)S(1)} %get-tuple-element.51), channel_id=1, source_target_pairs={{0,8},{2,10},{4,12},{6,14},{8,0},{10,2},{12,4},{14,6},{1,9},{3,11}... | collective-permute-start | bytes 393224 | tf_op jit(solution)/shard_map/ppermute | solution.py:199
  94.5 7.7 %collective-permute-start.10 = (f32[2,128,256]{1,2,0:T(8,128)S(1)}, f32[2,128,256]{1,2,0:T(8,128)S(1)}, u32[]{:S(2)}, u32[]{:S(2)}) collective-permute-start(f32[2,128,256]{1,2,0:T(8,128)S(1)} %pad_maximum_fusion.6), channel_id=1, source_target_pairs={{0,16},{16,0},{1,17},{17,1},{2,18},{18,2},{3,19},{19,3},{4,20},{20... | collective-permute-start | bytes 786440 | tf_op jit(solution)/shard_map/ppermute | solution.py:199
  98.7 7.6 %collective-permute-start.15 = (f32[2,128,256]{2,1,0:T(8,128)S(1)}, f32[2,128,256]{2,1,0:T(8,128)S(1)}, u32[]{:S(2)}, u32[]{:S(2)}) collective-permute-start(f32[2,128,256]{2,1,0:T(8,128)S(1)} %maximum_select_fusion.7), channel_id=1, source_target_pairs={{0,4},{2,6},{4,0},{6,2},{8,12},{10,14},{12,8},{14,10},{1,5},{3,7},... | collective-permute-start | bytes 786440 | tf_op jit(solution)/shard_map/ppermute | solution.py:199
  101.5 6.2 %collective-permute-start.18 = (f32[2,128,256]{2,1,0:T(8,128)S(1)}, f32[2,128,256]{2,1,0:T(8,128)S(1)}, u32[]{:S(2)}, u32[]{:S(2)}) collective-permute-start(f32[2,128,256]{2,1,0:T(8,128)S(1)} %maximum_select_fusion.9), channel_id=1, source_target_pairs={{0,2},{2,0},{4,6},{6,4},{8,10},{10,8},{12,14},{14,12},{1,3},{3,1},... | collective-permute-start | bytes 786440 | tf_op jit(solution)/shard_map/ppermute | solution.py:199
  102.2 11.1 %collective-permute-start.11 = (f32[2,128,256]{1,2,0:T(8,128)S(1)}, f32[2,128,256]{1,2,0:T(8,128)S(1)}, u32[]{:S(2)}, u32[]{:S(2)}) collective-permute-start(f32[2,128,256]{1,2,0:T(8,128)S(1)} %fusion.30), channel_id=1, source_target_pairs={{0,2},{2,0},{4,6},{6,4},{8,10},{10,8},{12,14},{14,12},{1,3},{3,1},... | collective-permute-start | bytes 786440 | tf_op jit(solution)/shard_map/ppermute | solution.py:199
  106.3 18.2 %collective-permute-start.16 = (f32[2,2,128,256]{3,2,0,1:T(8,128)S(1)}, f32[2,2,128,256]{3,2,0,1:T(8,128)S(1)}, u32[]{:S(2)}, u32[]{:S(2)}) collective-permute-start(f32[2,2,128,256]{3,2,0,1:T(8,128)S(1)} %maximum_select_fusion.4), channel_id=1, source_target_pairs={{0,2},{2,0},{4,6},{6,4},{8,10},{10,8},{12,14},{14,12},{1,3},{3,1},... | collective-permute-start | bytes 1572872 | tf_op jit(solution)/shard_map/ppermute | solution.py:199
  107.7 17.0 %collective-permute-start.19 = (f32[2,2,128,256]{3,2,0,1:T(8,128)S(1)}, f32[2,2,128,256]{3,2,0,1:T(8,128)S(1)}, u32[]{:S(2)}, u32[]{:S(2)}) collective-permute-start(f32[2,2,128,256]{3,2,0,1:T(8,128)S(1)} %maximum_select_fusion.6), channel_id=1, source_target_pairs={{0,4},{2,6},{4,0},{6,2},{8,12},{10,14},{12,8},{14,10},{1,5},{3,7},... | collective-permute-start | bytes 1572872 | tf_op jit(solution)/shard_map/ppermute | solution.py:199
  113.3 8.7 %collective-permute-start.12 = (f32[2,128,256]{1,2,0:T(8,128)S(1)}, f32[2,128,256]{1,2,0:T(8,128)S(1)}, u32[]{:S(2)}, u32[]{:S(2)}) collective-permute-start(f32[2,128,256]{1,2,0:T(8,128)S(1)} %fusion.36), channel_id=1, source_target_pairs={{0,4},{2,6},{4,0},{6,2},{8,12},{10,14},{12,8},{14,10},{1,5},{3,7},... | collective-permute-start | bytes 786440 | tf_op jit(solution)/shard_map/ppermute | solution.py:199
  122.1 8.8 %collective-permute-start.13 = (f32[2,128,256]{1,2,0:T(8,128)S(1)}, f32[2,128,256]{1,2,0:T(8,128)S(1)}, u32[]{:S(2)}, u32[]{:S(2)}) collective-permute-start(f32[2,128,256]{1,2,0:T(8,128)S(1)} %add.120), channel_id=1, source_target_pairs={{0,8},{2,10},{4,12},{6,14},{8,0},{10,2},{12,4},{14,6},{1,9},{3,11}... | collective-permute-start | bytes 786440 | tf_op jit(solution)/shard_map/ppermute | solution.py:199
  159.6 10.4 %collective-permute-start.20 = (f32[128,2048]{1,0:T(8,128)}, f32[128,2048]{1,0:T(8,128)}, u32[]{:S(2)}, u32[]{:S(2)}) collective-permute-start(f32[128,2048]{1,0:T(8,128)} %dynamic-slice_bitcast_fusion), channel_id=1, source_target_pairs={{0,16},{16,0},{1,17},{17,1},{2,18},{18,2},{3,19},{19,3},{4,20},{20... | collective-permute-start | bytes 3145736 | tf_op jit(solution)/shard_map/ppermute | solution.py:199
  (4 other events, 18.1 us)

commit v11 on v7

--- a/solution.py
+++ b/solution.py
@@ -186,33 +186,51 @@
     )
 
 
-def halving_steps(values, axis, order):
+def exchange_all(sends, axis, bits):
+    if len(sends) > 1 and len(set(bits)) == 1:
+        received = exchange(jnp.stack(sends), axis, bits[0])
+        return [received[i] for i in range(len(sends))]
+    return [exchange(send, axis, bit) for send, bit in zip(sends, bits)]
+
+
+def halving_steps(pieces, axis, orders):
     bits = axis_bits(axis)
-    chunk = values.shape[0] >> bits
-    data = values.reshape((2,) * bits + (chunk,) + values.shape[1:])
-    remaining = list(reversed(range(bits)))
-    for bit in order:
-        position = remaining.index(bit)
-        remaining.remove(bit)
-        mine = axis_bit(axis, bit)
-        keep = lax.dynamic_index_in_dim(data, mine, position, keepdims=False)
-        send = lax.dynamic_index_in_dim(data, 1 - mine, position, keepdims=False)
-        data = keep + exchange(send, axis, bit)
-    return data
-
-
-def doubling_steps(values, axis, order):
-    data = values
-    present = []
-    for bit in order:
-        position = sum(1 for other in present if other > bit)
-        present.insert(position, bit)
-        other = exchange(data, axis, bit)
-        first = axis_bit(axis, bit) == 0
-        data = jnp.where(
-            first, jnp.stack([data, other], axis=position), jnp.stack([other, data], axis=position)
-        )
-    return data
+    datas = [
+        piece.reshape((2,) * bits + (piece.shape[0] >> bits,) + piece.shape[1:]) for piece in pieces
+    ]
+    remaining = [list(reversed(range(bits))) for _ in pieces]
+    for step in range(bits):
+        keeps, sends, step_bits = [], [], []
+        for index, order in enumerate(orders):
+            bit = order[step]
+            position = remaining[index].index(bit)
+            remaining[index].remove(bit)
+            mine = axis_bit(axis, bit)
+            keeps.append(lax.dynamic_index_in_dim(datas[index], mine, position, keepdims=False))
+            sends.append(lax.dynamic_index_in_dim(datas[index], 1 - mine, position, keepdims=False))
+            step_bits.append(bit)
+        received = exchange_all(sends, axis, step_bits)
+        datas = [keep + other for keep, other in zip(keeps, received)]
+    return datas
+
+
+def doubling_steps(pieces, axis, orders):
+    datas = list(pieces)
+    present = [[] for _ in pieces]
+    for step in range(len(orders[0])):
+        step_bits = [order[step] for order in orders]
+        received = exchange_all(datas, axis, step_bits)
+        for index, bit in enumerate(step_bits):
+            position = sum(1 for other in present[index] if other > bit)
+            present[index].insert(position, bit)
+            first = axis_bit(axis, bit) == 0
+            data, other = datas[index], received[index]
+            datas[index] = jnp.where(
+                first,
+                jnp.stack([data, other], axis=position),
+                jnp.stack([other, data], axis=position),
+            )
+    return datas
 
 
 def bit_orders(axis):
@@ -227,18 +245,15 @@
     orders = bit_orders(axis)
     bits = axis_bits(axis)
     shaped = values.reshape((1 << bits, -1) + values.shape[1:])
-    pieces = jnp.split(shaped, len(orders), axis=1)
-    results = [
-        halving_steps(piece.reshape((-1,) + values.shape[1:]), axis, order)
-        for piece, order in zip(pieces, orders)
+    pieces = [
+        piece.reshape((-1,) + values.shape[1:]) for piece in jnp.split(shaped, len(orders), axis=1)
     ]
-    return jnp.concatenate(results, axis=0)
+    return jnp.concatenate(halving_steps(pieces, axis, orders), axis=0)
 
 
 def doubling_gather(values, axis):
     orders = [list(reversed(order)) for order in bit_orders(axis)]
-    pieces = jnp.split(values, len(orders), axis=0)
-    results = [doubling_steps(piece, axis, order) for piece, order in zip(pieces, orders)]
+    results = doubling_steps(jnp.split(values, len(orders), axis=0), axis, orders)
     stacked = jnp.concatenate(
         [result.reshape((-1,) + result.shape[-2:]) for result in results], axis=1
     )
@@ -247,8 +262,7 @@
 
 def doubling_gather_lanes(values, axis):
     orders = [list(reversed(order)) for order in bit_orders(axis)]
-    pieces = jnp.split(values, len(orders), axis=1)
-    results = [doubling_steps(piece, axis, order) for piece, order in zip(pieces, orders)]
+    results = doubling_steps(jnp.split(values, len(orders), axis=1), axis, orders)
     return jnp.concatenate(
         [result.reshape((-1,) + result.shape[-2:]) for result in results], axis=2
     )

time: 172 us -> 174 us (1.012)
  waiting for transfers between devices: 75.5 us -> 78.9 us
  starting transfers between devices: 20.6 us -> 18.8 us
    ppermute x21 -> x19, waiting for transfers between devices: 75.5 us -> 78.9 us  [exchange(): return lax.ppermute(values, axis, [(i, i ^ 1 << bit) for i in range(count)])]
    ppermute x21 -> x19, starting transfers between devices: 20.6 us -> 18.8 us  [exchange(): return lax.ppermute(values, axis, [(i, i ^ 1 << bit) for i in range(count)])]
  transfers between devices with their start and end apart: 21 -> 19, of which waited for: 17 -> 12; matrix products, arithmetic and copies ran while one was open for 4% -> 4% of each run, Pallas kernels for 0% -> 0%
where the time goes in v11:
time: 174 us; the launch traced here: 173 us
  waiting for transfers between devices  78.9 us (45%)
  Pallas kernels  48.8 us (28%)
  starting transfers between devices  18.8 us (11%)
  other arithmetic  12 us (7%)
  local copies, waits for them, and re-layouts  6.79 us (4%)
  matrix products  5.81 us (3%)
  between operations  1.8 us (1%)
    ppermute x19, waiting for transfers between devices, exchange(): return lax.ppermute(values, axis, [(i, i ^ 1 << bit) for i in range(count)])  78.9 us
    pallas_call x2, Pallas kernels, slot_pallas(): pl.pallas_call(kernel, grid_spec=grid_spec, out_shape=out_shapes, compile...  48.8 us
    ppermute x19, starting transfers between devices, exchange(): return lax.ppermute(values, axis, [(i, i ^ 1 << bit) for i in range(count)])  18.8 us
    unnamed x17, local copies, waits for them, and re-layouts  3.82 us
  transfers between devices with their start and end apart: 19, of which 12 were waited for; matrix products, arithmetic and copies ran while one was open for 4% of the time, Pallas kernels for 0%

profile of v11, /device:TPU:31, one launch (start us, length us, event | category | flops | bytes accessed | tf_op | source)
XLA Modules:
  0.0 172.9 jit_solution(12170375994770141592)
XLA Ops:
  2.1 1.8 %collective-permute-done.1 = f32[2048,128]{1,0:T(8,128)S(1)} collective-permute-done((f32[2048,128]{1,0:T(8,128)}, f32[2048,128]{1,0:T(8,128)S(1)}, u32[]{:S(2)}, u32[]{:S(2)}) %collective-permute-start.1) | collective-permute-done | bytes 1048608 | tf_op jit(solution)/shard_map/ppermute | solution.py:172
  3.9 1.7 %maximum_select_fusion = f32[2,2048,128]{2,1,0:T(8,128)S(1)} fusion(f32[1,2048,128]{2,1,0:T(8,128)S(1)} %bitcast.109, f32[1,2048,128]{2,1,0:T(8,128)} %bitcast.108, pred[]{:T(512)S(6)} %eq.21), kind=kLoop, calls=%fused_computation.6 | loop fusion | flops 1572864 | bytes 4194305 | tf_op jit(solution)/shard_map/jit(_where)/select_n | solution.py:228
  6.0 1.6 pad_maximum_fusion.panel_ref
  7.5 24.7 %shard_map.128 = (f32[4096,128]{1,0:T(8,128)}, s32[32,128,128]{2,1,0:T(8,128)}) custom-call(s32[1]{0:T(128)} %bitcast.live_ref, s32[512]{0:T(512)} %bitcast.116, s32[512]{0:T(512)} %bitcast.118, s32[512,16,128]{2,1,0:T(8,128)} %bitcast.96, bf16[4096,256]{1,0:T(8,128)(2,1)} %pad_maximum_fusion.panel_ref), custom_call_target="tpu_custom_call" | custom-call | tf_op jit(solution)/shard_map/pallas_call | solution.py:131
  32.3 2.4 %reduce_sum.9 = s32[32,128]{1,0:T(8,128)S(1)} reduce(s32[32,128,128]{2,1,0:T(8,128)} %get-tuple-element.10, s32[]{:T(128)} %constant.70.clone.1), dimensions={2}, to_apply=%region_0.1 | reduce | flops 520192 | bytes 2113540 | tf_op jit(solution)/shard_map/reduce_sum | solution.py:147
  36.1 13.3 %collective-permute-done.2 = f32[2,2,264,128]{3,2,1,0:T(8,128)S(1)} collective-permute-done((f32[2,2,264,128]{3,2,1,0:T(8,128)S(1)}, f32[2,2,264,128]{3,2,1,0:T(8,128)S(1)}, u32[]{:S(2)}, u32[]{:S(2)}) %collective-permute-start.2) | collective-permute-done | bytes 540704 | tf_op jit(solution)/shard_map/ppermute | solution.py:172
  50.8 6.6 %collective-permute-done.3 = f32[2,264,128]{2,1,0:T(8,128)S(1)} collective-permute-done((f32[2,264,128]{2,1,0:T(8,128)S(1)}, f32[2,264,128]{2,1,0:T(8,128)S(1)}, u32[]{:S(2)}, u32[]{:S(2)}) %collective-permute-start.3) | collective-permute-done | bytes 270368 | tf_op jit(solution)/shard_map/ppermute | solution.py:172
  58.0 14.0 %collective-permute-done.6 = f32[2,264,128]{2,1,0:T(8,128)S(1)} collective-permute-done((f32[2,264,128]{2,1,0:T(8,128)S(1)}, f32[2,264,128]{2,1,0:T(8,128)S(1)}, u32[]{:S(2)}, u32[]{:S(2)}) %collective-permute-start.6) | collective-permute-done | bytes 270368 | tf_op jit(solution)/shard_map/ppermute | solution.py:172
  72.5 6.3 %collective-permute-done.7 = f32[512,128]{1,0:T(8,128)S(1)} collective-permute-done((f32[512,128]{1,0:T(8,128)S(1)}, f32[512,128]{1,0:T(8,128)S(1)}, u32[]{:S(2)}, u32[]{:S(2)}) %collective-permute-start.7) | collective-permute-done | bytes 262176 | tf_op jit(solution)/shard_map/ppermute | solution.py:172
  79.4 1.3 multiply_multiply_fusion
  80.9 5.5 %collective-permute-done.8 = f32[512,128]{1,0:T(8,128)S(1)} collective-permute-done((f32[512,128]{1,0:T(8,128)S(1)}, f32[512,128]{1,0:T(8,128)S(1)}, u32[]{:S(2)}, u32[]{:S(2)}) %collective-permute-start.8) | collective-permute-done | bytes 262176 | tf_op jit(solution)/shard_map/ppermute | solution.py:172
  89.3 3.1 %collective-permute-start.9 = (f32[2,128,256]{1,2,0:T(8,128)S(1)}, f32[2,128,256]{1,2,0:T(8,128)S(1)}, u32[]{:S(2)}, u32[]{:S(2)}) collective-permute-start(f32[2,128,256]{1,2,0:T(8,128)S(1)} %pad_maximum_fusion.11), channel_id=1, source_target_pairs={{0,16},{16,0},{1,17},{17,1},{2,18},{18,2},{3,19},{19,3},{4,20},{20... | collective-permute-start | bytes 786440 | tf_op jit(solution)/shard_map/ppermute | solution.py:172
  92.4 8.6 %collective-permute-done.13 = f32[2,128,256]{2,1,0:T(8,128)S(1)} collective-permute-done((f32[2,128,256]{2,1,0:T(8,128)S(1)}, f32[2,128,256]{2,1,0:T(8,128)S(1)}, u32[]{:S(2)}, u32[]{:S(2)}) %collective-permute-start.13) | collective-permute-done | bytes 262176 | tf_op jit(solution)/shard_map/ppermute | solution.py:172
  101.3 1.5 collective-permute-start.10
  102.9 4.6 %collective-permute-done.14 = f32[2,128,256]{2,1,0:T(8,128)S(1)} collective-permute-done((f32[2,128,256]{2,1,0:T(8,128)S(1)}, f32[2,128,256]{2,1,0:T(8,128)S(1)}, u32[]{:S(2)}, u32[]{:S(2)}) %collective-permute-start.14) | collective-permute-done | bytes 262176 | tf_op jit(solution)/shard_map/ppermute | solution.py:172
  108.9 4.3 %collective-permute-done.10 = f32[2,128,256]{1,2,0:T(8,128)S(1)} collective-permute-done((f32[2,128,256]{1,2,0:T(8,128)S(1)}, f32[2,128,256]{1,2,0:T(8,128)S(1)}, u32[]{:S(2)}, u32[]{:S(2)}) %collective-permute-start.10) | collective-permute-done | bytes 262176 | tf_op jit(solution)/shard_map/ppermute | solution.py:172
  114.6 8.0 %collective-permute-done.11 = f32[2,128,256]{1,2,0:T(8,128)S(1)} collective-permute-done((f32[2,128,256]{1,2,0:T(8,128)S(1)}, f32[2,128,256]{1,2,0:T(8,128)S(1)}, u32[]{:S(2)}, u32[]{:S(2)}) %collective-permute-start.11) | collective-permute-done | bytes 262176 | tf_op jit(solution)/shard_map/ppermute | solution.py:172
  122.7 2.9 %collective-permute-start.12 = (f32[2,128,256]{1,2,0:T(8,128)S(1)}, f32[2,128,256]{1,2,0:T(8,128)S(1)}, u32[]{:S(2)}, u32[]{:S(2)}) collective-permute-start(f32[2,128,256]{1,2,0:T(8,128)S(1)} %add.129), channel_id=1, source_target_pairs={{0,8},{2,10},{4,12},{6,14},{8,0},{10,2},{12,4},{14,6},{1,9},{3,11}... | collective-permute-start | bytes 786440 | tf_op jit(solution)/shard_map/ppermute | solution.py:172
  126.3 5.8 %collective-permute-done.12 = f32[2,128,256]{1,2,0:T(8,128)S(1)} collective-permute-done((f32[2,128,256]{1,2,0:T(8,128)S(1)}, f32[2,128,256]{1,2,0:T(8,128)S(1)}, u32[]{:S(2)}, u32[]{:S(2)}) %collective-permute-start.12) | collective-permute-done | bytes 262176 | tf_op jit(solution)/shard_map/ppermute | solution.py:172
  132.6 1.5 pad_maximum_fusion.2.lifted_ref
  134.1 24.1 %shard_map.129 = f32[2,128,2048]{2,1,0:T(8,128)} custom-call(s32[1]{0:T(128)} %bitcast.live_ref, s32[512]{0:T(512)} %bitcast.117, s32[512]{0:T(512)} %bitcast.119, s32[512,16,128]{2,1,0:T(8,128)} %bitcast.97, bf16[8,256,512]{2,1,0:T(8,128)(2,1)} %pad_maximum_fusion.2.lifted_ref), custom_call_target="tpu_custom_call" | custom-call | tf_op jit(solution)/shard_map/pallas_call | solution.py:131
  158.2 2.4 %dynamic-slice_bitcast_fusion = f32[128,2048]{1,0:T(8,128)} fusion(f32[2,128,2048]{2,1,0:T(8,128)} %shard_map.129, s32[]{:T(128)S(6)} %select_n.227), kind=kLoop, calls=%fused_computation.20 | loop fusion | bytes 2097156 | tf_op jit(solution)/shard_map/jit(dynamic_index_in_dim)/squeeze | solution.py:210
  160.6 6.8 %collective-permute-start.18 = (f32[128,2048]{1,0:T(8,128)}, f32[128,2048]{1,0:T(8,128)}, u32[]{:S(2)}, u32[]{:S(2)}) collective-permute-start(f32[128,2048]{1,0:T(8,128)} %dynamic-slice_bitcast_fusion), channel_id=1, source_target_pairs={{0,16},{16,0},{1,17},{17,1},{2,18},{18,2},{3,19},{19,3},{4,20},{20... | collective-permute-start | bytes 3145736 | tf_op jit(solution)/shard_map/ppermute | solution.py:172
  170.3 1.3 fusion.3
  (93 shorter events, 17.0 us)
Async XLA Ops:
  0.6 78.8 %copy-start = (f32[256,256]{1,0:T(8,128)S(1)}, f32[256,256]{1,0:T(8,128)}, u32[]{:S(2)}) copy-start(f32[256,256]{1,0:T(8,128)} %param.11) | copy-start | bytes 786436
  0.6 3.2 %collective-permute-start.1 = (f32[2048,128]{1,0:T(8,128)}, f32[2048,128]{1,0:T(8,128)S(1)}, u32[]{:S(2)}, u32[]{:S(2)}) collective-permute-start(f32[2048,128]{1,0:T(8,128)} %param.9), channel_id=1, source_target_pairs={{0,16},{16,0},{1,17},{17,1},{2,18},{18,2},{3,19},{19,3},{4,20},{20... | collective-permute-start | bytes 3145736 | tf_op jit(solution)/shard_map/ppermute | solution.py:172
  35.8 13.5 %collective-permute-start.2 = (f32[2,2,264,128]{3,2,1,0:T(8,128)S(1)}, f32[2,2,264,128]{3,2,1,0:T(8,128)S(1)}, u32[]{:S(2)}, u32[]{:S(2)}) collective-permute-start(f32[2,2,264,128]{3,2,1,0:T(8,128)S(1)} %dynamic-slice_bitcast_fusion.2), channel_id=1, source_target_pairs={{0,2},{2,0},{4,6},{6,4},{8,10},{10,8},{12,14},{14,12},{1,3},{3,1},... | collective-permute-start | bytes 1622024 | tf_op jit(solution)/shard_map/ppermute | solution.py:172
  36.0 14.6 %collective-permute-start.4 = (f32[2,2,264,128]{3,2,1,0:T(8,128)S(1)}, f32[2,2,264,128]{3,2,1,0:T(8,128)S(1)}, u32[]{:S(2)}, u32[]{:S(2)}) collective-permute-start(f32[2,2,264,128]{3,2,1,0:T(8,128)S(1)} %dynamic-slice_bitcast_fusion.1), channel_id=1, source_target_pairs={{0,4},{2,6},{4,0},{6,2},{8,12},{10,14},{12,8},{14,10},{1,5},{3,7},... | collective-permute-start | bytes 1622024 | tf_op jit(solution)/shard_map/ppermute | solution.py:172
  50.5 7.3 %copy-start.4 = (f32[512,128]{1,0:T(8,128)S(1)}, f32[512,128]{1,0:T(8,128)}, u32[]{:S(2)}) copy-start(f32[512,128]{1,0:T(8,128)} %param.10) | copy-start | bytes 786436
  50.5 6.9 %collective-permute-start.3 = (f32[2,264,128]{2,1,0:T(8,128)S(1)}, f32[2,264,128]{2,1,0:T(8,128)S(1)}, u32[]{:S(2)}, u32[]{:S(2)}) collective-permute-start(f32[2,264,128]{2,1,0:T(8,128)S(1)} %dynamic-slice_bitcast_fusion.4), channel_id=1, source_target_pairs={{0,4},{2,6},{4,0},{6,2},{8,12},{10,14},{12,8},{14,10},{1,5},{3,7},... | collective-permute-start | bytes 811016 | tf_op jit(solution)/shard_map/ppermute | solution.py:172
  50.7 6.9 %collective-permute-start.5 = (f32[2,264,128]{2,1,0:T(8,128)S(1)}, f32[2,264,128]{2,1,0:T(8,128)S(1)}, u32[]{:S(2)}, u32[]{:S(2)}) collective-permute-start(f32[2,264,128]{2,1,0:T(8,128)S(1)} %dynamic-slice_bitcast_fusion.3), channel_id=1, source_target_pairs={{0,2},{2,0},{4,6},{6,4},{8,10},{10,8},{12,14},{14,12},{1,3},{3,1},... | collective-permute-start | bytes 811016 | tf_op jit(solution)/shard_map/ppermute | solution.py:172
  57.6 21.2 %copy-start.5 = (f32[256,256]{1,0:T(8,128)S(1)}, f32[256,256]{1,0:T(8,128)}, u32[]{:S(2)}) copy-start(f32[256,256]{1,0:T(8,128)} %param.12) | copy-start | bytes 786436
  57.7 14.3 %collective-permute-start.6 = (f32[2,264,128]{2,1,0:T(8,128)S(1)}, f32[2,264,128]{2,1,0:T(8,128)S(1)}, u32[]{:S(2)}, u32[]{:S(2)}) collective-permute-start(f32[2,264,128]{2,1,0:T(8,128)S(1)} %pad_maximum_fusion.9), channel_id=1, source_target_pairs={{0,8},{2,10},{4,12},{6,14},{8,0},{10,2},{12,4},{14,6},{1,9},{3,11}... | collective-permute-start | bytes 811016 | tf_op jit(solution)/shard_map/ppermute | solution.py:172
  57.8 14.6 %collective-permute-start = (f32[512,128]{1,0:T(8,128)S(1)}, f32[512,128]{1,0:T(8,128)S(1)}, u32[]{:S(2)}, u32[]{:S(2)}) collective-permute-start(f32[512,128]{1,0:T(8,128)S(1)} %copy-done.4), channel_id=1, source_target_pairs={{0,1},{1,0},{2,3},{3,2},{4,5},{5,4},{6,7},{7,6},{8,9},{9,8},{10,11... | collective-permute-start | bytes 786440 | tf_op jit(solution)/shard_map/ppermute | solution.py:172
  58.0 21.4 %copy-start.6 = (f32[512,128]{1,0:T(8,128)S(1)}, f32[512,128]{1,0:T(8,128)}, u32[]{:S(2)}) copy-start(f32[512,128]{1,0:T(8,128)} %param.13) | copy-start | bytes 786436
  72.2 6.6 %collective-permute-start.7 = (f32[512,128]{1,0:T(8,128)S(1)}, f32[512,128]{1,0:T(8,128)S(1)}, u32[]{:S(2)}, u32[]{:S(2)}) collective-permute-start(f32[512,128]{1,0:T(8,128)S(1)} %fusion.13), channel_id=1, source_target_pairs={{0,1},{1,0},{2,3},{3,2},{4,5},{5,4},{6,7},{7,6},{8,9},{9,8},{10,11... | collective-permute-start | bytes 786440 | tf_op jit(solution)/shard_map/ppermute | solution.py:172
  80.7 5.6 %collective-permute-start.8 = (f32[512,128]{1,0:T(8,128)S(1)}, f32[512,128]{1,0:T(8,128)S(1)}, u32[]{:S(2)}, u32[]{:S(2)}) collective-permute-start(f32[512,128]{1,0:T(8,128)S(1)} %get-tuple-element.57), channel_id=1, source_target_pairs={{0,1},{1,0},{2,3},{3,2},{4,5},{5,4},{6,7},{7,6},{8,9},{9,8},{10,11... | collective-permute-start | bytes 786440 | tf_op jit(solution)/shard_map/ppermute | solution.py:172
  87.2 13.8 %collective-permute-start.13 = (f32[2,128,256]{2,1,0:T(8,128)S(1)}, f32[2,128,256]{2,1,0:T(8,128)S(1)}, u32[]{:S(2)}, u32[]{:S(2)}) collective-permute-start(f32[2,128,256]{2,1,0:T(8,128)S(1)} %pad_maximum_fusion.7), channel_id=1, source_target_pairs={{0,8},{2,10},{4,12},{6,14},{8,0},{10,2},{12,4},{14,6},{1,9},{3,11}... | collective-permute-start | bytes 786440 | tf_op jit(solution)/shard_map/ppermute | solution.py:172
  89.3 12.0 %collective-permute-start.9 = (f32[2,128,256]{1,2,0:T(8,128)S(1)}, f32[2,128,256]{1,2,0:T(8,128)S(1)}, u32[]{:S(2)}, u32[]{:S(2)}) collective-permute-start(f32[2,128,256]{1,2,0:T(8,128)S(1)} %pad_maximum_fusion.11), channel_id=1, source_target_pairs={{0,16},{16,0},{1,17},{17,1},{2,18},{18,2},{3,19},{19,3},{4,20},{20... | collective-permute-start | bytes 786440 | tf_op jit(solution)/shard_map/ppermute | solution.py:172
  101.0 6.4 %collective-permute-start.14 = (f32[2,128,256]{2,1,0:T(8,128)S(1)}, f32[2,128,256]{2,1,0:T(8,128)S(1)}, u32[]{:S(2)}, u32[]{:S(2)}) collective-permute-start(f32[2,128,256]{2,1,0:T(8,128)S(1)} %fusion.11), channel_id=1, source_target_pairs={{0,4},{2,6},{4,0},{6,2},{8,12},{10,14},{12,8},{14,10},{1,5},{3,7},... | collective-permute-start | bytes 786440 | tf_op jit(solution)/shard_map/ppermute | solution.py:172
  101.2 6.5 %collective-permute-start.16 = (f32[2,128,256]{2,1,0:T(8,128)S(1)}, f32[2,128,256]{2,1,0:T(8,128)S(1)}, u32[]{:S(2)}, u32[]{:S(2)}) collective-permute-start(f32[2,128,256]{2,1,0:T(8,128)S(1)} %fusion.12), channel_id=1, source_target_pairs={{0,2},{2,0},{4,6},{6,4},{8,10},{10,8},{12,14},{14,12},{1,3},{3,1},... | collective-permute-start | bytes 786440 | tf_op jit(solution)/shard_map/ppermute | solution.py:172
  101.3 11.9 %collective-permute-start.10 = (f32[2,128,256]{1,2,0:T(8,128)S(1)}, f32[2,128,256]{1,2,0:T(8,128)S(1)}, u32[]{:S(2)}, u32[]{:S(2)}) collective-permute-start(f32[2,128,256]{1,2,0:T(8,128)S(1)} %fusion.32), channel_id=1, source_target_pairs={{0,2},{2,0},{4,6},{6,4},{8,10},{10,8},{12,14},{14,12},{1,3},{3,1},... | collective-permute-start | bytes 786440 | tf_op jit(solution)/shard_map/ppermute | solution.py:172
  107.5 18.0 %collective-permute-start.15 = (f32[2,2,128,256]{3,2,0,1:T(8,128)S(1)}, f32[2,2,128,256]{3,2,0,1:T(8,128)S(1)}, u32[]{:S(2)}, u32[]{:S(2)}) collective-permute-start(f32[2,2,128,256]{3,2,0,1:T(8,128)S(1)} %maximum_select_fusion.4), channel_id=1, source_target_pairs={{0,2},{2,0},{4,6},{6,4},{8,10},{10,8},{12,14},{14,12},{1,3},{3,1},... | collective-permute-start | bytes 1572872 | tf_op jit(solution)/shard_map/ppermute | solution.py:172
  107.7 18.1 %collective-permute-start.17 = (f32[2,2,128,256]{3,2,1,0:T(8,128)S(1)}, f32[2,2,128,256]{3,2,1,0:T(8,128)S(1)}, u32[]{:S(2)}, u32[]{:S(2)}) collective-permute-start(f32[2,2,128,256]{3,2,1,0:T(8,128)S(1)} %maximum_select_fusion.6), channel_id=1, source_target_pairs={{0,4},{2,6},{4,0},{6,2},{8,12},{10,14},{12,8},{14,10},{1,5},{3,7},... | collective-permute-start | bytes 1572872 | tf_op jit(solution)/shard_map/ppermute | solution.py:172
  113.3 9.3 %collective-permute-start.11 = (f32[2,128,256]{1,2,0:T(8,128)S(1)}, f32[2,128,256]{1,2,0:T(8,128)S(1)}, u32[]{:S(2)}, u32[]{:S(2)}) collective-permute-start(f32[2,128,256]{1,2,0:T(8,128)S(1)} %fusion.39), channel_id=1, source_target_pairs={{0,4},{2,6},{4,0},{6,2},{8,12},{10,14},{12,8},{14,10},{1,5},{3,7},... | collective-permute-start | bytes 786440 | tf_op jit(solution)/shard_map/ppermute | solution.py:172
  122.7 9.5 %collective-permute-start.12 = (f32[2,128,256]{1,2,0:T(8,128)S(1)}, f32[2,128,256]{1,2,0:T(8,128)S(1)}, u32[]{:S(2)}, u32[]{:S(2)}) collective-permute-start(f32[2,128,256]{1,2,0:T(8,128)S(1)} %add.129), channel_id=1, source_target_pairs={{0,8},{2,10},{4,12},{6,14},{8,0},{10,2},{12,4},{14,6},{1,9},{3,11}... | collective-permute-start | bytes 786440 | tf_op jit(solution)/shard_map/ppermute | solution.py:172
  158.2 12.1 %copy-start.1 = (f32[2,128,2048]{2,1,0:T(8,128)S(1)}, f32[2,128,2048]{2,1,0:T(8,128)}, u32[]{:S(2)}) copy-start(f32[2,128,2048]{2,1,0:T(8,128)} %shard_map.129) | copy-start | bytes 6291460
  160.6 9.7 %collective-permute-start.18 = (f32[128,2048]{1,0:T(8,128)}, f32[128,2048]{1,0:T(8,128)}, u32[]{:S(2)}, u32[]{:S(2)}) collective-permute-start(f32[128,2048]{1,0:T(8,128)} %dynamic-slice_bitcast_fusion), channel_id=1, source_target_pairs={{0,16},{16,0},{1,17},{17,1},{2,18},{18,2},{3,19},{19,3},{4,20},{20... | collective-permute-start | bytes 3145736 | tf_op jit(solution)/shard_map/ppermute | solution.py:172
  (2 other events, 3.4 us)

commit v12 on v7

--- a/solution.py
+++ b/solution.py
@@ -23,6 +23,12 @@
     shifts = lax.broadcasted_iota(jnp.int32, (word_rows, 8, edge), 1)
     bits = jnp.bitwise_and(jnp.right_shift(cube, shifts), 1)
     return bits.reshape(word_rows * 8, edge)
+
+
+def split_tile(tile, axis):
+    high = tile.astype(jnp.bfloat16)
+    low = (tile - high.astype(jnp.float32)).astype(jnp.bfloat16)
+    return jnp.concatenate([high, low], axis=axis)
 
 
 def unpack_block(words):
@@ -65,7 +71,7 @@
             bits = unpack_bits(jnp.bitwise_and(masks_ref[k], keep))
             bits_ref[row] += bits
             dense = bits.astype(jnp.float32).astype(jnp.bfloat16)
-            tile = panel_ref[pl.ds(pl.multiple_of(col * edge, edge), edge), :]
+            tile = split_tile(panel_ref[pl.ds(pl.multiple_of(col * edge, edge), edge), :], 1)
             prod = jnp.dot(dense, tile, preferred_element_type=jnp.float32)
             start = pl.multiple_of(row * edge, edge)
             totals_ref[pl.ds(start, edge), :] += prod[:, :half] + prod[:, half:]
@@ -96,10 +102,11 @@
             col = jnp.clip(cols_ref[slot], 0, col_limit)
             dense = slot_words(masks_ref, live_ref, base, k)
             row_start = pl.multiple_of((row % row_chunk) * edge, edge)
-            tile = lifted_ref[row // row_chunk, :, pl.ds(row_start, edge)]
+            tile = split_tile(lifted_ref[row // row_chunk, :, pl.ds(row_start, edge)], 0)
             prod = jnp.dot(tile, dense, preferred_element_type=jnp.float32)
             col_start = pl.multiple_of((col % col_chunk) * edge, edge)
-            out_ref[col // col_chunk, :, pl.ds(col_start, edge)] += prod[:half] + prod[half:]
+            relative = jnp.bitwise_xor(col // col_chunk, live_ref[1])
+            out_ref[relative, :, pl.ds(col_start, edge)] += prod[:half] + prod[half:]
             return carry
 
         lax.fori_loop(0, group, body, 0, unroll=UNROLL)
@@ -138,7 +145,7 @@
 
 def block_aggregate(live, block_rows, block_cols, packed_masks, panel_split, row_blocks):
     edge = packed_masks.shape[-1]
-    totals_shape = jax.ShapeDtypeStruct((row_blocks * edge, panel_split.shape[1] // 2), jnp.float32)
+    totals_shape = jax.ShapeDtypeStruct((row_blocks * edge, panel_split.shape[1]), jnp.float32)
     bits_shape = jax.ShapeDtypeStruct((row_blocks, edge, edge), jnp.int32)
     totals, bit_sums = slot_pallas(
         forward_kernel, live, block_rows, block_cols, packed_masks, panel_split,
@@ -149,8 +156,7 @@
 
 def block_transpose(live, block_rows, block_cols, packed_masks, lifted_chunks, cand_count):
     edge = packed_masks.shape[-1]
-    high = lax.reduce_precision(lifted_chunks, exponent_bits=8, mantissa_bits=7)
-    split_t = jnp.concatenate([high, lifted_chunks - high], axis=1).astype(jnp.bfloat16)
+    split_t = lifted_chunks
     width = lifted_chunks.shape[1]
     panel_cols = lifted_chunks.shape[0] * lifted_chunks.shape[2]
     out_shape = jax.ShapeDtypeStruct((cand_count, width, panel_cols // cand_count), jnp.float32)
@@ -252,6 +258,19 @@
     return jnp.concatenate(
         [result.reshape((-1,) + result.shape[-2:]) for result in results], axis=2
     )
+
+
+def halving_relative(chunks, axis):
+    bits = axis_bits(axis)
+    data = chunks.reshape((2,) * bits + chunks.shape[1:])
+    remaining = list(reversed(range(bits)))
+    for bit in range(bits):
+        position = remaining.index(bit)
+        remaining.remove(bit)
+        keep = lax.index_in_dim(data, 0, position, keepdims=False)
+        send = lax.index_in_dim(data, 1, position, keepdims=False)
+        data = keep + exchange(send, axis, bit)
+    return data
 
 
 def butterfly_sum(values, axes):
@@ -281,7 +300,9 @@
     packed_masks = block_mask.reshape(block_mask.shape[2:])
     block_rows = block_row.reshape(-1)
     block_cols = block_col.reshape(-1)
-    live = jnp.clip(block_live.reshape(1), 0, packed_masks.shape[0])
+    live = jnp.concatenate(
+        [jnp.clip(block_live.reshape(1), 0, packed_masks.shape[0]), lax.axis_index("cand").reshape(1)]
+    ).astype(jnp.int32)
     block_edge = packed_masks.shape[-1]
     cand_count = lax.axis_size("cand")
     test_count = lax.axis_size("test")
@@ -292,7 +313,7 @@
     panel = doubling_gather(x_test, "cand")
     cand_full = gather_axis(x_cand, "feat", 1)
     row_totals, row_counts = block_aggregate(
-        live, block_rows, block_cols, packed_masks, split_hi_lo(panel), row_blocks
+        live, block_rows, block_cols, packed_masks, panel, row_blocks
     )
     own_totals, degree = scatter_totals_and_counts(row_totals, row_counts, test_count)
     aggregated = own_totals / (1.0 + degree)[:, None]
@@ -320,7 +341,7 @@
     grad_w_self = grad_w_pair[0] / root_count
     grad_w_neigh = grad_w_pair[1] / root_count
     out_t = block_transpose(live, block_rows, block_cols, packed_masks, lifted_chunks, cand_count)
-    own_t = halving_scatter(out_t.reshape(-1, out_t.shape[2]), "cand")
+    own_t = halving_relative(out_t, "cand")
     grad_x_test = own_t.T
     return (output, grad_w_self, grad_w_neigh, grad_x_cand, grad_x_test)
 

time: 172 us -> 176 us (1.023)
  waiting for transfers between devices: 75.5 us -> 85.6 us
  starting transfers between devices: 20.6 us -> 11.7 us
  Pallas kernels: 48.8 us -> 51.5 us
    ppermute x21, waiting for transfers between devices: 75.5 us -> 85.6 us  [exchange(): return lax.ppermute(values, axis, [(i, i ^ 1 << bit) for i in range(count)])]
    ppermute x21, starting transfers between devices: 20.6 us -> 11.7 us  [exchange(): return lax.ppermute(values, axis, [(i, i ^ 1 << bit) for i in range(count)])]
    pallas_call x2, Pallas kernels: 48.8 us -> 51.5 us  [slot_pallas(): pl.pallas_call(kernel, grid_spec=grid_spec, out_shape=out_shapes, compile...]
    concatenate x2 -> x1, other arithmetic: 3.04 us -> 0.59 us  [local(): jnp.concatenate([jnp.clip(block_live.reshape(1), 0, packed_masks.shape[0]...]
    squeeze x0 -> x1, local copies, waits for them, and re-layouts: none -> 2.44 us  [halving_relative(): send = lax.index_in_dim(data, 1, position, keepdims=False)]
    squeeze x7 -> x6, local copies, waits for them, and re-layouts: 3.41 us -> 0.97 us  [halving_steps(): send = lax.dynamic_index_in_dim(data, 1 - mine, position, keepdims=False)]
  transfers between devices with their start and end apart: 21 -> 21, of which waited for: 17 -> 15; matrix products, arithmetic and copies ran while one was open for 4% -> 5% of each run, Pallas kernels for 0% -> 0%
where the time goes in v12:
time: 176 us; the launch traced here: 175 us
  waiting for transfers between devices  85.6 us (49%)
  Pallas kernels  51.5 us (29%)
  starting transfers between devices  11.7 us (7%)
  other arithmetic  11.4 us (6%)
  local copies, waits for them, and re-layouts  7.57 us (4%)
  matrix products  5.81 us (3%)
  between operations  1.77 us (1%)
    ppermute x21, waiting for transfers between devices, exchange(): return lax.ppermute(values, axis, [(i, i ^ 1 << bit) for i in range(count)])  85.6 us
    pallas_call x2, Pallas kernels, slot_pallas(): pl.pallas_call(kernel, grid_spec=grid_spec, out_shape=out_shapes, compile...  51.5 us
    ppermute x21, starting transfers between devices, exchange(): return lax.ppermute(values, axis, [(i, i ^ 1 << bit) for i in range(count)])  11.7 us
    unnamed x17, local copies, waits for them, and re-layouts  3.83 us
    select_n x11, other arithmetic, doubling_steps(): jnp.where(first, jnp.stack([data, other], axis=position), jnp.stack([othe...  3.54 us
  transfers between devices with their start and end apart: 21, of which 15 were waited for; matrix products, arithmetic and copies ran while one was open for 5% of the time, Pallas kernels for 0%

profile of v12, /device:TPU:31, one launch (start us, length us, event | category | flops | bytes accessed | tf_op | source)
XLA Modules:
  0.0 175.3 jit_solution(9372571907941609646)
XLA Ops:
  3.9 3.1 %maximum_select_fusion = f32[2,2048,128]{2,1,0:T(8,128)} fusion(f32[1,2048,128]{2,1,0:T(8,128)S(1)} %bitcast.113, f32[1,2048,128]{2,1,0:T(8,128)} %bitcast.112, pred[]{:T(512)S(6)} %eq.21), kind=kLoop, calls=%fused_computation | loop fusion | flops 1572864 | bytes 4194305 | tf_op jit(solution)/shard_map/jit(_where)/select_n | solution.py:218
  7.0 26.4 %shard_map.128 = (f32[4096,128]{1,0:T(8,128)}, s32[32,128,128]{2,1,0:T(8,128)}) custom-call(s32[2]{0:T(128)} %pad_add_fusion.live_ref, s32[512]{0:T(512)} %bitcast.121, s32[512]{0:T(512)} %bitcast.123, s32[512,16,128]{2,1,0:T(8,128)} %bitcast.96, f32[4096,128]{1,0:T(8,128)} %bitcast.98), custom_call_target="tpu_custom_call" | custom-call | tf_op jit(solution)/shard_map/pallas_call | solution.py:138
  33.4 2.4 %reduce_sum.9 = s32[32,128]{1,0:T(8,128)S(1)} reduce(s32[32,128,128]{2,1,0:T(8,128)} %get-tuple-element.10, s32[]{:T(128)} %constant.63.clone.1), dimensions={2}, to_apply=%region_0.1 | reduce | flops 520192 | bytes 2113540 | tf_op jit(solution)/shard_map/reduce_sum | solution.py:154
  38.1 12.4 %collective-permute-done.5 = f32[2,2,264,128]{3,2,1,0:T(8,128)S(1)} collective-permute-done((f32[2,2,264,128]{3,2,1,0:T(8,128)S(1)}, f32[2,2,264,128]{3,2,1,0:T(8,128)S(1)}, u32[]{:S(2)}, u32[]{:S(2)}) %collective-permute-start.5) | collective-permute-done | bytes 540704 | tf_op jit(solution)/shard_map/ppermute | solution.py:178
  52.9 5.6 %collective-permute-done.6 = f32[2,264,128]{2,1,0:T(8,128)S(1)} collective-permute-done((f32[2,264,128]{2,1,0:T(8,128)S(1)}, f32[2,264,128]{2,1,0:T(8,128)S(1)}, u32[]{:S(2)}, u32[]{:S(2)}) %collective-permute-start.6) | collective-permute-done | bytes 270368 | tf_op jit(solution)/shard_map/ppermute | solution.py:178
  58.8 2.4 %collective-permute-start.4 = (f32[264,128]{1,0:T(8,128)S(1)}, f32[264,128]{1,0:T(8,128)S(1)}, u32[]{:S(2)}, u32[]{:S(2)}) collective-permute-start(f32[264,128]{1,0:T(8,128)S(1)} %dynamic-slice_bitcast_fusion.5), channel_id=1, source_target_pairs={{0,8},{2,10},{4,12},{6,14},{8,0},{10,2},{12,4},{14,6},{1,9},{3,11}... | collective-permute-start | bytes 405512 | tf_op jit(solution)/shard_map/ppermute | solution.py:178
  61.2 9.4 %collective-permute-done.7 = f32[264,128]{1,0:T(8,128)S(1)} collective-permute-done((f32[264,128]{1,0:T(8,128)S(1)}, f32[264,128]{1,0:T(8,128)S(1)}, u32[]{:S(2)}, u32[]{:S(2)}) %collective-permute-start.7) | collective-permute-done | bytes 135200 | tf_op jit(solution)/shard_map/ppermute | solution.py:178
  70.6 2.9 %collective-permute-done.4 = f32[264,128]{1,0:T(8,128)S(1)} collective-permute-done((f32[264,128]{1,0:T(8,128)S(1)}, f32[264,128]{1,0:T(8,128)S(1)}, u32[]{:S(2)}, u32[]{:S(2)}) %collective-permute-start.4) | collective-permute-done | bytes 135200 | tf_op jit(solution)/shard_map/ppermute | solution.py:178
  74.0 6.8 %collective-permute-done.8 = f32[512,128]{1,0:T(8,128)S(1)} collective-permute-done((f32[512,128]{1,0:T(8,128)S(1)}, f32[512,128]{1,0:T(8,128)S(1)}, u32[]{:S(2)}, u32[]{:S(2)}) %collective-permute-start.8) | collective-permute-done | bytes 262176 | tf_op jit(solution)/shard_map/ppermute | solution.py:178
  81.5 1.3 multiply_multiply_fusion
  83.0 6.0 %collective-permute-done.9 = f32[512,128]{1,0:T(8,128)S(1)} collective-permute-done((f32[512,128]{1,0:T(8,128)S(1)}, f32[512,128]{1,0:T(8,128)S(1)}, u32[]{:S(2)}, u32[]{:S(2)}) %collective-permute-start.9) | collective-permute-done | bytes 262176 | tf_op jit(solution)/shard_map/ppermute | solution.py:178
  91.8 2.4 %collective-permute-start.14 = (f32[128,256]{1,0:T(8,128)S(1)}, f32[128,256]{1,0:T(8,128)S(1)}, u32[]{:S(2)}, u32[]{:S(2)}) collective-permute-start(f32[128,256]{1,0:T(8,128)S(1)} %get-tuple-element.48), channel_id=1, source_target_pairs={{0,8},{2,10},{4,12},{6,14},{8,0},{10,2},{12,4},{14,6},{1,9},{3,11}... | collective-permute-start | bytes 393224 | tf_op jit(solution)/shard_map/ppermute | solution.py:178
  94.3 3.1 %collective-permute-start.10 = (f32[2,128,256]{1,2,0:T(8,128)S(1)}, f32[2,128,256]{1,2,0:T(8,128)S(1)}, u32[]{:S(2)}, u32[]{:S(2)}) collective-permute-start(f32[2,128,256]{1,2,0:T(8,128)S(1)} %pad_maximum_fusion.4), channel_id=1, source_target_pairs={{0,16},{16,0},{1,17},{17,1},{2,18},{18,2},{3,19},{19,3},{4,20},{20... | collective-permute-start | bytes 786440 | tf_op jit(solution)/shard_map/ppermute | solution.py:178
  97.4 3.7 %collective-permute-done.17 = f32[128,256]{1,0:T(8,128)S(1)} collective-permute-done((f32[128,256]{1,0:T(8,128)S(1)}, f32[128,256]{1,0:T(8,128)S(1)}, u32[]{:S(2)}, u32[]{:S(2)}) %collective-permute-start.17) | collective-permute-done | bytes 131104 | tf_op jit(solution)/shard_map/ppermute | solution.py:178
  101.2 2.7 %collective-permute-done.14 = f32[128,256]{1,0:T(8,128)S(1)} collective-permute-done((f32[128,256]{1,0:T(8,128)S(1)}, f32[128,256]{1,0:T(8,128)S(1)}, u32[]{:S(2)}, u32[]{:S(2)}) %collective-permute-start.14) | collective-permute-done | bytes 131104 | tf_op jit(solution)/shard_map/ppermute | solution.py:178
  104.2 3.9 %collective-permute-done.18 = f32[2,128,256]{2,1,0:T(8,128)S(1)} collective-permute-done((f32[2,128,256]{2,1,0:T(8,128)S(1)}, f32[2,128,256]{2,1,0:T(8,128)S(1)}, u32[]{:S(2)}, u32[]{:S(2)}) %collective-permute-start.18) | collective-permute-done | bytes 262176 | tf_op jit(solution)/shard_map/ppermute | solution.py:178
  108.2 2.9 %collective-permute-done.15 = f32[2,128,256]{2,1,0:T(8,128)S(1)} collective-permute-done((f32[2,128,256]{2,1,0:T(8,128)S(1)}, f32[2,128,256]{2,1,0:T(8,128)S(1)}, u32[]{:S(2)}, u32[]{:S(2)}) %collective-permute-start.15) | collective-permute-done | bytes 262176 | tf_op jit(solution)/shard_map/ppermute | solution.py:178
  111.3 2.4 %collective-permute-done.11 = f32[2,128,256]{1,2,0:T(8,128)S(1)} collective-permute-done((f32[2,128,256]{1,2,0:T(8,128)S(1)}, f32[2,128,256]{1,2,0:T(8,128)S(1)}, u32[]{:S(2)}, u32[]{:S(2)}) %collective-permute-start.11) | collective-permute-done | bytes 262176 | tf_op jit(solution)/shard_map/ppermute | solution.py:178
  113.9 12.9 %collective-permute-done.12 = f32[2,128,256]{1,2,0:T(8,128)S(1)} collective-permute-done((f32[2,128,256]{1,2,0:T(8,128)S(1)}, f32[2,128,256]{1,2,0:T(8,128)S(1)}, u32[]{:S(2)}, u32[]{:S(2)}) %collective-permute-start.12) | collective-permute-done | bytes 262176 | tf_op jit(solution)/shard_map/ppermute | solution.py:178
  127.5 1.6 pad_maximum_fusion.lifted_ref
  129.1 12.7 %collective-permute-done.13 = f32[2,128,256]{1,2,0:T(8,128)S(1)} collective-permute-done((f32[2,128,256]{1,2,0:T(8,128)S(1)}, f32[2,128,256]{1,2,0:T(8,128)S(1)}, u32[]{:S(2)}, u32[]{:S(2)}) %collective-permute-start.13) | collective-permute-done | bytes 262176 | tf_op jit(solution)/shard_map/ppermute | solution.py:178
  141.8 25.1 %shard_map.129 = f32[2,128,2048]{2,1,0:T(8,128)} custom-call(s32[2]{0:T(128)} %pad_add_fusion.live_ref, s32[512]{0:T(512)} %bitcast.122, s32[512]{0:T(512)} %bitcast.124, s32[512,16,128]{2,1,0:T(8,128)} %bitcast.97, f32[8,128,512]{2,1,0:T(8,128)} %pad_maximum_fusion.lifted_ref), custom_call_target="tpu_custom_call" | custom-call | tf_op jit(solution)/shard_map/pallas_call | solution.py:138
  166.9 2.4 %slice_bitcast_fusion = f32[128,2048]{1,0:T(8,128)} fusion(f32[2,128,2048]{2,1,0:T(8,128)} %shard_map.129), kind=kLoop, calls=%fused_computation.8 | loop fusion | bytes 2097152 | tf_op jit(solution)/shard_map/squeeze | solution.py:271
  172.7 1.3 fusion.2
  (91 shorter events, 17.7 us)
Async XLA Ops:
  0.6 80.8 %copy-start = (f32[256,256]{1,0:T(8,128)S(1)}, f32[256,256]{1,0:T(8,128)}, u32[]{:S(2)}) copy-start(f32[256,256]{1,0:T(8,128)} %param.11) | copy-start | bytes 786436
  0.6 3.2 %collective-permute-start.1 = (f32[2048,128]{1,0:T(8,128)}, f32[2048,128]{1,0:T(8,128)S(1)}, u32[]{:S(2)}, u32[]{:S(2)}) collective-permute-start(f32[2048,128]{1,0:T(8,128)} %param.9), channel_id=1, source_target_pairs={{0,16},{16,0},{1,17},{17,1},{2,18},{18,2},{3,19},{19,3},{4,20},{20... | collective-permute-start | bytes 3145736 | tf_op jit(solution)/shard_map/ppermute | solution.py:178
  37.0 13.5 %collective-permute-start.5 = (f32[2,2,264,128]{3,2,1,0:T(8,128)S(1)}, f32[2,2,264,128]{3,2,1,0:T(8,128)S(1)}, u32[]{:S(2)}, u32[]{:S(2)}) collective-permute-start(f32[2,2,264,128]{3,2,1,0:T(8,128)S(1)} %dynamic-slice_bitcast_fusion), channel_id=1, source_target_pairs={{0,4},{2,6},{4,0},{6,2},{8,12},{10,14},{12,8},{14,10},{1,5},{3,7},... | collective-permute-start | bytes 1622024 | tf_op jit(solution)/shard_map/ppermute | solution.py:178
  37.9 13.8 %collective-permute-start.2 = (f32[2,2,264,128]{3,2,1,0:T(8,128)}, f32[2,2,264,128]{3,2,1,0:T(8,128)S(1)}, u32[]{:S(2)}, u32[]{:S(2)}) collective-permute-start(f32[2,2,264,128]{3,2,1,0:T(8,128)} %dynamic-slice_bitcast_fusion.1), channel_id=1, source_target_pairs={{0,2},{2,0},{4,6},{6,4},{8,10},{10,8},{12,14},{14,12},{1,3},{3,1},... | collective-permute-start | bytes 1622024 | tf_op jit(solution)/shard_map/ppermute | solution.py:178
  37.9 36.0 %collective-permute-start = (f32[512,128]{1,0:T(8,128)S(1)}, f32[512,128]{1,0:T(8,128)S(1)}, u32[]{:S(2)}, u32[]{:S(2)}) collective-permute-start(f32[512,128]{1,0:T(8,128)S(1)} %copy-done.4), channel_id=1, source_target_pairs={{0,1},{1,0},{2,3},{3,2},{4,5},{5,4},{6,7},{7,6},{8,9},{9,8},{10,11... | collective-permute-start | bytes 786440 | tf_op jit(solution)/shard_map/ppermute | solution.py:178
  51.6 6.9 %collective-permute-start.6 = (f32[2,264,128]{2,1,0:T(8,128)S(1)}, f32[2,264,128]{2,1,0:T(8,128)S(1)}, u32[]{:S(2)}, u32[]{:S(2)}) collective-permute-start(f32[2,264,128]{2,1,0:T(8,128)S(1)} %dynamic-slice_bitcast_fusion.2), channel_id=1, source_target_pairs={{0,2},{2,0},{4,6},{6,4},{8,10},{10,8},{12,14},{14,12},{1,3},{3,1},... | collective-permute-start | bytes 811016 | tf_op jit(solution)/shard_map/ppermute | solution.py:178
  51.8 6.9 %collective-permute-start.3 = (f32[2,264,128]{2,1,0:T(8,128)S(1)}, f32[2,264,128]{2,1,0:T(8,128)S(1)}, u32[]{:S(2)}, u32[]{:S(2)}) collective-permute-start(f32[2,264,128]{2,1,0:T(8,128)S(1)} %dynamic-slice_bitcast_fusion.3), channel_id=1, source_target_pairs={{0,4},{2,6},{4,0},{6,2},{8,12},{10,14},{12,8},{14,10},{1,5},{3,7},... | collective-permute-start | bytes 811016 | tf_op jit(solution)/shard_map/ppermute | solution.py:178
  58.6 22.3 %copy-start.5 = (f32[256,256]{1,0:T(8,128)S(1)}, f32[256,256]{1,0:T(8,128)}, u32[]{:S(2)}) copy-start(f32[256,256]{1,0:T(8,128)} %param.12) | copy-start | bytes 786436
  58.6 12.0 %collective-permute-start.7 = (f32[264,128]{1,0:T(8,128)S(1)}, f32[264,128]{1,0:T(8,128)S(1)}, u32[]{:S(2)}, u32[]{:S(2)}) collective-permute-start(f32[264,128]{1,0:T(8,128)S(1)} %dynamic-slice_bitcast_fusion.4), channel_id=1, source_target_pairs={{0,8},{2,10},{4,12},{6,14},{8,0},{10,2},{12,4},{14,6},{1,9},{3,11}... | collective-permute-start | bytes 405512 | tf_op jit(solution)/shard_map/ppermute | solution.py:178
  58.8 22.7 %copy-start.6 = (f32[512,128]{1,0:T(8,128)S(1)}, f32[512,128]{1,0:T(8,128)}, u32[]{:S(2)}) copy-start(f32[512,128]{1,0:T(8,128)} %param.13) | copy-start | bytes 786436
  58.8 14.7 %collective-permute-start.4 = (f32[264,128]{1,0:T(8,128)S(1)}, f32[264,128]{1,0:T(8,128)S(1)}, u32[]{:S(2)}, u32[]{:S(2)}) collective-permute-start(f32[264,128]{1,0:T(8,128)S(1)} %dynamic-slice_bitcast_fusion.5), channel_id=1, source_target_pairs={{0,8},{2,10},{4,12},{6,14},{8,0},{10,2},{12,4},{14,6},{1,9},{3,11}... | collective-permute-start | bytes 405512 | tf_op jit(solution)/shard_map/ppermute | solution.py:178
  73.6 7.2 %collective-permute-start.8 = (f32[512,128]{1,0:T(8,128)S(1)}, f32[512,128]{1,0:T(8,128)S(1)}, u32[]{:S(2)}, u32[]{:S(2)}) collective-permute-start(f32[512,128]{1,0:T(8,128)S(1)} %fusion.10), channel_id=1, source_target_pairs={{0,1},{1,0},{2,3},{3,2},{4,5},{5,4},{6,7},{7,6},{8,9},{9,8},{10,11... | collective-permute-start | bytes 786440 | tf_op jit(solution)/shard_map/ppermute | solution.py:178
  82.8 6.2 %collective-permute-start.9 = (f32[512,128]{1,0:T(8,128)S(1)}, f32[512,128]{1,0:T(8,128)S(1)}, u32[]{:S(2)}, u32[]{:S(2)}) collective-permute-start(f32[512,128]{1,0:T(8,128)S(1)} %get-tuple-element.49), channel_id=1, source_target_pairs={{0,1},{1,0},{2,3},{3,2},{4,5},{5,4},{6,7},{7,6},{8,9},{9,8},{10,11... | collective-permute-start | bytes 786440 | tf_op jit(solution)/shard_map/ppermute | solution.py:178
  90.8 10.3 %collective-permute-start.17 = (f32[128,256]{1,0:T(8,128)S(1)}, f32[128,256]{1,0:T(8,128)S(1)}, u32[]{:S(2)}, u32[]{:S(2)}) collective-permute-start(f32[128,256]{1,0:T(8,128)S(1)} %get-tuple-element.47), channel_id=1, source_target_pairs={{0,8},{2,10},{4,12},{6,14},{8,0},{10,2},{12,4},{14,6},{1,9},{3,11}... | collective-permute-start | bytes 393224 | tf_op jit(solution)/shard_map/ppermute | solution.py:178
  91.8 12.0 %collective-permute-start.14 = (f32[128,256]{1,0:T(8,128)S(1)}, f32[128,256]{1,0:T(8,128)S(1)}, u32[]{:S(2)}, u32[]{:S(2)}) collective-permute-start(f32[128,256]{1,0:T(8,128)S(1)} %get-tuple-element.48), channel_id=1, source_target_pairs={{0,8},{2,10},{4,12},{6,14},{8,0},{10,2},{12,4},{14,6},{1,9},{3,11}... | collective-permute-start | bytes 393224 | tf_op jit(solution)/shard_map/ppermute | solution.py:178
  94.3 9.8 %collective-permute-start.10 = (f32[2,128,256]{1,2,0:T(8,128)S(1)}, f32[2,128,256]{1,2,0:T(8,128)S(1)}, u32[]{:S(2)}, u32[]{:S(2)}) collective-permute-start(f32[2,128,256]{1,2,0:T(8,128)S(1)} %pad_maximum_fusion.4), channel_id=1, source_target_pairs={{0,16},{16,0},{1,17},{17,1},{2,18},{18,2},{3,19},{19,3},{4,20},{20... | collective-permute-start | bytes 786440 | tf_op jit(solution)/shard_map/ppermute | solution.py:178
  101.1 7.0 %collective-permute-start.18 = (f32[2,128,256]{2,1,0:T(8,128)S(1)}, f32[2,128,256]{2,1,0:T(8,128)S(1)}, u32[]{:S(2)}, u32[]{:S(2)}) collective-permute-start(f32[2,128,256]{2,1,0:T(8,128)S(1)} %maximum_select_fusion.9), channel_id=1, source_target_pairs={{0,2},{2,0},{4,6},{6,4},{8,10},{10,8},{12,14},{14,12},{1,3},{3,1},... | collective-permute-start | bytes 786440 | tf_op jit(solution)/shard_map/ppermute | solution.py:178
  103.9 7.3 %collective-permute-start.15 = (f32[2,128,256]{2,1,0:T(8,128)S(1)}, f32[2,128,256]{2,1,0:T(8,128)S(1)}, u32[]{:S(2)}, u32[]{:S(2)}) collective-permute-start(f32[2,128,256]{2,1,0:T(8,128)S(1)} %maximum_select_fusion.7), channel_id=1, source_target_pairs={{0,4},{2,6},{4,0},{6,2},{8,12},{10,14},{12,8},{14,10},{1,5},{3,7},... | collective-permute-start | bytes 786440 | tf_op jit(solution)/shard_map/ppermute | solution.py:178
  104.1 9.6 %collective-permute-start.11 = (f32[2,128,256]{1,2,0:T(8,128)S(1)}, f32[2,128,256]{1,2,0:T(8,128)S(1)}, u32[]{:S(2)}, u32[]{:S(2)}) collective-permute-start(f32[2,128,256]{1,2,0:T(8,128)S(1)} %fusion.29), channel_id=1, source_target_pairs={{0,2},{2,0},{4,6},{6,4},{8,10},{10,8},{12,14},{14,12},{1,3},{3,1},... | collective-permute-start | bytes 786440 | tf_op jit(solution)/shard_map/ppermute | solution.py:178
  108.1 18.9 %collective-permute-start.19 = (f32[2,2,128,256]{3,2,0,1:T(8,128)S(1)}, f32[2,2,128,256]{3,2,0,1:T(8,128)S(1)}, u32[]{:S(2)}, u32[]{:S(2)}) collective-permute-start(f32[2,2,128,256]{3,2,0,1:T(8,128)S(1)} %maximum_select_fusion.6), channel_id=1, source_target_pairs={{0,4},{2,6},{4,0},{6,2},{8,12},{10,14},{12,8},{14,10},{1,5},{3,7},... | collective-permute-start | bytes 1572872 | tf_op jit(solution)/shard_map/ppermute | solution.py:178
  111.2 16.0 %collective-permute-start.16 = (f32[2,2,128,256]{3,2,0,1:T(8,128)S(1)}, f32[2,2,128,256]{3,2,0,1:T(8,128)S(1)}, u32[]{:S(2)}, u32[]{:S(2)}) collective-permute-start(f32[2,2,128,256]{3,2,0,1:T(8,128)S(1)} %maximum_select_fusion.4), channel_id=1, source_target_pairs={{0,2},{2,0},{4,6},{6,4},{8,10},{10,8},{12,14},{14,12},{1,3},{3,1},... | collective-permute-start | bytes 1572872 | tf_op jit(solution)/shard_map/ppermute | solution.py:178
  113.7 13.1 %collective-permute-start.12 = (f32[2,128,256]{1,2,0:T(8,128)S(1)}, f32[2,128,256]{1,2,0:T(8,128)S(1)}, u32[]{:S(2)}, u32[]{:S(2)}) collective-permute-start(f32[2,128,256]{1,2,0:T(8,128)S(1)} %fusion.35), channel_id=1, source_target_pairs={{0,4},{2,6},{4,0},{6,2},{8,12},{10,14},{12,8},{14,10},{1,5},{3,7},... | collective-permute-start | bytes 786440 | tf_op jit(solution)/shard_map/ppermute | solution.py:178
  126.9 14.8 %collective-permute-start.13 = (f32[2,128,256]{1,2,0:T(8,128)S(1)}, f32[2,128,256]{1,2,0:T(8,128)S(1)}, u32[]{:S(2)}, u32[]{:S(2)}) collective-permute-start(f32[2,128,256]{1,2,0:T(8,128)S(1)} %add.112), channel_id=1, source_target_pairs={{0,8},{2,10},{4,12},{6,14},{8,0},{10,2},{12,4},{14,6},{1,9},{3,11}... | collective-permute-start | bytes 786440 | tf_op jit(solution)/shard_map/ppermute | solution.py:178
  169.3 3.3 %collective-permute-start.20 = (f32[128,2048]{1,0:T(8,128)}, f32[128,2048]{1,0:T(8,128)}, u32[]{:S(2)}, u32[]{:S(2)}) collective-permute-start(f32[128,2048]{1,0:T(8,128)} %slice_bitcast_fusion), channel_id=1, source_target_pairs={{0,16},{16,0},{1,17},{17,1},{2,18},{18,2},{3,19},{19,3},{4,20},{20... | collective-permute-start | bytes 3145736 | tf_op jit(solution)/shard_map/ppermute | solution.py:178
  (4 other events, 11.1 us)

commit v13 on v7

--- a/solution.py
+++ b/solution.py
@@ -310,7 +310,10 @@
     grad_full = gather_axis(grad_pre, "feat", 1)
     self_part = jnp.einsum("rk,rh->kh", x_cand, grad_full, precision=HIGHEST)
     neigh_part = jnp.einsum("rk,rh->kh", aggregated, grad_full, precision=HIGHEST)
-    grad_w_pair = butterfly_sum(jnp.stack([self_part, neigh_part]), ("cand", "test"))
+    grad_w_stack = butterfly_sum(jnp.stack([self_part, neigh_part]), ("cand",))
+    grad_w_rows = grad_w_stack.reshape(-1, grad_w_stack.shape[-1] // 2)
+    grad_w_rows = doubling_gather(halving_scatter(grad_w_rows, "test"), "test")
+    grad_w_pair = grad_w_rows.reshape(grad_w_stack.shape)
     root_count = math.sqrt(x_cand.shape[0] * cand_count * test_count)
     grad_x_cand = jnp.dot(grad_full, self_rows.T, precision=HIGHEST)
     grad_agg = jnp.dot(grad_full, neigh_rows.T, precision=HIGHEST)

time: 172 us -> 181 us (1.052)
  starting transfers between devices: 20.6 us -> 29.4 us
  other arithmetic: 11.9 us -> 17.5 us
  waiting for transfers between devices: 75.5 us -> 70.6 us
    ppermute x21 -> x30, starting transfers between devices: 20.6 us -> 29.4 us  [exchange(): return lax.ppermute(values, axis, [(i, i ^ 1 << bit) for i in range(count)])]
    select_n x11 -> x21, other arithmetic: 2.19 us -> 7.15 us  [doubling_steps(): jnp.where(first, jnp.stack([data, other], axis=position), jnp.stack([othe...]
    ppermute x21 -> x30, waiting for transfers between devices: 75.5 us -> 70.6 us  [exchange(): return lax.ppermute(values, axis, [(i, i ^ 1 << bit) for i in range(count)])]
    unnamed x17 -> x15, local copies, waits for them, and re-layouts: 3.82 us -> 2.34 us
  transfers between devices with their start and end apart: 21 -> 30, of which waited for: 17 -> 17; matrix products, arithmetic and copies ran while one was open for 4% -> 6% of each run, Pallas kernels for 0% -> 0%
where the time goes in v13:
time: 181 us
  waiting for transfers between devices  70.6 us (39%)
  Pallas kernels  48.9 us (27%)
  starting transfers between devices  29.4 us (16%)
  other arithmetic  17.5 us (10%)
  local copies, waits for them, and re-layouts  6.38 us (4%)
  matrix products  5.81 us (3%)
  between operations  1.9 us (1%)
    ppermute x30, waiting for transfers between devices, exchange(): return lax.ppermute(values, axis, [(i, i ^ 1 << bit) for i in range(count)])  70.6 us
    pallas_call x2, Pallas kernels, slot_pallas(): pl.pallas_call(kernel, grid_spec=grid_spec, out_shape=out_shapes, compile...  48.9 us
    ppermute x30, starting transfers between devices, exchange(): return lax.ppermute(values, axis, [(i, i ^ 1 << bit) for i in range(count)])  29.4 us
    select_n x21, other arithmetic, doubling_steps(): jnp.where(first, jnp.stack([data, other], axis=position), jnp.stack([othe...  7.15 us
  transfers between devices with their start and end apart: 30, of which 17 were waited for; matrix products, arithmetic and copies ran while one was open for 6% of the time, Pallas kernels for 0%

profile of v13, /device:TPU:31, one launch (start us, length us, event | category | flops | bytes accessed | tf_op | source)
XLA Modules:
  0.0 180.5 jit_solution(11059865401756247811)
XLA Ops:
  2.1 1.8 collective-permute-done.1
  3.9 1.7 maximum_select_fusion
  6.0 1.6 pad_maximum_fusion.panel_ref
  7.5 24.8 %shard_map.128 = (f32[4096,128]{1,0:T(8,128)}, s32[32,128,128]{2,1,0:T(8,128)}) custom-call(s32[1]{0:T(128)} %bitcast.live_ref, s32[512]{0:T(512)} %bitcast.191, s32[512]{0:T(512)} %bitcast.193, s32[512,16,128]{2,1,0:T(8,128)} %bitcast.145, bf16[4096,256]{1,0:T(8,128)(2,1)} %pad_maximum_fusion.panel_ref), custom_call_target="tpu_custom_call" | custom-call | tf_op jit(solution)/shard_map/pallas_call | solution.py:131
  32.3 2.4 %reduce_sum.9 = s32[32,128]{1,0:T(8,128)S(1)} reduce(s32[32,128,128]{2,1,0:T(8,128)} %get-tuple-element.10, s32[]{:T(128)} %constant.102.clone.1), dimensions={2}, to_apply=%region_0.1 | reduce | flops 520192 | bytes 2113540 | tf_op jit(solution)/shard_map/reduce_sum | solution.py:147
  37.1 12.4 %collective-permute-done.2 = f32[2,2,264,128]{3,2,1,0:T(8,128)S(1)} collective-permute-done((f32[2,2,264,128]{3,2,1,0:T(8,128)S(1)}, f32[2,2,264,128]{3,2,1,0:T(8,128)S(1)}, u32[]{:S(2)}, u32[]{:S(2)}) %collective-permute-start.2) | collective-permute-done | bytes 540704 | tf_op jit(solution)/shard_map/ppermute | solution.py:172
  51.8 5.6 %collective-permute-done.3 = f32[2,264,128]{2,1,0:T(8,128)S(1)} collective-permute-done((f32[2,264,128]{2,1,0:T(8,128)S(1)}, f32[2,264,128]{2,1,0:T(8,128)S(1)}, u32[]{:S(2)}, u32[]{:S(2)}) %collective-permute-start.3) | collective-permute-done | bytes 270368 | tf_op jit(solution)/shard_map/ppermute | solution.py:172
  57.7 2.4 %collective-permute-start.7 = (f32[264,128]{1,0:T(8,128)S(1)}, f32[264,128]{1,0:T(8,128)S(1)}, u32[]{:S(2)}, u32[]{:S(2)}) collective-permute-start(f32[264,128]{1,0:T(8,128)S(1)} %dynamic-slice_bitcast_fusion.5), channel_id=1, source_target_pairs={{0,8},{2,10},{4,12},{6,14},{8,0},{10,2},{12,4},{14,6},{1,9},{3,11}... | collective-permute-start | bytes 405512 | tf_op jit(solution)/shard_map/ppermute | solution.py:172
  60.1 9.7 %collective-permute-done.4 = f32[264,128]{1,0:T(8,128)S(1)} collective-permute-done((f32[264,128]{1,0:T(8,128)S(1)}, f32[264,128]{1,0:T(8,128)S(1)}, u32[]{:S(2)}, u32[]{:S(2)}) %collective-permute-start.4) | collective-permute-done | bytes 135200 | tf_op jit(solution)/shard_map/ppermute | solution.py:172
  69.8 2.9 %collective-permute-done.7 = f32[264,128]{1,0:T(8,128)S(1)} collective-permute-done((f32[264,128]{1,0:T(8,128)S(1)}, f32[264,128]{1,0:T(8,128)S(1)}, u32[]{:S(2)}, u32[]{:S(2)}) %collective-permute-start.7) | collective-permute-done | bytes 135200 | tf_op jit(solution)/shard_map/ppermute | solution.py:172
  73.1 7.1 %collective-permute-done.8 = f32[512,128]{1,0:T(8,128)S(1)} collective-permute-done((f32[512,128]{1,0:T(8,128)S(1)}, f32[512,128]{1,0:T(8,128)S(1)}, u32[]{:S(2)}, u32[]{:S(2)}) %collective-permute-start.8) | collective-permute-done | bytes 262176 | tf_op jit(solution)/shard_map/ppermute | solution.py:172
  82.4 6.3 %collective-permute-done.9 = f32[512,128]{1,0:T(8,128)S(1)} collective-permute-done((f32[512,128]{1,0:T(8,128)S(1)}, f32[512,128]{1,0:T(8,128)S(1)}, u32[]{:S(2)}, u32[]{:S(2)}) %collective-permute-start.9) | collective-permute-done | bytes 262176 | tf_op jit(solution)/shard_map/ppermute | solution.py:172
  91.6 2.4 %collective-permute-start.26 = (f32[128,256]{1,0:T(8,128)S(1)}, f32[128,256]{1,0:T(8,128)S(1)}, u32[]{:S(2)}, u32[]{:S(2)}) collective-permute-start(f32[128,256]{1,0:T(8,128)S(1)} %get-tuple-element.51), channel_id=1, source_target_pairs={{0,8},{2,10},{4,12},{6,14},{8,0},{10,2},{12,4},{14,6},{1,9},{3,11}... | collective-permute-start | bytes 393224 | tf_op jit(solution)/shard_map/ppermute | solution.py:172
  94.1 2.8 %collective-permute-start.10 = (f32[2,128,256]{1,2,0:T(8,128)S(1)}, f32[2,128,256]{1,2,0:T(8,128)S(1)}, u32[]{:S(2)}, u32[]{:S(2)}) collective-permute-start(f32[2,128,256]{1,2,0:T(8,128)S(1)} %pad_maximum_fusion.6), channel_id=1, source_target_pairs={{0,16},{16,0},{1,17},{17,1},{2,18},{18,2},{3,19},{19,3},{4,20},{20... | collective-permute-start | bytes 786440 | tf_op jit(solution)/shard_map/ppermute | solution.py:172
  99.0 2.0 %collective-permute-done.26 = f32[128,256]{1,0:T(8,128)S(1)} collective-permute-done((f32[128,256]{1,0:T(8,128)S(1)}, f32[128,256]{1,0:T(8,128)S(1)}, u32[]{:S(2)}, u32[]{:S(2)}) %collective-permute-start.26) | collective-permute-done | bytes 131104 | tf_op jit(solution)/shard_map/ppermute | solution.py:172
  103.0 5.7 %collective-permute-done.11 = f32[2,2,32,128]{3,2,1,0:T(8,128)S(1)} collective-permute-done((f32[2,2,32,128]{3,2,1,0:T(8,128)S(1)}, f32[2,2,32,128]{3,2,1,0:T(8,128)S(1)}, u32[]{:S(2)}, u32[]{:S(2)}) %collective-permute-start.11) | collective-permute-done | bytes 65568 | tf_op jit(solution)/shard_map/ppermute | solution.py:172
  109.5 2.1 %collective-permute-done.12 = f32[2,32,128]{2,1,0:T(8,128)S(1)} collective-permute-done((f32[2,32,128]{2,1,0:T(8,128)S(1)}, f32[2,32,128]{2,1,0:T(8,128)S(1)}, u32[]{:S(2)}, u32[]{:S(2)}) %collective-permute-start.12) | collective-permute-done | bytes 32800 | tf_op jit(solution)/shard_map/ppermute | solution.py:172
  111.7 2.4 %collective-permute-start.19 = (f32[32,128]{1,0:T(8,128)S(1)}, f32[32,128]{1,0:T(8,128)S(1)}, u32[]{:S(2)}, u32[]{:S(2)}) collective-permute-start(f32[32,128]{1,0:T(8,128)S(1)} %dynamic-slice_bitcast_fusion.11), channel_id=1, source_target_pairs={{0,8},{2,10},{4,12},{6,14},{8,0},{10,2},{12,4},{14,6},{1,9},{3,11}... | collective-permute-start | bytes 49160 | tf_op jit(solution)/shard_map/ppermute | solution.py:172
  115.3 2.3 %collective-permute-start.20 = (f32[32,128]{1,0:T(8,128)S(1)}, f32[32,128]{1,0:T(8,128)S(1)}, u32[]{:S(2)}, u32[]{:S(2)}) collective-permute-start(f32[32,128]{1,0:T(8,128)S(1)} %bitcast_add_fusion.11), channel_id=1, source_target_pairs={{0,8},{2,10},{4,12},{6,14},{8,0},{10,2},{12,4},{14,6},{1,9},{3,11}... | collective-permute-start | bytes 49160 | tf_op jit(solution)/shard_map/ppermute | solution.py:172
  123.5 6.8 %collective-permute-done.15 = f32[2,32,128]{2,1,0:T(8,128)S(1)} collective-permute-done((f32[2,32,128]{2,1,0:T(8,128)S(1)}, f32[2,32,128]{2,1,0:T(8,128)S(1)}, u32[]{:S(2)}, u32[]{:S(2)}) %collective-permute-start.15) | collective-permute-done | bytes 32800 | tf_op jit(solution)/shard_map/ppermute | solution.py:172
  131.3 3.3 %collective-permute-done.16 = f32[2,2,32,128]{3,2,0,1:T(8,128)S(1)} collective-permute-done((f32[2,2,32,128]{3,2,0,1:T(8,128)S(1)}, f32[2,2,32,128]{3,2,0,1:T(8,128)S(1)}, u32[]{:S(2)}, u32[]{:S(2)}) %collective-permute-start.16) | collective-permute-done | bytes 65568 | tf_op jit(solution)/shard_map/ppermute | solution.py:172
  140.7 24.1 %shard_map.129 = f32[2,128,2048]{2,1,0:T(8,128)} custom-call(s32[1]{0:T(128)} %bitcast.live_ref, s32[512]{0:T(512)} %bitcast.192, s32[512]{0:T(512)} %bitcast.194, s32[512,16,128]{2,1,0:T(8,128)} %bitcast.146, bf16[8,256,512]{2,1,0:T(8,128)(2,1)} %pad_maximum_fusion.2.lifted_ref), custom_call_target="tpu_custom_call" | custom-call | tf_op jit(solution)/shard_map/pallas_call | solution.py:131
  164.8 2.4 %dynamic-slice_bitcast_fusion = f32[128,2048]{1,0:T(8,128)} fusion(f32[2,128,2048]{2,1,0:T(8,128)} %shard_map.129, s32[]{:T(128)S(6)} %select_n.371), kind=kLoop, calls=%fused_computation.20 | loop fusion | bytes 2097156 | tf_op jit(solution)/shard_map/jit(dynamic_index_in_dim)/squeeze | solution.py:199
  167.2 8.0 %collective-permute-start.29 = (f32[128,2048]{1,0:T(8,128)}, f32[128,2048]{1,0:T(8,128)}, u32[]{:S(2)}, u32[]{:S(2)}) collective-permute-start(f32[128,2048]{1,0:T(8,128)} %dynamic-slice_bitcast_fusion), channel_id=1, source_target_pairs={{0,16},{16,0},{1,17},{17,1},{2,18},{18,2},{3,19},{19,3},{4,20},{20... | collective-permute-start | bytes 3145736 | tf_op jit(solution)/shard_map/ppermute | solution.py:172
  (138 shorter events, 35.7 us)
Async XLA Ops:
  35.9 13.5 %collective-permute-start.2 = (f32[2,2,264,128]{3,2,1,0:T(8,128)S(1)}, f32[2,2,264,128]{3,2,1,0:T(8,128)S(1)}, u32[]{:S(2)}, u32[]{:S(2)}) collective-permute-start(f32[2,2,264,128]{3,2,1,0:T(8,128)S(1)} %dynamic-slice_bitcast_fusion.2), channel_id=1, source_target_pairs={{0,2},{2,0},{4,6},{6,4},{8,10},{10,8},{12,14},{14,12},{1,3},{3,1},... | collective-permute-start | bytes 1622024 | tf_op jit(solution)/shard_map/ppermute | solution.py:172
  36.8 13.8 %collective-permute-start.5 = (f32[2,2,264,128]{3,2,1,0:T(8,128)}, f32[2,2,264,128]{3,2,1,0:T(8,128)S(1)}, u32[]{:S(2)}, u32[]{:S(2)}) collective-permute-start(f32[2,2,264,128]{3,2,1,0:T(8,128)} %dynamic-slice_bitcast_fusion.1), channel_id=1, source_target_pairs={{0,4},{2,6},{4,0},{6,2},{8,12},{10,14},{12,8},{14,10},{1,5},{3,7},... | collective-permute-start | bytes 1622024 | tf_op jit(solution)/shard_map/ppermute | solution.py:172
  36.8 36.3 %collective-permute-start = (f32[512,128]{1,0:T(8,128)S(1)}, f32[512,128]{1,0:T(8,128)S(1)}, u32[]{:S(2)}, u32[]{:S(2)}) collective-permute-start(f32[512,128]{1,0:T(8,128)S(1)} %copy-done.4), channel_id=1, source_target_pairs={{0,1},{1,0},{2,3},{3,2},{4,5},{5,4},{6,7},{7,6},{8,9},{9,8},{10,11... | collective-permute-start | bytes 786440 | tf_op jit(solution)/shard_map/ppermute | solution.py:172
  50.6 6.9 %collective-permute-start.3 = (f32[2,264,128]{2,1,0:T(8,128)S(1)}, f32[2,264,128]{2,1,0:T(8,128)S(1)}, u32[]{:S(2)}, u32[]{:S(2)}) collective-permute-start(f32[2,264,128]{2,1,0:T(8,128)S(1)} %dynamic-slice_bitcast_fusion.4), channel_id=1, source_target_pairs={{0,4},{2,6},{4,0},{6,2},{8,12},{10,14},{12,8},{14,10},{1,5},{3,7},... | collective-permute-start | bytes 811016 | tf_op jit(solution)/shard_map/ppermute | solution.py:172
  50.8 6.9 %collective-permute-start.6 = (f32[2,264,128]{2,1,0:T(8,128)S(1)}, f32[2,264,128]{2,1,0:T(8,128)S(1)}, u32[]{:S(2)}, u32[]{:S(2)}) collective-permute-start(f32[2,264,128]{2,1,0:T(8,128)S(1)} %dynamic-slice_bitcast_fusion.3), channel_id=1, source_target_pairs={{0,2},{2,0},{4,6},{6,4},{8,10},{10,8},{12,14},{14,12},{1,3},{3,1},... | collective-permute-start | bytes 811016 | tf_op jit(solution)/shard_map/ppermute | solution.py:172
  57.5 12.3 %collective-permute-start.4 = (f32[264,128]{1,0:T(8,128)S(1)}, f32[264,128]{1,0:T(8,128)S(1)}, u32[]{:S(2)}, u32[]{:S(2)}) collective-permute-start(f32[264,128]{1,0:T(8,128)S(1)} %dynamic-slice_bitcast_fusion.6), channel_id=1, source_target_pairs={{0,8},{2,10},{4,12},{6,14},{8,0},{10,2},{12,4},{14,6},{1,9},{3,11}... | collective-permute-start | bytes 405512 | tf_op jit(solution)/shard_map/ppermute | solution.py:172
  57.7 15.0 %collective-permute-start.7 = (f32[264,128]{1,0:T(8,128)S(1)}, f32[264,128]{1,0:T(8,128)S(1)}, u32[]{:S(2)}, u32[]{:S(2)}) collective-permute-start(f32[264,128]{1,0:T(8,128)S(1)} %dynamic-slice_bitcast_fusion.5), channel_id=1, source_target_pairs={{0,8},{2,10},{4,12},{6,14},{8,0},{10,2},{12,4},{14,6},{1,9},{3,11}... | collective-permute-start | bytes 405512 | tf_op jit(solution)/shard_map/ppermute | solution.py:172
  72.9 7.4 %collective-permute-start.8 = (f32[512,128]{1,0:T(8,128)S(1)}, f32[512,128]{1,0:T(8,128)S(1)}, u32[]{:S(2)}, u32[]{:S(2)}) collective-permute-start(f32[512,128]{1,0:T(8,128)S(1)} %fusion.11), channel_id=1, source_target_pairs={{0,1},{1,0},{2,3},{3,2},{4,5},{5,4},{6,7},{7,6},{8,9},{9,8},{10,11... | collective-permute-start | bytes 786440 | tf_op jit(solution)/shard_map/ppermute | solution.py:172
  82.3 6.5 %collective-permute-start.9 = (f32[512,128]{1,0:T(8,128)S(1)}, f32[512,128]{1,0:T(8,128)S(1)}, u32[]{:S(2)}, u32[]{:S(2)}) collective-permute-start(f32[512,128]{1,0:T(8,128)S(1)} %get-tuple-element.55), channel_id=1, source_target_pairs={{0,1},{1,0},{2,3},{3,2},{4,5},{5,4},{6,7},{7,6},{8,9},{9,8},{10,11... | collective-permute-start | bytes 786440 | tf_op jit(solution)/shard_map/ppermute | solution.py:172
  90.5 7.7 %collective-permute-start.23 = (f32[128,256]{1,0:T(8,128)S(1)}, f32[128,256]{1,0:T(8,128)S(1)}, u32[]{:S(2)}, u32[]{:S(2)}) collective-permute-start(f32[128,256]{1,0:T(8,128)S(1)} %get-tuple-element.52), channel_id=1, source_target_pairs={{0,8},{2,10},{4,12},{6,14},{8,0},{10,2},{12,4},{14,6},{1,9},{3,11}... | collective-permute-start | bytes 393224 | tf_op jit(solution)/shard_map/ppermute | solution.py:172
  91.6 9.4 %collective-permute-start.26 = (f32[128,256]{1,0:T(8,128)S(1)}, f32[128,256]{1,0:T(8,128)S(1)}, u32[]{:S(2)}, u32[]{:S(2)}) collective-permute-start(f32[128,256]{1,0:T(8,128)S(1)} %get-tuple-element.51), channel_id=1, source_target_pairs={{0,8},{2,10},{4,12},{6,14},{8,0},{10,2},{12,4},{14,6},{1,9},{3,11}... | collective-permute-start | bytes 393224 | tf_op jit(solution)/shard_map/ppermute | solution.py:172
  94.1 7.7 %collective-permute-start.10 = (f32[2,128,256]{1,2,0:T(8,128)S(1)}, f32[2,128,256]{1,2,0:T(8,128)S(1)}, u32[]{:S(2)}, u32[]{:S(2)}) collective-permute-start(f32[2,128,256]{1,2,0:T(8,128)S(1)} %pad_maximum_fusion.6), channel_id=1, source_target_pairs={{0,16},{16,0},{1,17},{17,1},{2,18},{18,2},{3,19},{19,3},{4,20},{20... | collective-permute-start | bytes 786440 | tf_op jit(solution)/shard_map/ppermute | solution.py:172
  98.9 19.7 %collective-permute-start.24 = (f32[2,128,256]{2,1,0:T(8,128)}, f32[2,128,256]{2,1,0:T(8,128)S(1)}, u32[]{:S(2)}, u32[]{:S(2)}) collective-permute-start(f32[2,128,256]{2,1,0:T(8,128)} %maximum_select_fusion.7), channel_id=1, source_target_pairs={{0,4},{2,6},{4,0},{6,2},{8,12},{10,14},{12,8},{14,10},{1,5},{3,7},... | collective-permute-start | bytes 786440 | tf_op jit(solution)/shard_map/ppermute | solution.py:172
  101.1 19.0 %collective-permute-start.27 = (f32[2,128,256]{2,1,0:T(8,128)S(1)}, f32[2,128,256]{2,1,0:T(8,128)S(1)}, u32[]{:S(2)}, u32[]{:S(2)}) collective-permute-start(f32[2,128,256]{2,1,0:T(8,128)S(1)} %maximum_select_fusion.9), channel_id=1, source_target_pairs={{0,2},{2,0},{4,6},{6,4},{8,10},{10,8},{12,14},{14,12},{1,3},{3,1},... | collective-permute-start | bytes 786440 | tf_op jit(solution)/shard_map/ppermute | solution.py:172
  102.0 6.7 %collective-permute-start.11 = (f32[2,2,32,128]{3,2,1,0:T(8,128)S(1)}, f32[2,2,32,128]{3,2,1,0:T(8,128)S(1)}, u32[]{:S(2)}, u32[]{:S(2)}) collective-permute-start(f32[2,2,32,128]{3,2,1,0:T(8,128)S(1)} %dynamic-slice_bitcast_fusion.8), channel_id=1, source_target_pairs={{0,2},{2,0},{4,6},{6,4},{8,10},{10,8},{12,14},{14,12},{1,3},{3,1},... | collective-permute-start | bytes 196616 | tf_op jit(solution)/shard_map/ppermute | solution.py:172
  103.0 5.8 %collective-permute-start.17 = (f32[2,2,32,128]{3,2,1,0:T(8,128)S(1)}, f32[2,2,32,128]{3,2,1,0:T(8,128)S(1)}, u32[]{:S(2)}, u32[]{:S(2)}) collective-permute-start(f32[2,2,32,128]{3,2,1,0:T(8,128)S(1)} %dynamic-slice_bitcast_fusion.7), channel_id=1, source_target_pairs={{0,4},{2,6},{4,0},{6,2},{8,12},{10,14},{12,8},{14,10},{1,5},{3,7},... | collective-permute-start | bytes 196616 | tf_op jit(solution)/shard_map/ppermute | solution.py:172
  115.3 4.8 %collective-permute-start.20 = (f32[32,128]{1,0:T(8,128)S(1)}, f32[32,128]{1,0:T(8,128)S(1)}, u32[]{:S(2)}, u32[]{:S(2)}) collective-permute-start(f32[32,128]{1,0:T(8,128)S(1)} %bitcast_add_fusion.11), channel_id=1, source_target_pairs={{0,8},{2,10},{4,12},{6,14},{8,0},{10,2},{12,4},{14,6},{1,9},{3,11}... | collective-permute-start | bytes 49160 | tf_op jit(solution)/shard_map/ppermute | solution.py:172
  119.5 16.0 %collective-permute-start.25 = (f32[2,2,128,256]{3,2,0,1:T(8,128)}, f32[2,2,128,256]{3,2,0,1:T(8,128)}, u32[]{:S(2)}, u32[]{:S(2)}) collective-permute-start(f32[2,2,128,256]{3,2,0,1:T(8,128)} %maximum_select_fusion.4), channel_id=1, source_target_pairs={{0,2},{2,0},{4,6},{6,4},{8,10},{10,8},{12,14},{14,12},{1,3},{3,1},... | collective-permute-start | bytes 1572872 | tf_op jit(solution)/shard_map/ppermute | solution.py:172
  121.0 16.0 %collective-permute-start.28 = (f32[2,2,128,256]{3,2,0,1:T(8,128)}, f32[2,2,128,256]{3,2,0,1:T(8,128)}, u32[]{:S(2)}, u32[]{:S(2)}) collective-permute-start(f32[2,2,128,256]{3,2,0,1:T(8,128)} %maximum_select_fusion.6), channel_id=1, source_target_pairs={{0,4},{2,6},{4,0},{6,2},{8,12},{10,14},{12,8},{14,10},{1,5},{3,7},... | collective-permute-start | bytes 1572872 | tf_op jit(solution)/shard_map/ppermute | solution.py:172
  121.1 9.2 %collective-permute-start.15 = (f32[2,32,128]{2,1,0:T(8,128)S(1)}, f32[2,32,128]{2,1,0:T(8,128)S(1)}, u32[]{:S(2)}, u32[]{:S(2)}) collective-permute-start(f32[2,32,128]{2,1,0:T(8,128)S(1)} %maximum_select_fusion.16), channel_id=1, source_target_pairs={{0,4},{2,6},{4,0},{6,2},{8,12},{10,14},{12,8},{14,10},{1,5},{3,7},... | collective-permute-start | bytes 98312 | tf_op jit(solution)/shard_map/ppermute | solution.py:172
  122.5 8.6 %collective-permute-start.21 = (f32[2,32,128]{2,1,0:T(8,128)S(1)}, f32[2,32,128]{2,1,0:T(8,128)S(1)}, u32[]{:S(2)}, u32[]{:S(2)}) collective-permute-start(f32[2,32,128]{2,1,0:T(8,128)S(1)} %maximum_select_fusion.18), channel_id=1, source_target_pairs={{0,2},{2,0},{4,6},{6,4},{8,10},{10,8},{12,14},{14,12},{1,3},{3,1},... | collective-permute-start | bytes 98312 | tf_op jit(solution)/shard_map/ppermute | solution.py:172
  130.3 4.3 %collective-permute-start.16 = (f32[2,2,32,128]{3,2,0,1:T(8,128)S(1)}, f32[2,2,32,128]{3,2,0,1:T(8,128)S(1)}, u32[]{:S(2)}, u32[]{:S(2)}) collective-permute-start(f32[2,2,32,128]{3,2,0,1:T(8,128)S(1)} %maximum_select_fusion.13), channel_id=1, source_target_pairs={{0,2},{2,0},{4,6},{6,4},{8,10},{10,8},{12,14},{14,12},{1,3},{3,1},... | collective-permute-start | bytes 196616 | tf_op jit(solution)/shard_map/ppermute | solution.py:172
  131.1 4.3 %collective-permute-start.22 = (f32[2,2,32,128]{3,2,1,0:T(8,128)S(1)}, f32[2,2,32,128]{3,2,1,0:T(8,128)S(1)}, u32[]{:S(2)}, u32[]{:S(2)}) collective-permute-start(f32[2,2,32,128]{3,2,1,0:T(8,128)S(1)} %maximum_select_fusion.14), channel_id=1, source_target_pairs={{0,4},{2,6},{4,0},{6,2},{8,12},{10,14},{12,8},{14,10},{1,5},{3,7},... | collective-permute-start | bytes 196616 | tf_op jit(solution)/shard_map/ppermute | solution.py:172
  167.2 10.6 %collective-permute-start.29 = (f32[128,2048]{1,0:T(8,128)}, f32[128,2048]{1,0:T(8,128)}, u32[]{:S(2)}, u32[]{:S(2)}) collective-permute-start(f32[128,2048]{1,0:T(8,128)} %dynamic-slice_bitcast_fusion), channel_id=1, source_target_pairs={{0,16},{16,0},{1,17},{17,1},{2,18},{18,2},{3,19},{19,3},{4,20},{20... | collective-permute-start | bytes 3145736 | tf_op jit(solution)/shard_map/ppermute | solution.py:172
  (13 other events, 164.3 us)

commit v14 on v7

--- a/solution.py
+++ b/solution.py
@@ -289,10 +289,19 @@
     half_width = x_cand.shape[1]
     row_blocks = x_cand.shape[0] * test_count // block_edge
     col_blocks = x_test.shape[0] * cand_count // block_edge
-    panel = doubling_gather(x_test, "cand")
+    if cand_count == 2:
+        own_split = split_hi_lo(x_test)
+        other_split = split_hi_lo(exchange(x_test, "cand", 0))
+        first = lax.axis_index("cand") == 0
+        panel_split = jnp.concatenate(
+            [jnp.where(first, own_split, other_split), jnp.where(first, other_split, own_split)],
+            axis=0,
+        )
+    else:
+        panel_split = split_hi_lo(doubling_gather(x_test, "cand"))
     cand_full = gather_axis(x_cand, "feat", 1)
     row_totals, row_counts = block_aggregate(
-        live, block_rows, block_cols, packed_masks, split_hi_lo(panel), row_blocks
+        live, block_rows, block_cols, packed_masks, panel_split, row_blocks
     )
     own_totals, degree = scatter_totals_and_counts(row_totals, row_counts, test_count)
     aggregated = own_totals / (1.0 + degree)[:, None]

time: 172 us -> 171 us (level)
    select_n x11 -> x10, other arithmetic: 2.19 us -> 0.44 us  [doubling_steps(): jnp.where(first, jnp.stack([data, other], axis=position), jnp.stack([othe...]
  transfers between devices with their start and end apart: 21 -> 21, of which waited for: 17 -> 15; matrix products, arithmetic and copies ran while one was open for 4% -> 5% of each run, Pallas kernels for 0% -> 0%
where the time goes in v14:
time: 171 us; the launch traced here: 170 us
  waiting for transfers between devices  74.1 us (43%)
  Pallas kernels  48.8 us (29%)
  starting transfers between devices  20.5 us (12%)
  other arithmetic  11.8 us (7%)
  local copies, waits for them, and re-layouts  7.57 us (4%)
  matrix products  5.81 us (3%)
  between operations  1.76 us (1%)
    ppermute x21, waiting for transfers between devices, exchange(): return lax.ppermute(values, axis, [(i, i ^ 1 << bit) for i in range(count)])  74.1 us
    pallas_call x2, Pallas kernels, slot_pallas(): pl.pallas_call(kernel, grid_spec=grid_spec, out_shape=out_shapes, compile...  48.8 us
    ppermute x21, starting transfers between devices, exchange(): return lax.ppermute(values, axis, [(i, i ^ 1 << bit) for i in range(count)])  20.5 us
    unnamed x17, local copies, waits for them, and re-layouts  3.82 us
  transfers between devices with their start and end apart: 21, of which 15 were waited for; matrix products, arithmetic and copies ran while one was open for 5% of the time, Pallas kernels for 0%

profile of v14, /device:TPU:31, one launch (start us, length us, event | category | flops | bytes accessed | tf_op | source)
XLA Modules:
  0.0 170.3 jit_solution(12635123372040360065)
XLA Ops:
  2.1 1.4 reduce-precision_convert_fusion.2
  4.5 1.5 pad_maximum_fusion.panel_ref
  6.0 24.7 %shard_map.128 = (f32[4096,128]{1,0:T(8,128)}, s32[32,128,128]{2,1,0:T(8,128)}) custom-call(s32[1]{0:T(128)} %bitcast.live_ref, s32[512]{0:T(512)} %bitcast.112, s32[512]{0:T(512)} %bitcast.114, s32[512,16,128]{2,1,0:T(8,128)} %bitcast.90, bf16[4096,256]{1,0:T(8,128)(2,1)} %pad_maximum_fusion.panel_ref), custom_call_target="tpu_custom_call" | custom-call | tf_op jit(solution)/shard_map/pallas_call | solution.py:131
  30.7 2.4 %reduce_sum.9 = s32[32,128]{1,0:T(8,128)S(1)} reduce(s32[32,128,128]{2,1,0:T(8,128)} %get-tuple-element.10, s32[]{:T(128)} %constant.70.clone.1), dimensions={2}, to_apply=%region_0.1 | reduce | flops 520192 | bytes 2113540 | tf_op jit(solution)/shard_map/reduce_sum | solution.py:147
  35.5 12.4 %collective-permute-done.2 = f32[2,2,264,128]{3,2,1,0:T(8,128)S(1)} collective-permute-done((f32[2,2,264,128]{3,2,1,0:T(8,128)S(1)}, f32[2,2,264,128]{3,2,1,0:T(8,128)S(1)}, u32[]{:S(2)}, u32[]{:S(2)}) %collective-permute-start.2) | collective-permute-done | bytes 540704 | tf_op jit(solution)/shard_map/ppermute | solution.py:172
  50.2 5.6 %collective-permute-done.3 = f32[2,264,128]{2,1,0:T(8,128)S(1)} collective-permute-done((f32[2,264,128]{2,1,0:T(8,128)S(1)}, f32[2,264,128]{2,1,0:T(8,128)S(1)}, u32[]{:S(2)}, u32[]{:S(2)}) %collective-permute-start.3) | collective-permute-done | bytes 270368 | tf_op jit(solution)/shard_map/ppermute | solution.py:172
  56.1 2.4 %collective-permute-start.7 = (f32[264,128]{1,0:T(8,128)S(1)}, f32[264,128]{1,0:T(8,128)S(1)}, u32[]{:S(2)}, u32[]{:S(2)}) collective-permute-start(f32[264,128]{1,0:T(8,128)S(1)} %dynamic-slice_bitcast_fusion.5), channel_id=1, source_target_pairs={{0,8},{2,10},{4,12},{6,14},{8,0},{10,2},{12,4},{14,6},{1,9},{3,11}... | collective-permute-start | bytes 405512 | tf_op jit(solution)/shard_map/ppermute | solution.py:172
  58.5 9.7 %collective-permute-done.4 = f32[264,128]{1,0:T(8,128)S(1)} collective-permute-done((f32[264,128]{1,0:T(8,128)S(1)}, f32[264,128]{1,0:T(8,128)S(1)}, u32[]{:S(2)}, u32[]{:S(2)}) %collective-permute-start.4) | collective-permute-done | bytes 135200 | tf_op jit(solution)/shard_map/ppermute | solution.py:172
  68.2 2.9 %collective-permute-done.7 = f32[264,128]{1,0:T(8,128)S(1)} collective-permute-done((f32[264,128]{1,0:T(8,128)S(1)}, f32[264,128]{1,0:T(8,128)S(1)}, u32[]{:S(2)}, u32[]{:S(2)}) %collective-permute-start.7) | collective-permute-done | bytes 135200 | tf_op jit(solution)/shard_map/ppermute | solution.py:172
  71.6 7.1 %collective-permute-done.8 = f32[512,128]{1,0:T(8,128)S(1)} collective-permute-done((f32[512,128]{1,0:T(8,128)S(1)}, f32[512,128]{1,0:T(8,128)S(1)}, u32[]{:S(2)}, u32[]{:S(2)}) %collective-permute-start.8) | collective-permute-done | bytes 262176 | tf_op jit(solution)/shard_map/ppermute | solution.py:172
  80.9 6.3 %collective-permute-done.9 = f32[512,128]{1,0:T(8,128)S(1)} collective-permute-done((f32[512,128]{1,0:T(8,128)S(1)}, f32[512,128]{1,0:T(8,128)S(1)}, u32[]{:S(2)}, u32[]{:S(2)}) %collective-permute-start.9) | collective-permute-done | bytes 262176 | tf_op jit(solution)/shard_map/ppermute | solution.py:172
  90.0 2.4 %collective-permute-start.17 = (f32[128,256]{1,0:T(8,128)S(1)}, f32[128,256]{1,0:T(8,128)S(1)}, u32[]{:S(2)}, u32[]{:S(2)}) collective-permute-start(f32[128,256]{1,0:T(8,128)S(1)} %get-tuple-element.55), channel_id=1, source_target_pairs={{0,8},{2,10},{4,12},{6,14},{8,0},{10,2},{12,4},{14,6},{1,9},{3,11}... | collective-permute-start | bytes 393224 | tf_op jit(solution)/shard_map/ppermute | solution.py:172
  92.4 2.8 %collective-permute-start.10 = (f32[2,128,256]{1,2,0:T(8,128)S(1)}, f32[2,128,256]{1,2,0:T(8,128)S(1)}, u32[]{:S(2)}, u32[]{:S(2)}) collective-permute-start(f32[2,128,256]{1,2,0:T(8,128)S(1)} %pad_maximum_fusion.8), channel_id=1, source_target_pairs={{0,16},{16,0},{1,17},{17,1},{2,18},{18,2},{3,19},{19,3},{4,20},{20... | collective-permute-start | bytes 786440 | tf_op jit(solution)/shard_map/ppermute | solution.py:172
  96.7 2.7 %collective-permute-done.17 = f32[128,256]{1,0:T(8,128)S(1)} collective-permute-done((f32[128,256]{1,0:T(8,128)S(1)}, f32[128,256]{1,0:T(8,128)S(1)}, u32[]{:S(2)}, u32[]{:S(2)}) %collective-permute-start.17) | collective-permute-done | bytes 131104 | tf_op jit(solution)/shard_map/ppermute | solution.py:172
  101.2 3.0 %collective-permute-done.15 = f32[2,128,256]{2,1,0:T(8,128)S(1)} collective-permute-done((f32[2,128,256]{2,1,0:T(8,128)S(1)}, f32[2,128,256]{2,1,0:T(8,128)S(1)}, u32[]{:S(2)}, u32[]{:S(2)}) %collective-permute-start.15) | collective-permute-done | bytes 262176 | tf_op jit(solution)/shard_map/ppermute | solution.py:172
  105.7 5.5 %collective-permute-done.11 = f32[2,128,256]{1,2,0:T(8,128)S(1)} collective-permute-done((f32[2,128,256]{1,2,0:T(8,128)S(1)}, f32[2,128,256]{1,2,0:T(8,128)S(1)}, u32[]{:S(2)}, u32[]{:S(2)}) %collective-permute-start.11) | collective-permute-done | bytes 262176 | tf_op jit(solution)/shard_map/ppermute | solution.py:172
  111.5 8.5 %collective-permute-done.12 = f32[2,128,256]{1,2,0:T(8,128)S(1)} collective-permute-done((f32[2,128,256]{1,2,0:T(8,128)S(1)}, f32[2,128,256]{1,2,0:T(8,128)S(1)}, u32[]{:S(2)}, u32[]{:S(2)}) %collective-permute-start.12) | collective-permute-done | bytes 262176 | tf_op jit(solution)/shard_map/ppermute | solution.py:172
  120.1 2.4 %collective-permute-done.16 = f32[2,2,128,256]{3,2,0,1:T(8,128)S(1)} collective-permute-done((f32[2,2,128,256]{3,2,0,1:T(8,128)S(1)}, f32[2,2,128,256]{3,2,0,1:T(8,128)S(1)}, u32[]{:S(2)}, u32[]{:S(2)}) %collective-permute-start.16) | collective-permute-done | bytes 524320 | tf_op jit(solution)/shard_map/ppermute | solution.py:172
  123.2 5.6 %collective-permute-done.13 = f32[2,128,256]{1,2,0:T(8,128)S(1)} collective-permute-done((f32[2,128,256]{1,2,0:T(8,128)S(1)}, f32[2,128,256]{1,2,0:T(8,128)S(1)}, u32[]{:S(2)}, u32[]{:S(2)}) %collective-permute-start.13) | collective-permute-done | bytes 262176 | tf_op jit(solution)/shard_map/ppermute | solution.py:172
  129.2 1.5 pad_maximum_fusion.2.lifted_ref
  130.7 24.1 %shard_map.129 = f32[2,128,2048]{2,1,0:T(8,128)} custom-call(s32[1]{0:T(128)} %bitcast.live_ref, s32[512]{0:T(512)} %bitcast.113, s32[512]{0:T(512)} %bitcast.115, s32[512,16,128]{2,1,0:T(8,128)} %bitcast.91, bf16[8,256,512]{2,1,0:T(8,128)(2,1)} %pad_maximum_fusion.2.lifted_ref), custom_call_target="tpu_custom_call" | custom-call | tf_op jit(solution)/shard_map/pallas_call | solution.py:131
  154.8 2.4 %dynamic-slice_bitcast_fusion = f32[128,2048]{1,0:T(8,128)} fusion(f32[2,128,2048]{2,1,0:T(8,128)} %shard_map.129, s32[]{:T(128)S(6)} %select_n.227), kind=kLoop, calls=%fused_computation.24 | loop fusion | bytes 2097156 | tf_op jit(solution)/shard_map/jit(dynamic_index_in_dim)/squeeze | solution.py:199
  157.3 7.5 %collective-permute-start.20 = (f32[128,2048]{1,0:T(8,128)}, f32[128,2048]{1,0:T(8,128)}, u32[]{:S(2)}, u32[]{:S(2)}) collective-permute-start(f32[128,2048]{1,0:T(8,128)} %dynamic-slice_bitcast_fusion), channel_id=1, source_target_pairs={{0,16},{16,0},{1,17},{17,1},{2,18},{18,2},{3,19},{19,3},{4,20},{20... | collective-permute-start | bytes 3145736 | tf_op jit(solution)/shard_map/ppermute | solution.py:172
  167.6 1.3 fusion.4
  (95 shorter events, 22.5 us)
Async XLA Ops:
  0.6 78.7 %copy-start = (f32[256,256]{1,0:T(8,128)S(1)}, f32[256,256]{1,0:T(8,128)}, u32[]{:S(2)}) copy-start(f32[256,256]{1,0:T(8,128)} %param.11) | copy-start | bytes 786436
  0.6 3.2 %collective-permute-start.1 = (f32[2048,128]{1,0:T(8,128)}, f32[2048,128]{1,0:T(8,128)S(1)}, u32[]{:S(2)}, u32[]{:S(2)}) collective-permute-start(f32[2048,128]{1,0:T(8,128)} %param.9), channel_id=1, source_target_pairs={{0,16},{16,0},{1,17},{17,1},{2,18},{18,2},{3,19},{19,3},{4,20},{20... | collective-permute-start | bytes 3145736 | tf_op jit(solution)/shard_map/ppermute | solution.py:172
  34.3 13.5 %collective-permute-start.2 = (f32[2,2,264,128]{3,2,1,0:T(8,128)S(1)}, f32[2,2,264,128]{3,2,1,0:T(8,128)S(1)}, u32[]{:S(2)}, u32[]{:S(2)}) collective-permute-start(f32[2,2,264,128]{3,2,1,0:T(8,128)S(1)} %dynamic-slice_bitcast_fusion.2), channel_id=1, source_target_pairs={{0,2},{2,0},{4,6},{6,4},{8,10},{10,8},{12,14},{14,12},{1,3},{3,1},... | collective-permute-start | bytes 1622024 | tf_op jit(solution)/shard_map/ppermute | solution.py:172
  35.2 13.8 %collective-permute-start.5 = (f32[2,2,264,128]{3,2,1,0:T(8,128)}, f32[2,2,264,128]{3,2,1,0:T(8,128)S(1)}, u32[]{:S(2)}, u32[]{:S(2)}) collective-permute-start(f32[2,2,264,128]{3,2,1,0:T(8,128)} %dynamic-slice_bitcast_fusion.1), channel_id=1, source_target_pairs={{0,4},{2,6},{4,0},{6,2},{8,12},{10,14},{12,8},{14,10},{1,5},{3,7},... | collective-permute-start | bytes 1622024 | tf_op jit(solution)/shard_map/ppermute | solution.py:172
  35.2 36.3 %collective-permute-start = (f32[512,128]{1,0:T(8,128)S(1)}, f32[512,128]{1,0:T(8,128)S(1)}, u32[]{:S(2)}, u32[]{:S(2)}) collective-permute-start(f32[512,128]{1,0:T(8,128)S(1)} %copy-done.4), channel_id=1, source_target_pairs={{0,1},{1,0},{2,3},{3,2},{4,5},{5,4},{6,7},{7,6},{8,9},{9,8},{10,11... | collective-permute-start | bytes 786440 | tf_op jit(solution)/shard_map/ppermute | solution.py:172
  49.0 6.9 %collective-permute-start.3 = (f32[2,264,128]{2,1,0:T(8,128)S(1)}, f32[2,264,128]{2,1,0:T(8,128)S(1)}, u32[]{:S(2)}, u32[]{:S(2)}) collective-permute-start(f32[2,264,128]{2,1,0:T(8,128)S(1)} %dynamic-slice_bitcast_fusion.4), channel_id=1, source_target_pairs={{0,4},{2,6},{4,0},{6,2},{8,12},{10,14},{12,8},{14,10},{1,5},{3,7},... | collective-permute-start | bytes 811016 | tf_op jit(solution)/shard_map/ppermute | solution.py:172
  49.2 6.9 %collective-permute-start.6 = (f32[2,264,128]{2,1,0:T(8,128)S(1)}, f32[2,264,128]{2,1,0:T(8,128)S(1)}, u32[]{:S(2)}, u32[]{:S(2)}) collective-permute-start(f32[2,264,128]{2,1,0:T(8,128)S(1)} %dynamic-slice_bitcast_fusion.3), channel_id=1, source_target_pairs={{0,2},{2,0},{4,6},{6,4},{8,10},{10,8},{12,14},{14,12},{1,3},{3,1},... | collective-permute-start | bytes 811016 | tf_op jit(solution)/shard_map/ppermute | solution.py:172
  55.9 22.8 %copy-start.5 = (f32[256,256]{1,0:T(8,128)S(1)}, f32[256,256]{1,0:T(8,128)}, u32[]{:S(2)}) copy-start(f32[256,256]{1,0:T(8,128)} %param.12) | copy-start | bytes 786436
  55.9 12.3 %collective-permute-start.4 = (f32[264,128]{1,0:T(8,128)S(1)}, f32[264,128]{1,0:T(8,128)S(1)}, u32[]{:S(2)}, u32[]{:S(2)}) collective-permute-start(f32[264,128]{1,0:T(8,128)S(1)} %dynamic-slice_bitcast_fusion.6), channel_id=1, source_target_pairs={{0,8},{2,10},{4,12},{6,14},{8,0},{10,2},{12,4},{14,6},{1,9},{3,11}... | collective-permute-start | bytes 405512 | tf_op jit(solution)/shard_map/ppermute | solution.py:172
  56.1 23.2 %copy-start.6 = (f32[512,128]{1,0:T(8,128)S(1)}, f32[512,128]{1,0:T(8,128)}, u32[]{:S(2)}) copy-start(f32[512,128]{1,0:T(8,128)} %param.13) | copy-start | bytes 786436
  56.1 15.0 %collective-permute-start.7 = (f32[264,128]{1,0:T(8,128)S(1)}, f32[264,128]{1,0:T(8,128)S(1)}, u32[]{:S(2)}, u32[]{:S(2)}) collective-permute-start(f32[264,128]{1,0:T(8,128)S(1)} %dynamic-slice_bitcast_fusion.5), channel_id=1, source_target_pairs={{0,8},{2,10},{4,12},{6,14},{8,0},{10,2},{12,4},{14,6},{1,9},{3,11}... | collective-permute-start | bytes 405512 | tf_op jit(solution)/shard_map/ppermute | solution.py:172
  71.3 7.4 %collective-permute-start.8 = (f32[512,128]{1,0:T(8,128)S(1)}, f32[512,128]{1,0:T(8,128)S(1)}, u32[]{:S(2)}, u32[]{:S(2)}) collective-permute-start(f32[512,128]{1,0:T(8,128)S(1)} %fusion.12), channel_id=1, source_target_pairs={{0,1},{1,0},{2,3},{3,2},{4,5},{5,4},{6,7},{7,6},{8,9},{9,8},{10,11... | collective-permute-start | bytes 786440 | tf_op jit(solution)/shard_map/ppermute | solution.py:172
  80.7 6.5 %collective-permute-start.9 = (f32[512,128]{1,0:T(8,128)S(1)}, f32[512,128]{1,0:T(8,128)S(1)}, u32[]{:S(2)}, u32[]{:S(2)}) collective-permute-start(f32[512,128]{1,0:T(8,128)S(1)} %get-tuple-element.57), channel_id=1, source_target_pairs={{0,1},{1,0},{2,3},{3,2},{4,5},{5,4},{6,7},{7,6},{8,9},{9,8},{10,11... | collective-permute-start | bytes 786440 | tf_op jit(solution)/shard_map/ppermute | solution.py:172
  88.9 7.7 %collective-permute-start.14 = (f32[128,256]{1,0:T(8,128)S(1)}, f32[128,256]{1,0:T(8,128)S(1)}, u32[]{:S(2)}, u32[]{:S(2)}) collective-permute-start(f32[128,256]{1,0:T(8,128)S(1)} %get-tuple-element.56), channel_id=1, source_target_pairs={{0,8},{2,10},{4,12},{6,14},{8,0},{10,2},{12,4},{14,6},{1,9},{3,11}... | collective-permute-start | bytes 393224 | tf_op jit(solution)/shard_map/ppermute | solution.py:172
  90.0 9.4 %collective-permute-start.17 = (f32[128,256]{1,0:T(8,128)S(1)}, f32[128,256]{1,0:T(8,128)S(1)}, u32[]{:S(2)}, u32[]{:S(2)}) collective-permute-start(f32[128,256]{1,0:T(8,128)S(1)} %get-tuple-element.55), channel_id=1, source_target_pairs={{0,8},{2,10},{4,12},{6,14},{8,0},{10,2},{12,4},{14,6},{1,9},{3,11}... | collective-permute-start | bytes 393224 | tf_op jit(solution)/shard_map/ppermute | solution.py:172
  92.4 7.7 %collective-permute-start.10 = (f32[2,128,256]{1,2,0:T(8,128)S(1)}, f32[2,128,256]{1,2,0:T(8,128)S(1)}, u32[]{:S(2)}, u32[]{:S(2)}) collective-permute-start(f32[2,128,256]{1,2,0:T(8,128)S(1)} %pad_maximum_fusion.8), channel_id=1, source_target_pairs={{0,16},{16,0},{1,17},{17,1},{2,18},{18,2},{3,19},{19,3},{4,20},{20... | collective-permute-start | bytes 786440 | tf_op jit(solution)/shard_map/ppermute | solution.py:172
  96.6 7.6 %collective-permute-start.15 = (f32[2,128,256]{2,1,0:T(8,128)S(1)}, f32[2,128,256]{2,1,0:T(8,128)S(1)}, u32[]{:S(2)}, u32[]{:S(2)}) collective-permute-start(f32[2,128,256]{2,1,0:T(8,128)S(1)} %maximum_select_fusion.6), channel_id=1, source_target_pairs={{0,4},{2,6},{4,0},{6,2},{8,12},{10,14},{12,8},{14,10},{1,5},{3,7},... | collective-permute-start | bytes 786440 | tf_op jit(solution)/shard_map/ppermute | solution.py:172
  99.4 6.2 %collective-permute-start.18 = (f32[2,128,256]{2,1,0:T(8,128)S(1)}, f32[2,128,256]{2,1,0:T(8,128)S(1)}, u32[]{:S(2)}, u32[]{:S(2)}) collective-permute-start(f32[2,128,256]{2,1,0:T(8,128)S(1)} %maximum_select_fusion.8), channel_id=1, source_target_pairs={{0,2},{2,0},{4,6},{6,4},{8,10},{10,8},{12,14},{14,12},{1,3},{3,1},... | collective-permute-start | bytes 786440 | tf_op jit(solution)/shard_map/ppermute | solution.py:172
  100.2 11.0 %collective-permute-start.11 = (f32[2,128,256]{1,2,0:T(8,128)S(1)}, f32[2,128,256]{1,2,0:T(8,128)S(1)}, u32[]{:S(2)}, u32[]{:S(2)}) collective-permute-start(f32[2,128,256]{1,2,0:T(8,128)S(1)} %fusion.31), channel_id=1, source_target_pairs={{0,2},{2,0},{4,6},{6,4},{8,10},{10,8},{12,14},{14,12},{1,3},{3,1},... | collective-permute-start | bytes 786440 | tf_op jit(solution)/shard_map/ppermute | solution.py:172
  104.2 18.2 %collective-permute-start.16 = (f32[2,2,128,256]{3,2,0,1:T(8,128)S(1)}, f32[2,2,128,256]{3,2,0,1:T(8,128)S(1)}, u32[]{:S(2)}, u32[]{:S(2)}) collective-permute-start(f32[2,2,128,256]{3,2,0,1:T(8,128)S(1)} %maximum_select_fusion.3), channel_id=1, source_target_pairs={{0,2},{2,0},{4,6},{6,4},{8,10},{10,8},{12,14},{14,12},{1,3},{3,1},... | collective-permute-start | bytes 1572872 | tf_op jit(solution)/shard_map/ppermute | solution.py:172
  105.6 17.0 %collective-permute-start.19 = (f32[2,2,128,256]{3,2,0,1:T(8,128)S(1)}, f32[2,2,128,256]{3,2,0,1:T(8,128)S(1)}, u32[]{:S(2)}, u32[]{:S(2)}) collective-permute-start(f32[2,2,128,256]{3,2,0,1:T(8,128)S(1)} %maximum_select_fusion.5), channel_id=1, source_target_pairs={{0,4},{2,6},{4,0},{6,2},{8,12},{10,14},{12,8},{14,10},{1,5},{3,7},... | collective-permute-start | bytes 1572872 | tf_op jit(solution)/shard_map/ppermute | solution.py:172
  111.3 8.7 %collective-permute-start.12 = (f32[2,128,256]{1,2,0:T(8,128)S(1)}, f32[2,128,256]{1,2,0:T(8,128)S(1)}, u32[]{:S(2)}, u32[]{:S(2)}) collective-permute-start(f32[2,128,256]{1,2,0:T(8,128)S(1)} %fusion.37), channel_id=1, source_target_pairs={{0,4},{2,6},{4,0},{6,2},{8,12},{10,14},{12,8},{14,10},{1,5},{3,7},... | collective-permute-start | bytes 786440 | tf_op jit(solution)/shard_map/ppermute | solution.py:172
  120.0 8.8 %collective-permute-start.13 = (f32[2,128,256]{1,2,0:T(8,128)S(1)}, f32[2,128,256]{1,2,0:T(8,128)S(1)}, u32[]{:S(2)}, u32[]{:S(2)}) collective-permute-start(f32[2,128,256]{1,2,0:T(8,128)S(1)} %add.120), channel_id=1, source_target_pairs={{0,8},{2,10},{4,12},{6,14},{8,0},{10,2},{12,4},{14,6},{1,9},{3,11}... | collective-permute-start | bytes 786440 | tf_op jit(solution)/shard_map/ppermute | solution.py:172
  157.3 10.3 %collective-permute-start.20 = (f32[128,2048]{1,0:T(8,128)}, f32[128,2048]{1,0:T(8,128)}, u32[]{:S(2)}, u32[]{:S(2)}) collective-permute-start(f32[128,2048]{1,0:T(8,128)} %dynamic-slice_bitcast_fusion), channel_id=1, source_target_pairs={{0,16},{16,0},{1,17},{17,1},{2,18},{18,2},{3,19},{19,3},{4,20},{20... | collective-permute-start | bytes 3145736 | tf_op jit(solution)/shard_map/ppermute | solution.py:172
  (4 other events, 18.1 us)

commit v15 on v14

--- a/solution.py
+++ b/solution.py
@@ -149,9 +149,8 @@
 
 def block_transpose(live, block_rows, block_cols, packed_masks, lifted_chunks, cand_count):
     edge = packed_masks.shape[-1]
-    high = lax.reduce_precision(lifted_chunks, exponent_bits=8, mantissa_bits=7)
-    split_t = jnp.concatenate([high, lifted_chunks - high], axis=1).astype(jnp.bfloat16)
-    width = lifted_chunks.shape[1]
+    split_t = lifted_chunks
+    width = lifted_chunks.shape[1] // 2
     panel_cols = lifted_chunks.shape[0] * lifted_chunks.shape[2]
     out_shape = jax.ShapeDtypeStruct((cand_count, width, panel_cols // cand_count), jnp.float32)
     (out_t,) = slot_pallas(
@@ -201,13 +200,15 @@
     return data
 
 
-def doubling_steps(values, axis, order):
+def doubling_steps(values, axis, order, finish=None):
     data = values
     present = []
-    for bit in order:
+    for step, bit in enumerate(order):
         position = sum(1 for other in present if other > bit)
         present.insert(position, bit)
         other = exchange(data, axis, bit)
+        if finish is not None and step == len(order) - 1:
+            data, other = finish(data), finish(other)
         first = axis_bit(axis, bit) == 0
         data = jnp.where(
             first, jnp.stack([data, other], axis=position), jnp.stack([other, data], axis=position)
@@ -245,10 +246,17 @@
     return stacked.reshape((-1,) + values.shape[1:])
 
 
+def split_rows(values):
+    high = lax.reduce_precision(values, exponent_bits=8, mantissa_bits=7)
+    return jnp.concatenate([high, values - high], axis=-2).astype(jnp.bfloat16)
+
+
 def doubling_gather_lanes(values, axis):
     orders = [list(reversed(order)) for order in bit_orders(axis)]
     pieces = jnp.split(values, len(orders), axis=1)
-    results = [doubling_steps(piece, axis, order) for piece, order in zip(pieces, orders)]
+    results = [
+        doubling_steps(piece, axis, order, split_rows) for piece, order in zip(pieces, orders)
+    ]
     return jnp.concatenate(
         [result.reshape((-1,) + result.shape[-2:]) for result in results], axis=2
     )

time: 171 us -> 171 us (level)
  starting transfers between devices: 20.5 us -> 22.4 us
    ppermute x21, starting transfers between devices: 20.5 us -> 22.4 us  [exchange(): return lax.ppermute(values, axis, [(i, i ^ 1 << bit) for i in range(count)])]
  transfers between devices with their start and end apart: 21 -> 21, of which waited for: 15 -> 16; matrix products, arithmetic and copies ran while one was open for 5% -> 6% of each run, Pallas kernels for 0% -> 0%
where the time goes in v15:
time: 171 us; the launch traced here: 170 us
  waiting for transfers between devices  72.6 us (42%)
  Pallas kernels  48.9 us (29%)
  starting transfers between devices  22.4 us (13%)
  other arithmetic  11.5 us (7%)
  local copies, waits for them, and re-layouts  7.53 us (4%)
  matrix products  5.81 us (3%)
    ppermute x21, waiting for transfers between devices, exchange(): return lax.ppermute(values, axis, [(i, i ^ 1 << bit) for i in range(count)])  72.6 us
    pallas_call x2, Pallas kernels, slot_pallas(): pl.pallas_call(kernel, grid_spec=grid_spec, out_shape=out_shapes, compile...  48.9 us
    ppermute x21, starting transfers between devices, exchange(): return lax.ppermute(values, axis, [(i, i ^ 1 << bit) for i in range(count)])  22.4 us
    unnamed x17, local copies, waits for them, and re-layouts  3.84 us
  transfers between devices with their start and end apart: 21, of which 16 were waited for; matrix products, arithmetic and copies ran while one was open for 6% of the time, Pallas kernels for 0%

profile of v15, /device:TPU:31, one launch (start us, length us, event | category | flops | bytes accessed | tf_op | source)
XLA Modules:
  0.0 170.4 jit_solution(4033540261147652781)
XLA Ops:
  2.1 1.4 reduce-precision_convert_fusion.1
  4.5 1.5 pad_maximum_fusion.panel_ref
  6.0 24.7 %shard_map.128 = (f32[4096,128]{1,0:T(8,128)}, s32[32,128,128]{2,1,0:T(8,128)}) custom-call(s32[1]{0:T(128)} %bitcast.live_ref, s32[512]{0:T(512)} %bitcast.110, s32[512]{0:T(512)} %bitcast.112, s32[512,16,128]{2,1,0:T(8,128)} %bitcast.94, bf16[4096,256]{1,0:T(8,128)(2,1)} %pad_maximum_fusion.panel_ref), custom_call_target="tpu_custom_call" | custom-call | tf_op jit(solution)/shard_map/pallas_call | solution.py:131
  30.8 2.4 %reduce_sum.9 = s32[32,128]{1,0:T(8,128)S(1)} reduce(s32[32,128,128]{2,1,0:T(8,128)} %get-tuple-element.10, s32[]{:T(128)} %constant.70.clone.1), dimensions={2}, to_apply=%region_0.1 | reduce | flops 520192 | bytes 2113540 | tf_op jit(solution)/shard_map/reduce_sum | solution.py:147
  35.7 12.1 %collective-permute-done.2 = f32[2,2,264,128]{3,2,1,0:T(8,128)S(1)} collective-permute-done((f32[2,2,264,128]{3,2,1,0:T(8,128)S(1)}, f32[2,2,264,128]{3,2,1,0:T(8,128)S(1)}, u32[]{:S(2)}, u32[]{:S(2)}) %collective-permute-start.2) | collective-permute-done | bytes 540704 | tf_op jit(solution)/shard_map/ppermute | solution.py:171
  50.3 5.6 %collective-permute-done.3 = f32[2,264,128]{2,1,0:T(8,128)S(1)} collective-permute-done((f32[2,264,128]{2,1,0:T(8,128)S(1)}, f32[2,264,128]{2,1,0:T(8,128)S(1)}, u32[]{:S(2)}, u32[]{:S(2)}) %collective-permute-start.3) | collective-permute-done | bytes 270368 | tf_op jit(solution)/shard_map/ppermute | solution.py:171
  56.6 1.9 %collective-permute-start.7 = (f32[264,128]{1,0:T(8,128)S(1)}, f32[264,128]{1,0:T(8,128)S(1)}, u32[]{:S(2)}, u32[]{:S(2)}) collective-permute-start(f32[264,128]{1,0:T(8,128)S(1)} %dynamic-slice_bitcast_fusion.5), channel_id=1, source_target_pairs={{0,8},{2,10},{4,12},{6,14},{8,0},{10,2},{12,4},{14,6},{1,9},{3,11}... | collective-permute-start | bytes 405512 | tf_op jit(solution)/shard_map/ppermute | solution.py:171
  58.5 9.7 %collective-permute-done.4 = f32[264,128]{1,0:T(8,128)S(1)} collective-permute-done((f32[264,128]{1,0:T(8,128)S(1)}, f32[264,128]{1,0:T(8,128)S(1)}, u32[]{:S(2)}, u32[]{:S(2)}) %collective-permute-start.4) | collective-permute-done | bytes 135200 | tf_op jit(solution)/shard_map/ppermute | solution.py:171
  68.2 2.9 %collective-permute-done.7 = f32[264,128]{1,0:T(8,128)S(1)} collective-permute-done((f32[264,128]{1,0:T(8,128)S(1)}, f32[264,128]{1,0:T(8,128)S(1)}, u32[]{:S(2)}, u32[]{:S(2)}) %collective-permute-start.7) | collective-permute-done | bytes 135200 | tf_op jit(solution)/shard_map/ppermute | solution.py:171
  71.6 7.1 %collective-permute-done.8 = f32[512,128]{1,0:T(8,128)S(1)} collective-permute-done((f32[512,128]{1,0:T(8,128)S(1)}, f32[512,128]{1,0:T(8,128)S(1)}, u32[]{:S(2)}, u32[]{:S(2)}) %collective-permute-start.8) | collective-permute-done | bytes 262176 | tf_op jit(solution)/shard_map/ppermute | solution.py:171
  80.9 6.3 %collective-permute-done.9 = f32[512,128]{1,0:T(8,128)S(1)} collective-permute-done((f32[512,128]{1,0:T(8,128)S(1)}, f32[512,128]{1,0:T(8,128)S(1)}, u32[]{:S(2)}, u32[]{:S(2)}) %collective-permute-start.9) | collective-permute-done | bytes 262176 | tf_op jit(solution)/shard_map/ppermute | solution.py:171
  90.1 2.4 %collective-permute-start.17 = (f32[128,256]{1,0:T(8,128)S(1)}, f32[128,256]{1,0:T(8,128)S(1)}, u32[]{:S(2)}, u32[]{:S(2)}) collective-permute-start(f32[128,256]{1,0:T(8,128)S(1)} %get-tuple-element.61), channel_id=1, source_target_pairs={{0,8},{2,10},{4,12},{6,14},{8,0},{10,2},{12,4},{14,6},{1,9},{3,11}... | collective-permute-start | bytes 393224 | tf_op jit(solution)/shard_map/ppermute | solution.py:171
  92.5 2.8 %collective-permute-start.10 = (f32[2,128,256]{1,2,0:T(8,128)S(1)}, f32[2,128,256]{1,2,0:T(8,128)S(1)}, u32[]{:S(2)}, u32[]{:S(2)}) collective-permute-start(f32[2,128,256]{1,2,0:T(8,128)S(1)} %pad_maximum_fusion.7), channel_id=1, source_target_pairs={{0,16},{16,0},{1,17},{17,1},{2,18},{18,2},{3,19},{19,3},{4,20},{20... | collective-permute-start | bytes 786440 | tf_op jit(solution)/shard_map/ppermute | solution.py:171
  96.8 2.7 %collective-permute-done.17 = f32[128,256]{1,0:T(8,128)S(1)} collective-permute-done((f32[128,256]{1,0:T(8,128)S(1)}, f32[128,256]{1,0:T(8,128)S(1)}, u32[]{:S(2)}, u32[]{:S(2)}) %collective-permute-start.17) | collective-permute-done | bytes 131104 | tf_op jit(solution)/shard_map/ppermute | solution.py:171
  101.2 3.1 %collective-permute-done.15 = f32[2,128,256]{2,1,0:T(8,128)S(1)} collective-permute-done((f32[2,128,256]{2,1,0:T(8,128)S(1)}, f32[2,128,256]{2,1,0:T(8,128)S(1)}, u32[]{:S(2)}, u32[]{:S(2)}) %collective-permute-start.15) | collective-permute-done | bytes 262176 | tf_op jit(solution)/shard_map/ppermute | solution.py:171
  105.7 5.6 %collective-permute-done.11 = f32[2,128,256]{1,2,0:T(8,128)S(1)} collective-permute-done((f32[2,128,256]{1,2,0:T(8,128)S(1)}, f32[2,128,256]{1,2,0:T(8,128)S(1)}, u32[]{:S(2)}, u32[]{:S(2)}) %collective-permute-start.11) | collective-permute-done | bytes 262176 | tf_op jit(solution)/shard_map/ppermute | solution.py:171
  111.5 1.5 collective-permute-start.19
  113.1 3.8 %collective-permute-done.12 = f32[2,128,256]{1,2,0:T(8,128)S(1)} collective-permute-done((f32[2,128,256]{1,2,0:T(8,128)S(1)}, f32[2,128,256]{1,2,0:T(8,128)S(1)}, u32[]{:S(2)}, u32[]{:S(2)}) %collective-permute-start.12) | collective-permute-done | bytes 262176 | tf_op jit(solution)/shard_map/ppermute | solution.py:171
  117.0 5.5 %collective-permute-done.16 = f32[2,2,128,256]{3,2,0,1:T(8,128)S(1)} collective-permute-done((f32[2,2,128,256]{3,2,0,1:T(8,128)S(1)}, f32[2,2,128,256]{3,2,0,1:T(8,128)S(1)}, u32[]{:S(2)}, u32[]{:S(2)}) %collective-permute-start.16) | collective-permute-done | bytes 524320 | tf_op jit(solution)/shard_map/ppermute | solution.py:171
  122.8 5.7 %collective-permute-done.19 = f32[2,2,128,256]{3,2,0,1:T(8,128)S(1)} collective-permute-done((f32[2,2,128,256]{3,2,0,1:T(8,128)S(1)}, f32[2,2,128,256]{3,2,0,1:T(8,128)S(1)}, u32[]{:S(2)}, u32[]{:S(2)}) %collective-permute-start.19) | collective-permute-done | bytes 524320 | tf_op jit(solution)/shard_map/ppermute | solution.py:171
  128.9 1.5 pad_maximum_fusion.1.lifted_ref
  130.5 24.1 %shard_map.129 = f32[2,128,2048]{2,1,0:T(8,128)} custom-call(s32[1]{0:T(128)} %bitcast.live_ref, s32[512]{0:T(512)} %bitcast.111, s32[512]{0:T(512)} %bitcast.113, s32[512,16,128]{2,1,0:T(8,128)} %bitcast.95, bf16[8,256,512]{2,1,0:T(8,128)(2,1)} %pad_maximum_fusion.1.lifted_ref), custom_call_target="tpu_custom_call" | custom-call | tf_op jit(solution)/shard_map/pallas_call | solution.py:131
  154.6 2.4 %dynamic-slice_bitcast_fusion = f32[128,2048]{1,0:T(8,128)} fusion(f32[2,128,2048]{2,1,0:T(8,128)} %shard_map.129, s32[]{:T(128)S(6)} %select_n.207), kind=kLoop, calls=%fused_computation.20 | loop fusion | bytes 2097156 | tf_op jit(solution)/shard_map/jit(dynamic_index_in_dim)/squeeze | solution.py:198
  157.0 7.8 %collective-permute-start.20 = (f32[128,2048]{1,0:T(8,128)}, f32[128,2048]{1,0:T(8,128)}, u32[]{:S(2)}, u32[]{:S(2)}) collective-permute-start(f32[128,2048]{1,0:T(8,128)} %dynamic-slice_bitcast_fusion), channel_id=1, source_target_pairs={{0,16},{16,0},{1,17},{17,1},{2,18},{18,2},{3,19},{19,3},{4,20},{20... | collective-permute-start | bytes 3145736 | tf_op jit(solution)/shard_map/ppermute | solution.py:171
  (93 shorter events, 24.0 us)
Async XLA Ops:
  0.6 78.8 %copy-start = (f32[256,256]{1,0:T(8,128)S(1)}, f32[256,256]{1,0:T(8,128)}, u32[]{:S(2)}) copy-start(f32[256,256]{1,0:T(8,128)} %param.11) | copy-start | bytes 786436
  0.6 3.2 %collective-permute-start.1 = (f32[2048,128]{1,0:T(8,128)}, f32[2048,128]{1,0:T(8,128)S(1)}, u32[]{:S(2)}, u32[]{:S(2)}) collective-permute-start(f32[2048,128]{1,0:T(8,128)} %param.9), channel_id=1, source_target_pairs={{0,16},{16,0},{1,17},{17,1},{2,18},{18,2},{3,19},{19,3},{4,20},{20... | collective-permute-start | bytes 3145736 | tf_op jit(solution)/shard_map/ppermute | solution.py:171
  34.4 13.5 %collective-permute-start.2 = (f32[2,2,264,128]{3,2,1,0:T(8,128)S(1)}, f32[2,2,264,128]{3,2,1,0:T(8,128)S(1)}, u32[]{:S(2)}, u32[]{:S(2)}) collective-permute-start(f32[2,2,264,128]{3,2,1,0:T(8,128)S(1)} %dynamic-slice_bitcast_fusion.2), channel_id=1, source_target_pairs={{0,2},{2,0},{4,6},{6,4},{8,10},{10,8},{12,14},{14,12},{1,3},{3,1},... | collective-permute-start | bytes 1622024 | tf_op jit(solution)/shard_map/ppermute | solution.py:171
  35.5 13.9 %collective-permute-start.5 = (f32[2,2,264,128]{3,2,1,0:T(8,128)}, f32[2,2,264,128]{3,2,1,0:T(8,128)S(1)}, u32[]{:S(2)}, u32[]{:S(2)}) collective-permute-start(f32[2,2,264,128]{3,2,1,0:T(8,128)} %dynamic-slice_bitcast_fusion.1), channel_id=1, source_target_pairs={{0,4},{2,6},{4,0},{6,2},{8,12},{10,14},{12,8},{14,10},{1,5},{3,7},... | collective-permute-start | bytes 1622024 | tf_op jit(solution)/shard_map/ppermute | solution.py:171
  35.5 36.1 %collective-permute-start = (f32[512,128]{1,0:T(8,128)S(1)}, f32[512,128]{1,0:T(8,128)S(1)}, u32[]{:S(2)}, u32[]{:S(2)}) collective-permute-start(f32[512,128]{1,0:T(8,128)S(1)} %copy-done.4), channel_id=1, source_target_pairs={{0,1},{1,0},{2,3},{3,2},{4,5},{5,4},{6,7},{7,6},{8,9},{9,8},{10,11... | collective-permute-start | bytes 786440 | tf_op jit(solution)/shard_map/ppermute | solution.py:171
  49.0 6.9 %collective-permute-start.3 = (f32[2,264,128]{2,1,0:T(8,128)S(1)}, f32[2,264,128]{2,1,0:T(8,128)S(1)}, u32[]{:S(2)}, u32[]{:S(2)}) collective-permute-start(f32[2,264,128]{2,1,0:T(8,128)S(1)} %dynamic-slice_bitcast_fusion.4), channel_id=1, source_target_pairs={{0,4},{2,6},{4,0},{6,2},{8,12},{10,14},{12,8},{14,10},{1,5},{3,7},... | collective-permute-start | bytes 811016 | tf_op jit(solution)/shard_map/ppermute | solution.py:171
  49.5 7.1 %collective-permute-start.6 = (f32[2,264,128]{2,1,0:T(8,128)S(1)}, f32[2,264,128]{2,1,0:T(8,128)S(1)}, u32[]{:S(2)}, u32[]{:S(2)}) collective-permute-start(f32[2,264,128]{2,1,0:T(8,128)S(1)} %dynamic-slice_bitcast_fusion.3), channel_id=1, source_target_pairs={{0,2},{2,0},{4,6},{6,4},{8,10},{10,8},{12,14},{14,12},{1,3},{3,1},... | collective-permute-start | bytes 811016 | tf_op jit(solution)/shard_map/ppermute | solution.py:171
  56.0 22.8 %copy-start.5 = (f32[256,256]{1,0:T(8,128)S(1)}, f32[256,256]{1,0:T(8,128)}, u32[]{:S(2)}) copy-start(f32[256,256]{1,0:T(8,128)} %param.12) | copy-start | bytes 786436
  56.0 12.3 %collective-permute-start.4 = (f32[264,128]{1,0:T(8,128)S(1)}, f32[264,128]{1,0:T(8,128)S(1)}, u32[]{:S(2)}, u32[]{:S(2)}) collective-permute-start(f32[264,128]{1,0:T(8,128)S(1)} %dynamic-slice_bitcast_fusion.6), channel_id=1, source_target_pairs={{0,8},{2,10},{4,12},{6,14},{8,0},{10,2},{12,4},{14,6},{1,9},{3,11}... | collective-permute-start | bytes 405512 | tf_op jit(solution)/shard_map/ppermute | solution.py:171
  56.6 22.8 %copy-start.6 = (f32[512,128]{1,0:T(8,128)S(1)}, f32[512,128]{1,0:T(8,128)}, u32[]{:S(2)}) copy-start(f32[512,128]{1,0:T(8,128)} %param.13) | copy-start | bytes 786436
  56.6 14.5 %collective-permute-start.7 = (f32[264,128]{1,0:T(8,128)S(1)}, f32[264,128]{1,0:T(8,128)S(1)}, u32[]{:S(2)}, u32[]{:S(2)}) collective-permute-start(f32[264,128]{1,0:T(8,128)S(1)} %dynamic-slice_bitcast_fusion.5), channel_id=1, source_target_pairs={{0,8},{2,10},{4,12},{6,14},{8,0},{10,2},{12,4},{14,6},{1,9},{3,11}... | collective-permute-start | bytes 405512 | tf_op jit(solution)/shard_map/ppermute | solution.py:171
  71.3 7.4 %collective-permute-start.8 = (f32[512,128]{1,0:T(8,128)S(1)}, f32[512,128]{1,0:T(8,128)S(1)}, u32[]{:S(2)}, u32[]{:S(2)}) collective-permute-start(f32[512,128]{1,0:T(8,128)S(1)} %fusion.23), channel_id=1, source_target_pairs={{0,1},{1,0},{2,3},{3,2},{4,5},{5,4},{6,7},{7,6},{8,9},{9,8},{10,11... | collective-permute-start | bytes 786440 | tf_op jit(solution)/shard_map/ppermute | solution.py:171
  80.7 6.5 %collective-permute-start.9 = (f32[512,128]{1,0:T(8,128)S(1)}, f32[512,128]{1,0:T(8,128)S(1)}, u32[]{:S(2)}, u32[]{:S(2)}) collective-permute-start(f32[512,128]{1,0:T(8,128)S(1)} %get-tuple-element.63), channel_id=1, source_target_pairs={{0,1},{1,0},{2,3},{3,2},{4,5},{5,4},{6,7},{7,6},{8,9},{9,8},{10,11... | collective-permute-start | bytes 786440 | tf_op jit(solution)/shard_map/ppermute | solution.py:171
  89.0 7.7 %collective-permute-start.14 = (f32[128,256]{1,0:T(8,128)S(1)}, f32[128,256]{1,0:T(8,128)S(1)}, u32[]{:S(2)}, u32[]{:S(2)}) collective-permute-start(f32[128,256]{1,0:T(8,128)S(1)} %get-tuple-element.62), channel_id=1, source_target_pairs={{0,8},{2,10},{4,12},{6,14},{8,0},{10,2},{12,4},{14,6},{1,9},{3,11}... | collective-permute-start | bytes 393224 | tf_op jit(solution)/shard_map/ppermute | solution.py:171
  90.1 9.4 %collective-permute-start.17 = (f32[128,256]{1,0:T(8,128)S(1)}, f32[128,256]{1,0:T(8,128)S(1)}, u32[]{:S(2)}, u32[]{:S(2)}) collective-permute-start(f32[128,256]{1,0:T(8,128)S(1)} %get-tuple-element.61), channel_id=1, source_target_pairs={{0,8},{2,10},{4,12},{6,14},{8,0},{10,2},{12,4},{14,6},{1,9},{3,11}... | collective-permute-start | bytes 393224 | tf_op jit(solution)/shard_map/ppermute | solution.py:171
  92.5 8.4 %collective-permute-start.10 = (f32[2,128,256]{1,2,0:T(8,128)S(1)}, f32[2,128,256]{1,2,0:T(8,128)S(1)}, u32[]{:S(2)}, u32[]{:S(2)}) collective-permute-start(f32[2,128,256]{1,2,0:T(8,128)S(1)} %pad_maximum_fusion.7), channel_id=1, source_target_pairs={{0,16},{16,0},{1,17},{17,1},{2,18},{18,2},{3,19},{19,3},{4,20},{20... | collective-permute-start | bytes 786440 | tf_op jit(solution)/shard_map/ppermute | solution.py:171
  96.7 7.6 %collective-permute-start.15 = (f32[2,128,256]{2,1,0:T(8,128)S(1)}, f32[2,128,256]{2,1,0:T(8,128)S(1)}, u32[]{:S(2)}, u32[]{:S(2)}) collective-permute-start(f32[2,128,256]{2,1,0:T(8,128)S(1)} %maximum_select_fusion.4), channel_id=1, source_target_pairs={{0,4},{2,6},{4,0},{6,2},{8,12},{10,14},{12,8},{14,10},{1,5},{3,7},... | collective-permute-start | bytes 786440 | tf_op jit(solution)/shard_map/ppermute | solution.py:171
  99.5 11.9 %collective-permute-start.18 = (f32[2,128,256]{2,1,0:T(8,128)S(1)}, f32[2,128,256]{2,1,0:T(8,128)S(1)}, u32[]{:S(2)}, u32[]{:S(2)}) collective-permute-start(f32[2,128,256]{2,1,0:T(8,128)S(1)} %maximum_select_fusion.6), channel_id=1, source_target_pairs={{0,2},{2,0},{4,6},{6,4},{8,10},{10,8},{12,14},{14,12},{1,3},{3,1},... | collective-permute-start | bytes 786440 | tf_op jit(solution)/shard_map/ppermute | solution.py:171
  100.9 10.4 %collective-permute-start.11 = (f32[2,128,256]{1,2,0:T(8,128)S(1)}, f32[2,128,256]{1,2,0:T(8,128)S(1)}, u32[]{:S(2)}, u32[]{:S(2)}) collective-permute-start(f32[2,128,256]{1,2,0:T(8,128)S(1)} %fusion.42), channel_id=1, source_target_pairs={{0,2},{2,0},{4,6},{6,4},{8,10},{10,8},{12,14},{14,12},{1,3},{3,1},... | collective-permute-start | bytes 786440 | tf_op jit(solution)/shard_map/ppermute | solution.py:171
  104.3 18.2 %collective-permute-start.16 = (f32[2,2,128,256]{3,2,0,1:T(8,128)S(1)}, f32[2,2,128,256]{3,2,0,1:T(8,128)S(1)}, u32[]{:S(2)}, u32[]{:S(2)}) collective-permute-start(f32[2,2,128,256]{3,2,0,1:T(8,128)S(1)} %get-tuple-element.34), channel_id=1, source_target_pairs={{0,2},{2,0},{4,6},{6,4},{8,10},{10,8},{12,14},{14,12},{1,3},{3,1},... | collective-permute-start | bytes 1572872 | tf_op jit(solution)/shard_map/ppermute | solution.py:171
  111.3 5.6 %collective-permute-start.12 = (f32[2,128,256]{1,2,0:T(8,128)S(1)}, f32[2,128,256]{1,2,0:T(8,128)S(1)}, u32[]{:S(2)}, u32[]{:S(2)}) collective-permute-start(f32[2,128,256]{1,2,0:T(8,128)S(1)} %fusion.46), channel_id=1, source_target_pairs={{0,4},{2,6},{4,0},{6,2},{8,12},{10,14},{12,8},{14,10},{1,5},{3,7},... | collective-permute-start | bytes 786440 | tf_op jit(solution)/shard_map/ppermute | solution.py:171
  111.5 17.0 %collective-permute-start.19 = (f32[2,2,128,256]{3,2,0,1:T(8,128)S(1)}, f32[2,2,128,256]{3,2,0,1:T(8,128)S(1)}, u32[]{:S(2)}, u32[]{:S(2)}) collective-permute-start(f32[2,2,128,256]{3,2,0,1:T(8,128)S(1)} %get-tuple-element.36), channel_id=1, source_target_pairs={{0,4},{2,6},{4,0},{6,2},{8,12},{10,14},{12,8},{14,10},{1,5},{3,7},... | collective-permute-start | bytes 1572872 | tf_op jit(solution)/shard_map/ppermute | solution.py:171
  116.9 13.5 %collective-permute-start.13 = (f32[2,128,256]{1,2,0:T(8,128)S(1)}, f32[2,128,256]{1,2,0:T(8,128)S(1)}, u32[]{:S(2)}, u32[]{:S(2)}) collective-permute-start(f32[2,128,256]{1,2,0:T(8,128)S(1)} %add.120), channel_id=1, source_target_pairs={{0,8},{2,10},{4,12},{6,14},{8,0},{10,2},{12,4},{14,6},{1,9},{3,11}... | collective-permute-start | bytes 786440 | tf_op jit(solution)/shard_map/ppermute | solution.py:171
  157.0 10.7 %collective-permute-start.20 = (f32[128,2048]{1,0:T(8,128)}, f32[128,2048]{1,0:T(8,128)}, u32[]{:S(2)}, u32[]{:S(2)}) collective-permute-start(f32[128,2048]{1,0:T(8,128)} %dynamic-slice_bitcast_fusion), channel_id=1, source_target_pairs={{0,16},{16,0},{1,17},{17,1},{2,18},{18,2},{3,19},{19,3},{4,20},{20... | collective-permute-start | bytes 3145736 | tf_op jit(solution)/shard_map/ppermute | solution.py:171
  (4 other events, 18.7 us)

commit v16 on v15

--- a/solution.py
+++ b/solution.py
@@ -99,10 +99,20 @@
             tile = lifted_ref[row // row_chunk, :, pl.ds(row_start, edge)]
             prod = jnp.dot(tile, dense, preferred_element_type=jnp.float32)
             col_start = pl.multiple_of((col % col_chunk) * edge, edge)
-            out_ref[col // col_chunk, :, pl.ds(col_start, edge)] += prod[:half] + prod[half:]
+            chunk = jnp.bitwise_xor(col // col_chunk, live_ref[1])
+            out_ref[chunk, :, pl.ds(col_start, edge)] += prod[:half] + prod[half:]
             return carry
 
         lax.fori_loop(0, group, body, 0, unroll=UNROLL)
+
+
+def backward_pair_kernel(live_ref, rows_ref, cols_ref, masks_ref, lifted_ref, own_ref, other_ref, acc_ref):
+    backward_kernel(live_ref, rows_ref, cols_ref, masks_ref, lifted_ref, acc_ref)
+
+    @pl.when(pl.program_id(0) == pl.num_programs(0) - 1)
+    def _():
+        own_ref[...] = acc_ref[0]
+        other_ref[...] = acc_ref[1]
 
 
 def mask_spec(packed_masks, group):
@@ -148,15 +158,32 @@
 
 
 def block_transpose(live, block_rows, block_cols, packed_masks, lifted_chunks, cand_count):
-    edge = packed_masks.shape[-1]
     split_t = lifted_chunks
     width = lifted_chunks.shape[1] // 2
     panel_cols = lifted_chunks.shape[0] * lifted_chunks.shape[2]
-    out_shape = jax.ShapeDtypeStruct((cand_count, width, panel_cols // cand_count), jnp.float32)
-    (out_t,) = slot_pallas(
-        backward_kernel, live, block_rows, block_cols, packed_masks, split_t, [out_shape]
-    )
-    return out_t
+    acc_shape = (cand_count, width, panel_cols // cand_count)
+    if cand_count != 2:
+        out_shape = jax.ShapeDtypeStruct(acc_shape, jnp.float32)
+        (out_t,) = slot_pallas(
+            backward_kernel, live, block_rows, block_cols, packed_masks, split_t, [out_shape]
+        )
+        return [out_t]
+    slot_total = packed_masks.shape[0]
+    group = min(SLOT_GROUP, slot_total)
+    half_shape = jax.ShapeDtypeStruct(acc_shape[1:], jnp.float32)
+    grid_spec = pltpu.PrefetchScalarGridSpec(
+        num_scalar_prefetch=3,
+        grid=(slot_total // group,),
+        in_specs=[mask_spec(packed_masks, group), whole_spec(split_t.shape)],
+        out_specs=[whole_spec(acc_shape[1:]), whole_spec(acc_shape[1:])],
+        scratch_shapes=[pltpu.VMEM(acc_shape, jnp.float32)],
+    )
+    return pl.pallas_call(
+        backward_pair_kernel,
+        grid_spec=grid_spec,
+        out_shape=[half_shape, half_shape],
+        compiler_params=pltpu.CompilerParams(dimension_semantics=("arbitrary",)),
+    )(live, block_rows, block_cols, packed_masks, split_t)
 
 
 def axis_bits(axis):
@@ -262,6 +289,19 @@
     )
 
 
+def halving_relative(chunks, axis):
+    bits = axis_bits(axis)
+    data = chunks.reshape((2,) * bits + chunks.shape[1:])
+    remaining = list(reversed(range(bits)))
+    for bit in range(bits):
+        position = remaining.index(bit)
+        remaining.remove(bit)
+        keep = lax.index_in_dim(data, 0, position, keepdims=False)
+        send = lax.index_in_dim(data, 1, position, keepdims=False)
+        data = keep + exchange(send, axis, bit)
+    return data
+
+
 def butterfly_sum(values, axes):
     for axis in axes:
         for bit in range(axis_bits(axis)):
@@ -289,7 +329,9 @@
     packed_masks = block_mask.reshape(block_mask.shape[2:])
     block_rows = block_row.reshape(-1)
     block_cols = block_col.reshape(-1)
-    live = jnp.clip(block_live.reshape(1), 0, packed_masks.shape[0])
+    live = jnp.concatenate(
+        [jnp.clip(block_live.reshape(1), 0, packed_masks.shape[0]), lax.axis_index("cand").reshape(1)]
+    ).astype(jnp.int32)
     block_edge = packed_masks.shape[-1]
     cand_count = lax.axis_size("cand")
     test_count = lax.axis_size("test")
@@ -336,8 +378,11 @@
     grad_w_pair, lifted_chunks = lax.optimization_barrier((grad_w_pair, lifted_chunks))
     grad_w_self = grad_w_pair[0] / root_count
     grad_w_neigh = grad_w_pair[1] / root_count
-    out_t = block_transpose(live, block_rows, block_cols, packed_masks, lifted_chunks, cand_count)
-    own_t = halving_scatter(out_t.reshape(-1, out_t.shape[2]), "cand")
+    outs = block_transpose(live, block_rows, block_cols, packed_masks, lifted_chunks, cand_count)
+    if len(outs) == 2:
+        own_t = outs[0] + exchange(outs[1], "cand", 0)
+    else:
+        own_t = halving_relative(outs[0], "cand")
     grad_x_test = own_t.T
     return (output, grad_w_self, grad_w_neigh, grad_x_cand, grad_x_test)
 

time: 171 us -> 169 us (0.988)
  local copies, waits for them, and re-layouts: 7.53 us -> 5.07 us
    pallas_call x0 -> x1, Pallas kernels: none -> 25.2 us  [block_transpose(): pl.pallas_call(backward_pair_kernel, grid_spec=grid_spec, out_shape=[half...]
    pallas_call x2 -> x1, Pallas kernels: 48.9 us -> 24.8 us  [slot_pallas(): pl.pallas_call(kernel, grid_spec=grid_spec, out_shape=out_shapes, compile...]
    squeeze x7 -> x6, local copies, waits for them, and re-layouts: 3.41 us -> 0.97 us  [halving_steps(): send = lax.dynamic_index_in_dim(data, 1 - mine, position, keepdims=False)]
  transfers between devices with their start and end apart: 21 -> 21, of which waited for: 16 -> 15; matrix products, arithmetic and copies ran while one was open for 6% -> 7% of each run, Pallas kernels for 0% -> 0%
where the time goes in v16:
time: 169 us
  waiting for transfers between devices  72.4 us (43%)
  Pallas kernels  50 us (30%)
  starting transfers between devices  22.7 us (13%)
  other arithmetic  10.9 us (6%)
  matrix products  5.82 us (3%)
  local copies, waits for them, and re-layouts  5.07 us (3%)
  between operations  1.71 us (1%)
    ppermute x21, waiting for transfers between devices, exchange(): return lax.ppermute(values, axis, [(i, i ^ 1 << bit) for i in range(count)])  72.4 us
    pallas_call x1, Pallas kernels, block_transpose(): pl.pallas_call(backward_pair_kernel, grid_spec=grid_spec, out_shape=[half...  25.2 us
    pallas_call x1, Pallas kernels, slot_pallas(): pl.pallas_call(kernel, grid_spec=grid_spec, out_shape=out_shapes, compile...  24.8 us
    ppermute x21, starting transfers between devices, exchange(): return lax.ppermute(values, axis, [(i, i ^ 1 << bit) for i in range(count)])  22.7 us
    unnamed x17, local copies, waits for them, and re-layouts  3.83 us
  transfers between devices with their start and end apart: 21, of which 15 were waited for; matrix products, arithmetic and copies ran while one was open for 7% of the time, Pallas kernels for 0%

profile of v16, /device:TPU:31, one launch (start us, length us, event | category | flops | bytes accessed | tf_op | source)
XLA Modules:
  0.0 168.6 jit_solution(3202274011135450179)
XLA Ops:
  2.7 1.4 reduce-precision_convert_fusion.1
  4.8 1.5 pad_maximum_fusion.panel_ref
  6.3 24.8 %shard_map.128 = (f32[4096,128]{1,0:T(8,128)}, s32[32,128,128]{2,1,0:T(8,128)}) custom-call(s32[2]{0:T(128)} %pad_add_fusion.live_ref, s32[512]{0:T(512)} %bitcast.105, s32[512]{0:T(512)} %bitcast.107, s32[512,16,128]{2,1,0:T(8,128)} %bitcast.89, bf16[4096,256]{1,0:T(8,128)(2,1)} %pad_maximum_fusion.panel_ref), custom_call_target="tpu_custom_call" | custom-call | tf_op jit(solution)/shard_map/pallas_call | solution.py:141
  31.0 2.4 %reduce_sum.9 = s32[32,128]{1,0:T(8,128)S(1)} reduce(s32[32,128,128]{2,1,0:T(8,128)} %get-tuple-element.12, s32[]{:T(128)} %constant.63.clone.1), dimensions={2}, to_apply=%region_0.1 | reduce | flops 520192 | bytes 2113540 | tf_op jit(solution)/shard_map/reduce_sum | solution.py:157
  36.0 12.4 %collective-permute-done.2 = f32[2,2,264,128]{3,2,1,0:T(8,128)S(1)} collective-permute-done((f32[2,2,264,128]{3,2,1,0:T(8,128)S(1)}, f32[2,2,264,128]{3,2,1,0:T(8,128)S(1)}, u32[]{:S(2)}, u32[]{:S(2)}) %collective-permute-start.2) | collective-permute-done | bytes 540704 | tf_op jit(solution)/shard_map/ppermute | solution.py:198
  50.8 5.9 %collective-permute-done.3 = f32[2,264,128]{2,1,0:T(8,128)S(1)} collective-permute-done((f32[2,264,128]{2,1,0:T(8,128)S(1)}, f32[2,264,128]{2,1,0:T(8,128)S(1)}, u32[]{:S(2)}, u32[]{:S(2)}) %collective-permute-start.3) | collective-permute-done | bytes 270368 | tf_op jit(solution)/shard_map/ppermute | solution.py:198
  57.4 1.9 %collective-permute-start.7 = (f32[264,128]{1,0:T(8,128)S(1)}, f32[264,128]{1,0:T(8,128)S(1)}, u32[]{:S(2)}, u32[]{:S(2)}) collective-permute-start(f32[264,128]{1,0:T(8,128)S(1)} %dynamic-slice_bitcast_fusion.4), channel_id=1, source_target_pairs={{0,8},{2,10},{4,12},{6,14},{8,0},{10,2},{12,4},{14,6},{1,9},{3,11}... | collective-permute-start | bytes 405512 | tf_op jit(solution)/shard_map/ppermute | solution.py:198
  59.4 9.7 %collective-permute-done.4 = f32[264,128]{1,0:T(8,128)S(1)} collective-permute-done((f32[264,128]{1,0:T(8,128)S(1)}, f32[264,128]{1,0:T(8,128)S(1)}, u32[]{:S(2)}, u32[]{:S(2)}) %collective-permute-start.4) | collective-permute-done | bytes 135200 | tf_op jit(solution)/shard_map/ppermute | solution.py:198
  69.1 2.9 %collective-permute-done.7 = f32[264,128]{1,0:T(8,128)S(1)} collective-permute-done((f32[264,128]{1,0:T(8,128)S(1)}, f32[264,128]{1,0:T(8,128)S(1)}, u32[]{:S(2)}, u32[]{:S(2)}) %collective-permute-start.7) | collective-permute-done | bytes 135200 | tf_op jit(solution)/shard_map/ppermute | solution.py:198
  72.6 6.9 %collective-permute-done.8 = f32[512,128]{1,0:T(8,128)S(1)} collective-permute-done((f32[512,128]{1,0:T(8,128)S(1)}, f32[512,128]{1,0:T(8,128)S(1)}, u32[]{:S(2)}, u32[]{:S(2)}) %collective-permute-start.8) | collective-permute-done | bytes 262176 | tf_op jit(solution)/shard_map/ppermute | solution.py:198
  81.9 6.1 %collective-permute-done.9 = f32[512,128]{1,0:T(8,128)S(1)} collective-permute-done((f32[512,128]{1,0:T(8,128)S(1)}, f32[512,128]{1,0:T(8,128)S(1)}, u32[]{:S(2)}, u32[]{:S(2)}) %collective-permute-start.9) | collective-permute-done | bytes 262176 | tf_op jit(solution)/shard_map/ppermute | solution.py:198
  90.9 2.4 %collective-permute-start.17 = (f32[128,256]{1,0:T(8,128)S(1)}, f32[128,256]{1,0:T(8,128)S(1)}, u32[]{:S(2)}, u32[]{:S(2)}) collective-permute-start(f32[128,256]{1,0:T(8,128)S(1)} %get-tuple-element.65), channel_id=1, source_target_pairs={{0,8},{2,10},{4,12},{6,14},{8,0},{10,2},{12,4},{14,6},{1,9},{3,11}... | collective-permute-start | bytes 393224 | tf_op jit(solution)/shard_map/ppermute | solution.py:198
  93.3 2.8 %collective-permute-start.10 = (f32[2,128,256]{1,2,0:T(8,128)S(1)}, f32[2,128,256]{1,2,0:T(8,128)S(1)}, u32[]{:S(2)}, u32[]{:S(2)}) collective-permute-start(f32[2,128,256]{1,2,0:T(8,128)S(1)} %pad_maximum_fusion.7), channel_id=1, source_target_pairs={{0,16},{16,0},{1,17},{17,1},{2,18},{18,2},{3,19},{19,3},{4,20},{20... | collective-permute-start | bytes 786440 | tf_op jit(solution)/shard_map/ppermute | solution.py:198
  96.2 1.3 collective-permute-done.14
  97.6 2.7 %collective-permute-done.17 = f32[128,256]{1,0:T(8,128)S(1)} collective-permute-done((f32[128,256]{1,0:T(8,128)S(1)}, f32[128,256]{1,0:T(8,128)S(1)}, u32[]{:S(2)}, u32[]{:S(2)}) %collective-permute-start.17) | collective-permute-done | bytes 131104 | tf_op jit(solution)/shard_map/ppermute | solution.py:198
  102.0 3.1 %collective-permute-done.15 = f32[2,128,256]{2,1,0:T(8,128)S(1)} collective-permute-done((f32[2,128,256]{2,1,0:T(8,128)S(1)}, f32[2,128,256]{2,1,0:T(8,128)S(1)}, u32[]{:S(2)}, u32[]{:S(2)}) %collective-permute-start.15) | collective-permute-done | bytes 262176 | tf_op jit(solution)/shard_map/ppermute | solution.py:198
  106.5 5.6 %collective-permute-done.11 = f32[2,128,256]{1,2,0:T(8,128)S(1)} collective-permute-done((f32[2,128,256]{1,2,0:T(8,128)S(1)}, f32[2,128,256]{1,2,0:T(8,128)S(1)}, u32[]{:S(2)}, u32[]{:S(2)}) %collective-permute-start.11) | collective-permute-done | bytes 262176 | tf_op jit(solution)/shard_map/ppermute | solution.py:198
  112.3 1.5 collective-permute-start.19
  113.9 3.8 %collective-permute-done.12 = f32[2,128,256]{1,2,0:T(8,128)S(1)} collective-permute-done((f32[2,128,256]{1,2,0:T(8,128)S(1)}, f32[2,128,256]{1,2,0:T(8,128)S(1)}, u32[]{:S(2)}, u32[]{:S(2)}) %collective-permute-start.12) | collective-permute-done | bytes 262176 | tf_op jit(solution)/shard_map/ppermute | solution.py:198
  117.8 5.5 %collective-permute-done.16 = f32[2,2,128,256]{3,2,0,1:T(8,128)S(1)} collective-permute-done((f32[2,2,128,256]{3,2,0,1:T(8,128)S(1)}, f32[2,2,128,256]{3,2,0,1:T(8,128)S(1)}, u32[]{:S(2)}, u32[]{:S(2)}) %collective-permute-start.16) | collective-permute-done | bytes 524320 | tf_op jit(solution)/shard_map/ppermute | solution.py:198
  123.6 5.6 %collective-permute-done.19 = f32[2,2,128,256]{3,2,0,1:T(8,128)S(1)} collective-permute-done((f32[2,2,128,256]{3,2,0,1:T(8,128)S(1)}, f32[2,2,128,256]{3,2,0,1:T(8,128)S(1)}, u32[]{:S(2)}, u32[]{:S(2)}) %collective-permute-start.19) | collective-permute-done | bytes 524320 | tf_op jit(solution)/shard_map/ppermute | solution.py:198
  129.7 1.5 pad_maximum_fusion.1.lifted_ref
  131.3 25.2 %shard_map.129 = (f32[128,2048]{1,0:T(8,128)}, f32[128,2048]{1,0:T(8,128)}) custom-call(s32[2]{0:T(128)} %pad_add_fusion.live_ref, s32[512]{0:T(512)} %bitcast.106, s32[512]{0:T(512)} %bitcast.108, s32[512,16,128]{2,1,0:T(8,128)} %bitcast.90, bf16[8,256,512]{2,1,0:T(8,128)(2,1)} %pad_maximum_fusion.1.lifted_ref), custom_call_target="tpu_custom_call" | custom-call | tf_op jit(solution)/shard_map/pallas_call | solution.py:181
  156.5 7.8 %collective-permute-start.20 = (f32[128,2048]{1,0:T(8,128)}, f32[128,2048]{1,0:T(8,128)S(1)}, u32[]{:S(2)}, u32[]{:S(2)}) collective-permute-start(f32[128,2048]{1,0:T(8,128)} %get-tuple-element.16), channel_id=1, source_target_pairs={{0,16},{16,0},{1,17},{17,1},{2,18},{18,2},{3,19},{19,3},{4,20},{20... | collective-permute-start | bytes 3145736 | tf_op jit(solution)/shard_map/ppermute | solution.py:198
  (93 shorter events, 22.0 us)
Async XLA Ops:
  0.6 79.6 %copy-start = (f32[256,256]{1,0:T(8,128)S(1)}, f32[256,256]{1,0:T(8,128)}, u32[]{:S(2)}) copy-start(f32[256,256]{1,0:T(8,128)} %param.11) | copy-start | bytes 786436
  0.6 3.5 %collective-permute-start.1 = (f32[2048,128]{1,0:T(8,128)}, f32[2048,128]{1,0:T(8,128)S(1)}, u32[]{:S(2)}, u32[]{:S(2)}) collective-permute-start(f32[2048,128]{1,0:T(8,128)} %param.9), channel_id=1, source_target_pairs={{0,16},{16,0},{1,17},{17,1},{2,18},{18,2},{3,19},{19,3},{4,20},{20... | collective-permute-start | bytes 3145736 | tf_op jit(solution)/shard_map/ppermute | solution.py:198
  34.6 13.8 %collective-permute-start.2 = (f32[2,2,264,128]{3,2,1,0:T(8,128)S(1)}, f32[2,2,264,128]{3,2,1,0:T(8,128)S(1)}, u32[]{:S(2)}, u32[]{:S(2)}) collective-permute-start(f32[2,2,264,128]{3,2,1,0:T(8,128)S(1)} %dynamic-slice_bitcast_fusion.1), channel_id=1, source_target_pairs={{0,2},{2,0},{4,6},{6,4},{8,10},{10,8},{12,14},{14,12},{1,3},{3,1},... | collective-permute-start | bytes 1622024 | tf_op jit(solution)/shard_map/ppermute | solution.py:198
  35.7 14.1 %collective-permute-start.5 = (f32[2,2,264,128]{3,2,1,0:T(8,128)}, f32[2,2,264,128]{3,2,1,0:T(8,128)S(1)}, u32[]{:S(2)}, u32[]{:S(2)}) collective-permute-start(f32[2,2,264,128]{3,2,1,0:T(8,128)} %dynamic-slice_bitcast_fusion), channel_id=1, source_target_pairs={{0,4},{2,6},{4,0},{6,2},{8,12},{10,14},{12,8},{14,10},{1,5},{3,7},... | collective-permute-start | bytes 1622024 | tf_op jit(solution)/shard_map/ppermute | solution.py:198
  35.7 36.8 %collective-permute-start = (f32[512,128]{1,0:T(8,128)S(1)}, f32[512,128]{1,0:T(8,128)S(1)}, u32[]{:S(2)}, u32[]{:S(2)}) collective-permute-start(f32[512,128]{1,0:T(8,128)S(1)} %copy-done.4), channel_id=1, source_target_pairs={{0,1},{1,0},{2,3},{3,2},{4,5},{5,4},{6,7},{7,6},{8,9},{9,8},{10,11... | collective-permute-start | bytes 786440 | tf_op jit(solution)/shard_map/ppermute | solution.py:198
  49.6 7.2 %collective-permute-start.3 = (f32[2,264,128]{2,1,0:T(8,128)S(1)}, f32[2,264,128]{2,1,0:T(8,128)S(1)}, u32[]{:S(2)}, u32[]{:S(2)}) collective-permute-start(f32[2,264,128]{2,1,0:T(8,128)S(1)} %dynamic-slice_bitcast_fusion.3), channel_id=1, source_target_pairs={{0,4},{2,6},{4,0},{6,2},{8,12},{10,14},{12,8},{14,10},{1,5},{3,7},... | collective-permute-start | bytes 811016 | tf_op jit(solution)/shard_map/ppermute | solution.py:198
  50.0 7.4 %collective-permute-start.6 = (f32[2,264,128]{2,1,0:T(8,128)S(1)}, f32[2,264,128]{2,1,0:T(8,128)S(1)}, u32[]{:S(2)}, u32[]{:S(2)}) collective-permute-start(f32[2,264,128]{2,1,0:T(8,128)S(1)} %dynamic-slice_bitcast_fusion.2), channel_id=1, source_target_pairs={{0,2},{2,0},{4,6},{6,4},{8,10},{10,8},{12,14},{14,12},{1,3},{3,1},... | collective-permute-start | bytes 811016 | tf_op jit(solution)/shard_map/ppermute | solution.py:198
  56.8 22.8 %copy-start.5 = (f32[256,256]{1,0:T(8,128)S(1)}, f32[256,256]{1,0:T(8,128)}, u32[]{:S(2)}) copy-start(f32[256,256]{1,0:T(8,128)} %param.12) | copy-start | bytes 786436
  56.8 12.3 %collective-permute-start.4 = (f32[264,128]{1,0:T(8,128)S(1)}, f32[264,128]{1,0:T(8,128)S(1)}, u32[]{:S(2)}, u32[]{:S(2)}) collective-permute-start(f32[264,128]{1,0:T(8,128)S(1)} %dynamic-slice_bitcast_fusion.5), channel_id=1, source_target_pairs={{0,8},{2,10},{4,12},{6,14},{8,0},{10,2},{12,4},{14,6},{1,9},{3,11}... | collective-permute-start | bytes 405512 | tf_op jit(solution)/shard_map/ppermute | solution.py:198
  57.4 22.8 %copy-start.6 = (f32[512,128]{1,0:T(8,128)S(1)}, f32[512,128]{1,0:T(8,128)}, u32[]{:S(2)}) copy-start(f32[512,128]{1,0:T(8,128)} %param.13) | copy-start | bytes 786436
  57.4 14.5 %collective-permute-start.7 = (f32[264,128]{1,0:T(8,128)S(1)}, f32[264,128]{1,0:T(8,128)S(1)}, u32[]{:S(2)}, u32[]{:S(2)}) collective-permute-start(f32[264,128]{1,0:T(8,128)S(1)} %dynamic-slice_bitcast_fusion.4), channel_id=1, source_target_pairs={{0,8},{2,10},{4,12},{6,14},{8,0},{10,2},{12,4},{14,6},{1,9},{3,11}... | collective-permute-start | bytes 405512 | tf_op jit(solution)/shard_map/ppermute | solution.py:198
  72.1 7.4 %collective-permute-start.8 = (f32[512,128]{1,0:T(8,128)S(1)}, f32[512,128]{1,0:T(8,128)S(1)}, u32[]{:S(2)}, u32[]{:S(2)}) collective-permute-start(f32[512,128]{1,0:T(8,128)S(1)} %fusion.22), channel_id=1, source_target_pairs={{0,1},{1,0},{2,3},{3,2},{4,5},{5,4},{6,7},{7,6},{8,9},{9,8},{10,11... | collective-permute-start | bytes 786440 | tf_op jit(solution)/shard_map/ppermute | solution.py:198
  81.5 6.5 %collective-permute-start.9 = (f32[512,128]{1,0:T(8,128)S(1)}, f32[512,128]{1,0:T(8,128)S(1)}, u32[]{:S(2)}, u32[]{:S(2)}) collective-permute-start(f32[512,128]{1,0:T(8,128)S(1)} %get-tuple-element.67), channel_id=1, source_target_pairs={{0,1},{1,0},{2,3},{3,2},{4,5},{5,4},{6,7},{7,6},{8,9},{9,8},{10,11... | collective-permute-start | bytes 786440 | tf_op jit(solution)/shard_map/ppermute | solution.py:198
  89.8 7.7 %collective-permute-start.14 = (f32[128,256]{1,0:T(8,128)S(1)}, f32[128,256]{1,0:T(8,128)S(1)}, u32[]{:S(2)}, u32[]{:S(2)}) collective-permute-start(f32[128,256]{1,0:T(8,128)S(1)} %get-tuple-element.66), channel_id=1, source_target_pairs={{0,8},{2,10},{4,12},{6,14},{8,0},{10,2},{12,4},{14,6},{1,9},{3,11}... | collective-permute-start | bytes 393224 | tf_op jit(solution)/shard_map/ppermute | solution.py:198
  90.9 9.4 %collective-permute-start.17 = (f32[128,256]{1,0:T(8,128)S(1)}, f32[128,256]{1,0:T(8,128)S(1)}, u32[]{:S(2)}, u32[]{:S(2)}) collective-permute-start(f32[128,256]{1,0:T(8,128)S(1)} %get-tuple-element.65), channel_id=1, source_target_pairs={{0,8},{2,10},{4,12},{6,14},{8,0},{10,2},{12,4},{14,6},{1,9},{3,11}... | collective-permute-start | bytes 393224 | tf_op jit(solution)/shard_map/ppermute | solution.py:198
  93.3 8.3 %collective-permute-start.10 = (f32[2,128,256]{1,2,0:T(8,128)S(1)}, f32[2,128,256]{1,2,0:T(8,128)S(1)}, u32[]{:S(2)}, u32[]{:S(2)}) collective-permute-start(f32[2,128,256]{1,2,0:T(8,128)S(1)} %pad_maximum_fusion.7), channel_id=1, source_target_pairs={{0,16},{16,0},{1,17},{17,1},{2,18},{18,2},{3,19},{19,3},{4,20},{20... | collective-permute-start | bytes 786440 | tf_op jit(solution)/shard_map/ppermute | solution.py:198
  97.5 7.6 %collective-permute-start.15 = (f32[2,128,256]{2,1,0:T(8,128)S(1)}, f32[2,128,256]{2,1,0:T(8,128)S(1)}, u32[]{:S(2)}, u32[]{:S(2)}) collective-permute-start(f32[2,128,256]{2,1,0:T(8,128)S(1)} %maximum_select_fusion.4), channel_id=1, source_target_pairs={{0,4},{2,6},{4,0},{6,2},{8,12},{10,14},{12,8},{14,10},{1,5},{3,7},... | collective-permute-start | bytes 786440 | tf_op jit(solution)/shard_map/ppermute | solution.py:198
  100.3 11.9 %collective-permute-start.18 = (f32[2,128,256]{2,1,0:T(8,128)S(1)}, f32[2,128,256]{2,1,0:T(8,128)S(1)}, u32[]{:S(2)}, u32[]{:S(2)}) collective-permute-start(f32[2,128,256]{2,1,0:T(8,128)S(1)} %maximum_select_fusion.6), channel_id=1, source_target_pairs={{0,2},{2,0},{4,6},{6,4},{8,10},{10,8},{12,14},{14,12},{1,3},{3,1},... | collective-permute-start | bytes 786440 | tf_op jit(solution)/shard_map/ppermute | solution.py:198
  101.7 10.4 %collective-permute-start.11 = (f32[2,128,256]{1,2,0:T(8,128)S(1)}, f32[2,128,256]{1,2,0:T(8,128)S(1)}, u32[]{:S(2)}, u32[]{:S(2)}) collective-permute-start(f32[2,128,256]{1,2,0:T(8,128)S(1)} %fusion.41), channel_id=1, source_target_pairs={{0,2},{2,0},{4,6},{6,4},{8,10},{10,8},{12,14},{14,12},{1,3},{3,1},... | collective-permute-start | bytes 786440 | tf_op jit(solution)/shard_map/ppermute | solution.py:198
  105.1 18.2 %collective-permute-start.16 = (f32[2,2,128,256]{3,2,0,1:T(8,128)S(1)}, f32[2,2,128,256]{3,2,0,1:T(8,128)S(1)}, u32[]{:S(2)}, u32[]{:S(2)}) collective-permute-start(f32[2,2,128,256]{3,2,0,1:T(8,128)S(1)} %get-tuple-element.38), channel_id=1, source_target_pairs={{0,2},{2,0},{4,6},{6,4},{8,10},{10,8},{12,14},{14,12},{1,3},{3,1},... | collective-permute-start | bytes 1572872 | tf_op jit(solution)/shard_map/ppermute | solution.py:198
  112.1 5.6 %collective-permute-start.12 = (f32[2,128,256]{1,2,0:T(8,128)S(1)}, f32[2,128,256]{1,2,0:T(8,128)S(1)}, u32[]{:S(2)}, u32[]{:S(2)}) collective-permute-start(f32[2,128,256]{1,2,0:T(8,128)S(1)} %fusion.45), channel_id=1, source_target_pairs={{0,4},{2,6},{4,0},{6,2},{8,12},{10,14},{12,8},{14,10},{1,5},{3,7},... | collective-permute-start | bytes 786440 | tf_op jit(solution)/shard_map/ppermute | solution.py:198
  112.3 17.0 %collective-permute-start.19 = (f32[2,2,128,256]{3,2,0,1:T(8,128)S(1)}, f32[2,2,128,256]{3,2,0,1:T(8,128)S(1)}, u32[]{:S(2)}, u32[]{:S(2)}) collective-permute-start(f32[2,2,128,256]{3,2,0,1:T(8,128)S(1)} %get-tuple-element.40), channel_id=1, source_target_pairs={{0,4},{2,6},{4,0},{6,2},{8,12},{10,14},{12,8},{14,10},{1,5},{3,7},... | collective-permute-start | bytes 1572872 | tf_op jit(solution)/shard_map/ppermute | solution.py:198
  117.8 13.5 %collective-permute-start.13 = (f32[2,128,256]{1,2,0:T(8,128)S(1)}, f32[2,128,256]{1,2,0:T(8,128)S(1)}, u32[]{:S(2)}, u32[]{:S(2)}) collective-permute-start(f32[2,128,256]{1,2,0:T(8,128)S(1)} %add.112), channel_id=1, source_target_pairs={{0,8},{2,10},{4,12},{6,14},{8,0},{10,2},{12,4},{14,6},{1,9},{3,11}... | collective-permute-start | bytes 786440 | tf_op jit(solution)/shard_map/ppermute | solution.py:198
  156.5 10.6 %collective-permute-start.20 = (f32[128,2048]{1,0:T(8,128)}, f32[128,2048]{1,0:T(8,128)S(1)}, u32[]{:S(2)}, u32[]{:S(2)}) collective-permute-start(f32[128,2048]{1,0:T(8,128)} %get-tuple-element.16), channel_id=1, source_target_pairs={{0,16},{16,0},{1,17},{17,1},{2,18},{18,2},{3,19},{19,3},{4,20},{20... | collective-permute-start | bytes 3145736 | tf_op jit(solution)/shard_map/ppermute | solution.py:198
  (4 other events, 16.2 us)

commit v17 on v16

--- a/solution.py
+++ b/solution.py
@@ -40,6 +40,16 @@
 def slot_words(masks_ref, live_ref, base, k):
     keep = jnp.where(base + k < live_ref[0], -1, 0).astype(jnp.int32)
     return unpack_block(jnp.bitwise_and(masks_ref[k], keep)).astype(jnp.bfloat16)
+
+
+def forward_counts_kernel(
+    live_ref, rows_ref, cols_ref, masks_ref, panel_ref, totals_ref, counts_ref, bits_ref
+):
+    forward_kernel(live_ref, rows_ref, cols_ref, masks_ref, panel_ref, totals_ref, bits_ref)
+
+    @pl.when(pl.program_id(0) == pl.num_programs(0) - 1)
+    def _():
+        counts_ref[...] = jnp.sum(bits_ref[...], axis=-1).astype(jnp.float32)
 
 
 def forward_kernel(live_ref, rows_ref, cols_ref, masks_ref, panel_ref, totals_ref, bits_ref):
@@ -147,14 +157,26 @@
 
 
 def block_aggregate(live, block_rows, block_cols, packed_masks, panel_split, row_blocks):
-    edge = packed_masks.shape[-1]
-    totals_shape = jax.ShapeDtypeStruct((row_blocks * edge, panel_split.shape[1] // 2), jnp.float32)
-    bits_shape = jax.ShapeDtypeStruct((row_blocks, edge, edge), jnp.int32)
-    totals, bit_sums = slot_pallas(
-        forward_kernel, live, block_rows, block_cols, packed_masks, panel_split,
-        [totals_shape, bits_shape],
-    )
-    return totals, jnp.sum(bit_sums, axis=-1).astype(jnp.float32).reshape(-1)
+    slot_total, _, edge = packed_masks.shape
+    group = min(SLOT_GROUP, slot_total)
+    totals_shape = (row_blocks * edge, panel_split.shape[1] // 2)
+    grid_spec = pltpu.PrefetchScalarGridSpec(
+        num_scalar_prefetch=3,
+        grid=(slot_total // group,),
+        in_specs=[mask_spec(packed_masks, group), whole_spec(panel_split.shape)],
+        out_specs=[whole_spec(totals_shape), whole_spec((row_blocks, edge))],
+        scratch_shapes=[pltpu.VMEM((row_blocks, edge, edge), jnp.int32)],
+    )
+    totals, counts = pl.pallas_call(
+        forward_counts_kernel,
+        grid_spec=grid_spec,
+        out_shape=[
+            jax.ShapeDtypeStruct(totals_shape, jnp.float32),
+            jax.ShapeDtypeStruct((row_blocks, edge), jnp.float32),
+        ],
+        compiler_params=pltpu.CompilerParams(dimension_semantics=("arbitrary",)),
+    )(live, block_rows, block_cols, packed_masks, panel_split)
+    return totals, counts.reshape(-1)
 
 
 def block_transpose(live, block_rows, block_cols, packed_masks, lifted_chunks, cand_count):

time: 169 us -> 167 us (0.988)
  starting transfers between devices: 22.7 us -> 17.8 us
  waiting for transfers between devices: 72.4 us -> 75.5 us
    ppermute x21, starting transfers between devices: 22.7 us -> 17.8 us  [exchange(): return lax.ppermute(values, axis, [(i, i ^ 1 << bit) for i in range(count)])]
    ppermute x21, waiting for transfers between devices: 72.4 us -> 75.5 us  [exchange(): return lax.ppermute(values, axis, [(i, i ^ 1 << bit) for i in range(count)])]
    reduce_sum x1 -> x0, other arithmetic: 2.35 us -> none  [block_aggregate(): return (totals, jnp.sum(bit_sums, axis=-1).astype(jnp.float32).reshape(-1))]
    unnamed x17 -> x15, local copies, waits for them, and re-layouts: 3.83 us -> 2.86 us
where the time goes in v17:
time: 167 us; the launch traced here: 166 us
  waiting for transfers between devices  75.5 us (45%)
  Pallas kernels  50.6 us (30%)
  starting transfers between devices  17.8 us (11%)
  other arithmetic  10.2 us (6%)
  matrix products  5.82 us (3%)
  local copies, waits for them, and re-layouts  4.93 us (3%)
  between operations  1.69 us (1%)
    ppermute x21, waiting for transfers between devices, exchange(): return lax.ppermute(values, axis, [(i, i ^ 1 << bit) for i in range(count)])  75.5 us
    pallas_call x1, Pallas kernels, block_aggregate(): pl.pallas_call(forward_counts_kernel, grid_spec=grid_spec, out_shape=[jax...  25.3 us
    pallas_call x1, Pallas kernels, block_transpose(): pl.pallas_call(backward_pair_kernel, grid_spec=grid_spec, out_shape=[half...  25.2 us
    ppermute x21, starting transfers between devices, exchange(): return lax.ppermute(values, axis, [(i, i ^ 1 << bit) for i in range(count)])  17.8 us
  transfers between devices with their start and end apart: 21, of which 15 were waited for; matrix products, arithmetic and copies ran while one was open for 7% of the time, Pallas kernels for 0%

profile of v17, /device:TPU:31, one launch (start us, length us, event | category | flops | bytes accessed | tf_op | source)
XLA Modules:
  0.0 166.5 jit_solution(5534711440483176647)
XLA Ops:
  2.7 1.4 reduce-precision_convert_fusion.1
  4.8 1.5 pad_maximum_fusion.panel_ref
  6.3 25.3 %shard_map.128 = (f32[4096,128]{1,0:T(8,128)}, f32[32,128]{1,0:T(8,128)}) custom-call(s32[2]{0:T(128)} %pad_add_fusion.live_ref, s32[512]{0:T(512)} %bitcast.105, s32[512]{0:T(512)} %bitcast.107, s32[512,16,128]{2,1,0:T(8,128)} %bitcast.89, bf16[4096,256]{1,0:T(8,128)(2,1)} %pad_maximum_fusion.panel_ref), custom_call_target="tpu_custom_call" | custom-call | tf_op jit(solution)/shard_map/pallas_call | solution.py:170
  31.6 1.7 %fusion.42 = (f32[8,264,128]{2,1,0:T(8,128)S(1)}, f32[8,264,128]{2,1,0:T(8,128)S(1)}) fusion(f32[8,512,128]{2,1,0:T(8,128)} %bitcast.91, f32[264]{0:T(512)S(1)} %pad_slice_fusion, f32[8,4,128]{2,1,0:T(4,128)} %bitcast.104), kind=kLoop, calls=%fused_computation.107 | loop fusion | flops 540672 | bytes 5358624 | tf_op jit(solution)/shard_map/split | solution.py:280
  35.6 12.6 %collective-permute-done.2 = f32[2,2,264,128]{3,2,1,0:T(8,128)S(1)} collective-permute-done((f32[2,2,264,128]{3,2,1,0:T(8,128)}, f32[2,2,264,128]{3,2,1,0:T(8,128)S(1)}, u32[]{:S(2)}, u32[]{:S(2)}) %collective-permute-start.2) | collective-permute-done | bytes 540704 | tf_op jit(solution)/shard_map/ppermute | solution.py:220
  51.4 4.0 %collective-permute-done.3 = f32[2,264,128]{2,1,0:T(8,128)S(1)} collective-permute-done((f32[2,264,128]{2,1,0:T(8,128)S(1)}, f32[2,264,128]{2,1,0:T(8,128)S(1)}, u32[]{:S(2)}, u32[]{:S(2)}) %collective-permute-start.3) | collective-permute-done | bytes 270368 | tf_op jit(solution)/shard_map/ppermute | solution.py:220
  55.6 1.5 collective-permute-done.6
  58.1 9.3 %collective-permute-done.4 = f32[264,128]{1,0:T(8,128)S(1)} collective-permute-done((f32[264,128]{1,0:T(8,128)S(1)}, f32[264,128]{1,0:T(8,128)S(1)}, u32[]{:S(2)}, u32[]{:S(2)}) %collective-permute-start.4) | collective-permute-done | bytes 135200 | tf_op jit(solution)/shard_map/ppermute | solution.py:220
  67.4 2.9 %collective-permute-done.7 = f32[264,128]{1,0:T(8,128)S(1)} collective-permute-done((f32[264,128]{1,0:T(8,128)S(1)}, f32[264,128]{1,0:T(8,128)S(1)}, u32[]{:S(2)}, u32[]{:S(2)}) %collective-permute-start.7) | collective-permute-done | bytes 135200 | tf_op jit(solution)/shard_map/ppermute | solution.py:220
  70.9 6.5 %collective-permute-done.8 = f32[512,128]{1,0:T(8,128)S(1)} collective-permute-done((f32[512,128]{1,0:T(8,128)S(1)}, f32[512,128]{1,0:T(8,128)S(1)}, u32[]{:S(2)}, u32[]{:S(2)}) %collective-permute-start.8) | collective-permute-done | bytes 262176 | tf_op jit(solution)/shard_map/ppermute | solution.py:220
  78.2 1.3 multiply_multiply_fusion
  79.9 5.7 %collective-permute-done.9 = f32[512,128]{1,0:T(8,128)S(1)} collective-permute-done((f32[512,128]{1,0:T(8,128)S(1)}, f32[512,128]{1,0:T(8,128)S(1)}, u32[]{:S(2)}, u32[]{:S(2)}) %collective-permute-start.9) | collective-permute-done | bytes 262176 | tf_op jit(solution)/shard_map/ppermute | solution.py:220
  88.4 2.4 %collective-permute-start.17 = (f32[128,256]{1,0:T(8,128)S(1)}, f32[128,256]{1,0:T(8,128)S(1)}, u32[]{:S(2)}, u32[]{:S(2)}) collective-permute-start(f32[128,256]{1,0:T(8,128)S(1)} %get-tuple-element.65), channel_id=1, source_target_pairs={{0,8},{2,10},{4,12},{6,14},{8,0},{10,2},{12,4},{14,6},{1,9},{3,11}... | collective-permute-start | bytes 393224 | tf_op jit(solution)/shard_map/ppermute | solution.py:220
  90.9 3.2 %collective-permute-start.10 = (f32[2,128,256]{1,2,0:T(8,128)S(1)}, f32[2,128,256]{1,2,0:T(8,128)S(1)}, u32[]{:S(2)}, u32[]{:S(2)}) collective-permute-start(f32[2,128,256]{1,2,0:T(8,128)S(1)} %pad_maximum_fusion.7), channel_id=1, source_target_pairs={{0,16},{16,0},{1,17},{17,1},{2,18},{18,2},{3,19},{19,3},{4,20},{20... | collective-permute-start | bytes 786440 | tf_op jit(solution)/shard_map/ppermute | solution.py:220
  94.1 2.6 %collective-permute-done.14 = f32[128,256]{1,0:T(8,128)S(1)} collective-permute-done((f32[128,256]{1,0:T(8,128)S(1)}, f32[128,256]{1,0:T(8,128)S(1)}, u32[]{:S(2)}, u32[]{:S(2)}) %collective-permute-start.14) | collective-permute-done | bytes 131104 | tf_op jit(solution)/shard_map/ppermute | solution.py:220
  96.8 2.7 %collective-permute-done.17 = f32[128,256]{1,0:T(8,128)S(1)} collective-permute-done((f32[128,256]{1,0:T(8,128)S(1)}, f32[128,256]{1,0:T(8,128)S(1)}, u32[]{:S(2)}, u32[]{:S(2)}) %collective-permute-start.17) | collective-permute-done | bytes 131104 | tf_op jit(solution)/shard_map/ppermute | solution.py:220
  101.3 5.0 %collective-permute-done.18 = f32[2,128,256]{2,1,0:T(8,128)S(1)} collective-permute-done((f32[2,128,256]{2,1,0:T(8,128)S(1)}, f32[2,128,256]{2,1,0:T(8,128)S(1)}, u32[]{:S(2)}, u32[]{:S(2)}) %collective-permute-start.18) | collective-permute-done | bytes 262176 | tf_op jit(solution)/shard_map/ppermute | solution.py:220
  106.5 5.4 %collective-permute-done.11 = f32[2,128,256]{1,2,0:T(8,128)S(1)} collective-permute-done((f32[2,128,256]{1,2,0:T(8,128)S(1)}, f32[2,128,256]{1,2,0:T(8,128)S(1)}, u32[]{:S(2)}, u32[]{:S(2)}) %collective-permute-start.11) | collective-permute-done | bytes 262176 | tf_op jit(solution)/shard_map/ppermute | solution.py:220
  112.3 9.3 %collective-permute-done.12 = f32[2,128,256]{1,2,0:T(8,128)S(1)} collective-permute-done((f32[2,128,256]{1,2,0:T(8,128)S(1)}, f32[2,128,256]{1,2,0:T(8,128)S(1)}, u32[]{:S(2)}, u32[]{:S(2)}) %collective-permute-start.12) | collective-permute-done | bytes 262176 | tf_op jit(solution)/shard_map/ppermute | solution.py:220
  122.0 1.4 collective-permute-done.16
  123.9 1.5 pad_maximum_fusion.1.lifted_ref
  125.5 5.8 %collective-permute-done.13 = f32[2,128,256]{1,2,0:T(8,128)S(1)} collective-permute-done((f32[2,128,256]{1,2,0:T(8,128)S(1)}, f32[2,128,256]{1,2,0:T(8,128)S(1)}, u32[]{:S(2)}, u32[]{:S(2)}) %collective-permute-start.13) | collective-permute-done | bytes 262176 | tf_op jit(solution)/shard_map/ppermute | solution.py:220
  131.3 25.2 %shard_map.129 = (f32[128,2048]{1,0:T(8,128)}, f32[128,2048]{1,0:T(8,128)}) custom-call(s32[2]{0:T(128)} %pad_add_fusion.live_ref, s32[512]{0:T(512)} %bitcast.106, s32[512]{0:T(512)} %bitcast.108, s32[512,16,128]{2,1,0:T(8,128)} %bitcast.90, bf16[8,256,512]{2,1,0:T(8,128)(2,1)} %pad_maximum_fusion.1.lifted_ref), custom_call_target="tpu_custom_call" | custom-call | tf_op jit(solution)/shard_map/pallas_call | solution.py:203
  156.5 5.6 %collective-permute-start.20 = (f32[128,2048]{1,0:T(8,128)}, f32[128,2048]{1,0:T(8,128)S(1)}, u32[]{:S(2)}, u32[]{:S(2)}) collective-permute-start(f32[128,2048]{1,0:T(8,128)} %get-tuple-element.16), channel_id=1, source_target_pairs={{0,16},{16,0},{1,17},{17,1},{2,18},{18,2},{3,19},{19,3},{4,20},{20... | collective-permute-start | bytes 3145736 | tf_op jit(solution)/shard_map/ppermute | solution.py:220
  (89 shorter events, 20.7 us)
Async XLA Ops:
  0.6 77.5 %copy-start = (f32[256,256]{1,0:T(8,128)S(1)}, f32[256,256]{1,0:T(8,128)}, u32[]{:S(2)}) copy-start(f32[256,256]{1,0:T(8,128)} %param.11) | copy-start | bytes 786436
  0.6 3.5 %collective-permute-start.1 = (f32[2048,128]{1,0:T(8,128)}, f32[2048,128]{1,0:T(8,128)S(1)}, u32[]{:S(2)}, u32[]{:S(2)}) collective-permute-start(f32[2048,128]{1,0:T(8,128)} %param.9), channel_id=1, source_target_pairs={{0,16},{16,0},{1,17},{17,1},{2,18},{18,2},{3,19},{19,3},{4,20},{20... | collective-permute-start | bytes 3145736 | tf_op jit(solution)/shard_map/ppermute | solution.py:220
  34.2 14.0 %collective-permute-start.2 = (f32[2,2,264,128]{3,2,1,0:T(8,128)}, f32[2,2,264,128]{3,2,1,0:T(8,128)S(1)}, u32[]{:S(2)}, u32[]{:S(2)}) collective-permute-start(f32[2,2,264,128]{3,2,1,0:T(8,128)} %dynamic-slice_bitcast_fusion.1), channel_id=1, source_target_pairs={{0,2},{2,0},{4,6},{6,4},{8,10},{10,8},{12,14},{14,12},{1,3},{3,1},... | collective-permute-start | bytes 1622024 | tf_op jit(solution)/shard_map/ppermute | solution.py:220
  35.3 13.8 %collective-permute-start.5 = (f32[2,2,264,128]{3,2,1,0:T(8,128)}, f32[2,2,264,128]{3,2,1,0:T(8,128)}, u32[]{:S(2)}, u32[]{:S(2)}) collective-permute-start(f32[2,2,264,128]{3,2,1,0:T(8,128)} %dynamic-slice_bitcast_fusion), channel_id=1, source_target_pairs={{0,4},{2,6},{4,0},{6,2},{8,12},{10,14},{12,8},{14,10},{1,5},{3,7},... | collective-permute-start | bytes 1622024 | tf_op jit(solution)/shard_map/ppermute | solution.py:220
  35.3 35.6 %collective-permute-start = (f32[512,128]{1,0:T(8,128)S(1)}, f32[512,128]{1,0:T(8,128)S(1)}, u32[]{:S(2)}, u32[]{:S(2)}) collective-permute-start(f32[512,128]{1,0:T(8,128)S(1)} %copy-done.2), channel_id=1, source_target_pairs={{0,1},{1,0},{2,3},{3,2},{4,5},{5,4},{6,7},{7,6},{8,9},{9,8},{10,11... | collective-permute-start | bytes 786440 | tf_op jit(solution)/shard_map/ppermute | solution.py:220
  48.3 7.2 %collective-permute-start.3 = (f32[2,264,128]{2,1,0:T(8,128)S(1)}, f32[2,264,128]{2,1,0:T(8,128)S(1)}, u32[]{:S(2)}, u32[]{:S(2)}) collective-permute-start(f32[2,264,128]{2,1,0:T(8,128)S(1)} %dynamic-slice_bitcast_fusion.3), channel_id=1, source_target_pairs={{0,4},{2,6},{4,0},{6,2},{8,12},{10,14},{12,8},{14,10},{1,5},{3,7},... | collective-permute-start | bytes 811016 | tf_op jit(solution)/shard_map/ppermute | solution.py:220
  50.3 6.9 %collective-permute-start.6 = (f32[2,264,128]{2,1,0:T(8,128)S(1)}, f32[2,264,128]{2,1,0:T(8,128)S(1)}, u32[]{:S(2)}, u32[]{:S(2)}) collective-permute-start(f32[2,264,128]{2,1,0:T(8,128)S(1)} %dynamic-slice_bitcast_fusion.2), channel_id=1, source_target_pairs={{0,2},{2,0},{4,6},{6,4},{8,10},{10,8},{12,14},{14,12},{1,3},{3,1},... | collective-permute-start | bytes 811016 | tf_op jit(solution)/shard_map/ppermute | solution.py:220
  55.5 22.0 %copy-start.3 = (f32[256,256]{1,0:T(8,128)S(1)}, f32[256,256]{1,0:T(8,128)}, u32[]{:S(2)}) copy-start(f32[256,256]{1,0:T(8,128)} %param.12) | copy-start | bytes 786436
  55.6 11.8 %collective-permute-start.4 = (f32[264,128]{1,0:T(8,128)S(1)}, f32[264,128]{1,0:T(8,128)S(1)}, u32[]{:S(2)}, u32[]{:S(2)}) collective-permute-start(f32[264,128]{1,0:T(8,128)S(1)} %dynamic-slice_bitcast_fusion.5), channel_id=1, source_target_pairs={{0,8},{2,10},{4,12},{6,14},{8,0},{10,2},{12,4},{14,6},{1,9},{3,11}... | collective-permute-start | bytes 405512 | tf_op jit(solution)/shard_map/ppermute | solution.py:220
  57.2 21.0 %copy-start.5 = (f32[512,128]{1,0:T(8,128)S(1)}, f32[512,128]{1,0:T(8,128)}, u32[]{:S(2)}) copy-start(f32[512,128]{1,0:T(8,128)} %param.13) | copy-start | bytes 786436
  57.2 13.1 %collective-permute-start.7 = (f32[264,128]{1,0:T(8,128)S(1)}, f32[264,128]{1,0:T(8,128)S(1)}, u32[]{:S(2)}, u32[]{:S(2)}) collective-permute-start(f32[264,128]{1,0:T(8,128)S(1)} %dynamic-slice_bitcast_fusion.4), channel_id=1, source_target_pairs={{0,8},{2,10},{4,12},{6,14},{8,0},{10,2},{12,4},{14,6},{1,9},{3,11}... | collective-permute-start | bytes 405512 | tf_op jit(solution)/shard_map/ppermute | solution.py:220
  70.5 7.0 %collective-permute-start.8 = (f32[512,128]{1,0:T(8,128)S(1)}, f32[512,128]{1,0:T(8,128)S(1)}, u32[]{:S(2)}, u32[]{:S(2)}) collective-permute-start(f32[512,128]{1,0:T(8,128)S(1)} %fusion.22), channel_id=1, source_target_pairs={{0,1},{1,0},{2,3},{3,2},{4,5},{5,4},{6,7},{7,6},{8,9},{9,8},{10,11... | collective-permute-start | bytes 786440 | tf_op jit(solution)/shard_map/ppermute | solution.py:220
  79.5 6.1 %collective-permute-start.9 = (f32[512,128]{1,0:T(8,128)S(1)}, f32[512,128]{1,0:T(8,128)S(1)}, u32[]{:S(2)}, u32[]{:S(2)}) collective-permute-start(f32[512,128]{1,0:T(8,128)S(1)} %get-tuple-element.67), channel_id=1, source_target_pairs={{0,1},{1,0},{2,3},{3,2},{4,5},{5,4},{6,7},{7,6},{8,9},{9,8},{10,11... | collective-permute-start | bytes 786440 | tf_op jit(solution)/shard_map/ppermute | solution.py:220
  87.4 9.4 %collective-permute-start.14 = (f32[128,256]{1,0:T(8,128)S(1)}, f32[128,256]{1,0:T(8,128)S(1)}, u32[]{:S(2)}, u32[]{:S(2)}) collective-permute-start(f32[128,256]{1,0:T(8,128)S(1)} %get-tuple-element.66), channel_id=1, source_target_pairs={{0,8},{2,10},{4,12},{6,14},{8,0},{10,2},{12,4},{14,6},{1,9},{3,11}... | collective-permute-start | bytes 393224 | tf_op jit(solution)/shard_map/ppermute | solution.py:220
  88.4 11.1 %collective-permute-start.17 = (f32[128,256]{1,0:T(8,128)S(1)}, f32[128,256]{1,0:T(8,128)S(1)}, u32[]{:S(2)}, u32[]{:S(2)}) collective-permute-start(f32[128,256]{1,0:T(8,128)S(1)} %get-tuple-element.65), channel_id=1, source_target_pairs={{0,8},{2,10},{4,12},{6,14},{8,0},{10,2},{12,4},{14,6},{1,9},{3,11}... | collective-permute-start | bytes 393224 | tf_op jit(solution)/shard_map/ppermute | solution.py:220
  90.9 9.1 %collective-permute-start.10 = (f32[2,128,256]{1,2,0:T(8,128)S(1)}, f32[2,128,256]{1,2,0:T(8,128)S(1)}, u32[]{:S(2)}, u32[]{:S(2)}) collective-permute-start(f32[2,128,256]{1,2,0:T(8,128)S(1)} %pad_maximum_fusion.7), channel_id=1, source_target_pairs={{0,16},{16,0},{1,17},{17,1},{2,18},{18,2},{3,19},{19,3},{4,20},{20... | collective-permute-start | bytes 786440 | tf_op jit(solution)/shard_map/ppermute | solution.py:220
  96.8 9.6 %collective-permute-start.15 = (f32[2,128,256]{2,1,0:T(8,128)S(1)}, f32[2,128,256]{2,1,0:T(8,128)S(1)}, u32[]{:S(2)}, u32[]{:S(2)}) collective-permute-start(f32[2,128,256]{2,1,0:T(8,128)S(1)} %maximum_select_fusion.4), channel_id=1, source_target_pairs={{0,4},{2,6},{4,0},{6,2},{8,12},{10,14},{12,8},{14,10},{1,5},{3,7},... | collective-permute-start | bytes 786440 | tf_op jit(solution)/shard_map/ppermute | solution.py:220
  99.6 6.7 %collective-permute-start.18 = (f32[2,128,256]{2,1,0:T(8,128)S(1)}, f32[2,128,256]{2,1,0:T(8,128)S(1)}, u32[]{:S(2)}, u32[]{:S(2)}) collective-permute-start(f32[2,128,256]{2,1,0:T(8,128)S(1)} %maximum_select_fusion.6), channel_id=1, source_target_pairs={{0,2},{2,0},{4,6},{6,4},{8,10},{10,8},{12,14},{14,12},{1,3},{3,1},... | collective-permute-start | bytes 786440 | tf_op jit(solution)/shard_map/ppermute | solution.py:220
  100.0 11.9 %collective-permute-start.11 = (f32[2,128,256]{1,2,0:T(8,128)S(1)}, f32[2,128,256]{1,2,0:T(8,128)S(1)}, u32[]{:S(2)}, u32[]{:S(2)}) collective-permute-start(f32[2,128,256]{1,2,0:T(8,128)S(1)} %fusion.41), channel_id=1, source_target_pairs={{0,2},{2,0},{4,6},{6,4},{8,10},{10,8},{12,14},{14,12},{1,3},{3,1},... | collective-permute-start | bytes 786440 | tf_op jit(solution)/shard_map/ppermute | solution.py:220
  106.3 15.4 %collective-permute-start.19 = (f32[2,2,128,256]{3,2,0,1:T(8,128)S(1)}, f32[2,2,128,256]{3,2,0,1:T(8,128)S(1)}, u32[]{:S(2)}, u32[]{:S(2)}) collective-permute-start(f32[2,2,128,256]{3,2,0,1:T(8,128)S(1)} %get-tuple-element.40), channel_id=1, source_target_pairs={{0,4},{2,6},{4,0},{6,2},{8,12},{10,14},{12,8},{14,10},{1,5},{3,7},... | collective-permute-start | bytes 1572872 | tf_op jit(solution)/shard_map/ppermute | solution.py:220
  111.9 9.7 %collective-permute-start.12 = (f32[2,128,256]{1,2,0:T(8,128)S(1)}, f32[2,128,256]{1,2,0:T(8,128)S(1)}, u32[]{:S(2)}, u32[]{:S(2)}) collective-permute-start(f32[2,128,256]{1,2,0:T(8,128)S(1)} %fusion.45), channel_id=1, source_target_pairs={{0,4},{2,6},{4,0},{6,2},{8,12},{10,14},{12,8},{14,10},{1,5},{3,7},... | collective-permute-start | bytes 786440 | tf_op jit(solution)/shard_map/ppermute | solution.py:220
  112.0 11.4 %collective-permute-start.16 = (f32[2,2,128,256]{3,2,0,1:T(8,128)S(1)}, f32[2,2,128,256]{3,2,0,1:T(8,128)S(1)}, u32[]{:S(2)}, u32[]{:S(2)}) collective-permute-start(f32[2,2,128,256]{3,2,0,1:T(8,128)S(1)} %get-tuple-element.38), channel_id=1, source_target_pairs={{0,2},{2,0},{4,6},{6,4},{8,10},{10,8},{12,14},{14,12},{1,3},{3,1},... | collective-permute-start | bytes 1572872 | tf_op jit(solution)/shard_map/ppermute | solution.py:220
  121.6 9.6 %collective-permute-start.13 = (f32[2,128,256]{1,2,0:T(8,128)S(1)}, f32[2,128,256]{1,2,0:T(8,128)S(1)}, u32[]{:S(2)}, u32[]{:S(2)}) collective-permute-start(f32[2,128,256]{1,2,0:T(8,128)S(1)} %add.112), channel_id=1, source_target_pairs={{0,8},{2,10},{4,12},{6,14},{8,0},{10,2},{12,4},{14,6},{1,9},{3,11}... | collective-permute-start | bytes 786440 | tf_op jit(solution)/shard_map/ppermute | solution.py:220
  156.5 8.5 %collective-permute-start.20 = (f32[128,2048]{1,0:T(8,128)}, f32[128,2048]{1,0:T(8,128)S(1)}, u32[]{:S(2)}, u32[]{:S(2)}) collective-permute-start(f32[128,2048]{1,0:T(8,128)} %get-tuple-element.16), channel_id=1, source_target_pairs={{0,16},{16,0},{1,17},{17,1},{2,18},{18,2},{3,19},{19,3},{4,20},{20... | collective-permute-start | bytes 3145736 | tf_op jit(solution)/shard_map/ppermute | solution.py:220
  (3 other events, 19.0 us)
